TPU v7x, 512 devices: a whole 4x4x16 slice. The times are simulated.
512 devices in a mesh: sect: 8 (over x, y_hi), blk: 64 (over z, y_lo, core).
Axes of the slice: x: 4, y: 4 (y_hi: 2, y_lo: 2; y = y_hi * 2 + y_lo), z: 16, core: 2. Of those that a mesh axis runs over, the one named last changes fastest.
Arguments:
- bits: int32 [8, 1024], P('sect', 'blk'), may hold values from 0 to 1
- labels: int32 [128], replicated, may hold values from 0 to 127, each once
- left: bfloat16 [1024, 16384], P('blk')
- tensors: bfloat16 [8, 2, 128, 128, 128], P('sect', None, 'blk')
Outputs:
- prob: float32 [8, 1024], P('sect', 'blk')
- logprob: float32 [8, 1024], P('sect', 'blk')
Inputs may be any that keep to these rules, and one draw needn't show every extreme that they name: Every charge labels exactly one block.
All inputs are finite; a program needn't handle non-finite values.
Results may differ from a plain program's by a relative error of at most 0.0003.
Values may be sent and summed in bfloat16 or wider, within the bound.
No kernel may reach another device: no remote copies, remote signals or barrier semaphores. Data moves between devices by JAX's collectives and lax.ppermute only.
A program may use at most 64 MiB of HBM per device.

v0:
```python
import jax
import jax.numpy as jnp
from jax import lax
from jax.sharding import PartitionSpec as P


def passed_along(value, axis, steps):
    count = lax.axis_size(axis)
    first, last = (max(0, -steps), min(count, count - steps))
    return lax.ppermute(value, axis, [(source, source + steps) for source in range(first, last)])


def charge_order(labels, left, block):
    count_blocks = labels.shape[0]
    samples_here = left.shape[0]
    blocks = left.reshape(samples_here, count_blocks, block)
    index = jnp.arange(count_blocks, dtype=jnp.int32)
    pick = (labels[None, :] == index[:, None]).astype(jnp.bfloat16)
    ordered = jnp.einsum("ci,rik->rck", pick, blocks, preferred_element_type=jnp.float32)
    return ordered.astype(jnp.bfloat16)


def site_images(state, weights, block):
    count_rows = state.shape[0]
    blocks = state.reshape(count_rows, weights.shape[1], block)
    return jnp.einsum(
        "rck,bckl->brcl",
        blocks,
        weights,
        preferred_element_type=jnp.float32,
        precision=lax.Precision.HIGHEST,
    )


def run_sections(start_rows, site_bits, advance, count):
    segment = lax.axis_index("sect")
    segments = lax.axis_size("sect")
    mrows = start_rows.shape[1]

    def one_step(step, carry):
        state, total, prob_out, log_out = carry
        group = step - segment
        valid = (group >= 0) & (group < count)
        slot = jnp.clip(group, 0, count - 1)
        first = segment == 0
        start_now = lax.dynamic_index_in_dim(start_rows, slot, 0, keepdims=False)
        state = jnp.where(first, start_now, state)
        total = jnp.where(first, jnp.zeros_like(total), total)
        bit_rows = lax.dynamic_index_in_dim(site_bits, slot, 0, keepdims=False)
        prob, next_state = advance(state, bit_rows)
        total = total + jnp.log(prob)
        old_prob = lax.dynamic_index_in_dim(prob_out, slot, 0, keepdims=False)
        old_log = lax.dynamic_index_in_dim(log_out, slot, 0, keepdims=False)
        prob_out = lax.dynamic_update_index_in_dim(
            prob_out, jnp.where(valid, prob, old_prob), slot, 0
        )
        log_out = lax.dynamic_update_index_in_dim(
            log_out, jnp.where(valid, total, old_log), slot, 0
        )
        state, total = passed_along((next_state, total), "sect", 1)
        return (state, total, prob_out, log_out)

    empty = jnp.zeros((count, mrows), jnp.float32)
    init = (start_rows[0], jnp.zeros((mrows,), jnp.float32), empty, empty)
    result = lax.fori_loop(0, count + segments - 1, one_step, init)
    return (result[2], result[3])


def body(bits, labels, left, tensors):
    block = tensors.shape[-1]
    count_blocks = labels.shape[0]
    width = count_blocks * block
    rows = bits.shape[1]
    ordered = charge_order(labels, left, block)
    count = 1
    whole = lax.all_gather(tensors, "blk", axis=2, tiled=True)[0]

    def advance(state, bit_rows):
        image = site_images(state, whole, block)
        stay = image[0]
        raised = jnp.roll(image[1], 1, axis=1)
        norm_zero = jnp.sum(stay * stay, axis=(1, 2))
        norm_one = jnp.sum(raised * raised, axis=(1, 2))
        choose = bit_rows == 1
        chosen_norm = jnp.where(choose, norm_one, norm_zero)
        prob = chosen_norm / (norm_zero + norm_one)
        chosen = jnp.where(choose[:, None, None], raised, stay)
        scaled = chosen * lax.rsqrt(chosen_norm / width + 1e-06)[:, None, None]
        return (prob, scaled.reshape(state.shape[0], width))

    mrows = rows // count
    start_rows = ordered.astype(jnp.float32).reshape(count, mrows, width)
    site_bits = bits[0].reshape(count, mrows)
    prob_out, log_out = run_sections(start_rows, site_bits, advance, count)
    return (prob_out, log_out)


def solution(mesh):
    in_specs = (P("sect", "blk"), P(), P("blk", None), P("sect", None, "blk", None, None))
    out_specs = (P("sect", "blk"), P("sect", "blk"))
    return jax.shard_map(body, mesh=mesh, in_specs=in_specs, out_specs=out_specs, check_vma=False)
```

profile of v0, /device:TPU:4, one launch (start us, length us, event | category | flops | bytes accessed | tf_op | source)
XLA Modules:
  0.0 439.7 jit_solution(6856353192765204653)
XLA Ops:
  7.2 1.6 copy.15
  8.8 1.1 copy.22
  10.0 0.9 fusion.7
  10.9 0.6 copy.29
  11.5 1.2 reshape.91
  12.8 130.8 %all-gather.2.cloned.1.call-done = bf16[1,2,128,128,128]{4,3,1,0,2:T(8,128)(2,1)} async-done(((bf16[1,2,2,128,128]{4,3,1,0,2:T(8,128)(2,1)}), bf16[1,2,128,128,128]{4,3,1,0,2:T(8,128)(2,1)}) %all-gather.2.cloned.1.call-update) | async-done | bytes 8388624 | tf_op jit(solution)/shard_map/all_gather | solution.py:76
  143.6 288.7 %while.21 = (s32[]{:T(128)}, f32[16,16384]{1,0:T(8,128)S(1)}, f32[16]{0:T(128)S(1)}, f32[1,16]{1,0:T(1,128)S(1)}, f32[1,16]{1,0:T(1,128)S(1)}, /*index=5*/s32[1,...) while((s32[]{:T(128)}, f32[16,16384]{1,0:T(8,128)S(1)}, ...), condition=%wide.region_3.4_spmd.clone, body=%wide.region_0.3_spmd.clone.sunk | while | flops 807403776 | bytes 34604904 | solution.py:65
  143.6 1.3 fusion.21
  145.2 6.5 %convolution_bitcast_fusion.2 = f32[2,16,128,128]{3,1,0,2:T(8,128)S(1)} fusion(bf16[2,128,128,128]{3,2,0,1:T(8,128)(2,1)} %get-tuple-element.370, f32[16,128,128,1]{2,1,0,3:T(8,128)S(1)} %bitcast.81), kind=kOutput, calls=%fused_computation.clone.1 | convolution fusion | flops 805306368 | bytes 11534336 | tf_op jit(solution)/shard_map/while/body/eval_jaxpr/rck,bckl->brcl/dot_general | solution.py:26
  151.7 0.4 multiply_reduce_fusion.4
  152.8 0.6 fusion.23
  153.4 4.6 %collective-permute-start = (f32[16,16384]{1,0:T(8,128)S(1)}, f32[16,16384]{1,0:T(8,128)S(1)}, u32[]{:S(2)}, u32[]{:S(2)}) collective-permute-start(f32[16,16384]{1,0:T(8,128)S(1)} %fusion.23), channel_id=1, source_target_pairs={{0,64},{64,128},{128,192},{192,256},{256,320},{320,384},{384,448},... | collective-permute-start | bytes 3145736 | tf_op jit(solution)/shard_map/while/body/eval_jaxpr/ppermute | solution.py:10
  158.1 3.3 collective-permute-start.1
  161.4 21.6 %collective-permute-done.1 = f32[16]{0:T(128)S(1)} collective-permute-done((f32[16]{0:T(128)S(1)}, f32[16]{0:T(128)S(1)}, u32[]{:S(2)}, u32[]{:S(2)}) %collective-permute-start.1) | collective-permute-done | bytes 96 | tf_op jit(solution)/shard_map/while/body/eval_jaxpr/ppermute | solution.py:10
  183.1 1.3 fusion.21
  184.6 6.5 %convolution_bitcast_fusion.2 = f32[2,16,128,128]{3,1,0,2:T(8,128)S(1)} fusion(bf16[2,128,128,128]{3,2,0,1:T(8,128)(2,1)} %get-tuple-element.370, f32[16,128,128,1]{2,1,0,3:T(8,128)S(1)} %bitcast.81), kind=kOutput, calls=%fused_computation.clone.1 | convolution fusion | flops 805306368 | bytes 11534336 | tf_op jit(solution)/shard_map/while/body/eval_jaxpr/rck,bckl->brcl/dot_general | solution.py:26
  191.1 0.4 multiply_reduce_fusion.4
  192.2 0.6 fusion.23
  192.9 3.7 collective-permute-start
  196.6 4.2 collective-permute-start.1
  200.9 20.8 %collective-permute-done.1 = f32[16]{0:T(128)S(1)} collective-permute-done((f32[16]{0:T(128)S(1)}, f32[16]{0:T(128)S(1)}, u32[]{:S(2)}, u32[]{:S(2)}) %collective-permute-start.1) | collective-permute-done | bytes 96 | tf_op jit(solution)/shard_map/while/body/eval_jaxpr/ppermute | solution.py:10
  221.7 1.3 fusion.21
  223.2 6.5 %convolution_bitcast_fusion.2 = f32[2,16,128,128]{3,1,0,2:T(8,128)S(1)} fusion(bf16[2,128,128,128]{3,2,0,1:T(8,128)(2,1)} %get-tuple-element.370, f32[16,128,128,1]{2,1,0,3:T(8,128)S(1)} %bitcast.81), kind=kOutput, calls=%fused_computation.clone.1 | convolution fusion | flops 805306368 | bytes 11534336 | tf_op jit(solution)/shard_map/while/body/eval_jaxpr/rck,bckl->brcl/dot_general | solution.py:26
  229.7 0.4 multiply_reduce_fusion.4
  230.8 0.6 fusion.23
  231.4 2.8 collective-permute-start
  234.3 5.1 %collective-permute-start.1 = (f32[16]{0:T(128)S(1)}, f32[16]{0:T(128)S(1)}, u32[]{:S(2)}, u32[]{:S(2)}) collective-permute-start(f32[16]{0:T(128)S(1)} %get-tuple-element.336), channel_id=1, source_target_pairs={{0,64},{64,128},{128,192},{192,256},{256,320},{320,384},{384,448},... | collective-permute-start | bytes 200 | tf_op jit(solution)/shard_map/while/body/eval_jaxpr/ppermute | solution.py:10
  239.5 19.8 %collective-permute-done.1 = f32[16]{0:T(128)S(1)} collective-permute-done((f32[16]{0:T(128)S(1)}, f32[16]{0:T(128)S(1)}, u32[]{:S(2)}, u32[]{:S(2)}) %collective-permute-start.1) | collective-permute-done | bytes 96 | tf_op jit(solution)/shard_map/while/body/eval_jaxpr/ppermute | solution.py:10
  259.2 1.3 fusion.21
  260.8 6.5 %convolution_bitcast_fusion.2 = f32[2,16,128,128]{3,1,0,2:T(8,128)S(1)} fusion(bf16[2,128,128,128]{3,2,0,1:T(8,128)(2,1)} %get-tuple-element.370, f32[16,128,128,1]{2,1,0,3:T(8,128)S(1)} %bitcast.81), kind=kOutput, calls=%fused_computation.clone.1 | convolution fusion | flops 805306368 | bytes 11534336 | tf_op jit(solution)/shard_map/while/body/eval_jaxpr/rck,bckl->brcl/dot_general | solution.py:26
  267.3 0.4 multiply_reduce_fusion.4
  268.4 0.6 fusion.23
  269.0 1.9 collective-permute-start
  271.0 6.0 %collective-permute-start.1 = (f32[16]{0:T(128)S(1)}, f32[16]{0:T(128)S(1)}, u32[]{:S(2)}, u32[]{:S(2)}) collective-permute-start(f32[16]{0:T(128)S(1)} %get-tuple-element.336), channel_id=1, source_target_pairs={{0,64},{64,128},{128,192},{192,256},{256,320},{320,384},{384,448},... | collective-permute-start | bytes 200 | tf_op jit(solution)/shard_map/while/body/eval_jaxpr/ppermute | solution.py:10
  277.1 18.8 %collective-permute-done.1 = f32[16]{0:T(128)S(1)} collective-permute-done((f32[16]{0:T(128)S(1)}, f32[16]{0:T(128)S(1)}, u32[]{:S(2)}, u32[]{:S(2)}) %collective-permute-start.1) | collective-permute-done | bytes 96 | tf_op jit(solution)/shard_map/while/body/eval_jaxpr/ppermute | solution.py:10
  295.8 1.3 fusion.21
  297.4 6.5 %convolution_bitcast_fusion.2 = f32[2,16,128,128]{3,1,0,2:T(8,128)S(1)} fusion(bf16[2,128,128,128]{3,2,0,1:T(8,128)(2,1)} %get-tuple-element.370, f32[16,128,128,1]{2,1,0,3:T(8,128)S(1)} %bitcast.81), kind=kOutput, calls=%fused_computation.clone.1 | convolution fusion | flops 805306368 | bytes 11534336 | tf_op jit(solution)/shard_map/while/body/eval_jaxpr/rck,bckl->brcl/dot_general | solution.py:26
  303.9 0.4 multiply_reduce_fusion.4
  305.0 0.6 fusion.23
  305.6 1.9 collective-permute-start
  307.6 6.1 %collective-permute-start.1 = (f32[16]{0:T(128)S(1)}, f32[16]{0:T(128)S(1)}, u32[]{:S(2)}, u32[]{:S(2)}) collective-permute-start(f32[16]{0:T(128)S(1)} %get-tuple-element.336), channel_id=1, source_target_pairs={{0,64},{64,128},{128,192},{192,256},{256,320},{320,384},{384,448},... | collective-permute-start | bytes 200 | tf_op jit(solution)/shard_map/while/body/eval_jaxpr/ppermute | solution.py:10
  313.6 17.8 %collective-permute-done.1 = f32[16]{0:T(128)S(1)} collective-permute-done((f32[16]{0:T(128)S(1)}, f32[16]{0:T(128)S(1)}, u32[]{:S(2)}, u32[]{:S(2)}) %collective-permute-start.1) | collective-permute-done | bytes 96 | tf_op jit(solution)/shard_map/while/body/eval_jaxpr/ppermute | solution.py:10
  331.4 1.3 fusion.21
  333.0 6.5 %convolution_bitcast_fusion.2 = f32[2,16,128,128]{3,1,0,2:T(8,128)S(1)} fusion(bf16[2,128,128,128]{3,2,0,1:T(8,128)(2,1)} %get-tuple-element.370, f32[16,128,128,1]{2,1,0,3:T(8,128)S(1)} %bitcast.81), kind=kOutput, calls=%fused_computation.clone.1 | convolution fusion | flops 805306368 | bytes 11534336 | tf_op jit(solution)/shard_map/while/body/eval_jaxpr/rck,bckl->brcl/dot_general | solution.py:26
  339.5 0.4 multiply_reduce_fusion.4
  340.6 0.6 fusion.23
  341.2 1.9 collective-permute-start
  343.2 6.1 %collective-permute-start.1 = (f32[16]{0:T(128)S(1)}, f32[16]{0:T(128)S(1)}, u32[]{:S(2)}, u32[]{:S(2)}) collective-permute-start(f32[16]{0:T(128)S(1)} %get-tuple-element.336), channel_id=1, source_target_pairs={{0,64},{64,128},{128,192},{192,256},{256,320},{320,384},{384,448},... | collective-permute-start | bytes 200 | tf_op jit(solution)/shard_map/while/body/eval_jaxpr/ppermute | solution.py:10
  349.3 16.8 %collective-permute-done.1 = f32[16]{0:T(128)S(1)} collective-permute-done((f32[16]{0:T(128)S(1)}, f32[16]{0:T(128)S(1)}, u32[]{:S(2)}, u32[]{:S(2)}) %collective-permute-start.1) | collective-permute-done | bytes 96 | tf_op jit(solution)/shard_map/while/body/eval_jaxpr/ppermute | solution.py:10
  366.1 1.3 fusion.21
  367.6 6.5 %convolution_bitcast_fusion.2 = f32[2,16,128,128]{3,1,0,2:T(8,128)S(1)} fusion(bf16[2,128,128,128]{3,2,0,1:T(8,128)(2,1)} %get-tuple-element.370, f32[16,128,128,1]{2,1,0,3:T(8,128)S(1)} %bitcast.81), kind=kOutput, calls=%fused_computation.clone.1 | convolution fusion | flops 805306368 | bytes 11534336 | tf_op jit(solution)/shard_map/while/body/eval_jaxpr/rck,bckl->brcl/dot_general | solution.py:26
  374.1 0.4 multiply_reduce_fusion.4
  375.2 0.6 fusion.23
  375.9 1.9 collective-permute-start
  377.8 6.1 %collective-permute-start.1 = (f32[16]{0:T(128)S(1)}, f32[16]{0:T(128)S(1)}, u32[]{:S(2)}, u32[]{:S(2)}) collective-permute-start(f32[16]{0:T(128)S(1)} %get-tuple-element.336), channel_id=1, source_target_pairs={{0,64},{64,128},{128,192},{192,256},{256,320},{320,384},{384,448},... | collective-permute-start | bytes 200 | tf_op jit(solution)/shard_map/while/body/eval_jaxpr/ppermute | solution.py:10
  383.9 15.8 %collective-permute-done.1 = f32[16]{0:T(128)S(1)} collective-permute-done((f32[16]{0:T(128)S(1)}, f32[16]{0:T(128)S(1)}, u32[]{:S(2)}, u32[]{:S(2)}) %collective-permute-start.1) | collective-permute-done | bytes 96 | tf_op jit(solution)/shard_map/while/body/eval_jaxpr/ppermute | solution.py:10
  399.7 1.3 fusion.21
  401.2 6.5 %convolution_bitcast_fusion.2 = f32[2,16,128,128]{3,1,0,2:T(8,128)S(1)} fusion(bf16[2,128,128,128]{3,2,0,1:T(8,128)(2,1)} %get-tuple-element.370, f32[16,128,128,1]{2,1,0,3:T(8,128)S(1)} %bitcast.81), kind=kOutput, calls=%fused_computation.clone.1 | convolution fusion | flops 805306368 | bytes 11534336 | tf_op jit(solution)/shard_map/while/body/eval_jaxpr/rck,bckl->brcl/dot_general | solution.py:26
  407.7 0.4 multiply_reduce_fusion.4
  408.8 0.6 fusion.23
  409.5 1.9 collective-permute-start
  411.4 6.1 %collective-permute-start.1 = (f32[16]{0:T(128)S(1)}, f32[16]{0:T(128)S(1)}, u32[]{:S(2)}, u32[]{:S(2)}) collective-permute-start(f32[16]{0:T(128)S(1)} %get-tuple-element.336), channel_id=1, source_target_pairs={{0,64},{64,128},{128,192},{192,256},{256,320},{320,384},{384,448},... | collective-permute-start | bytes 200 | tf_op jit(solution)/shard_map/while/body/eval_jaxpr/ppermute | solution.py:10
  417.5 14.8 %collective-permute-done.1 = f32[16]{0:T(128)S(1)} collective-permute-done((f32[16]{0:T(128)S(1)}, f32[16]{0:T(128)S(1)}, u32[]{:S(2)}, u32[]{:S(2)}) %collective-permute-start.1) | collective-permute-done | bytes 96 | tf_op jit(solution)/shard_map/while/body/eval_jaxpr/ppermute | solution.py:10
  432.3 0.5 copy-done.1
  (96 shorter events, 7.6 us)
Async XLA Ops:
  7.2 136.5 %all-gather.2.cloned.1.call-start = ((), (), s32[]{:S(2)}) async-start(), calls=%async_computation | async-start | bytes 8519680 | tf_op jit(solution)/shard_map/all_gather | solution.py:76
  151.6 0.8 copy-start
  153.4 29.7 %collective-permute-start = (f32[16,16384]{1,0:T(8,128)S(1)}, f32[16,16384]{1,0:T(8,128)S(1)}, u32[]{:S(2)}, u32[]{:S(2)}) collective-permute-start(f32[16,16384]{1,0:T(8,128)S(1)} %fusion.23), channel_id=1, source_target_pairs={{0,64},{64,128},{128,192},{192,256},{256,320},{320,384},{384,448},... | collective-permute-start | bytes 3145736 | tf_op jit(solution)/shard_map/while/body/eval_jaxpr/ppermute | solution.py:10
  158.1 25.0 %collective-permute-start.1 = (f32[16]{0:T(128)S(1)}, f32[16]{0:T(128)S(1)}, u32[]{:S(2)}, u32[]{:S(2)}) collective-permute-start(f32[16]{0:T(128)S(1)} %get-tuple-element.336), channel_id=1, source_target_pairs={{0,64},{64,128},{128,192},{192,256},{256,320},{320,384},{384,448},... | collective-permute-start | bytes 200 | tf_op jit(solution)/shard_map/while/body/eval_jaxpr/ppermute | solution.py:10
  191.1 0.8 copy-start
  192.9 28.8 %collective-permute-start = (f32[16,16384]{1,0:T(8,128)S(1)}, f32[16,16384]{1,0:T(8,128)S(1)}, u32[]{:S(2)}, u32[]{:S(2)}) collective-permute-start(f32[16,16384]{1,0:T(8,128)S(1)} %fusion.23), channel_id=1, source_target_pairs={{0,64},{64,128},{128,192},{192,256},{256,320},{320,384},{384,448},... | collective-permute-start | bytes 3145736 | tf_op jit(solution)/shard_map/while/body/eval_jaxpr/ppermute | solution.py:10
  196.6 25.0 %collective-permute-start.1 = (f32[16]{0:T(128)S(1)}, f32[16]{0:T(128)S(1)}, u32[]{:S(2)}, u32[]{:S(2)}) collective-permute-start(f32[16]{0:T(128)S(1)} %get-tuple-element.336), channel_id=1, source_target_pairs={{0,64},{64,128},{128,192},{192,256},{256,320},{320,384},{384,448},... | collective-permute-start | bytes 200 | tf_op jit(solution)/shard_map/while/body/eval_jaxpr/ppermute | solution.py:10
  229.7 0.8 copy-start
  231.4 27.8 %collective-permute-start = (f32[16,16384]{1,0:T(8,128)S(1)}, f32[16,16384]{1,0:T(8,128)S(1)}, u32[]{:S(2)}, u32[]{:S(2)}) collective-permute-start(f32[16,16384]{1,0:T(8,128)S(1)} %fusion.23), channel_id=1, source_target_pairs={{0,64},{64,128},{128,192},{192,256},{256,320},{320,384},{384,448},... | collective-permute-start | bytes 3145736 | tf_op jit(solution)/shard_map/while/body/eval_jaxpr/ppermute | solution.py:10
  234.3 24.9 %collective-permute-start.1 = (f32[16]{0:T(128)S(1)}, f32[16]{0:T(128)S(1)}, u32[]{:S(2)}, u32[]{:S(2)}) collective-permute-start(f32[16]{0:T(128)S(1)} %get-tuple-element.336), channel_id=1, source_target_pairs={{0,64},{64,128},{128,192},{192,256},{256,320},{320,384},{384,448},... | collective-permute-start | bytes 200 | tf_op jit(solution)/shard_map/while/body/eval_jaxpr/ppermute | solution.py:10
  267.3 0.8 copy-start
  269.0 26.8 %collective-permute-start = (f32[16,16384]{1,0:T(8,128)S(1)}, f32[16,16384]{1,0:T(8,128)S(1)}, u32[]{:S(2)}, u32[]{:S(2)}) collective-permute-start(f32[16,16384]{1,0:T(8,128)S(1)} %fusion.23), channel_id=1, source_target_pairs={{0,64},{64,128},{128,192},{192,256},{256,320},{320,384},{384,448},... | collective-permute-start | bytes 3145736 | tf_op jit(solution)/shard_map/while/body/eval_jaxpr/ppermute | solution.py:10
  271.0 24.9 %collective-permute-start.1 = (f32[16]{0:T(128)S(1)}, f32[16]{0:T(128)S(1)}, u32[]{:S(2)}, u32[]{:S(2)}) collective-permute-start(f32[16]{0:T(128)S(1)} %get-tuple-element.336), channel_id=1, source_target_pairs={{0,64},{64,128},{128,192},{192,256},{256,320},{320,384},{384,448},... | collective-permute-start | bytes 200 | tf_op jit(solution)/shard_map/while/body/eval_jaxpr/ppermute | solution.py:10
  303.9 0.8 copy-start
  305.6 25.8 %collective-permute-start = (f32[16,16384]{1,0:T(8,128)S(1)}, f32[16,16384]{1,0:T(8,128)S(1)}, u32[]{:S(2)}, u32[]{:S(2)}) collective-permute-start(f32[16,16384]{1,0:T(8,128)S(1)} %fusion.23), channel_id=1, source_target_pairs={{0,64},{64,128},{128,192},{192,256},{256,320},{320,384},{384,448},... | collective-permute-start | bytes 3145736 | tf_op jit(solution)/shard_map/while/body/eval_jaxpr/ppermute | solution.py:10
  307.6 23.9 %collective-permute-start.1 = (f32[16]{0:T(128)S(1)}, f32[16]{0:T(128)S(1)}, u32[]{:S(2)}, u32[]{:S(2)}) collective-permute-start(f32[16]{0:T(128)S(1)} %get-tuple-element.336), channel_id=1, source_target_pairs={{0,64},{64,128},{128,192},{192,256},{256,320},{320,384},{384,448},... | collective-permute-start | bytes 200 | tf_op jit(solution)/shard_map/while/body/eval_jaxpr/ppermute | solution.py:10
  339.5 0.8 copy-start
  341.2 24.8 %collective-permute-start = (f32[16,16384]{1,0:T(8,128)S(1)}, f32[16,16384]{1,0:T(8,128)S(1)}, u32[]{:S(2)}, u32[]{:S(2)}) collective-permute-start(f32[16,16384]{1,0:T(8,128)S(1)} %fusion.23), channel_id=1, source_target_pairs={{0,64},{64,128},{128,192},{192,256},{256,320},{320,384},{384,448},... | collective-permute-start | bytes 3145736 | tf_op jit(solution)/shard_map/while/body/eval_jaxpr/ppermute | solution.py:10
  343.2 22.9 %collective-permute-start.1 = (f32[16]{0:T(128)S(1)}, f32[16]{0:T(128)S(1)}, u32[]{:S(2)}, u32[]{:S(2)}) collective-permute-start(f32[16]{0:T(128)S(1)} %get-tuple-element.336), channel_id=1, source_target_pairs={{0,64},{64,128},{128,192},{192,256},{256,320},{320,384},{384,448},... | collective-permute-start | bytes 200 | tf_op jit(solution)/shard_map/while/body/eval_jaxpr/ppermute | solution.py:10
  374.1 0.8 copy-start
  375.9 23.8 %collective-permute-start = (f32[16,16384]{1,0:T(8,128)S(1)}, f32[16,16384]{1,0:T(8,128)S(1)}, u32[]{:S(2)}, u32[]{:S(2)}) collective-permute-start(f32[16,16384]{1,0:T(8,128)S(1)} %fusion.23), channel_id=1, source_target_pairs={{0,64},{64,128},{128,192},{192,256},{256,320},{320,384},{384,448},... | collective-permute-start | bytes 3145736 | tf_op jit(solution)/shard_map/while/body/eval_jaxpr/ppermute | solution.py:10
  377.8 21.9 %collective-permute-start.1 = (f32[16]{0:T(128)S(1)}, f32[16]{0:T(128)S(1)}, u32[]{:S(2)}, u32[]{:S(2)}) collective-permute-start(f32[16]{0:T(128)S(1)} %get-tuple-element.336), channel_id=1, source_target_pairs={{0,64},{64,128},{128,192},{192,256},{256,320},{320,384},{384,448},... | collective-permute-start | bytes 200 | tf_op jit(solution)/shard_map/while/body/eval_jaxpr/ppermute | solution.py:10
  407.7 0.8 copy-start
  409.5 22.8 %collective-permute-start = (f32[16,16384]{1,0:T(8,128)S(1)}, f32[16,16384]{1,0:T(8,128)S(1)}, u32[]{:S(2)}, u32[]{:S(2)}) collective-permute-start(f32[16,16384]{1,0:T(8,128)S(1)} %fusion.23), channel_id=1, source_target_pairs={{0,64},{64,128},{128,192},{192,256},{256,320},{320,384},{384,448},... | collective-permute-start | bytes 3145736 | tf_op jit(solution)/shard_map/while/body/eval_jaxpr/ppermute | solution.py:10
  411.4 20.9 %collective-permute-start.1 = (f32[16]{0:T(128)S(1)}, f32[16]{0:T(128)S(1)}, u32[]{:S(2)}, u32[]{:S(2)}) collective-permute-start(f32[16]{0:T(128)S(1)} %get-tuple-element.336), channel_id=1, source_target_pairs={{0,64},{64,128},{128,192},{192,256},{256,320},{320,384},{384,448},... | collective-permute-start | bytes 200 | tf_op jit(solution)/shard_map/while/body/eval_jaxpr/ppermute | solution.py:10
  432.3 0.5 copy-start.1
  432.3 0.5 copy-start.2
Sparse Core Ops, SparseCore 0:
  10.1 133.4 all-gather.1
where the time goes:
time: 441 us; the launch traced here: 440 us
  waiting for transfers between devices  277 us (63%)
  starting transfers between devices  63.9 us (14%)
  matrix products  52.6 us (12%)
  other arithmetic  21.2 us (5%)
  between operations  14.1 us (3%)
  local copies, waits for them, and re-layouts  10 us (2%)
    ppermute x16, waiting for transfers between devices, passed_along(): lax.ppermute(value, axis, [(source, source + steps) for source in range(f...  146 us
    all_gather x1, waiting for transfers between devices, body(): whole = lax.all_gather(tensors, 'blk', axis=2, tiled=True)[0]  131 us
    ppermute x16, starting transfers between devices, passed_along(): lax.ppermute(value, axis, [(source, source + steps) for source in range(f...  63.8 us
    dot_general x8, matrix products, site_images(): jnp.einsum('rck,bckl->brcl', blocks, weights, preferred_element_type=jnp....  51.7 us
    while x8, other arithmetic  10.6 us
  transfers between devices with their start and end apart: 17, of which 9 were waited for; matrix products, arithmetic and copies ran while one was open for 1% of the time, Pallas kernels for 0%

commit v1 on v0

v1 whole, which is shorter than its diff:
```python
import jax
import jax.numpy as jnp
from jax import lax
from jax.sharding import PartitionSpec as P


def charge_blocks(labels, rows, block):
    count_blocks = labels.shape[0]
    blocks = rows.reshape(rows.shape[0], count_blocks, block)
    index = jnp.arange(count_blocks, dtype=jnp.int32)
    pick = (labels[None, :] == index[:, None]).astype(blocks.dtype)
    ordered = jnp.einsum("ci,rik->rck", pick, blocks, preferred_element_type=jnp.float32)
    return ordered.astype(blocks.dtype)


def body(bits, labels, left, tensors):
    sect = lax.axis_index("sect")
    blk = lax.axis_index("blk")
    n_sect = lax.axis_size("sect")
    n_blk = lax.axis_size("blk")
    block = tensors.shape[-1]
    count_blocks = labels.shape[0]
    width = count_blocks * block
    sites = bits.shape[0] * n_sect
    per_blk = left.shape[0]
    pick_rows = per_blk // n_sect
    local_blocks = tensors.shape[2]

    weights = lax.all_gather(tensors[0], "sect", axis=0, tiled=False)

    all_bits = lax.all_gather(bits, ("sect", "blk"), axis=0, tiled=False)
    all_bits = all_bits.reshape(n_sect, n_blk, bits.shape[0], per_blk)[:, :, 0, :]
    all_bits = all_bits.reshape(sites, n_blk, n_sect, pick_rows)
    group_bits = lax.dynamic_index_in_dim(all_bits, sect, 2, keepdims=False)
    group_bits = group_bits.reshape(sites, n_blk * pick_rows)

    mine = lax.dynamic_slice_in_dim(left, sect * pick_rows, pick_rows, 0)
    ordered = charge_blocks(labels, mine, block)
    ordered = ordered.reshape(pick_rows, n_blk, local_blocks, block)
    spread = lax.all_to_all(ordered, "blk", 1, 1, tiled=False)
    rows = n_blk * pick_rows
    state = jnp.transpose(spread, (1, 0, 2, 3)).reshape(rows, local_blocks, block)
    state = state.astype(jnp.float32)

    total = jnp.zeros((rows,), jnp.float32)
    shift = [(j, (j + 1) % n_blk) for j in range(n_blk)]
    probs = []
    logs = []
    for site in range(sites):
        image = jnp.einsum(
            "rck,bckl->brcl",
            state,
            weights[site].astype(jnp.float32),
            preferred_element_type=jnp.float32,
            precision=lax.Precision.HIGHEST,
        )
        stay = image[0]
        rise = image[1]
        part = jnp.stack([jnp.sum(stay * stay, axis=(1, 2)), jnp.sum(rise * rise, axis=(1, 2))])
        norms = lax.psum(part, "blk")
        came = lax.ppermute(rise[:, local_blocks - 1], "blk", shift)
        raised = jnp.concatenate([came[:, None], rise[:, : local_blocks - 1]], axis=1)
        norm_zero = norms[0]
        norm_one = norms[1]
        choose = group_bits[site] == 1
        chosen_norm = jnp.where(choose, norm_one, norm_zero)
        prob = chosen_norm / (norm_zero + norm_one)
        total = total + jnp.log(prob)
        probs.append(prob)
        logs.append(total)
        if site + 1 < sites:
            chosen = jnp.where(choose[:, None, None], raised, stay)
            state = chosen * lax.rsqrt(chosen_norm / width + 1e-06)[:, None, None]

    result = jnp.stack([jnp.stack(probs), jnp.stack(logs)], axis=1)
    result = result.reshape(sites, 2, n_blk, pick_rows)
    result = lax.dynamic_index_in_dim(result, blk, 2, keepdims=False)
    result = result.reshape(n_sect, bits.shape[0], 2, pick_rows)
    back = lax.all_to_all(result, "sect", 0, 0, tiled=False)
    back = back[:, 0]
    out = jnp.transpose(back, (1, 0, 2)).reshape(2, bits.shape[0], n_sect * pick_rows)
    return (out[0], out[1])


def solution(mesh):
    in_specs = (P("sect", "blk"), P(), P("blk", None), P("sect", None, "blk", None, None))
    out_specs = (P("sect", "blk"), P("sect", "blk"))
    return jax.shard_map(body, mesh=mesh, in_specs=in_specs, out_specs=out_specs, check_vma=False)
```

time: 441 us -> 1630 us (3.70)
  the two profiles are of different devices: /device:TPU:4 before, /device:TPU:2 now
where the time goes in v1:
time: 1630 us
  blocking collectives  1530 us (94%)
  waiting for transfers between devices  40 us (2%)
  starting transfers between devices  30.6 us (2%)
    psum x8, blocking collectives, body(): norms = lax.psum(part, 'blk')  838 us
    all_gather x1, blocking collectives, body(): all_bits = lax.all_gather(bits, ('sect', 'blk'), axis=0, tiled=False)  601 us
    all_to_all x1, blocking collectives, body(): back = lax.all_to_all(result, 'sect', 0, 0, tiled=False)  88.8 us
    ppermute x7, waiting for transfers between devices, body(): came = lax.ppermute(rise[:, local_blocks - 1], 'blk', shift)  39.3 us
  transfers between devices with their start and end apart: 9, of which 7 were waited for; matrix products, arithmetic and copies ran while one was open for 0% of the time, Pallas kernels for 0%

profile of v1, /device:TPU:2, one launch (start us, length us, event | category | flops | bytes accessed | tf_op | source)
XLA Modules:
  0.0 1625.8 jit_solution(1893576394552230806)
XLA Ops:
  7.2 0.7 all-gather.4.cloned.1.call-update
  7.9 0.3 copy-done
  8.3 0.6 copy-done.1
  8.9 0.2 convolution_convert_fusion
  9.0 0.7 copy.162
  9.7 17.1 %all-to-all-start = ((bf16[2,64,2,128]{3,2,0,1:T(2,128)(2,1)}), bf16[2,64,2,128]{3,2,0,1:T(2,128)(2,1)S(1)}, u32[]{:S(2)}, u32[]{:S(2)}) async-start(bf16[2,64,2,128]{3,2,0,1:T(2,128)(2,1)} %copy.162), calls=%async_computation | async-start | bytes 131072 | tf_op jit(solution)/shard_map/all_to_all | solution.py:40
  26.8 0.6 copy-done.2
  27.5 600.8 %all-gather.1 = s32[512,1,16]{2,1,0:T(1,128)S(1)} all-gather(s32[1,1,16]{2,1,0:T(1,128)S(1)} %bitcast.420), channel_id=2, replica_groups=mesh['sect'=8,'blk'=64] {'sect','blk'}, dimensions={0}, use_global_device_ids=true | all-gather | bytes 32832 | tf_op jit(solution)/shard_map/all_gather | solution.py:31
  628.7 0.1 eq.230
  628.8 0.1 eq.224
  629.1 0.2 eq.233
  629.2 0.1 eq.229
  629.5 0.2 eq.236
  629.7 0.1 eq.232
  629.9 0.2 eq.239
  630.1 0.1 eq.235
  630.3 0.2 eq.242
  630.5 0.1 eq.238
  630.8 0.2 eq.245
  630.9 0.1 eq.241
  631.2 0.2 eq.248
  631.3 0.1 eq.244
  631.6 0.1 eq.247
  631.8 1.4 fusion.92
  633.3 0.2 convolution_bitcast_fusion.7
  633.6 105.0 %psum.56 = f32[2,128]{1,0:T(2,128)S(1)} all-reduce(f32[2,128]{1,0:T(2,128)S(1)} %pad_maximum_fusion), channel_id=1, replica_groups=mesh['sect'=8,'blk'=64] {'blk'}, use_global_device_ids=true, to_apply=%region_2.3 | all-reduce | flops 256 | bytes 2048 | tf_op jit(solution)/shard_map/psum | solution.py:60
  738.6 1.9 collective-permute-start
  740.7 0.1 copy.251
  740.8 0.1 copy.248
  741.0 0.1 copy.245
  741.1 0.1 copy.242
  741.3 0.1 copy.239
  741.4 0.1 copy.236
  741.5 4.8 collective-permute-done
  746.3 0.3 convolution_bitcast_fusion.6
  746.7 104.7 %psum.57 = f32[2,128]{1,0:T(2,128)S(1)} all-reduce(f32[2,128]{1,0:T(2,128)S(1)} %pad_maximum_fusion.1), channel_id=1, replica_groups=mesh['sect'=8,'blk'=64] {'blk'}, use_global_device_ids=true, to_apply=%region_5.6 | all-reduce | flops 256 | bytes 2048 | tf_op jit(solution)/shard_map/psum | solution.py:60
  851.4 1.9 collective-permute-start.1
  853.3 5.8 collective-permute-done.1
  859.1 0.3 convolution_bitcast_fusion.5
  859.5 104.7 %psum.58 = f32[2,128]{1,0:T(2,128)S(1)} all-reduce(f32[2,128]{1,0:T(2,128)S(1)} %pad_maximum_fusion.2), channel_id=1, replica_groups=mesh['sect'=8,'blk'=64] {'blk'}, use_global_device_ids=true, to_apply=%region_8.9 | all-reduce | flops 256 | bytes 2048 | tf_op jit(solution)/shard_map/psum | solution.py:60
  964.2 1.9 collective-permute-start.2
  966.1 5.8 collective-permute-done.2
  971.8 0.3 convolution_bitcast_fusion.4
  972.2 104.7 %psum.59 = f32[2,128]{1,0:T(2,128)S(1)} all-reduce(f32[2,128]{1,0:T(2,128)S(1)} %pad_maximum_fusion.3), channel_id=1, replica_groups=mesh['sect'=8,'blk'=64] {'blk'}, use_global_device_ids=true, to_apply=%region_11.12 | all-reduce | flops 256 | bytes 2048 | tf_op jit(solution)/shard_map/psum | solution.py:60
  1076.9 1.9 collective-permute-start.3
  1078.9 5.8 collective-permute-done.3
  1084.6 0.3 convolution_bitcast_fusion.3
  1085.0 104.7 %psum.60 = f32[2,128]{1,0:T(2,128)S(1)} all-reduce(f32[2,128]{1,0:T(2,128)S(1)} %pad_maximum_fusion.4), channel_id=1, replica_groups=mesh['sect'=8,'blk'=64] {'blk'}, use_global_device_ids=true, to_apply=%region_14.15 | all-reduce | flops 256 | bytes 2048 | tf_op jit(solution)/shard_map/psum | solution.py:60
  1189.7 1.9 collective-permute-start.4
  1191.6 5.8 collective-permute-done.4
  1197.4 0.3 convolution_bitcast_fusion.2
  1197.8 104.7 %psum.61 = f32[2,128]{1,0:T(2,128)S(1)} all-reduce(f32[2,128]{1,0:T(2,128)S(1)} %pad_maximum_fusion.5), channel_id=1, replica_groups=mesh['sect'=8,'blk'=64] {'blk'}, use_global_device_ids=true, to_apply=%region_17.18 | all-reduce | flops 256 | bytes 2048 | tf_op jit(solution)/shard_map/psum | solution.py:60
  1302.5 1.9 collective-permute-start.5
  1304.4 5.8 collective-permute-done.5
  1310.1 0.3 convolution_bitcast_fusion.1
  1310.5 104.7 %psum.62 = f32[2,128]{1,0:T(2,128)S(1)} all-reduce(f32[2,128]{1,0:T(2,128)S(1)} %pad_maximum_fusion.6), channel_id=1, replica_groups=mesh['sect'=8,'blk'=64] {'blk'}, use_global_device_ids=true, to_apply=%region_20.21 | all-reduce | flops 256 | bytes 2048 | tf_op jit(solution)/shard_map/psum | solution.py:60
  1415.2 1.9 collective-permute-start.6
  1417.2 5.8 collective-permute-done.6
  1422.9 0.3 convolution_bitcast_fusion
  1423.3 104.7 %psum.63 = f32[2,128]{1,0:T(2,128)S(1)} all-reduce(f32[2,128]{1,0:T(2,128)S(1)} %pad_maximum_fusion.7), channel_id=1, replica_groups=mesh['sect'=8,'blk'=64] {'blk'}, use_global_device_ids=true, to_apply=%region_23.24 | all-reduce | flops 256 | bytes 2048 | tf_op jit(solution)/shard_map/psum | solution.py:60
  1528.5 0.2 copy.230
  1528.7 88.8 %all_to_all.10 = f32[8,1,2,2]{3,2,1,0:T(2,128)S(1)} all-to-all(f32[8,1,2,2]{3,2,1,0:T(2,128)S(1)} %bitcast.394), channel_id=1, replica_groups=mesh['sect'=8,'blk'=64] {'sect'}, dimensions={0} | all-to-all | bytes 256 | tf_op jit(solution)/shard_map/all_to_all | solution.py:79
  1617.7 0.6 squeeze.199
  1618.4 0.6 squeeze.198
  (79 shorter events, 3.1 us)
Async XLA Ops:
  7.2 1.0 copy-start
  7.2 624.7 %all-gather.4.cloned.1.call-start = ((), (), s32[]{:S(2)}) async-start(), calls=%async_computation.2 | async-start | bytes 1179648 | tf_op jit(solution)/shard_map/all_gather | solution.py:29
  8.2 0.7 copy-start.1
  9.7 622.1 %all-to-all-start = ((bf16[2,64,2,128]{3,2,0,1:T(2,128)(2,1)}), bf16[2,64,2,128]{3,2,0,1:T(2,128)(2,1)S(1)}, u32[]{:S(2)}, u32[]{:S(2)}) async-start(bf16[2,64,2,128]{3,2,0,1:T(2,128)(2,1)} %copy.162), calls=%async_computation | async-start | bytes 131072 | tf_op jit(solution)/shard_map/all_to_all | solution.py:40
  26.8 0.7 copy-start.2
  738.6 7.7 collective-permute-start
  851.4 7.7 collective-permute-start.1
  964.2 7.7 collective-permute-start.2
  1076.9 7.7 collective-permute-start.3
  1189.7 7.7 collective-permute-start.4
  1302.5 7.7 collective-permute-start.5
  1415.2 7.7 collective-permute-start.6
Sparse Core Ops, SparseCore 0:
  11.2 67.0 all-gather.3

commit v2 on v0

v2 whole, which is shorter than its diff:
```python
import jax
import jax.numpy as jnp
from jax import lax
from jax.sharding import PartitionSpec as P


def charge_order(labels, left, block):
    count_blocks = labels.shape[0]
    samples_here = left.shape[0]
    blocks = left.reshape(samples_here, count_blocks, block)
    index = jnp.arange(count_blocks, dtype=jnp.int32)
    pick = (labels[None, :] == index[:, None]).astype(jnp.bfloat16)
    ordered = jnp.einsum("ci,rik->rck", pick, blocks, preferred_element_type=jnp.float32)
    return ordered.astype(jnp.bfloat16)


def body(bits, labels, left, tensors):
    block = tensors.shape[-1]
    count_blocks = labels.shape[0]
    width = count_blocks * block
    rows = bits.shape[1]
    segment = lax.axis_index("sect")
    segments = lax.axis_size("sect")
    whole = lax.all_gather(tensors, "blk", axis=2, tiled=True)[0]
    choose = bits[0] == 1

    state = charge_order(labels, left, block).astype(jnp.float32)
    total = jnp.zeros((rows,), jnp.float32)
    prob_out = jnp.zeros((rows,), jnp.float32)
    log_out = jnp.zeros((rows,), jnp.float32)
    for step in range(segments):
        rounded = lax.reduce_precision(state, exponent_bits=8, mantissa_bits=7)
        high = rounded.astype(jnp.bfloat16)
        low = (state - rounded).astype(jnp.bfloat16)
        parts = jnp.concatenate([high, low], axis=0).reshape(2 * rows, count_blocks, block)
        both = jnp.einsum("rck,bckl->brcl", parts, whole, preferred_element_type=jnp.float32)
        image = both[:, :rows] + both[:, rows:]
        stay = image[0]
        raised = jnp.roll(image[1], 1, axis=1)
        norm_zero = jnp.sum(stay * stay, axis=(1, 2))
        norm_one = jnp.sum(raised * raised, axis=(1, 2))
        chosen_norm = jnp.where(choose, norm_one, norm_zero)
        prob = chosen_norm / (norm_zero + norm_one)
        total = total + jnp.log(prob)
        here = segment == step
        prob_out = jnp.where(here, prob, prob_out)
        log_out = jnp.where(here, total, log_out)
        if step + 1 < segments:
            chosen = jnp.where(choose[:, None, None], raised, stay)
            scaled = chosen * lax.rsqrt(chosen_norm / width + 1e-06)[:, None, None]
            extra = jnp.zeros((1, width), jnp.float32).at[0, :rows].set(total)
            sent = jnp.concatenate([scaled.reshape(rows, width), extra], axis=0)
            came = lax.ppermute(sent, "sect", [(step, step + 1)])
            state = came[:rows]
            total = came[rows, :rows]
    return (prob_out[None], log_out[None])


def solution(mesh):
    in_specs = (P("sect", "blk"), P(), P("blk", None), P("sect", None, "blk", None, None))
    out_specs = (P("sect", "blk"), P("sect", "blk"))
    return jax.shard_map(body, mesh=mesh, in_specs=in_specs, out_specs=out_specs, check_vma=False)
```

time: 441 us -> 451 us (1.023)
  the two profiles are of different devices: /device:TPU:4 before, /device:TPU:22 now
where the time goes in v2:
time: 451 us
  waiting for transfers between devices  377 us (84%)
  other arithmetic  23.4 us (5%)
  matrix products  20.9 us (5%)
  between operations  14.8 us (3%)
  local copies, waits for them, and re-layouts  8.03 us (2%)
  starting transfers between devices  6.43 us (1%)
    ppermute x7, waiting for transfers between devices, body(): came = lax.ppermute(sent, 'sect', [(step, step + 1)])  246 us
    all_gather x1, waiting for transfers between devices, body(): whole = lax.all_gather(tensors, 'blk', axis=2, tiled=True)[0]  131 us
    dot_general x8, matrix products, body(): jnp.einsum('rck,bckl->brcl', parts, whole, preferred_element_type=jnp.flo...  19.9 us
  transfers between devices with their start and end apart: 8, of which 2 were waited for; matrix products, arithmetic and copies ran while one was open for 1% of the time, Pallas kernels for 0%

profile of v2, /device:TPU:22, one launch (start us, length us, event | category | flops | bytes accessed | tf_op | source)
XLA Modules:
  0.0 450.9 jit_solution(7525638271096546561)
XLA Ops:
  7.2 1.6 copy.31
  8.8 1.1 copy.85
  10.0 0.6 compare_reduce_fusion
  10.6 1.0 reduce-precision_convert_fusion.7
  11.7 131.1 %all-gather.2.cloned.1.call-done = bf16[1,2,128,128,128]{4,3,1,0,2:T(8,128)(2,1)} async-done(((bf16[1,2,2,128,128]{4,3,1,0,2:T(8,128)(2,1)}), bf16[1,2,128,128,128]{4,3,1,0,2:T(8,128)(2,1)}) %all-gather.2.cloned.1.call-update) | async-done | bytes 8388624 | tf_op jit(solution)/shard_map/all_gather | solution.py:24
  142.8 5.0 %fusion.16 = f32[2,32,128,128]{3,1,0,2:T(8,128)S(1)} fusion(bf16[1,2,128,128,128]{4,3,1,0,2:T(8,128)(2,1)} %all-gather.2.cloned.1.call-done, bf16[32,128,128,1]{2,1,0,3:T(8,128)(2,1)S(1)} %maximum_bitcast_fusion), kind=kOutput, calls=%fused_computation.16 | convolution fusion | flops 268435456 | bytes 13631488 | tf_op jit(solution)/shard_map/rck,bckl->brcl/dot_general | solution.py:36
  147.9 0.4 slice_add_fusion.7
  148.3 0.4 fusion.99
  148.7 0.3 copy.34
  149.1 0.3 fusion.73
  149.3 1.0 broadcast_select_fusion.20
  150.3 0.6 fusion.56
  151.1 0.9 collective-permute-start
  152.5 0.7 slice-done.1
  153.2 1.7 fusion.19
  154.8 0.4 slice_add_fusion.6
  155.2 0.4 fusion.98
  155.7 0.3 copy.37
  156.0 0.3 fusion.72
  156.3 0.6 fusion.55
  156.9 0.7 broadcast_select_fusion.19
  157.7 0.9 collective-permute-start.1
  159.1 1.6 fusion.22
  160.8 0.4 slice_add_fusion.5
  161.2 0.4 fusion.97
  161.6 0.3 copy.40
  162.3 0.6 fusion.54
  162.9 0.7 broadcast_select_fusion.18
  163.7 0.8 collective-permute-start.2
  164.9 1.6 fusion.25
  166.6 0.4 slice_add_fusion.4
  167.0 0.4 fusion.96
  167.4 0.3 copy.43
  168.0 0.6 fusion.53
  168.7 0.7 broadcast_select_fusion.17
  169.5 0.8 collective-permute-start.3
  170.7 1.6 fusion.28
  172.3 0.4 slice_add_fusion.3
  172.7 0.4 fusion.95
  173.2 0.3 copy.46
  173.8 0.6 fusion.52
  174.5 0.7 broadcast_select_fusion.16
  175.3 1.0 collective-permute-start.4
  176.7 1.6 fusion.31
  178.4 0.4 slice_add_fusion.2
  178.7 0.4 fusion.94
  179.2 0.3 copy.49
  179.8 0.6 fusion.51
  180.5 0.7 broadcast_select_fusion.15
  181.3 0.8 collective-permute-start.5
  182.5 1.6 fusion.34
  184.1 0.4 slice_add_fusion.1
  184.5 0.4 fusion.93
  185.0 0.3 copy.52
  185.6 0.6 fusion.50
  186.3 0.7 broadcast_select_fusion.14
  187.0 1.3 collective-permute-start.6
  188.4 246.2 %collective-permute-done.6 = f32[17,16384]{1,0:T(8,128)} collective-permute-done((f32[17,16384]{1,0:T(8,128)S(1)}, f32[17,16384]{1,0:T(8,128)}, u32[]{:S(2)}, u32[]{:S(2)}) %collective-permute-start.6) | collective-permute-done | bytes 1114144 | tf_op jit(solution)/shard_map/ppermute | solution.py:53
  434.5 1.3 reduce-precision_convert_fusion
  436.2 5.0 %fusion.37 = f32[2,32,128,128]{3,1,0,2:T(8,128)S(1)} fusion(bf16[1,2,128,128,128]{4,3,1,0,2:T(8,128)(2,1)} %all-gather.2.cloned.1.call-done, bf16[32,128,128,1]{2,1,0,3:T(8,128)(2,1)S(1)} %bitcast.287), kind=kOutput, calls=%fused_computation.23 | convolution fusion | flops 268435456 | bytes 13631488 | tf_op jit(solution)/shard_map/rck,bckl->brcl/dot_general | solution.py:36
  441.2 0.4 slice_add_fusion
  441.6 0.3 slice_bitcast_fusion
  442.2 0.5 broadcast_select_fusion.22
  442.8 1.2 broadcast_select_fusion.21
  (82 shorter events, 6.0 us)
Async XLA Ops:
  7.2 135.7 %all-gather.2.cloned.1.call-start = ((), (), s32[]{:S(2)}) async-start(), calls=%async_computation | async-start | bytes 8519680 | tf_op jit(solution)/shard_map/all_gather | solution.py:24
  9.9 1.7 copy-start.5
  148.7 3.7 slice-start
  151.0 2.2 slice-start.1
  151.1 0.9 collective-permute-start
  157.7 1.0 collective-permute-start.1
  158.7 4.2 copy-start
  163.7 0.8 collective-permute-start.2
  164.5 4.2 copy-start.1
  169.5 0.8 collective-permute-start.3
  170.2 4.2 copy-start.2
  175.3 1.0 collective-permute-start.4
  176.3 4.2 copy-start.3
  181.3 0.8 collective-permute-start.5
  182.0 4.2 copy-start.4
  187.0 247.5 %collective-permute-start.6 = (f32[17,16384]{1,0:T(8,128)S(1)}, f32[17,16384]{1,0:T(8,128)}, u32[]{:S(2)}, u32[]{:S(2)}) collective-permute-start(f32[17,16384]{1,0:T(8,128)S(1)} %select_maximum_fusion), channel_id=1, source_target_pairs={{384,448},{385,449},{386,450},{387,451},{388,452},{389,453},{390,4... | collective-permute-start | bytes 3342344 | tf_op jit(solution)/shard_map/ppermute | solution.py:53
Sparse Core Ops, SparseCore 0:
  10.1 132.6 all-gather.1

commit v3 on v2

v3 whole, which is shorter than its diff:
```python
import jax
import jax.numpy as jnp
from jax import lax
from jax.sharding import PartitionSpec as P

MICRO = 2


def charge_order(labels, left, block):
    count_blocks = labels.shape[0]
    samples_here = left.shape[0]
    blocks = left.reshape(samples_here, count_blocks, block)
    index = jnp.arange(count_blocks, dtype=jnp.int32)
    pick = (labels[None, :] == index[:, None]).astype(jnp.bfloat16)
    ordered = jnp.einsum("ci,rik->rck", pick, blocks, preferred_element_type=jnp.float32)
    return ordered.astype(jnp.bfloat16)


def site_images(state, weights, block):
    count_rows = state.shape[0]
    rounded = lax.reduce_precision(state, exponent_bits=8, mantissa_bits=7)
    high = rounded.astype(jnp.bfloat16)
    low = (state - rounded).astype(jnp.bfloat16)
    parts = jnp.concatenate([high, low], axis=0).reshape(2 * count_rows, weights.shape[1], block)
    both = jnp.einsum("rck,bckl->brcl", parts, weights, preferred_element_type=jnp.float32)
    return both[:, :count_rows] + both[:, count_rows:]


def body(bits, labels, left, tensors):
    block = tensors.shape[-1]
    count_blocks = labels.shape[0]
    width = count_blocks * block
    rows = bits.shape[1]
    segment = lax.axis_index("sect")
    segments = lax.axis_size("sect")
    n_blk = lax.axis_size("blk")
    whole = lax.all_gather(tensors, "blk", axis=2, tiled=True)[0]

    flip = [(b, b ^ 2) for b in range(n_blk)]
    odd = segment % 2 == 1
    carried_bits = jnp.where(odd, lax.ppermute(bits, "blk", flip), bits)[0]
    hop = [(s * n_blk + b, (s + 1) * n_blk + (b ^ 2)) for s in range(segments - 1) for b in range(n_blk)]

    count = MICRO
    mrows = rows // count
    start_rows = charge_order(labels, left, block).astype(jnp.float32).reshape(count, mrows, width)
    site_bits = (carried_bits == 1).reshape(count, mrows)

    def advance(state, choose):
        image = site_images(state, whole, block)
        stay = image[0]
        raised = jnp.roll(image[1], 1, axis=1)
        norm_zero = jnp.sum(stay * stay, axis=(1, 2))
        norm_one = jnp.sum(raised * raised, axis=(1, 2))
        chosen_norm = jnp.where(choose, norm_one, norm_zero)
        prob = chosen_norm / (norm_zero + norm_one)
        chosen = jnp.where(choose[:, None, None], raised, stay)
        scaled = chosen * lax.rsqrt(chosen_norm / width + 1e-06)[:, None, None]
        return (prob, scaled.reshape(mrows, width))

    def one_step(step, carry, send):
        state, total, prob_out, log_out = carry
        group = step - segment
        valid = (group >= 0) & (group < count)
        slot = jnp.clip(group, 0, count - 1)
        first = segment == 0
        state = jnp.where(first, lax.dynamic_index_in_dim(start_rows, slot, 0, keepdims=False), state)
        total = jnp.where(first, jnp.zeros_like(total), total)
        choose = lax.dynamic_index_in_dim(site_bits, slot, 0, keepdims=False)
        prob, next_state = advance(state, choose)
        total = total + jnp.log(prob)
        old_prob = lax.dynamic_index_in_dim(prob_out, slot, 0, keepdims=False)
        old_log = lax.dynamic_index_in_dim(log_out, slot, 0, keepdims=False)
        prob_out = lax.dynamic_update_index_in_dim(prob_out, jnp.where(valid, prob, old_prob), slot, 0)
        log_out = lax.dynamic_update_index_in_dim(log_out, jnp.where(valid, total, old_log), slot, 0)
        if send:
            extra = jnp.zeros((1, width), jnp.float32).at[0, :mrows].set(total)
            sent = jnp.concatenate([next_state, extra], axis=0)
            came = lax.ppermute(sent, ("sect", "blk"), hop)
            state = came[:mrows]
            total = came[mrows, :mrows]
        return (state, total, prob_out, log_out)

    empty = jnp.zeros((count, mrows), jnp.float32)
    init = (start_rows[0], jnp.zeros((mrows,), jnp.float32), empty, empty)
    steps = count + segments - 1
    carry = lax.fori_loop(0, steps - 1, lambda step, carry: one_step(step, carry, True), init)
    carry = one_step(steps - 1, carry, False)
    result = jnp.stack([carry[2].reshape(rows), carry[3].reshape(rows)])
    result = jnp.where(odd, lax.ppermute(result, "blk", flip), result)
    return (result[0][None], result[1][None])


def solution(mesh):
    in_specs = (P("sect", "blk"), P(), P("blk", None), P("sect", None, "blk", None, None))
    out_specs = (P("sect", "blk"), P("sect", "blk"))
    return jax.shard_map(body, mesh=mesh, in_specs=in_specs, out_specs=out_specs, check_vma=False)
```

time: 451 us -> 445 us (0.987)
  the two profiles are of different devices: /device:TPU:22 before, /device:TPU:2 now
where the time goes in v3:
time: 445 us; the launch traced here: 443 us
  waiting for transfers between devices  321 us (72%)
  matrix products  43.3 us (10%)
  starting transfers between devices  25.2 us (6%)
  local copies, waits for them, and re-layouts  19.9 us (4%)
  other arithmetic  18.8 us (4%)
  between operations  14.2 us (3%)
    ppermute x8, waiting for transfers between devices, one_step(): came = lax.ppermute(sent, ('sect', 'blk'), hop)  190 us
    all_gather x1, waiting for transfers between devices, body(): whole = lax.all_gather(tensors, 'blk', axis=2, tiled=True)[0]  128 us
    dot_general x9, matrix products, site_images(): jnp.einsum('rck,bckl->brcl', parts, weights, preferred_element_type=jnp.f...  42.4 us
    ppermute x8, starting transfers between devices, one_step(): came = lax.ppermute(sent, ('sect', 'blk'), hop)  19.8 us
    another operation x16, other arithmetic  9.47 us
  transfers between devices with their start and end apart: 11, of which 10 were waited for; matrix products, arithmetic and copies ran while one was open for 1% of the time, Pallas kernels for 0%

profile of v3, /device:TPU:2, one launch (start us, length us, event | category | flops | bytes accessed | tf_op | source)
XLA Modules:
  0.0 443.1 jit_solution(5987685315972397245)
XLA Ops:
  7.2 1.6 copy.11
  8.8 3.5 collective-permute-start.1
  12.3 1.1 copy.20
  13.5 0.9 fusion.10
  15.0 0.7 compare_reduce_fusion.1
  15.8 127.9 %all-gather.2.cloned.1.call-done = bf16[1,2,128,128,128]{4,3,1,0,2:T(8,128)(2,1)} async-done(((bf16[1,2,2,128,128]{4,3,1,0,2:T(8,128)(2,1)}), bf16[1,2,128,128,128]{4,3,1,0,2:T(8,128)(2,1)}) %all-gather.2.cloned.1.call-update) | async-done | bytes 8388624 | tf_op jit(solution)/shard_map/all_gather | solution.py:37
  143.7 280.7 %while.22 = (s32[]{:T(128)}, f32[8,16384]{1,0:T(8,128)S(1)}, f32[8]{0:T(128)S(1)}, f32[2,8]{1,0:T(2,128)S(1)}, f32[2,8]{1,0:T(2,128)S(1)}, /*index=5*/s32[]{:T(1...) while((s32[]{:T(128)}, f32[8,16384]{1,0:T(8,128)S(1)}, ...), condition=%wide.region_4.5_spmd, body=%wide.region_0.4_spmd.sunk | while | flops 137674880 | bytes 27067452 | solution.py:87
  143.9 4.7 %convolution_bitcast_fusion.3 = f32[2,16,128,128]{3,1,0,2:T(8,128)S(1)} fusion(bf16[2,128,128,128]{3,2,0,1:T(8,128)(2,1)} %get-tuple-element.400, bf16[16,128,128,1]{2,1,0,3:T(8,128)(2,1)S(1)} %bitcast.130), kind=kOutput, calls=%fused_computation.clone.1 | convolution fusion | flops 134217728 | bytes 11010048 | tf_op jit(solution)/shard_map/while/body/eval_jaxpr/rck,bckl->brcl/dot_general | solution.py:25
  149.0 0.6 compare_reduce_fusion.3
  150.1 0.6 fusion.37
  150.7 4.3 collective-permute-start
  155.1 25.0 %collective-permute-done = f32[9,16384]{1,0:T(8,128)} collective-permute-done((f32[9,16384]{1,0:T(8,128)S(1)}, f32[9,16384]{1,0:T(8,128)}, u32[]{:S(2)}, u32[]{:S(2)}) %collective-permute-start) | collective-permute-done | bytes 589856 | tf_op jit(solution)/shard_map/while/body/eval_jaxpr/ppermute | solution.py:79
  180.1 1.1 slice.192
  181.2 0.7 slice_bitcast_fusion.7
  182.1 4.7 %convolution_bitcast_fusion.3 = f32[2,16,128,128]{3,1,0,2:T(8,128)S(1)} fusion(bf16[2,128,128,128]{3,2,0,1:T(8,128)(2,1)} %get-tuple-element.400, bf16[16,128,128,1]{2,1,0,3:T(8,128)(2,1)S(1)} %bitcast.130), kind=kOutput, calls=%fused_computation.clone.1 | convolution fusion | flops 134217728 | bytes 11010048 | tf_op jit(solution)/shard_map/while/body/eval_jaxpr/rck,bckl->brcl/dot_general | solution.py:25
  187.3 0.6 compare_reduce_fusion.3
  188.3 0.6 fusion.37
  188.9 3.4 collective-permute-start
  192.4 25.1 %collective-permute-done = f32[9,16384]{1,0:T(8,128)} collective-permute-done((f32[9,16384]{1,0:T(8,128)S(1)}, f32[9,16384]{1,0:T(8,128)}, u32[]{:S(2)}, u32[]{:S(2)}) %collective-permute-start) | collective-permute-done | bytes 589856 | tf_op jit(solution)/shard_map/while/body/eval_jaxpr/ppermute | solution.py:79
  217.5 1.1 slice.192
  218.6 0.7 slice_bitcast_fusion.7
  219.5 4.7 %convolution_bitcast_fusion.3 = f32[2,16,128,128]{3,1,0,2:T(8,128)S(1)} fusion(bf16[2,128,128,128]{3,2,0,1:T(8,128)(2,1)} %get-tuple-element.400, bf16[16,128,128,1]{2,1,0,3:T(8,128)(2,1)S(1)} %bitcast.130), kind=kOutput, calls=%fused_computation.clone.1 | convolution fusion | flops 134217728 | bytes 11010048 | tf_op jit(solution)/shard_map/while/body/eval_jaxpr/rck,bckl->brcl/dot_general | solution.py:25
  224.7 0.6 compare_reduce_fusion.3
  225.7 0.6 fusion.37
  226.4 2.5 collective-permute-start
  229.0 25.1 %collective-permute-done = f32[9,16384]{1,0:T(8,128)} collective-permute-done((f32[9,16384]{1,0:T(8,128)S(1)}, f32[9,16384]{1,0:T(8,128)}, u32[]{:S(2)}, u32[]{:S(2)}) %collective-permute-start) | collective-permute-done | bytes 589856 | tf_op jit(solution)/shard_map/while/body/eval_jaxpr/ppermute | solution.py:79
  254.0 1.1 slice.192
  255.1 0.7 slice_bitcast_fusion.7
  256.0 4.7 %convolution_bitcast_fusion.3 = f32[2,16,128,128]{3,1,0,2:T(8,128)S(1)} fusion(bf16[2,128,128,128]{3,2,0,1:T(8,128)(2,1)} %get-tuple-element.400, bf16[16,128,128,1]{2,1,0,3:T(8,128)(2,1)S(1)} %bitcast.130), kind=kOutput, calls=%fused_computation.clone.1 | convolution fusion | flops 134217728 | bytes 11010048 | tf_op jit(solution)/shard_map/while/body/eval_jaxpr/rck,bckl->brcl/dot_general | solution.py:25
  261.2 0.6 compare_reduce_fusion.3
  262.2 0.6 fusion.37
  262.8 1.9 collective-permute-start
  264.9 24.7 %collective-permute-done = f32[9,16384]{1,0:T(8,128)} collective-permute-done((f32[9,16384]{1,0:T(8,128)S(1)}, f32[9,16384]{1,0:T(8,128)}, u32[]{:S(2)}, u32[]{:S(2)}) %collective-permute-start) | collective-permute-done | bytes 589856 | tf_op jit(solution)/shard_map/while/body/eval_jaxpr/ppermute | solution.py:79
  289.6 1.1 slice.192
  290.7 0.7 slice_bitcast_fusion.7
  291.6 4.7 %convolution_bitcast_fusion.3 = f32[2,16,128,128]{3,1,0,2:T(8,128)S(1)} fusion(bf16[2,128,128,128]{3,2,0,1:T(8,128)(2,1)} %get-tuple-element.400, bf16[16,128,128,1]{2,1,0,3:T(8,128)(2,1)S(1)} %bitcast.130), kind=kOutput, calls=%fused_computation.clone.1 | convolution fusion | flops 134217728 | bytes 11010048 | tf_op jit(solution)/shard_map/while/body/eval_jaxpr/rck,bckl->brcl/dot_general | solution.py:25
  296.7 0.6 compare_reduce_fusion.3
  297.8 0.6 fusion.37
  298.4 1.9 collective-permute-start
  300.4 23.8 %collective-permute-done = f32[9,16384]{1,0:T(8,128)} collective-permute-done((f32[9,16384]{1,0:T(8,128)S(1)}, f32[9,16384]{1,0:T(8,128)}, u32[]{:S(2)}, u32[]{:S(2)}) %collective-permute-start) | collective-permute-done | bytes 589856 | tf_op jit(solution)/shard_map/while/body/eval_jaxpr/ppermute | solution.py:79
  324.2 1.1 slice.192
  325.3 0.7 slice_bitcast_fusion.7
  326.2 4.7 %convolution_bitcast_fusion.3 = f32[2,16,128,128]{3,1,0,2:T(8,128)S(1)} fusion(bf16[2,128,128,128]{3,2,0,1:T(8,128)(2,1)} %get-tuple-element.400, bf16[16,128,128,1]{2,1,0,3:T(8,128)(2,1)S(1)} %bitcast.130), kind=kOutput, calls=%fused_computation.clone.1 | convolution fusion | flops 134217728 | bytes 11010048 | tf_op jit(solution)/shard_map/while/body/eval_jaxpr/rck,bckl->brcl/dot_general | solution.py:25
  331.4 0.6 compare_reduce_fusion.3
  332.4 0.6 fusion.37
  333.1 1.9 collective-permute-start
  335.1 22.9 %collective-permute-done = f32[9,16384]{1,0:T(8,128)} collective-permute-done((f32[9,16384]{1,0:T(8,128)S(1)}, f32[9,16384]{1,0:T(8,128)}, u32[]{:S(2)}, u32[]{:S(2)}) %collective-permute-start) | collective-permute-done | bytes 589856 | tf_op jit(solution)/shard_map/while/body/eval_jaxpr/ppermute | solution.py:79
  358.0 1.1 slice.192
  359.0 0.7 slice_bitcast_fusion.7
  359.9 4.7 %convolution_bitcast_fusion.3 = f32[2,16,128,128]{3,1,0,2:T(8,128)S(1)} fusion(bf16[2,128,128,128]{3,2,0,1:T(8,128)(2,1)} %get-tuple-element.400, bf16[16,128,128,1]{2,1,0,3:T(8,128)(2,1)S(1)} %bitcast.130), kind=kOutput, calls=%fused_computation.clone.1 | convolution fusion | flops 134217728 | bytes 11010048 | tf_op jit(solution)/shard_map/while/body/eval_jaxpr/rck,bckl->brcl/dot_general | solution.py:25
  365.1 0.6 compare_reduce_fusion.3
  366.8 1.9 collective-permute-start
  368.8 22.0 %collective-permute-done = f32[9,16384]{1,0:T(8,128)} collective-permute-done((f32[9,16384]{1,0:T(8,128)S(1)}, f32[9,16384]{1,0:T(8,128)}, u32[]{:S(2)}, u32[]{:S(2)}) %collective-permute-start) | collective-permute-done | bytes 589856 | tf_op jit(solution)/shard_map/while/body/eval_jaxpr/ppermute | solution.py:79
  390.8 1.1 slice.192
  391.8 0.7 slice_bitcast_fusion.7
  392.7 4.7 %convolution_bitcast_fusion.3 = f32[2,16,128,128]{3,1,0,2:T(8,128)S(1)} fusion(bf16[2,128,128,128]{3,2,0,1:T(8,128)(2,1)} %get-tuple-element.400, bf16[16,128,128,1]{2,1,0,3:T(8,128)(2,1)S(1)} %bitcast.130), kind=kOutput, calls=%fused_computation.clone.1 | convolution fusion | flops 134217728 | bytes 11010048 | tf_op jit(solution)/shard_map/while/body/eval_jaxpr/rck,bckl->brcl/dot_general | solution.py:25
  397.9 0.6 compare_reduce_fusion.3
  399.6 1.9 collective-permute-start
  401.6 21.0 %collective-permute-done = f32[9,16384]{1,0:T(8,128)} collective-permute-done((f32[9,16384]{1,0:T(8,128)S(1)}, f32[9,16384]{1,0:T(8,128)}, u32[]{:S(2)}, u32[]{:S(2)}) %collective-permute-start) | collective-permute-done | bytes 589856 | tf_op jit(solution)/shard_map/while/body/eval_jaxpr/ppermute | solution.py:79
  422.6 1.1 slice.192
  423.7 0.7 slice_bitcast_fusion.7
  424.6 4.7 %convolution_bitcast_fusion.1 = f32[2,16,128,128]{3,1,0,2:T(8,128)S(1)} fusion(bf16[16,128,128,1]{2,1,0,3:T(8,128)(2,1)S(1)} %bitcast.132, bf16[1,2,128,128,128]{4,3,1,0,2:T(8,128)(2,1)} %bitcast.129), kind=kOutput, calls=%fused_computation.35 | convolution fusion | flops 134217728 | bytes 11010048 | tf_op jit(solution)/shard_map/rck,bckl->brcl/dot_general | solution.py:25
  430.3 1.9 collective-permute-start.2
  432.2 3.5 collective-permute-done.2
  (149 shorter events, 13.0 us)
Async XLA Ops:
  7.2 136.5 %all-gather.2.cloned.1.call-start = ((), (), s32[]{:S(2)}) async-start(), calls=%async_computation | async-start | bytes 8519680 | tf_op jit(solution)/shard_map/all_gather | solution.py:37
  8.8 6.2 %collective-permute-start.1 = (s32[1,16]{1,0:T(1,128)}, s32[1,16]{1,0:T(1,128)S(1)}, u32[]{:S(2)}, u32[]{:S(2)}) collective-permute-start(s32[1,16]{1,0:T(1,128)} %param.8), channel_id=1, source_target_pairs={{0,2},{1,3},{2,0},{3,1},{4,6},{5,7},{6,4},{7,5},{8,10},{9,11},{10,... | collective-permute-start | bytes 200 | tf_op jit(solution)/shard_map/ppermute | solution.py:41
  150.7 29.4 %collective-permute-start = (f32[9,16384]{1,0:T(8,128)S(1)}, f32[9,16384]{1,0:T(8,128)}, u32[]{:S(2)}, u32[]{:S(2)}) collective-permute-start(f32[9,16384]{1,0:T(8,128)S(1)} %select_maximum_fusion.2), channel_id=1, source_target_pairs={{0,66},{1,67},{2,64},{3,65},{4,70},{5,71},{6,68},{7,69},{8,74},{9,... | collective-permute-start | bytes 1769480 | tf_op jit(solution)/shard_map/while/body/eval_jaxpr/ppermute | solution.py:79
  188.9 28.6 %collective-permute-start = (f32[9,16384]{1,0:T(8,128)S(1)}, f32[9,16384]{1,0:T(8,128)}, u32[]{:S(2)}, u32[]{:S(2)}) collective-permute-start(f32[9,16384]{1,0:T(8,128)S(1)} %select_maximum_fusion.2), channel_id=1, source_target_pairs={{0,66},{1,67},{2,64},{3,65},{4,70},{5,71},{6,68},{7,69},{8,74},{9,... | collective-permute-start | bytes 1769480 | tf_op jit(solution)/shard_map/while/body/eval_jaxpr/ppermute | solution.py:79
  226.4 27.7 %collective-permute-start = (f32[9,16384]{1,0:T(8,128)S(1)}, f32[9,16384]{1,0:T(8,128)}, u32[]{:S(2)}, u32[]{:S(2)}) collective-permute-start(f32[9,16384]{1,0:T(8,128)S(1)} %select_maximum_fusion.2), channel_id=1, source_target_pairs={{0,66},{1,67},{2,64},{3,65},{4,70},{5,71},{6,68},{7,69},{8,74},{9,... | collective-permute-start | bytes 1769480 | tf_op jit(solution)/shard_map/while/body/eval_jaxpr/ppermute | solution.py:79
  262.8 26.7 %collective-permute-start = (f32[9,16384]{1,0:T(8,128)S(1)}, f32[9,16384]{1,0:T(8,128)}, u32[]{:S(2)}, u32[]{:S(2)}) collective-permute-start(f32[9,16384]{1,0:T(8,128)S(1)} %select_maximum_fusion.2), channel_id=1, source_target_pairs={{0,66},{1,67},{2,64},{3,65},{4,70},{5,71},{6,68},{7,69},{8,74},{9,... | collective-permute-start | bytes 1769480 | tf_op jit(solution)/shard_map/while/body/eval_jaxpr/ppermute | solution.py:79
  298.4 25.8 %collective-permute-start = (f32[9,16384]{1,0:T(8,128)S(1)}, f32[9,16384]{1,0:T(8,128)}, u32[]{:S(2)}, u32[]{:S(2)}) collective-permute-start(f32[9,16384]{1,0:T(8,128)S(1)} %select_maximum_fusion.2), channel_id=1, source_target_pairs={{0,66},{1,67},{2,64},{3,65},{4,70},{5,71},{6,68},{7,69},{8,74},{9,... | collective-permute-start | bytes 1769480 | tf_op jit(solution)/shard_map/while/body/eval_jaxpr/ppermute | solution.py:79
  333.1 24.9 %collective-permute-start = (f32[9,16384]{1,0:T(8,128)S(1)}, f32[9,16384]{1,0:T(8,128)}, u32[]{:S(2)}, u32[]{:S(2)}) collective-permute-start(f32[9,16384]{1,0:T(8,128)S(1)} %select_maximum_fusion.2), channel_id=1, source_target_pairs={{0,66},{1,67},{2,64},{3,65},{4,70},{5,71},{6,68},{7,69},{8,74},{9,... | collective-permute-start | bytes 1769480 | tf_op jit(solution)/shard_map/while/body/eval_jaxpr/ppermute | solution.py:79
  366.8 24.0 %collective-permute-start = (f32[9,16384]{1,0:T(8,128)S(1)}, f32[9,16384]{1,0:T(8,128)}, u32[]{:S(2)}, u32[]{:S(2)}) collective-permute-start(f32[9,16384]{1,0:T(8,128)S(1)} %select_maximum_fusion.2), channel_id=1, source_target_pairs={{0,66},{1,67},{2,64},{3,65},{4,70},{5,71},{6,68},{7,69},{8,74},{9,... | collective-permute-start | bytes 1769480 | tf_op jit(solution)/shard_map/while/body/eval_jaxpr/ppermute | solution.py:79
  399.6 23.1 %collective-permute-start = (f32[9,16384]{1,0:T(8,128)S(1)}, f32[9,16384]{1,0:T(8,128)}, u32[]{:S(2)}, u32[]{:S(2)}) collective-permute-start(f32[9,16384]{1,0:T(8,128)S(1)} %select_maximum_fusion.2), channel_id=1, source_target_pairs={{0,66},{1,67},{2,64},{3,65},{4,70},{5,71},{6,68},{7,69},{8,74},{9,... | collective-permute-start | bytes 1769480 | tf_op jit(solution)/shard_map/while/body/eval_jaxpr/ppermute | solution.py:79
  430.3 5.5 %collective-permute-start.2 = (f32[2,16]{1,0:T(2,128)S(1)}, f32[2,16]{1,0:T(2,128)S(1)}, u32[]{:S(2)}, u32[]{:S(2)}) collective-permute-start(f32[2,16]{1,0:T(2,128)S(1)} %pad_maximum_fusion.1), channel_id=1, source_target_pairs={{0,2},{1,3},{2,0},{3,1},{4,6},{5,7},{6,4},{7,5},{8,10},{9,11},{10,... | collective-permute-start | bytes 392 | tf_op jit(solution)/shard_map/ppermute | solution.py:90
Sparse Core Ops, SparseCore 0:
  10.1 133.4 all-gather.1

commit v4 on v1

v4 whole, which is shorter than its diff:
```python
import jax
import jax.numpy as jnp
from jax import lax
from jax.sharding import Mesh
from jax.sharding import PartitionSpec as P

PARTS = 8


def charge_order(labels, rows, block):
    count_blocks = labels.shape[0]
    blocks = rows.reshape(rows.shape[0], count_blocks, block)
    index = jnp.arange(count_blocks, dtype=jnp.int32)
    pick = (labels[None, :] == index[:, None]).astype(blocks.dtype)
    ordered = jnp.einsum("ci,rik->rck", pick, blocks, preferred_element_type=jnp.float32)
    return ordered.astype(blocks.dtype)


def site_images(state, weights):
    count_rows = state.shape[0]
    rounded = lax.reduce_precision(state, exponent_bits=8, mantissa_bits=7)
    high = rounded.astype(jnp.bfloat16)
    low = (state - rounded).astype(jnp.bfloat16)
    parts = jnp.concatenate([high, low], axis=0)
    both = jnp.einsum("rck,bckl->brcl", parts, weights, preferred_element_type=jnp.float32)
    return both[:, :count_rows] + both[:, count_rows:]


def body(bits, labels, left, tensors):
    sect = lax.axis_index("sect")
    bhi = lax.axis_index("bhi")
    n_sect = lax.axis_size("sect")
    n_hi = lax.axis_size("bhi")
    n_lo = lax.axis_size("blo")
    block = tensors.shape[-1]
    count_blocks = labels.shape[0]
    width = count_blocks * block
    sites = bits.shape[0] * n_sect
    per_dev = left.shape[0]
    pick = per_dev // n_sect
    mine = count_blocks // n_hi

    slabs = lax.all_gather(tensors[0], "sect", axis=0, tiled=False)

    pieces = bits[0].reshape(n_sect, pick)
    pieces = lax.all_to_all(pieces, "sect", 0, 0, tiled=False)
    carried_bits = lax.all_gather(pieces, "bhi", axis=0, tiled=False)
    carried_bits = jnp.transpose(carried_bits, (1, 0, 2)).reshape(sites, n_hi * pick)

    rows = lax.dynamic_slice_in_dim(left, sect * pick, pick, 0)
    ordered = charge_order(labels, rows, block).reshape(pick, n_hi, mine, block)
    spread = lax.all_to_all(ordered, "bhi", 1, 1, tiled=False)
    count_rows = n_hi * pick
    state = jnp.transpose(spread, (1, 0, 2, 3)).reshape(count_rows, mine, block).astype(jnp.float32)

    total = jnp.zeros((count_rows,), jnp.float32)
    shift = [(q, (q + 1) % n_hi) for q in range(n_hi)]
    probs = []
    logs = []
    for site in range(sites):
        weights = lax.all_gather(slabs[site], "blo", axis=1, tiled=True)
        image = site_images(state, weights)
        stay = image[0]
        rise = image[1]
        part = jnp.stack([jnp.sum(stay * stay, axis=(1, 2)), jnp.sum(rise * rise, axis=(1, 2))])
        norms = lax.psum(part, "bhi")
        came = lax.ppermute(rise[:, mine - 1], "bhi", shift)
        raised = jnp.concatenate([came[:, None], rise[:, : mine - 1]], axis=1)
        norm_zero = norms[0]
        norm_one = norms[1]
        choose = carried_bits[site] == 1
        chosen_norm = jnp.where(choose, norm_one, norm_zero)
        prob = chosen_norm / (norm_zero + norm_one)
        total = total + jnp.log(prob)
        probs.append(prob)
        logs.append(total)
        if site + 1 < sites:
            chosen = jnp.where(choose[:, None, None], raised, stay)
            state = chosen * lax.rsqrt(chosen_norm / width + 1e-06)[:, None, None]

    result = jnp.stack([jnp.stack(probs), jnp.stack(logs)], axis=1)
    result = lax.dynamic_slice_in_dim(result, bhi * pick, pick, 2)
    back = lax.all_to_all(result, "sect", 0, 0, tiled=False)
    out = jnp.transpose(back, (1, 0, 2)).reshape(2, bits.shape[0], n_sect * pick)
    return (out[0], out[1])


def solution(mesh):
    n_sect, n_blk = mesh.devices.shape
    fine = Mesh(mesh.devices.reshape(n_sect, PARTS, n_blk // PARTS), ("sect", "bhi", "blo"))
    blk = ("bhi", "blo")
    in_specs = (P("sect", blk), P(), P(blk, None), P("sect", None, blk, None, None))
    out_specs = (P("sect", blk), P("sect", blk))
    return jax.shard_map(body, mesh=fine, in_specs=in_specs, out_specs=out_specs, check_vma=False)
```

time: 1630 us -> 385 us (0.24)
  blocking collectives: 1530 us -> 211 us
  waiting for transfers between devices: 40 us -> 94.2 us
    psum x8, blocking collectives: 838 us -> 165 us  [body(): norms = lax.psum(part, 'bhi')]
    all_gather x1, blocking collectives: 601 us -> 32.3 us  [body(): carried_bits = lax.all_gather(pieces, 'bhi', axis=0, tiled=False)]
    all_gather x1 -> x9, waiting for transfers between devices: 0.02 us -> 84.1 us  [the longest x1 70.3 us: body(): slabs = lax.all_gather(tensors[0], 'sect', axis=0, tiled=False)]
    all_to_all x1, blocking collectives: 88.8 us -> 12.8 us  [body(): back = lax.all_to_all(result, 'sect', 0, 0, tiled=False)]
    ppermute x7, waiting for transfers between devices: 39.3 us -> 4.51 us  [body(): came = lax.ppermute(rise[:, mine - 1], 'bhi', shift)]
  transfers between devices with their start and end apart: 9 -> 18, of which waited for: 7 -> 6; matrix products, arithmetic and copies ran while one was open for 0% -> 6% of each run, Pallas kernels for 0% -> 0%
where the time goes in v4:
time: 385 us; the launch traced here: 384 us
  blocking collectives  211 us (55%)
  waiting for transfers between devices  94.2 us (24%)
  starting transfers between devices  36.9 us (10%)
  between operations  14.4 us (4%)
  local copies, waits for them, and re-layouts  13 us (3%)
  matrix products  12.2 us (3%)
    psum x8, blocking collectives, body(): norms = lax.psum(part, 'bhi')  165 us
    all_gather x1, waiting for transfers between devices, body(): slabs = lax.all_gather(tensors[0], 'sect', axis=0, tiled=False)  70.3 us
    all_gather x1, blocking collectives, body(): carried_bits = lax.all_gather(pieces, 'bhi', axis=0, tiled=False)  32.3 us
    ppermute x7, starting transfers between devices, body(): came = lax.ppermute(rise[:, mine - 1], 'bhi', shift)  19.8 us
    all_gather x8, waiting for transfers between devices, body(): weights = lax.all_gather(slabs[site], 'blo', axis=1, tiled=True)  13.8 us
    all_to_all x1, blocking collectives, body(): back = lax.all_to_all(result, 'sect', 0, 0, tiled=False)  12.8 us
    all_to_all x1, starting transfers between devices, body(): spread = lax.all_to_all(ordered, 'bhi', 1, 1, tiled=False)  12.2 us
    dot_general x8, matrix products, site_images(): jnp.einsum('rck,bckl->brcl', parts, weights, preferred_element_type=jnp.f...  12.1 us
  transfers between devices with their start and end apart: 18, of which 6 were waited for; matrix products, arithmetic and copies ran while one was open for 6% of the time, Pallas kernels for 0%

profile of v4, /device:TPU:2, one launch (start us, length us, event | category | flops | bytes accessed | tf_op | source)
XLA Modules:
  0.0 384.2 jit_solution(2618559293923504255)
XLA Ops:
  7.2 0.7 all-gather.19.cloned.1.call-update
  8.0 70.3 %all-gather.19.cloned.1.call-done = bf16[8,2,2,128,128]{4,3,2,1,0:T(8,128)(2,1)} async-done(((bf16[1,2,2,128,128]{4,3,2,1,0:T(8,128)(2,1)}), bf16[8,2,2,128,128]{4,3,2,1,0:T(8,128)(2,1)}) %all-gather.19.cloned.1.call-update) | async-done | bytes 1048592 | tf_op jit(solution)/shard_map/all_gather | solution.py:43
  78.2 1.4 fusion.75
  79.6 0.7 copy.132
  80.3 0.7 copy.136
  81.1 0.7 copy.140
  81.8 0.6 copy.144
  82.5 0.7 copy.148
  83.3 0.6 copy.152
  84.0 0.7 copy.156
  84.7 0.5 broadcast.265
  85.3 0.1 copy-done.2
  85.4 0.7 reduce.13
  86.0 0.7 all_to_all.12
  86.7 4.5 %all-to-all-start = ((s32[8,1,2]{2,1,0:T(1,128)}), s32[8,1,2]{2,1,0:T(1,128)S(1)}, u32[]{:S(2)}, u32[]{:S(2)}) async-start(s32[8,1,2]{2,1,0:T(1,128)} %bitcast), calls=%async_computation | async-start | bytes 8192 | tf_op jit(solution)/shard_map/all_to_all | solution.py:46
  91.3 0.6 copy-done.1
  91.9 0.2 convolution_convert_fusion
  92.1 0.6 copy.130
  92.7 4.8 %all-to-all-done = s32[8,1,2]{2,1,0:T(1,128)S(1)} async-done(((s32[8,1,2]{2,1,0:T(1,128)}), s32[8,1,2]{2,1,0:T(1,128)S(1)}, u32[]{:S(2)}, u32[]{:S(2)}) %all-to-all-start) | async-done | bytes 96 | tf_op jit(solution)/shard_map/all_to_all | solution.py:46
  97.4 12.2 %all-to-all-start.1 = ((bf16[2,8,16,128]{3,2,0,1:T(8,128)(2,1)}), bf16[2,8,16,128]{3,2,0,1:T(8,128)(2,1)S(1)}, u32[]{:S(2)}, u32[]{:S(2)}) async-start(bf16[2,8,16,128]{3,2,0,1:T(8,128)(2,1)} %copy.130), calls=%async_computation.1 | async-start | bytes 131072 | tf_op jit(solution)/shard_map/all_to_all | solution.py:52
  109.7 32.3 %all-gather = s32[64,1,2]{2,1,0:T(1,128)S(1)} all-gather(s32[8,1,2]{2,1,0:T(1,128)S(1)} %all-to-all-done), channel_id=2, replica_groups=mesh['sect'=8,'bhi'=8,'blo'=8] {'bhi'}, dimensions={0}, use_global_device_ids=true | all-gather | bytes 576 | tf_op jit(solution)/shard_map/all_gather | solution.py:47
  142.0 0.1 copy.128
  144.4 0.7 copy.160
  145.1 1.5 convolution_bitcast_fusion.7
  146.7 0.1 multiply_reduce_fusion.13
  146.8 17.7 %psum.56 = f32[2,16]{1,0:T(2,128)S(1)} all-reduce(f32[2,16]{1,0:T(2,128)S(1)} %pad_maximum_fusion), channel_id=1, replica_groups=mesh['sect'=8,'bhi'=8,'blo'=8] {'bhi'}, use_global_device_ids=true, to_apply=%region_2.0 | all-reduce | flops 32 | bytes 256 | tf_op jit(solution)/shard_map/psum | solution.py:66
  164.5 3.1 collective-permute-start
  167.7 4.5 %collective-permute-done = f32[16,128]{1,0:T(8,128)S(1)} collective-permute-done((f32[16,128]{1,0:T(8,128)S(1)}, f32[16,128]{1,0:T(8,128)S(1)}, u32[]{:S(2)}, u32[]{:S(2)}) %collective-permute-start) | collective-permute-done | bytes 8224 | tf_op jit(solution)/shard_map/ppermute | solution.py:67
  172.3 1.5 convolution_bitcast_fusion.6
  173.8 0.1 multiply_reduce_fusion.11
  174.0 1.9 collective-permute-start.1
  176.0 20.0 %psum.57 = f32[2,16]{1,0:T(2,128)S(1)} all-reduce(f32[2,16]{1,0:T(2,128)S(1)} %pad_maximum_fusion.1), channel_id=1, replica_groups=mesh['sect'=8,'bhi'=8,'blo'=8] {'bhi'}, use_global_device_ids=true, to_apply=%region_5.6 | all-reduce | flops 32 | bytes 256 | tf_op jit(solution)/shard_map/psum | solution.py:66
  196.1 0.1 reduce-precision_convert_fusion.5
  196.2 1.6 convolution_bitcast_fusion.5
  197.8 0.1 multiply_reduce_fusion.9
  198.0 1.9 collective-permute-start.2
  199.9 20.1 %psum.58 = f32[2,16]{1,0:T(2,128)S(1)} all-reduce(f32[2,16]{1,0:T(2,128)S(1)} %pad_maximum_fusion.2), channel_id=1, replica_groups=mesh['sect'=8,'bhi'=8,'blo'=8] {'bhi'}, use_global_device_ids=true, to_apply=%region_8.9 | all-reduce | flops 32 | bytes 256 | tf_op jit(solution)/shard_map/psum | solution.py:66
  220.1 0.1 reduce-precision_convert_fusion.4
  220.2 1.5 convolution_bitcast_fusion.4
  221.8 0.1 multiply_reduce_fusion.7
  221.9 1.9 collective-permute-start.3
  223.9 20.1 %psum.59 = f32[2,16]{1,0:T(2,128)S(1)} all-reduce(f32[2,16]{1,0:T(2,128)S(1)} %pad_maximum_fusion.3), channel_id=1, replica_groups=mesh['sect'=8,'bhi'=8,'blo'=8] {'bhi'}, use_global_device_ids=true, to_apply=%region_11.12 | all-reduce | flops 32 | bytes 256 | tf_op jit(solution)/shard_map/psum | solution.py:66
  244.1 1.5 convolution_bitcast_fusion.3
  245.7 0.1 multiply_reduce_fusion.5
  245.8 1.9 collective-permute-start.4
  247.8 21.1 %psum.60 = f32[2,16]{1,0:T(2,128)S(1)} all-reduce(f32[2,16]{1,0:T(2,128)S(1)} %pad_maximum_fusion.4), channel_id=1, replica_groups=mesh['sect'=8,'bhi'=8,'blo'=8] {'bhi'}, use_global_device_ids=true, to_apply=%region_14.15 | all-reduce | flops 32 | bytes 256 | tf_op jit(solution)/shard_map/psum | solution.py:66
  268.9 0.1 reduce-precision_convert_fusion.2
  269.0 4.5 %all-gather.31.cloned.1.call-done = bf16[1,2,16,128,128]{4,3,1,0,2:T(8,128)(2,1)} async-done(((bf16[1,2,2,128,128]{4,3,1,0,2:T(8,128)(2,1)}), bf16[1,2,16,128,128]{4,3,1,0,2:T(8,128)(2,1)}) %all-gather.31.cloned.1.call-update) | async-done | bytes 1048592 | tf_op jit(solution)/shard_map/all_gather | solution.py:61
  273.5 1.5 convolution_bitcast_fusion.2
  275.1 0.1 multiply_reduce_fusion.3
  275.2 4.5 %collective-permute-start.5 = (f32[16,128]{1,0:T(8,128)S(1)}, f32[16,128]{1,0:T(8,128)S(1)}, u32[]{:S(2)}, u32[]{:S(2)}) collective-permute-start(f32[16,128]{1,0:T(8,128)S(1)} %slice_bitcast_fusion.15), channel_id=1, source_target_pairs={{0,8},{8,16},{16,24},{24,32},{32,40},{40,48},{48,56},{56,0},{1,9},... | collective-permute-start | bytes 24584 | tf_op jit(solution)/shard_map/ppermute | solution.py:67
  279.7 22.0 %psum.61 = f32[2,16]{1,0:T(2,128)S(1)} all-reduce(f32[2,16]{1,0:T(2,128)S(1)} %pad_maximum_fusion.5), channel_id=1, replica_groups=mesh['sect'=8,'bhi'=8,'blo'=8] {'bhi'}, use_global_device_ids=true, to_apply=%region_17.18 | all-reduce | flops 32 | bytes 256 | tf_op jit(solution)/shard_map/psum | solution.py:66
  301.9 4.6 %all-gather.33.cloned.1.call-done = bf16[1,2,16,128,128]{4,3,1,0,2:T(8,128)(2,1)} async-done(((bf16[1,2,2,128,128]{4,3,1,0,2:T(8,128)(2,1)}), bf16[1,2,16,128,128]{4,3,1,0,2:T(8,128)(2,1)}) %all-gather.33.cloned.1.call-update) | async-done | bytes 1048592 | tf_op jit(solution)/shard_map/all_gather | solution.py:61
  306.4 1.5 convolution_bitcast_fusion.1
  308.0 4.5 %collective-permute-start.6 = (f32[16,128]{1,0:T(8,128)S(1)}, f32[16,128]{1,0:T(8,128)S(1)}, u32[]{:S(2)}, u32[]{:S(2)}) collective-permute-start(f32[16,128]{1,0:T(8,128)S(1)} %slice_bitcast_fusion.14), channel_id=1, source_target_pairs={{0,8},{8,16},{16,24},{24,32},{32,40},{40,48},{48,56},{56,0},{1,9},... | collective-permute-start | bytes 24584 | tf_op jit(solution)/shard_map/ppermute | solution.py:67
  312.5 0.1 multiply_reduce_fusion.1
  312.6 22.0 %psum.62 = f32[2,16]{1,0:T(2,128)S(1)} all-reduce(f32[2,16]{1,0:T(2,128)S(1)} %pad_maximum_fusion.6), channel_id=1, replica_groups=mesh['sect'=8,'bhi'=8,'blo'=8] {'bhi'}, use_global_device_ids=true, to_apply=%region_20.21 | all-reduce | flops 32 | bytes 256 | tf_op jit(solution)/shard_map/psum | solution.py:66
  334.8 4.6 %all-gather.35.cloned.1.call-done = bf16[1,2,16,128,128]{4,3,1,0,2:T(8,128)(2,1)} async-done(((bf16[1,2,2,128,128]{4,3,1,0,2:T(8,128)(2,1)}), bf16[1,2,16,128,128]{4,3,1,0,2:T(8,128)(2,1)}) %all-gather.35.cloned.1.call-update) | async-done | bytes 1048592 | tf_op jit(solution)/shard_map/all_gather | solution.py:61
  339.4 1.5 convolution_bitcast_fusion
  340.9 0.1 fusion.17
  341.1 22.4 %psum.63 = f32[2,16]{1,0:T(2,128)S(1)} all-reduce(f32[2,16]{1,0:T(2,128)S(1)} %pad_maximum_fusion.7), channel_id=1, replica_groups=mesh['sect'=8,'bhi'=8,'blo'=8] {'bhi'}, use_global_device_ids=true, to_apply=%region_23.24 | all-reduce | flops 32 | bytes 256 | tf_op jit(solution)/shard_map/psum | solution.py:66
  363.7 12.8 %all_to_all.19 = f32[8,2,2]{2,1,0:T(2,128)S(1)} all-to-all(f32[8,2,2]{2,1,0:T(2,128)S(1)} %copy.161), channel_id=1, replica_groups=mesh['sect'=8,'bhi'=8,'blo'=8] {'sect'}, dimensions={0} | all-to-all | bytes 256 | tf_op jit(solution)/shard_map/all_to_all | solution.py:83
  376.5 0.6 squeeze.190
  377.1 0.6 squeeze.191
  (116 shorter events, 4.2 us)
Async XLA Ops:
  7.2 84.1 %copy-start = (bf16[16,16384]{1,0:T(8,128)(2,1)S(1)}, bf16[16,16384]{1,0:T(8,128)(2,1)}, u32[]{:S(2)}) copy-start(bf16[16,16384]{1,0:T(8,128)(2,1)} %param.6) | copy-start | bytes 1572868
  7.2 71.1 %all-gather.19.cloned.1.call-start = ((), (), s32[]{:S(2)}) async-start(), calls=%async_computation.3 | async-start | bytes 1179648 | tf_op jit(solution)/shard_map/all_gather | solution.py:43
  7.9 137.2 %all-gather.21.cloned.1.call-start = ((), (), s32[]{:S(2)}) async-start(), calls=%async_computation.4 | async-start | bytes 1179648 | tf_op jit(solution)/shard_map/all_gather | solution.py:61
  80.3 92.0 %all-gather.23.cloned.1.call-start = ((), (), s32[]{:S(2)}) async-start(), calls=%async_computation.5 | async-start | bytes 1179648 | tf_op jit(solution)/shard_map/all_gather | solution.py:61
  81.0 115.2 %all-gather.25.cloned.1.call-start = ((), (), s32[]{:S(2)}) async-start(), calls=%async_computation.6 | async-start | bytes 1179648 | tf_op jit(solution)/shard_map/all_gather | solution.py:61
  81.8 138.5 %all-gather.27.cloned.1.call-start = ((), (), s32[]{:S(2)}) async-start(), calls=%async_computation.7 | async-start | bytes 1179648 | tf_op jit(solution)/shard_map/all_gather | solution.py:61
  82.5 161.6 %all-gather.29.cloned.1.call-start = ((), (), s32[]{:S(2)}) async-start(), calls=%async_computation.8 | async-start | bytes 1179648 | tf_op jit(solution)/shard_map/all_gather | solution.py:61
  83.2 190.3 %all-gather.31.cloned.1.call-start = ((), (), s32[]{:S(2)}) async-start(), calls=%async_computation.9 | async-start | bytes 1179648 | tf_op jit(solution)/shard_map/all_gather | solution.py:61
  84.0 222.5 %all-gather.33.cloned.1.call-start = ((), (), s32[]{:S(2)}) async-start(), calls=%async_computation.10 | async-start | bytes 1179648 | tf_op jit(solution)/shard_map/all_gather | solution.py:61
  84.7 0.7 copy-start.2
  86.7 10.7 %all-to-all-start = ((s32[8,1,2]{2,1,0:T(1,128)}), s32[8,1,2]{2,1,0:T(1,128)S(1)}, u32[]{:S(2)}, u32[]{:S(2)}) async-start(s32[8,1,2]{2,1,0:T(1,128)} %bitcast), calls=%async_computation | async-start | bytes 8192 | tf_op jit(solution)/shard_map/all_to_all | solution.py:46
  91.3 0.7 copy-start.1
  97.4 46.8 %all-to-all-start.1 = ((bf16[2,8,16,128]{3,2,0,1:T(8,128)(2,1)}), bf16[2,8,16,128]{3,2,0,1:T(8,128)(2,1)S(1)}, u32[]{:S(2)}, u32[]{:S(2)}) async-start(bf16[2,8,16,128]{3,2,0,1:T(8,128)(2,1)} %copy.130), calls=%async_computation.1 | async-start | bytes 131072 | tf_op jit(solution)/shard_map/all_to_all | solution.py:52
  109.6 229.8 %all-gather.35.cloned.1.call-start = ((), (), s32[]{:S(2)}) async-start(), calls=%async_computation.11 | async-start | bytes 1179648 | tf_op jit(solution)/shard_map/all_gather | solution.py:61
  164.5 7.6 %collective-permute-start = (f32[16,128]{1,0:T(8,128)S(1)}, f32[16,128]{1,0:T(8,128)S(1)}, u32[]{:S(2)}, u32[]{:S(2)}) collective-permute-start(f32[16,128]{1,0:T(8,128)S(1)} %slice_bitcast_fusion.20), channel_id=1, source_target_pairs={{0,8},{8,16},{16,24},{24,32},{32,40},{40,48},{48,56},{56,0},{1,9},... | collective-permute-start | bytes 24584 | tf_op jit(solution)/shard_map/ppermute | solution.py:67
  174.0 22.1 %collective-permute-start.1 = (f32[16,128]{1,0:T(8,128)S(1)}, f32[16,128]{1,0:T(8,128)S(1)}, u32[]{:S(2)}, u32[]{:S(2)}) collective-permute-start(f32[16,128]{1,0:T(8,128)S(1)} %slice_bitcast_fusion.19), channel_id=1, source_target_pairs={{0,8},{8,16},{16,24},{24,32},{32,40},{40,48},{48,56},{56,0},{1,9},... | collective-permute-start | bytes 24584 | tf_op jit(solution)/shard_map/ppermute | solution.py:67
  198.0 22.1 %collective-permute-start.2 = (f32[16,128]{1,0:T(8,128)S(1)}, f32[16,128]{1,0:T(8,128)S(1)}, u32[]{:S(2)}, u32[]{:S(2)}) collective-permute-start(f32[16,128]{1,0:T(8,128)S(1)} %slice_bitcast_fusion.18), channel_id=1, source_target_pairs={{0,8},{8,16},{16,24},{24,32},{32,40},{40,48},{48,56},{56,0},{1,9},... | collective-permute-start | bytes 24584 | tf_op jit(solution)/shard_map/ppermute | solution.py:67
  221.9 22.1 %collective-permute-start.3 = (f32[16,128]{1,0:T(8,128)S(1)}, f32[16,128]{1,0:T(8,128)S(1)}, u32[]{:S(2)}, u32[]{:S(2)}) collective-permute-start(f32[16,128]{1,0:T(8,128)S(1)} %slice_bitcast_fusion.17), channel_id=1, source_target_pairs={{0,8},{8,16},{16,24},{24,32},{32,40},{40,48},{48,56},{56,0},{1,9},... | collective-permute-start | bytes 24584 | tf_op jit(solution)/shard_map/ppermute | solution.py:67
  245.8 23.0 %collective-permute-start.4 = (f32[16,128]{1,0:T(8,128)S(1)}, f32[16,128]{1,0:T(8,128)S(1)}, u32[]{:S(2)}, u32[]{:S(2)}) collective-permute-start(f32[16,128]{1,0:T(8,128)S(1)} %slice_bitcast_fusion.16), channel_id=1, source_target_pairs={{0,8},{8,16},{16,24},{24,32},{32,40},{40,48},{48,56},{56,0},{1,9},... | collective-permute-start | bytes 24584 | tf_op jit(solution)/shard_map/ppermute | solution.py:67
  275.2 26.5 %collective-permute-start.5 = (f32[16,128]{1,0:T(8,128)S(1)}, f32[16,128]{1,0:T(8,128)S(1)}, u32[]{:S(2)}, u32[]{:S(2)}) collective-permute-start(f32[16,128]{1,0:T(8,128)S(1)} %slice_bitcast_fusion.15), channel_id=1, source_target_pairs={{0,8},{8,16},{16,24},{24,32},{32,40},{40,48},{48,56},{56,0},{1,9},... | collective-permute-start | bytes 24584 | tf_op jit(solution)/shard_map/ppermute | solution.py:67
  308.0 26.7 %collective-permute-start.6 = (f32[16,128]{1,0:T(8,128)S(1)}, f32[16,128]{1,0:T(8,128)S(1)}, u32[]{:S(2)}, u32[]{:S(2)}) collective-permute-start(f32[16,128]{1,0:T(8,128)S(1)} %slice_bitcast_fusion.14), channel_id=1, source_target_pairs={{0,8},{8,16},{16,24},{24,32},{32,40},{40,48},{48,56},{56,0},{1,9},... | collective-permute-start | bytes 24584 | tf_op jit(solution)/shard_map/ppermute | solution.py:67
Sparse Core Ops, SparseCore 0:
  11.2 66.9 all-gather.18
  80.4 28.6 all-gather.20
  111.3 31.0 all-gather.22
  144.3 30.7 all-gather.24
  177.1 30.7 all-gather.26
  209.9 30.6 all-gather.28
  242.8 30.6 all-gather.30
  275.6 30.7 all-gather.32
  308.6 30.7 all-gather.34

commit v5 on v4

--- a/solution.py
+++ b/solution.py
@@ -42,16 +42,17 @@
 
     slabs = lax.all_gather(tensors[0], "sect", axis=0, tiled=False)
 
-    pieces = bits[0].reshape(n_sect, pick)
-    pieces = lax.all_to_all(pieces, "sect", 0, 0, tiled=False)
-    carried_bits = lax.all_gather(pieces, "bhi", axis=0, tiled=False)
-    carried_bits = jnp.transpose(carried_bits, (1, 0, 2)).reshape(sites, n_hi * pick)
+    pieces = lax.all_to_all(bits[0].reshape(n_sect, pick), "sect", 0, 0, tiled=False)
+    row_bits = jnp.transpose(pieces).astype(left.dtype)
 
     rows = lax.dynamic_slice_in_dim(left, sect * pick, pick, 0)
-    ordered = charge_order(labels, rows, block).reshape(pick, n_hi, mine, block)
-    spread = lax.all_to_all(ordered, "bhi", 1, 1, tiled=False)
+    ordered = charge_order(labels, rows, block).reshape(pick, n_hi, mine * block)
+    tagged = jnp.broadcast_to(row_bits[:, None, :], (pick, n_hi, sites))
+    spread = lax.all_to_all(jnp.concatenate([ordered, tagged], axis=2), "bhi", 1, 1, tiled=False)
     count_rows = n_hi * pick
-    state = jnp.transpose(spread, (1, 0, 2, 3)).reshape(count_rows, mine, block).astype(jnp.float32)
+    spread = jnp.transpose(spread, (1, 0, 2)).reshape(count_rows, mine * block + sites)
+    state = spread[:, : mine * block].reshape(count_rows, mine, block).astype(jnp.float32)
+    carried_bits = jnp.transpose(spread[:, mine * block :])
 
     total = jnp.zeros((count_rows,), jnp.float32)
     shift = [(q, (q + 1) % n_hi) for q in range(n_hi)]

time: 385 us -> 385 us (level)
  blocking collectives: 211 us -> 183 us
  waiting for transfers between devices: 94.2 us -> 113 us
  starting transfers between devices: 36.9 us -> 44.9 us
    all_gather x1 -> x0, blocking collectives: 32.3 us -> none  [body(): carried_bits = lax.all_gather(pieces, 'bhi', axis=0, tiled=False)]
    all_to_all x2, waiting for transfers between devices: 4.76 us -> 18.5 us  [the longest x1 13.4 us: body(): lax.all_to_all(jnp.concatenate([ordered, tagged], axis=2), 'bhi', 1, 1, t...]
    ppermute x7, starting transfers between devices: 19.8 us -> 27.8 us  [body(): came = lax.ppermute(rise[:, mine - 1], 'bhi', shift)]
    all_gather x8, waiting for transfers between devices: 13.8 us -> 19.5 us  [body(): weights = lax.all_gather(slabs[site], 'blo', axis=1, tiled=True)]
    psum x8, blocking collectives: 165 us -> 170 us  [body(): norms = lax.psum(part, 'bhi')]
  transfers between devices with their start and end apart: 18 -> 18, of which waited for: 6 -> 9; matrix products, arithmetic and copies ran while one was open for 6% -> 6% of each run, Pallas kernels for 0% -> 0%
where the time goes in v5:
time: 385 us; the launch traced here: 384 us
  blocking collectives  183 us (48%)
  waiting for transfers between devices  113 us (29%)
  starting transfers between devices  44.9 us (12%)
  between operations  14.5 us (4%)
  local copies, waits for them, and re-layouts  13.3 us (3%)
  matrix products  12.2 us (3%)
    psum x8, blocking collectives, body(): norms = lax.psum(part, 'bhi')  170 us
    all_gather x1, waiting for transfers between devices, body(): slabs = lax.all_gather(tensors[0], 'sect', axis=0, tiled=False)  70.3 us
    ppermute x7, starting transfers between devices, body(): came = lax.ppermute(rise[:, mine - 1], 'bhi', shift)  27.8 us
    all_gather x8, waiting for transfers between devices, body(): weights = lax.all_gather(slabs[site], 'blo', axis=1, tiled=True)  19.5 us
    all_to_all x1, waiting for transfers between devices, body(): lax.all_to_all(jnp.concatenate([ordered, tagged], axis=2), 'bhi', 1, 1, t...  13.4 us
    all_to_all x1, blocking collectives, body(): back = lax.all_to_all(result, 'sect', 0, 0, tiled=False)  12.8 us
    all_to_all x1, starting transfers between devices, body(): lax.all_to_all(jnp.concatenate([ordered, tagged], axis=2), 'bhi', 1, 1, t...  12.2 us
    dot_general x8, matrix products, site_images(): jnp.einsum('rck,bckl->brcl', parts, weights, preferred_element_type=jnp.f...  12 us
  transfers between devices with their start and end apart: 18, of which 9 were waited for; matrix products, arithmetic and copies ran while one was open for 6% of the time, Pallas kernels for 0%

profile of v5, /device:TPU:2, one launch (start us, length us, event | category | flops | bytes accessed | tf_op | source)
XLA Modules:
  0.0 384.1 jit_solution(10083996544783171045)
XLA Ops:
  7.2 0.7 all-gather.18.cloned.1.call-update
  8.0 70.3 %all-gather.18.cloned.1.call-done = bf16[8,2,2,128,128]{4,3,2,1,0:T(8,128)(2,1)} async-done(((bf16[1,2,2,128,128]{4,3,2,1,0:T(8,128)(2,1)}), bf16[8,2,2,128,128]{4,3,2,1,0:T(8,128)(2,1)}) %all-gather.18.cloned.1.call-update) | async-done | bytes 1048592 | tf_op jit(solution)/shard_map/all_gather | solution.py:43
  78.2 1.4 fusion.62
  79.6 0.7 copy.120
  80.3 0.7 copy.123
  81.1 0.7 copy.126
  81.8 0.6 copy.129
  82.5 0.7 copy.132
  83.3 0.6 copy.135
  84.0 0.7 copy.138
  84.7 0.5 broadcast.258
  85.4 0.7 reduce.55
  86.0 0.7 all_to_all.12
  86.7 4.5 %all-to-all-start = ((s32[8,1,2]{2,1,0:T(1,128)}), s32[8,1,2]{2,1,0:T(1,128)S(1)}, u32[]{:S(2)}, u32[]{:S(2)}) async-start(s32[8,1,2]{2,1,0:T(1,128)} %bitcast.2), calls=%async_computation | async-start | bytes 8192 | tf_op jit(solution)/shard_map/all_to_all | solution.py:45
  91.3 0.6 copy-done.1
  91.9 0.2 fusion
  92.3 5.2 %all-to-all-done = s32[8,1,2]{2,1,0:T(1,128)S(1)} async-done(((s32[8,1,2]{2,1,0:T(1,128)}), s32[8,1,2]{2,1,0:T(1,128)S(1)}, u32[]{:S(2)}, u32[]{:S(2)}) %all-to-all-start) | async-done | bytes 96 | tf_op jit(solution)/shard_map/all_to_all | solution.py:45
  97.5 0.7 copy.117
  98.2 12.2 %all-to-all-start.1 = ((bf16[2,8,2056]{2,0,1:T(2,128)(2,1)}), bf16[2,8,2056]{2,0,1:T(2,128)(2,1)S(1)}, u32[]{:S(2)}, u32[]{:S(2)}) async-start(bf16[2,8,2056]{2,0,1:T(2,128)(2,1)} %copy.117), calls=%async_computation.1 | async-start | bytes 139264 | tf_op jit(solution)/shard_map/all_to_all | solution.py:51
  110.5 13.4 %all-to-all-done.1 = bf16[2,8,2056]{2,0,1:T(2,128)(2,1)S(1)} async-done(((bf16[2,8,2056]{2,0,1:T(2,128)(2,1)}), bf16[2,8,2056]{2,0,1:T(2,128)(2,1)S(1)}, u32[]{:S(2)}, u32[]{:S(2)}) %all-to-all-start.1) | async-done | bytes 65824 | tf_op jit(solution)/shard_map/all_to_all | solution.py:51
  123.9 0.3 fusion.53
  124.2 0.7 copy.141
  124.9 1.5 convolution_bitcast_fusion.7
  126.5 0.1 multiply_reduce_fusion.13
  126.7 17.1 %psum.56 = f32[2,16]{0,1:T(8,128)S(1)} all-reduce(f32[2,16]{0,1:T(8,128)S(1)} %copy.122), channel_id=1, replica_groups=mesh['sect'=8,'bhi'=8,'blo'=8] {'bhi'}, use_global_device_ids=true, to_apply=%region_2.0 | all-reduce | flops 32 | bytes 256 | tf_op jit(solution)/shard_map/psum | solution.py:67
  143.8 0.2 slice_reduce_fusion.12
  144.0 4.0 %collective-permute-start = (f32[16,128]{1,0:T(8,128)S(1)}, f32[16,128]{1,0:T(8,128)S(1)}, u32[]{:S(2)}, u32[]{:S(2)}) collective-permute-start(f32[16,128]{1,0:T(8,128)S(1)} %slice_bitcast_fusion.20), channel_id=1, source_target_pairs={{0,8},{8,16},{16,24},{24,32},{32,40},{40,48},{48,56},{56,0},{1,9},... | collective-permute-start | bytes 24584 | tf_op jit(solution)/shard_map/ppermute | solution.py:68
  148.0 3.6 collective-permute-done
  151.8 1.5 convolution_bitcast_fusion.6
  153.4 0.1 multiply_reduce_fusion.11
  153.5 2.9 collective-permute-start.1
  156.5 19.4 %psum.57 = f32[2,16]{0,1:T(8,128)S(1)} all-reduce(f32[2,16]{0,1:T(8,128)S(1)} %copy.125), channel_id=1, replica_groups=mesh['sect'=8,'bhi'=8,'blo'=8] {'bhi'}, use_global_device_ids=true, to_apply=%region_5.6 | all-reduce | flops 32 | bytes 256 | tf_op jit(solution)/shard_map/psum | solution.py:67
  175.8 0.2 slice_reduce_fusion.10
  176.2 1.5 convolution_bitcast_fusion.5
  177.8 0.1 multiply_reduce_fusion.9
  177.9 3.1 collective-permute-start.2
  181.1 22.3 %psum.58 = f32[2,16]{0,1:T(8,128)S(1)} all-reduce(f32[2,16]{0,1:T(8,128)S(1)} %copy.128), channel_id=1, replica_groups=mesh['sect'=8,'bhi'=8,'blo'=8] {'bhi'}, use_global_device_ids=true, to_apply=%region_8.9 | all-reduce | flops 32 | bytes 256 | tf_op jit(solution)/shard_map/psum | solution.py:67
  203.4 0.2 slice_reduce_fusion.8
  203.7 3.7 all-gather.26.cloned.1.call-done
  207.4 1.5 convolution_bitcast_fusion.4
  209.1 4.4 %collective-permute-start.3 = (f32[16,128]{1,0:T(8,128)S(1)}, f32[16,128]{1,0:T(8,128)S(1)}, u32[]{:S(2)}, u32[]{:S(2)}) collective-permute-start(f32[16,128]{1,0:T(8,128)S(1)} %slice_bitcast_fusion.17), channel_id=1, source_target_pairs={{0,8},{8,16},{16,24},{24,32},{32,40},{40,48},{48,56},{56,0},{1,9},... | collective-permute-start | bytes 24584 | tf_op jit(solution)/shard_map/ppermute | solution.py:68
  213.6 22.3 %psum.59 = f32[2,16]{0,1:T(8,128)S(1)} all-reduce(f32[2,16]{0,1:T(8,128)S(1)} %copy.131), channel_id=1, replica_groups=mesh['sect'=8,'bhi'=8,'blo'=8] {'bhi'}, use_global_device_ids=true, to_apply=%region_11.12 | all-reduce | flops 32 | bytes 256 | tf_op jit(solution)/shard_map/psum | solution.py:67
  236.0 0.2 slice_reduce_fusion.6
  236.3 3.9 %all-gather.28.cloned.1.call-done = bf16[1,2,16,128,128]{4,3,1,0,2:T(8,128)(2,1)} async-done(((bf16[1,2,2,128,128]{4,3,1,0,2:T(8,128)(2,1)}), bf16[1,2,16,128,128]{4,3,1,0,2:T(8,128)(2,1)}) %all-gather.28.cloned.1.call-update) | async-done | bytes 1048592 | tf_op jit(solution)/shard_map/all_gather | solution.py:62
  240.2 1.5 convolution_bitcast_fusion.3
  241.9 4.5 %collective-permute-start.4 = (f32[16,128]{1,0:T(8,128)S(1)}, f32[16,128]{1,0:T(8,128)S(1)}, u32[]{:S(2)}, u32[]{:S(2)}) collective-permute-start(f32[16,128]{1,0:T(8,128)S(1)} %slice_bitcast_fusion.16), channel_id=1, source_target_pairs={{0,8},{8,16},{16,24},{24,32},{32,40},{40,48},{48,56},{56,0},{1,9},... | collective-permute-start | bytes 24584 | tf_op jit(solution)/shard_map/ppermute | solution.py:68
  246.5 22.2 %psum.60 = f32[2,16]{0,1:T(8,128)S(1)} all-reduce(f32[2,16]{0,1:T(8,128)S(1)} %copy.134), channel_id=1, replica_groups=mesh['sect'=8,'bhi'=8,'blo'=8] {'bhi'}, use_global_device_ids=true, to_apply=%region_14.15 | all-reduce | flops 32 | bytes 256 | tf_op jit(solution)/shard_map/psum | solution.py:67
  268.7 0.2 slice_reduce_fusion.4
  269.1 3.9 %all-gather.30.cloned.1.call-done = bf16[1,2,16,128,128]{4,3,1,0,2:T(8,128)(2,1)} async-done(((bf16[1,2,2,128,128]{4,3,1,0,2:T(8,128)(2,1)}), bf16[1,2,16,128,128]{4,3,1,0,2:T(8,128)(2,1)}) %all-gather.30.cloned.1.call-update) | async-done | bytes 1048592 | tf_op jit(solution)/shard_map/all_gather | solution.py:62
  273.0 1.5 convolution_bitcast_fusion.2
  274.7 4.5 %collective-permute-start.5 = (f32[16,128]{1,0:T(8,128)S(1)}, f32[16,128]{1,0:T(8,128)S(1)}, u32[]{:S(2)}, u32[]{:S(2)}) collective-permute-start(f32[16,128]{1,0:T(8,128)S(1)} %slice_bitcast_fusion.15), channel_id=1, source_target_pairs={{0,8},{8,16},{16,24},{24,32},{32,40},{40,48},{48,56},{56,0},{1,9},... | collective-permute-start | bytes 24584 | tf_op jit(solution)/shard_map/ppermute | solution.py:68
  279.3 22.2 %psum.61 = f32[2,16]{0,1:T(8,128)S(1)} all-reduce(f32[2,16]{0,1:T(8,128)S(1)} %copy.137), channel_id=1, replica_groups=mesh['sect'=8,'bhi'=8,'blo'=8] {'bhi'}, use_global_device_ids=true, to_apply=%region_17.18 | all-reduce | flops 32 | bytes 256 | tf_op jit(solution)/shard_map/psum | solution.py:67
  301.5 0.2 slice_reduce_fusion.2
  301.9 3.9 %all-gather.32.cloned.1.call-done = bf16[1,2,16,128,128]{4,3,1,0,2:T(8,128)(2,1)} async-done(((bf16[1,2,2,128,128]{4,3,1,0,2:T(8,128)(2,1)}), bf16[1,2,16,128,128]{4,3,1,0,2:T(8,128)(2,1)}) %all-gather.32.cloned.1.call-update) | async-done | bytes 1048592 | tf_op jit(solution)/shard_map/all_gather | solution.py:62
  305.8 1.5 convolution_bitcast_fusion.1
  307.4 4.5 %collective-permute-start.6 = (f32[16,128]{1,0:T(8,128)S(1)}, f32[16,128]{1,0:T(8,128)S(1)}, u32[]{:S(2)}, u32[]{:S(2)}) collective-permute-start(f32[16,128]{1,0:T(8,128)S(1)} %slice_bitcast_fusion.14), channel_id=1, source_target_pairs={{0,8},{8,16},{16,24},{24,32},{32,40},{40,48},{48,56},{56,0},{1,9},... | collective-permute-start | bytes 24584 | tf_op jit(solution)/shard_map/ppermute | solution.py:68
  312.1 22.2 %psum.62 = f32[2,16]{0,1:T(8,128)S(1)} all-reduce(f32[2,16]{0,1:T(8,128)S(1)} %copy.140), channel_id=1, replica_groups=mesh['sect'=8,'bhi'=8,'blo'=8] {'bhi'}, use_global_device_ids=true, to_apply=%region_20.21 | all-reduce | flops 32 | bytes 256 | tf_op jit(solution)/shard_map/psum | solution.py:67
  334.3 0.2 slice_reduce_fusion
  334.7 3.9 %all-gather.34.cloned.1.call-done = bf16[1,2,16,128,128]{4,3,1,0,2:T(8,128)(2,1)} async-done(((bf16[1,2,2,128,128]{4,3,1,0,2:T(8,128)(2,1)}), bf16[1,2,16,128,128]{4,3,1,0,2:T(8,128)(2,1)}) %all-gather.34.cloned.1.call-update) | async-done | bytes 1048592 | tf_op jit(solution)/shard_map/all_gather | solution.py:62
  338.6 1.5 convolution_bitcast_fusion
  340.4 22.6 %psum.63 = f32[2,16]{0,1:T(8,128)S(1)} all-reduce(f32[2,16]{0,1:T(8,128)S(1)} %copy.142), channel_id=1, replica_groups=mesh['sect'=8,'bhi'=8,'blo'=8] {'bhi'}, use_global_device_ids=true, to_apply=%region_23.24 | all-reduce | flops 32 | bytes 256 | tf_op jit(solution)/shard_map/psum | solution.py:67
  363.5 12.8 %all_to_all.19 = f32[8,2,2]{2,1,0:T(2,128)S(1)} all-to-all(f32[8,2,2]{2,1,0:T(2,128)S(1)} %copy.145), channel_id=1, replica_groups=mesh['sect'=8,'bhi'=8,'blo'=8] {'sect'}, dimensions={0} | all-to-all | bytes 256 | tf_op jit(solution)/shard_map/all_to_all | solution.py:84
  376.4 0.6 squeeze.190
  377.0 0.6 squeeze.191
  (114 shorter events, 4.4 us)
Async XLA Ops:
  7.2 84.1 %copy-start = (bf16[16,16384]{1,0:T(8,128)(2,1)S(1)}, bf16[16,16384]{1,0:T(8,128)(2,1)}, u32[]{:S(2)}) copy-start(bf16[16,16384]{1,0:T(8,128)(2,1)} %param.6) | copy-start | bytes 1572868
  7.2 71.1 %all-gather.18.cloned.1.call-start = ((), (), s32[]{:S(2)}) async-start(), calls=%async_computation.3 | async-start | bytes 1179648 | tf_op jit(solution)/shard_map/all_gather | solution.py:43
  7.9 117.0 %all-gather.20.cloned.1.call-start = ((), (), s32[]{:S(2)}) async-start(), calls=%async_computation.4 | async-start | bytes 1179648 | tf_op jit(solution)/shard_map/all_gather | solution.py:62
  80.3 71.5 %all-gather.22.cloned.1.call-start = ((), (), s32[]{:S(2)}) async-start(), calls=%async_computation.5 | async-start | bytes 1179648 | tf_op jit(solution)/shard_map/all_gather | solution.py:62
  81.0 95.2 %all-gather.24.cloned.1.call-start = ((), (), s32[]{:S(2)}) async-start(), calls=%async_computation.6 | async-start | bytes 1179648 | tf_op jit(solution)/shard_map/all_gather | solution.py:62
  81.8 125.6 %all-gather.26.cloned.1.call-start = ((), (), s32[]{:S(2)}) async-start(), calls=%async_computation.7 | async-start | bytes 1179648 | tf_op jit(solution)/shard_map/all_gather | solution.py:62
  82.5 157.7 %all-gather.28.cloned.1.call-start = ((), (), s32[]{:S(2)}) async-start(), calls=%async_computation.8 | async-start | bytes 1179648 | tf_op jit(solution)/shard_map/all_gather | solution.py:62
  83.2 189.8 %all-gather.30.cloned.1.call-start = ((), (), s32[]{:S(2)}) async-start(), calls=%async_computation.9 | async-start | bytes 1179648 | tf_op jit(solution)/shard_map/all_gather | solution.py:62
  84.0 221.8 %all-gather.32.cloned.1.call-start = ((), (), s32[]{:S(2)}) async-start(), calls=%async_computation.10 | async-start | bytes 1179648 | tf_op jit(solution)/shard_map/all_gather | solution.py:62
  84.7 0.7 copy-start.2
  86.7 10.7 %all-to-all-start = ((s32[8,1,2]{2,1,0:T(1,128)}), s32[8,1,2]{2,1,0:T(1,128)S(1)}, u32[]{:S(2)}, u32[]{:S(2)}) async-start(s32[8,1,2]{2,1,0:T(1,128)} %bitcast.2), calls=%async_computation | async-start | bytes 8192 | tf_op jit(solution)/shard_map/all_to_all | solution.py:45
  91.2 0.7 copy-start.1
  98.2 25.6 %all-to-all-start.1 = ((bf16[2,8,2056]{2,0,1:T(2,128)(2,1)}), bf16[2,8,2056]{2,0,1:T(2,128)(2,1)S(1)}, u32[]{:S(2)}, u32[]{:S(2)}) async-start(bf16[2,8,2056]{2,0,1:T(2,128)(2,1)} %copy.117), calls=%async_computation.1 | async-start | bytes 139264 | tf_op jit(solution)/shard_map/all_to_all | solution.py:51
  110.4 228.2 %all-gather.34.cloned.1.call-start = ((), (), s32[]{:S(2)}) async-start(), calls=%async_computation.11 | async-start | bytes 1179648 | tf_op jit(solution)/shard_map/all_gather | solution.py:62
  144.0 7.7 %collective-permute-start = (f32[16,128]{1,0:T(8,128)S(1)}, f32[16,128]{1,0:T(8,128)S(1)}, u32[]{:S(2)}, u32[]{:S(2)}) collective-permute-start(f32[16,128]{1,0:T(8,128)S(1)} %slice_bitcast_fusion.20), channel_id=1, source_target_pairs={{0,8},{8,16},{16,24},{24,32},{32,40},{40,48},{48,56},{56,0},{1,9},... | collective-permute-start | bytes 24584 | tf_op jit(solution)/shard_map/ppermute | solution.py:68
  153.5 22.5 %collective-permute-start.1 = (f32[16,128]{1,0:T(8,128)S(1)}, f32[16,128]{1,0:T(8,128)S(1)}, u32[]{:S(2)}, u32[]{:S(2)}) collective-permute-start(f32[16,128]{1,0:T(8,128)S(1)} %slice_bitcast_fusion.19), channel_id=1, source_target_pairs={{0,8},{8,16},{16,24},{24,32},{32,40},{40,48},{48,56},{56,0},{1,9},... | collective-permute-start | bytes 24584 | tf_op jit(solution)/shard_map/ppermute | solution.py:68
  177.9 25.7 %collective-permute-start.2 = (f32[16,128]{1,0:T(8,128)S(1)}, f32[16,128]{1,0:T(8,128)S(1)}, u32[]{:S(2)}, u32[]{:S(2)}) collective-permute-start(f32[16,128]{1,0:T(8,128)S(1)} %slice_bitcast_fusion.18), channel_id=1, source_target_pairs={{0,8},{8,16},{16,24},{24,32},{32,40},{40,48},{48,56},{56,0},{1,9},... | collective-permute-start | bytes 24584 | tf_op jit(solution)/shard_map/ppermute | solution.py:68
  209.1 27.1 %collective-permute-start.3 = (f32[16,128]{1,0:T(8,128)S(1)}, f32[16,128]{1,0:T(8,128)S(1)}, u32[]{:S(2)}, u32[]{:S(2)}) collective-permute-start(f32[16,128]{1,0:T(8,128)S(1)} %slice_bitcast_fusion.17), channel_id=1, source_target_pairs={{0,8},{8,16},{16,24},{24,32},{32,40},{40,48},{48,56},{56,0},{1,9},... | collective-permute-start | bytes 24584 | tf_op jit(solution)/shard_map/ppermute | solution.py:68
  241.9 27.0 %collective-permute-start.4 = (f32[16,128]{1,0:T(8,128)S(1)}, f32[16,128]{1,0:T(8,128)S(1)}, u32[]{:S(2)}, u32[]{:S(2)}) collective-permute-start(f32[16,128]{1,0:T(8,128)S(1)} %slice_bitcast_fusion.16), channel_id=1, source_target_pairs={{0,8},{8,16},{16,24},{24,32},{32,40},{40,48},{48,56},{56,0},{1,9},... | collective-permute-start | bytes 24584 | tf_op jit(solution)/shard_map/ppermute | solution.py:68
  274.7 27.0 %collective-permute-start.5 = (f32[16,128]{1,0:T(8,128)S(1)}, f32[16,128]{1,0:T(8,128)S(1)}, u32[]{:S(2)}, u32[]{:S(2)}) collective-permute-start(f32[16,128]{1,0:T(8,128)S(1)} %slice_bitcast_fusion.15), channel_id=1, source_target_pairs={{0,8},{8,16},{16,24},{24,32},{32,40},{40,48},{48,56},{56,0},{1,9},... | collective-permute-start | bytes 24584 | tf_op jit(solution)/shard_map/ppermute | solution.py:68
  307.4 27.2 %collective-permute-start.6 = (f32[16,128]{1,0:T(8,128)S(1)}, f32[16,128]{1,0:T(8,128)S(1)}, u32[]{:S(2)}, u32[]{:S(2)}) collective-permute-start(f32[16,128]{1,0:T(8,128)S(1)} %slice_bitcast_fusion.14), channel_id=1, source_target_pairs={{0,8},{8,16},{16,24},{24,32},{32,40},{40,48},{48,56},{56,0},{1,9},... | collective-permute-start | bytes 24584 | tf_op jit(solution)/shard_map/ppermute | solution.py:68
Sparse Core Ops, SparseCore 0:
  11.2 66.9 all-gather.17
  80.4 28.6 all-gather.19
  111.3 30.9 all-gather.21
  144.3 30.4 all-gather.23
  176.8 30.5 all-gather.25
  209.4 30.7 all-gather.27
  242.3 30.5 all-gather.29
  275.1 30.6 all-gather.31
  307.9 30.6 all-gather.33

commit v6 on v5

--- a/solution.py
+++ b/solution.py
@@ -58,8 +58,14 @@
     shift = [(q, (q + 1) % n_hi) for q in range(n_hi)]
     probs = []
     logs = []
+    batches = [[0]] + [list(range(k, min(k + 2, sites))) for k in range(1, sites, 2)]
+    gathered = {}
+    for batch in batches:
+        got = lax.all_gather(slabs[batch[0] : batch[-1] + 1], "blo", axis=2, tiled=True)
+        for index, site in enumerate(batch):
+            gathered[site] = got[index]
     for site in range(sites):
-        weights = lax.all_gather(slabs[site], "blo", axis=1, tiled=True)
+        weights = gathered[site]
         image = site_images(state, weights)
         stay = image[0]
         rise = image[1]

time: 385 us -> 335 us (0.87)
  the two profiles are of different devices: /device:TPU:2 before, /device:TPU:64 now
where the time goes in v6:
time: 335 us; the launch traced here: 334 us
  blocking collectives  147 us (44%)
  waiting for transfers between devices  91.8 us (27%)
  starting transfers between devices  56.3 us (17%)
  between operations  14.8 us (4%)
  local copies, waits for them, and re-layouts  11.6 us (3%)
  matrix products  8.97 us (3%)
  other arithmetic  3.4 us (1%)
    psum x8, blocking collectives, body(): norms = lax.psum(part, 'bhi')  135 us
    all_gather x1, waiting for transfers between devices, body(): slabs = lax.all_gather(tensors[0], 'sect', axis=0, tiled=False)  69.8 us
    ppermute x7, starting transfers between devices, body(): came = lax.ppermute(rise[:, mine - 1], 'bhi', shift)  39.8 us
    all_to_all x1, blocking collectives, body(): back = lax.all_to_all(result, 'sect', 0, 0, tiled=False)  12.6 us
    all_to_all x1, starting transfers between devices, body(): lax.all_to_all(jnp.concatenate([ordered, tagged], axis=2), 'bhi', 1, 1, t...  12.6 us
    all_to_all x1, waiting for transfers between devices, body(): lax.all_to_all(jnp.concatenate([ordered, tagged], axis=2), 'bhi', 1, 1, t...  11.3 us
    dot_general x8, matrix products, site_images(): jnp.einsum('rck,bckl->brcl', parts, weights, preferred_element_type=jnp.f...  8.78 us
    all_to_all x1, waiting for transfers between devices, body(): lax.all_to_all(bits[0].reshape(n_sect, pick), 'sect', 0, 0, tiled=False)  7.03 us
  transfers between devices with their start and end apart: 15, of which 4 were waited for; matrix products, arithmetic and copies ran while one was open for 5% of the time, Pallas kernels for 0%

profile of v6, /device:TPU:64, one launch (start us, length us, event | category | flops | bytes accessed | tf_op | source)
XLA Modules:
  0.0 334.0 jit_solution(12761818312474624732)
XLA Ops:
  7.2 0.7 all-gather.7.cloned.1.call-update
  8.0 69.8 %all-gather.7.cloned.1.call-done = bf16[8,2,2,128,128]{4,3,2,1,0:T(8,128)(2,1)} async-done(((bf16[1,2,2,128,128]{4,3,2,1,0:T(8,128)(2,1)}), bf16[8,2,2,128,128]{4,3,2,1,0:T(8,128)(2,1)}) %all-gather.7.cloned.1.call-update) | async-done | bytes 1048592 | tf_op jit(solution)/shard_map/all_gather | solution.py:43
  77.8 1.0 fusion.56
  78.7 0.7 copy.117
  79.5 1.2 fusion.57
  80.7 0.7 copy.150
  81.5 0.7 copy.153
  82.3 0.7 copy.156
  83.0 0.5 broadcast.258
  83.5 0.7 reduce.55
  84.2 0.7 all_to_all.12
  84.9 3.7 %all-to-all-start = ((s32[8,1,2]{2,1,0:T(1,128)}), s32[8,1,2]{2,1,0:T(1,128)S(1)}, u32[]{:S(2)}, u32[]{:S(2)}) async-start(s32[8,1,2]{2,1,0:T(1,128)} %bitcast.2), calls=%async_computation | async-start | bytes 8192 | tf_op jit(solution)/shard_map/all_to_all | solution.py:45
  88.7 0.2 fusion
  88.9 0.1 copy.111
  89.1 7.0 %all-to-all-done = s32[8,1,2]{2,1,0:T(1,128)S(1)} async-done(((s32[8,1,2]{2,1,0:T(1,128)}), s32[8,1,2]{2,1,0:T(1,128)S(1)}, u32[]{:S(2)}, u32[]{:S(2)}) %all-to-all-start) | async-done | bytes 96 | tf_op jit(solution)/shard_map/all_to_all | solution.py:45
  96.2 0.7 copy.114
  96.9 12.6 %all-to-all-start.1 = ((bf16[2,8,2056]{2,0,1:T(2,128)(2,1)}), bf16[2,8,2056]{2,0,1:T(2,128)(2,1)S(1)}, u32[]{:S(2)}, u32[]{:S(2)}) async-start(bf16[2,8,2056]{2,0,1:T(2,128)(2,1)} %copy.114), calls=%async_computation.1 | async-start | bytes 139264 | tf_op jit(solution)/shard_map/all_to_all | solution.py:51
  109.5 11.3 %all-to-all-done.1 = bf16[2,8,2056]{2,0,1:T(2,128)(2,1)S(1)} async-done(((bf16[2,8,2056]{2,0,1:T(2,128)(2,1)}), bf16[2,8,2056]{2,0,1:T(2,128)(2,1)S(1)}, u32[]{:S(2)}, u32[]{:S(2)}) %all-to-all-start.1) | async-done | bytes 65824 | tf_op jit(solution)/shard_map/all_to_all | solution.py:51
  120.8 0.3 fusion.47
  121.1 0.7 copy.135
  121.8 1.5 convolution_bitcast_fusion.7
  123.4 0.1 multiply_reduce_fusion.13
  123.6 18.6 %psum.56 = f32[2,16]{0,1:T(8,128)S(1)} all-reduce(f32[2,16]{0,1:T(8,128)S(1)} %copy.119), channel_id=1, replica_groups=mesh['sect'=8,'bhi'=8,'blo'=8] {'bhi'}, use_global_device_ids=true, to_apply=%region_2.0 | all-reduce | flops 32 | bytes 256 | tf_op jit(solution)/shard_map/psum | solution.py:73
  142.3 0.2 slice_reduce_fusion.12
  142.4 3.6 %collective-permute-start = (f32[16,128]{1,0:T(8,128)S(1)}, f32[16,128]{1,0:T(8,128)S(1)}, u32[]{:S(2)}, u32[]{:S(2)}) collective-permute-start(f32[16,128]{1,0:T(8,128)S(1)} %slice_bitcast_fusion.32), channel_id=1, source_target_pairs={{0,8},{8,16},{16,24},{24,32},{32,40},{40,48},{48,56},{56,0},{1,9},... | collective-permute-start | bytes 24584 | tf_op jit(solution)/shard_map/ppermute | solution.py:74
  146.1 2.8 collective-permute-done
  149.0 1.6 convolution_bitcast_fusion.6
  150.8 0.1 multiply_reduce_fusion.11
  150.9 4.8 %collective-permute-start.1 = (f32[16,128]{1,0:T(8,128)S(1)}, f32[16,128]{1,0:T(8,128)S(1)}, u32[]{:S(2)}, u32[]{:S(2)}) collective-permute-start(f32[16,128]{1,0:T(8,128)S(1)} %slice_bitcast_fusion.31), channel_id=1, source_target_pairs={{0,8},{8,16},{16,24},{24,32},{32,40},{40,48},{48,56},{56,0},{1,9},... | collective-permute-start | bytes 24584 | tf_op jit(solution)/shard_map/ppermute | solution.py:74
  155.8 16.2 %psum.57 = f32[2,16]{0,1:T(8,128)S(1)} all-reduce(f32[2,16]{0,1:T(8,128)S(1)} %copy.122), channel_id=1, replica_groups=mesh['sect'=8,'bhi'=8,'blo'=8] {'bhi'}, use_global_device_ids=true, to_apply=%region_5.6 | all-reduce | flops 32 | bytes 256 | tf_op jit(solution)/shard_map/psum | solution.py:73
  172.0 0.2 slice_reduce_fusion.10
  172.3 0.3 convolution_bitcast_fusion.5
  172.7 0.1 multiply_reduce_fusion.9
  172.8 6.1 %collective-permute-start.2 = (f32[16,128]{1,0:T(8,128)S(1)}, f32[16,128]{1,0:T(8,128)S(1)}, u32[]{:S(2)}, u32[]{:S(2)}) collective-permute-start(f32[16,128]{1,0:T(8,128)S(1)} %slice_bitcast_fusion.30), channel_id=1, source_target_pairs={{0,8},{8,16},{16,24},{24,32},{32,40},{40,48},{48,56},{56,0},{1,9},... | collective-permute-start | bytes 24584 | tf_op jit(solution)/shard_map/ppermute | solution.py:74
  179.1 15.9 %psum.58 = f32[2,16]{0,1:T(8,128)S(1)} all-reduce(f32[2,16]{0,1:T(8,128)S(1)} %copy.124), channel_id=1, replica_groups=mesh['sect'=8,'bhi'=8,'blo'=8] {'bhi'}, use_global_device_ids=true, to_apply=%region_8.9 | all-reduce | flops 32 | bytes 256 | tf_op jit(solution)/shard_map/psum | solution.py:73
  195.0 0.2 slice_reduce_fusion.8
  195.4 1.6 convolution_bitcast_fusion.4
  197.1 0.1 multiply_reduce_fusion.7
  197.2 6.3 %collective-permute-start.3 = (f32[16,128]{1,0:T(8,128)S(1)}, f32[16,128]{1,0:T(8,128)S(1)}, u32[]{:S(2)}, u32[]{:S(2)}) collective-permute-start(f32[16,128]{1,0:T(8,128)S(1)} %slice_bitcast_fusion.29), channel_id=1, source_target_pairs={{0,8},{8,16},{16,24},{24,32},{32,40},{40,48},{48,56},{56,0},{1,9},... | collective-permute-start | bytes 24584 | tf_op jit(solution)/shard_map/ppermute | solution.py:74
  203.6 16.0 %psum.59 = f32[2,16]{0,1:T(8,128)S(1)} all-reduce(f32[2,16]{0,1:T(8,128)S(1)} %copy.127), channel_id=1, replica_groups=mesh['sect'=8,'bhi'=8,'blo'=8] {'bhi'}, use_global_device_ids=true, to_apply=%region_11.12 | all-reduce | flops 32 | bytes 256 | tf_op jit(solution)/shard_map/psum | solution.py:73
  219.7 0.2 slice_reduce_fusion.6
  219.9 0.1 reduce-precision_convert_fusion.3
  220.0 0.3 convolution_bitcast_fusion.3
  220.4 0.1 multiply_reduce_fusion.5
  220.5 6.3 %collective-permute-start.4 = (f32[16,128]{1,0:T(8,128)S(1)}, f32[16,128]{1,0:T(8,128)S(1)}, u32[]{:S(2)}, u32[]{:S(2)}) collective-permute-start(f32[16,128]{1,0:T(8,128)S(1)} %slice_bitcast_fusion.28), channel_id=1, source_target_pairs={{0,8},{8,16},{16,24},{24,32},{32,40},{40,48},{48,56},{56,0},{1,9},... | collective-permute-start | bytes 24584 | tf_op jit(solution)/shard_map/ppermute | solution.py:74
  226.9 16.0 %psum.60 = f32[2,16]{0,1:T(8,128)S(1)} all-reduce(f32[2,16]{0,1:T(8,128)S(1)} %copy.129), channel_id=1, replica_groups=mesh['sect'=8,'bhi'=8,'blo'=8] {'bhi'}, use_global_device_ids=true, to_apply=%region_14.15 | all-reduce | flops 32 | bytes 256 | tf_op jit(solution)/shard_map/psum | solution.py:73
  242.9 0.2 slice_reduce_fusion.4
  243.3 1.7 convolution_bitcast_fusion.2
  245.0 0.1 multiply_reduce_fusion.3
  245.1 6.3 %collective-permute-start.5 = (f32[16,128]{1,0:T(8,128)S(1)}, f32[16,128]{1,0:T(8,128)S(1)}, u32[]{:S(2)}, u32[]{:S(2)}) collective-permute-start(f32[16,128]{1,0:T(8,128)S(1)} %slice_bitcast_fusion.27), channel_id=1, source_target_pairs={{0,8},{8,16},{16,24},{24,32},{32,40},{40,48},{48,56},{56,0},{1,9},... | collective-permute-start | bytes 24584 | tf_op jit(solution)/shard_map/ppermute | solution.py:74
  251.5 15.9 %psum.61 = f32[2,16]{0,1:T(8,128)S(1)} all-reduce(f32[2,16]{0,1:T(8,128)S(1)} %copy.132), channel_id=1, replica_groups=mesh['sect'=8,'bhi'=8,'blo'=8] {'bhi'}, use_global_device_ids=true, to_apply=%region_17.18 | all-reduce | flops 32 | bytes 256 | tf_op jit(solution)/shard_map/psum | solution.py:73
  267.5 0.2 slice_reduce_fusion.2
  267.8 0.3 convolution_bitcast_fusion.1
  268.1 6.3 %collective-permute-start.6 = (f32[16,128]{1,0:T(8,128)S(1)}, f32[16,128]{1,0:T(8,128)S(1)}, u32[]{:S(2)}, u32[]{:S(2)}) collective-permute-start(f32[16,128]{1,0:T(8,128)S(1)} %slice_bitcast_fusion.26), channel_id=1, source_target_pairs={{0,8},{8,16},{16,24},{24,32},{32,40},{40,48},{48,56},{56,0},{1,9},... | collective-permute-start | bytes 24584 | tf_op jit(solution)/shard_map/ppermute | solution.py:74
  274.5 0.1 multiply_reduce_fusion.1
  274.7 16.0 %psum.62 = f32[2,16]{0,1:T(8,128)S(1)} all-reduce(f32[2,16]{0,1:T(8,128)S(1)} %copy.134), channel_id=1, replica_groups=mesh['sect'=8,'bhi'=8,'blo'=8] {'bhi'}, use_global_device_ids=true, to_apply=%region_20.21 | all-reduce | flops 32 | bytes 256 | tf_op jit(solution)/shard_map/psum | solution.py:73
  290.7 0.2 slice_reduce_fusion
  291.1 1.5 convolution_bitcast_fusion
  292.6 0.1 fusion.12
  292.8 19.9 %psum.63 = f32[2,16]{0,1:T(8,128)S(1)} all-reduce(f32[2,16]{0,1:T(8,128)S(1)} %copy.136), channel_id=1, replica_groups=mesh['sect'=8,'bhi'=8,'blo'=8] {'bhi'}, use_global_device_ids=true, to_apply=%region_23.24 | all-reduce | flops 32 | bytes 256 | tf_op jit(solution)/shard_map/psum | solution.py:73
  312.8 0.1 log_add_fusion
  313.3 12.6 %all_to_all.19 = f32[8,2,2]{2,1,0:T(2,128)S(1)} all-to-all(f32[8,2,2]{2,1,0:T(2,128)S(1)} %copy.139), channel_id=1, replica_groups=mesh['sect'=8,'bhi'=8,'blo'=8] {'sect'}, dimensions={0} | all-to-all | bytes 256 | tf_op jit(solution)/shard_map/all_to_all | solution.py:90
  325.9 0.6 squeeze.190
  326.5 0.6 squeeze.191
  (109 shorter events, 3.1 us)
Async XLA Ops:
  7.2 81.5 %copy-start = (bf16[16,16384]{1,0:T(8,128)(2,1)S(1)}, bf16[16,16384]{1,0:T(8,128)(2,1)}, u32[]{:S(2)}) copy-start(bf16[16,16384]{1,0:T(8,128)(2,1)} %param.6) | copy-start | bytes 1572868
  7.2 70.6 %all-gather.7.cloned.1.call-start = ((), (), s32[]{:S(2)}) async-start(), calls=%async_computation.3 | async-start | bytes 1179648 | tf_op jit(solution)/shard_map/all_gather | solution.py:43
  7.9 113.9 %all-gather.9.cloned.1.call-start = ((), (), s32[]{:S(2)}) async-start(), calls=%async_computation.4 | async-start | bytes 1179648 | tf_op jit(solution)/shard_map/all_gather | solution.py:64
  79.4 4.1 %copy-start.5 = (s32[1,16]{1,0:T(1,128)S(1)}, s32[1,16]{1,0:T(1,128)}, u32[]{:S(2)}) copy-start(s32[1,16]{1,0:T(1,128)} %param.4) | copy-start | bytes 196
  79.4 9.3 %copy-start.4 = (s32[128]{0:T(128)S(1)}, s32[128]{0:T(128)}, u32[]{:S(2)}) copy-start(s32[128]{0:T(128)} %param.5) | copy-start | bytes 1540
  79.4 69.6 %all-gather.11.cloned.1.call-start = ((), (), s32[]{:S(2)}) async-start(), calls=%async_computation.5 | async-start | bytes 2359296 | tf_op jit(solution)/shard_map/all_gather | solution.py:64
  81.4 113.9 %all-gather.13.cloned.1.call-start = ((), (), s32[]{:S(2)}) async-start(), calls=%async_computation.6 | async-start | bytes 2359296 | tf_op jit(solution)/shard_map/all_gather | solution.py:64
  82.2 161.0 %all-gather.15.cloned.1.call-start = ((), (), s32[]{:S(2)}) async-start(), calls=%async_computation.7 | async-start | bytes 2359296 | tf_op jit(solution)/shard_map/all_gather | solution.py:64
  84.9 11.2 %all-to-all-start = ((s32[8,1,2]{2,1,0:T(1,128)}), s32[8,1,2]{2,1,0:T(1,128)S(1)}, u32[]{:S(2)}, u32[]{:S(2)}) async-start(s32[8,1,2]{2,1,0:T(1,128)} %bitcast.2), calls=%async_computation | async-start | bytes 8192 | tf_op jit(solution)/shard_map/all_to_all | solution.py:45
  96.9 23.8 %all-to-all-start.1 = ((bf16[2,8,2056]{2,0,1:T(2,128)(2,1)}), bf16[2,8,2056]{2,0,1:T(2,128)(2,1)S(1)}, u32[]{:S(2)}, u32[]{:S(2)}) async-start(bf16[2,8,2056]{2,0,1:T(2,128)(2,1)} %copy.114), calls=%async_computation.1 | async-start | bytes 139264 | tf_op jit(solution)/shard_map/all_to_all | solution.py:51
  109.5 181.6 %all-gather.17.cloned.1.call-start = ((), (), s32[]{:S(2)}) async-start(), calls=%async_computation.8 | async-start | bytes 1179648 | tf_op jit(solution)/shard_map/all_gather | solution.py:64
  142.4 6.4 %collective-permute-start = (f32[16,128]{1,0:T(8,128)S(1)}, f32[16,128]{1,0:T(8,128)S(1)}, u32[]{:S(2)}, u32[]{:S(2)}) collective-permute-start(f32[16,128]{1,0:T(8,128)S(1)} %slice_bitcast_fusion.32), channel_id=1, source_target_pairs={{0,8},{8,16},{16,24},{24,32},{32,40},{40,48},{48,56},{56,0},{1,9},... | collective-permute-start | bytes 24584 | tf_op jit(solution)/shard_map/ppermute | solution.py:74
  149.0 23.3 %copy-start.3 = (bf16[2,2,16,128,128]{4,3,1,2,0:T(8,128)(2,1)S(1)}, bf16[2,2,16,128,128]{4,3,1,2,0:T(8,128)(2,1)}, u32[]{:S(2)}) copy-start(bf16[2,2,16,128,128]{4,3,1,2,0:T(8,128)(2,1)} %all-gather.11.cloned.1.call-done) | copy-start | bytes 6291460
  150.9 21.3 %collective-permute-start.1 = (f32[16,128]{1,0:T(8,128)S(1)}, f32[16,128]{1,0:T(8,128)S(1)}, u32[]{:S(2)}, u32[]{:S(2)}) collective-permute-start(f32[16,128]{1,0:T(8,128)S(1)} %slice_bitcast_fusion.31), channel_id=1, source_target_pairs={{0,8},{8,16},{16,24},{24,32},{32,40},{40,48},{48,56},{56,0},{1,9},... | collective-permute-start | bytes 24584 | tf_op jit(solution)/shard_map/ppermute | solution.py:74
  172.8 22.4 %collective-permute-start.2 = (f32[16,128]{1,0:T(8,128)S(1)}, f32[16,128]{1,0:T(8,128)S(1)}, u32[]{:S(2)}, u32[]{:S(2)}) collective-permute-start(f32[16,128]{1,0:T(8,128)S(1)} %slice_bitcast_fusion.30), channel_id=1, source_target_pairs={{0,8},{8,16},{16,24},{24,32},{32,40},{40,48},{48,56},{56,0},{1,9},... | collective-permute-start | bytes 24584 | tf_op jit(solution)/shard_map/ppermute | solution.py:74
  195.4 24.7 %copy-start.2 = (bf16[2,2,16,128,128]{4,3,1,2,0:T(8,128)(2,1)S(1)}, bf16[2,2,16,128,128]{4,3,1,2,0:T(8,128)(2,1)}, u32[]{:S(2)}) copy-start(bf16[2,2,16,128,128]{4,3,1,2,0:T(8,128)(2,1)} %all-gather.13.cloned.1.call-done) | copy-start | bytes 6291460
  197.2 22.7 %collective-permute-start.3 = (f32[16,128]{1,0:T(8,128)S(1)}, f32[16,128]{1,0:T(8,128)S(1)}, u32[]{:S(2)}, u32[]{:S(2)}) collective-permute-start(f32[16,128]{1,0:T(8,128)S(1)} %slice_bitcast_fusion.29), channel_id=1, source_target_pairs={{0,8},{8,16},{16,24},{24,32},{32,40},{40,48},{48,56},{56,0},{1,9},... | collective-permute-start | bytes 24584 | tf_op jit(solution)/shard_map/ppermute | solution.py:74
  220.5 22.6 %collective-permute-start.4 = (f32[16,128]{1,0:T(8,128)S(1)}, f32[16,128]{1,0:T(8,128)S(1)}, u32[]{:S(2)}, u32[]{:S(2)}) collective-permute-start(f32[16,128]{1,0:T(8,128)S(1)} %slice_bitcast_fusion.28), channel_id=1, source_target_pairs={{0,8},{8,16},{16,24},{24,32},{32,40},{40,48},{48,56},{56,0},{1,9},... | collective-permute-start | bytes 24584 | tf_op jit(solution)/shard_map/ppermute | solution.py:74
  243.2 24.5 %copy-start.1 = (bf16[2,2,16,128,128]{4,3,1,2,0:T(8,128)(2,1)S(1)}, bf16[2,2,16,128,128]{4,3,1,2,0:T(8,128)(2,1)}, u32[]{:S(2)}) copy-start(bf16[2,2,16,128,128]{4,3,1,2,0:T(8,128)(2,1)} %all-gather.15.cloned.1.call-done) | copy-start | bytes 6291460
  245.1 22.6 %collective-permute-start.5 = (f32[16,128]{1,0:T(8,128)S(1)}, f32[16,128]{1,0:T(8,128)S(1)}, u32[]{:S(2)}, u32[]{:S(2)}) collective-permute-start(f32[16,128]{1,0:T(8,128)S(1)} %slice_bitcast_fusion.27), channel_id=1, source_target_pairs={{0,8},{8,16},{16,24},{24,32},{32,40},{40,48},{48,56},{56,0},{1,9},... | collective-permute-start | bytes 24584 | tf_op jit(solution)/shard_map/ppermute | solution.py:74
  268.1 22.8 %collective-permute-start.6 = (f32[16,128]{1,0:T(8,128)S(1)}, f32[16,128]{1,0:T(8,128)S(1)}, u32[]{:S(2)}, u32[]{:S(2)}) collective-permute-start(f32[16,128]{1,0:T(8,128)S(1)} %slice_bitcast_fusion.26), channel_id=1, source_target_pairs={{0,8},{8,16},{16,24},{24,32},{32,40},{40,48},{48,56},{56,0},{1,9},... | collective-permute-start | bytes 24584 | tf_op jit(solution)/shard_map/ppermute | solution.py:74
Sparse Core Ops, SparseCore 0:
  11.2 66.4 all-gather.6
  79.9 28.4 all-gather.8
  110.5 35.1 all-gather.10
  147.8 32.5 all-gather.12
  182.3 33.1 all-gather.14
  217.5 30.6 all-gather.16

commit v7 on v6

--- a/solution.py
+++ b/solution.py
@@ -46,7 +46,8 @@
     row_bits = jnp.transpose(pieces).astype(left.dtype)
 
     rows = lax.dynamic_slice_in_dim(left, sect * pick, pick, 0)
-    ordered = charge_order(labels, rows, block).reshape(pick, n_hi, mine * block)
+    ordered = charge_order(labels, rows, block).reshape(pick, n_lo, n_hi, mine // n_lo, block)
+    ordered = jnp.transpose(ordered, (0, 2, 1, 3, 4)).reshape(pick, n_hi, mine * block)
     tagged = jnp.broadcast_to(row_bits[:, None, :], (pick, n_hi, sites))
     spread = lax.all_to_all(jnp.concatenate([ordered, tagged], axis=2), "bhi", 1, 1, tiled=False)
     count_rows = n_hi * pick
@@ -71,8 +72,11 @@
         rise = image[1]
         part = jnp.stack([jnp.sum(stay * stay, axis=(1, 2)), jnp.sum(rise * rise, axis=(1, 2))])
         norms = lax.psum(part, "bhi")
-        came = lax.ppermute(rise[:, mine - 1], "bhi", shift)
-        raised = jnp.concatenate([came[:, None], rise[:, : mine - 1]], axis=1)
+        rise4 = rise.reshape(count_rows, n_lo, mine // n_lo, block)
+        send = rise4[:, :, mine // n_lo - 1]
+        send = jnp.where(bhi == n_hi - 1, jnp.roll(send, 1, axis=1), send)
+        came = lax.ppermute(send, "bhi", shift)
+        raised = jnp.stack([came, rise4[:, :, 0]], axis=2).reshape(count_rows, mine, block)
         norm_zero = norms[0]
         norm_one = norms[1]
         choose = carried_bits[site] == 1
@@ -94,8 +98,8 @@
 
 def solution(mesh):
     n_sect, n_blk = mesh.devices.shape
-    fine = Mesh(mesh.devices.reshape(n_sect, PARTS, n_blk // PARTS), ("sect", "bhi", "blo"))
-    blk = ("bhi", "blo")
+    fine = Mesh(mesh.devices.reshape(n_sect, n_blk // PARTS, PARTS), ("sect", "blo", "bhi"))
+    blk = ("blo", "bhi")
     in_specs = (P("sect", blk), P(), P(blk, None), P("sect", None, blk, None, None))
     out_specs = (P("sect", blk), P("sect", blk))
     return jax.shard_map(body, mesh=fine, in_specs=in_specs, out_specs=out_specs, check_vma=False)

time: 335 us -> 410 us (1.22)
  the two profiles are of different devices: /device:TPU:64 before, /device:TPU:1 now
where the time goes in v7:
time: 410 us; the launch traced here: 409 us
  waiting for transfers between devices  210 us (51%)
  blocking collectives  119 us (29%)
  starting transfers between devices  40.8 us (10%)
  between operations  14.9 us (4%)
  local copies, waits for them, and re-layouts  11.5 us (3%)
  matrix products  8.93 us (2%)
  other arithmetic  4.41 us (1%)
    all_gather x5, waiting for transfers between devices, body(): lax.all_gather(slabs[batch[0]:batch[-1] + 1], 'blo', axis=2, tiled=True)  126 us
    psum x8, blocking collectives, body(): norms = lax.psum(part, 'bhi')  105 us
    all_gather x1, waiting for transfers between devices, body(): slabs = lax.all_gather(tensors[0], 'sect', axis=0, tiled=False)  70.5 us
    ppermute x7, starting transfers between devices, body(): came = lax.ppermute(send, 'bhi', shift)  30.5 us
    all_to_all x1, blocking collectives, body(): back = lax.all_to_all(result, 'sect', 0, 0, tiled=False)  13.8 us
    dot_general x8, matrix products, site_images(): jnp.einsum('rck,bckl->brcl', parts, weights, preferred_element_type=jnp.f...  8.77 us
  transfers between devices with their start and end apart: 15, of which 9 were waited for; matrix products, arithmetic and copies ran while one was open for 5% of the time, Pallas kernels for 0%

profile of v7, /device:TPU:1, one launch (start us, length us, event | category | flops | bytes accessed | tf_op | source)
XLA Modules:
  0.0 409.0 jit_solution(703974313832476605)
XLA Ops:
  7.2 0.7 all-gather.7.cloned.1.call-update
  8.0 70.5 %all-gather.7.cloned.1.call-done = bf16[8,2,2,128,128]{4,3,2,1,0:T(8,128)(2,1)} async-done(((bf16[1,2,2,128,128]{4,3,2,1,0:T(8,128)(2,1)}), bf16[8,2,2,128,128]{4,3,2,1,0:T(8,128)(2,1)}) %all-gather.7.cloned.1.call-update) | async-done | bytes 1048592 | tf_op jit(solution)/shard_map/all_gather | solution.py:43
  78.4 1.0 fusion.55
  79.4 0.7 copy.161
  80.1 1.2 fusion.56
  81.3 0.7 copy.205
  82.1 0.7 copy.210
  82.9 0.7 copy.215
  83.7 0.5 broadcast.258
  84.2 0.7 reduce.62
  84.9 0.7 all_to_all.12
  85.5 3.3 all-to-all-start
  89.0 0.2 convolution_convert_fusion
  89.2 6.1 %all-to-all-done = s32[8,1,2]{2,1,0:T(1,128)S(1)} async-done(((s32[8,1,2]{2,1,0:T(1,128)}), s32[8,1,2]{2,1,0:T(1,128)S(1)}, u32[]{:S(2)}, u32[]{:S(2)}) %all-to-all-start) | async-done | bytes 96 | tf_op jit(solution)/shard_map/all_to_all | solution.py:45
  95.4 0.7 copy.158
  96.1 6.8 %all-to-all-start.1 = ((bf16[2,8,2056]{2,0,1:T(2,128)(2,1)}), bf16[2,8,2056]{2,0,1:T(2,128)(2,1)S(1)}, u32[]{:S(2)}, u32[]{:S(2)}) async-start(bf16[2,8,2056]{2,0,1:T(2,128)(2,1)} %copy.158), calls=%async_computation.1 | async-start | bytes 139264 | tf_op jit(solution)/shard_map/all_to_all | solution.py:52
  102.8 5.0 %all-to-all-done.1 = bf16[2,8,2056]{2,0,1:T(2,128)(2,1)S(1)} async-done(((bf16[2,8,2056]{2,0,1:T(2,128)(2,1)}), bf16[2,8,2056]{2,0,1:T(2,128)(2,1)S(1)}, u32[]{:S(2)}, u32[]{:S(2)}) %all-to-all-start.1) | async-done | bytes 65824 | tf_op jit(solution)/shard_map/all_to_all | solution.py:52
  107.9 0.3 fusion.46
  108.2 0.7 copy.191
  108.9 21.3 %all-gather.9.cloned.1.call-done = bf16[1,2,16,128,128]{4,3,1,0,2:T(8,128)(2,1)} async-done(((bf16[1,2,2,128,128]{4,3,1,0,2:T(8,128)(2,1)}), bf16[1,2,16,128,128]{4,3,1,0,2:T(8,128)(2,1)}) %all-gather.9.cloned.1.call-update) | async-done | bytes 1048592 | tf_op jit(solution)/shard_map/all_gather | solution.py:65
  130.2 1.5 convolution_bitcast_fusion.7
  131.8 0.1 fusion.63
  132.2 15.5 %psum.56 = f32[2,16]{0,1:T(8,128)S(1)} all-reduce(f32[2,16]{0,1:T(8,128)S(1)} %copy.162), channel_id=1, replica_groups=mesh['sect'=8,'blo'=8,'bhi'=8] {'bhi'}, use_global_device_ids=true, to_apply=%region_2.0 | all-reduce | flops 32 | bytes 256 | tf_op jit(solution)/shard_map/psum | solution.py:74
  147.6 0.2 slice_reduce_fusion.12
  147.8 1.9 collective-permute-start
  149.8 1.4 collective-permute-done
  151.3 42.6 %all-gather.11.cloned.1.call-done = bf16[2,2,16,128,128]{4,3,1,2,0:T(8,128)(2,1)} async-done(((bf16[2,2,2,128,128]{4,3,1,2,0:T(8,128)(2,1)}), bf16[2,2,16,128,128]{4,3,1,2,0:T(8,128)(2,1)}) %all-gather.11.cloned.1.call-update) | async-done | bytes 2097168 | tf_op jit(solution)/shard_map/all_gather | solution.py:65
  193.9 1.6 convolution_bitcast_fusion.6
  195.6 0.1 fusion.62
  195.9 5.2 %collective-permute-start.1 = (f32[16,8,128]{2,0,1:T(8,128)S(1)}, f32[16,8,128]{2,0,1:T(8,128)S(1)}, u32[]{:S(2)}, u32[]{:S(2)}) collective-permute-start(f32[16,8,128]{2,0,1:T(8,128)S(1)} %maximum_select_fusion.1), channel_id=1, source_target_pairs={{0,1},{1,2},{2,3},{3,4},{4,5},{5,6},{6,7},{7,0},{8,9},{9,10},{10,1... | collective-permute-start | bytes 196616 | tf_op jit(solution)/shard_map/ppermute | solution.py:78
  201.2 9.7 %psum.57 = f32[2,16]{0,1:T(8,128)S(1)} all-reduce(f32[2,16]{0,1:T(8,128)S(1)} %copy.165), channel_id=1, replica_groups=mesh['sect'=8,'blo'=8,'bhi'=8] {'bhi'}, use_global_device_ids=true, to_apply=%region_5.6 | all-reduce | flops 32 | bytes 256 | tf_op jit(solution)/shard_map/psum | solution.py:74
  210.9 0.2 slice_reduce_fusion.10
  211.2 0.3 convolution_bitcast_fusion.5
  211.6 0.1 fusion.61
  211.9 4.2 %collective-permute-start.2 = (f32[16,8,128]{2,0,1:T(8,128)S(1)}, f32[16,8,128]{2,0,1:T(8,128)S(1)}, u32[]{:S(2)}, u32[]{:S(2)}) collective-permute-start(f32[16,8,128]{2,0,1:T(8,128)S(1)} %maximum_select_fusion.2), channel_id=1, source_target_pairs={{0,1},{1,2},{2,3},{3,4},{4,5},{5,6},{6,7},{7,0},{8,9},{9,10},{10,1... | collective-permute-start | bytes 196616 | tf_op jit(solution)/shard_map/ppermute | solution.py:78
  216.2 14.4 %psum.58 = f32[2,16]{0,1:T(8,128)S(1)} all-reduce(f32[2,16]{0,1:T(8,128)S(1)} %copy.169), channel_id=1, replica_groups=mesh['sect'=8,'blo'=8,'bhi'=8] {'bhi'}, use_global_device_ids=true, to_apply=%region_8.9 | all-reduce | flops 32 | bytes 256 | tf_op jit(solution)/shard_map/psum | solution.py:74
  230.6 0.2 slice_reduce_fusion.8
  230.9 26.3 %all-gather.13.cloned.1.call-done = bf16[2,2,16,128,128]{4,3,1,2,0:T(8,128)(2,1)} async-done(((bf16[2,2,2,128,128]{4,3,1,2,0:T(8,128)(2,1)}), bf16[2,2,16,128,128]{4,3,1,2,0:T(8,128)(2,1)}) %all-gather.13.cloned.1.call-update) | async-done | bytes 2097168 | tf_op jit(solution)/shard_map/all_gather | solution.py:65
  257.2 1.6 convolution_bitcast_fusion.4
  258.9 0.1 fusion.60
  259.2 5.2 %collective-permute-start.3 = (f32[16,8,128]{2,0,1:T(8,128)S(1)}, f32[16,8,128]{2,0,1:T(8,128)S(1)}, u32[]{:S(2)}, u32[]{:S(2)}) collective-permute-start(f32[16,8,128]{2,0,1:T(8,128)S(1)} %maximum_select_fusion.3), channel_id=1, source_target_pairs={{0,1},{1,2},{2,3},{3,4},{4,5},{5,6},{6,7},{7,0},{8,9},{9,10},{10,1... | collective-permute-start | bytes 196616 | tf_op jit(solution)/shard_map/ppermute | solution.py:78
  264.5 11.0 %psum.59 = f32[2,16]{0,1:T(8,128)S(1)} all-reduce(f32[2,16]{0,1:T(8,128)S(1)} %copy.174), channel_id=1, replica_groups=mesh['sect'=8,'blo'=8,'bhi'=8] {'bhi'}, use_global_device_ids=true, to_apply=%region_11.12 | all-reduce | flops 32 | bytes 256 | tf_op jit(solution)/shard_map/psum | solution.py:74
  275.5 0.2 slice_reduce_fusion.6
  275.9 0.3 convolution_bitcast_fusion.3
  276.5 3.6 collective-permute-start.4
  280.3 16.3 %psum.60 = f32[2,16]{0,1:T(8,128)S(1)} all-reduce(f32[2,16]{0,1:T(8,128)S(1)} %copy.178), channel_id=1, replica_groups=mesh['sect'=8,'blo'=8,'bhi'=8] {'bhi'}, use_global_device_ids=true, to_apply=%region_14.15 | all-reduce | flops 32 | bytes 256 | tf_op jit(solution)/shard_map/psum | solution.py:74
  296.5 0.2 slice_reduce_fusion.4
  296.9 23.3 %all-gather.15.cloned.1.call-done = bf16[2,2,16,128,128]{4,3,1,2,0:T(8,128)(2,1)} async-done(((bf16[2,2,2,128,128]{4,3,1,2,0:T(8,128)(2,1)}), bf16[2,2,16,128,128]{4,3,1,2,0:T(8,128)(2,1)}) %all-gather.15.cloned.1.call-update) | async-done | bytes 2097168 | tf_op jit(solution)/shard_map/all_gather | solution.py:65
  320.2 1.7 convolution_bitcast_fusion.2
  322.2 6.1 %collective-permute-start.5 = (f32[16,8,128]{2,0,1:T(8,128)S(1)}, f32[16,8,128]{2,0,1:T(8,128)S(1)}, u32[]{:S(2)}, u32[]{:S(2)}) collective-permute-start(f32[16,8,128]{2,0,1:T(8,128)S(1)} %maximum_select_fusion.5), channel_id=1, source_target_pairs={{0,1},{1,2},{2,3},{3,4},{4,5},{5,6},{6,7},{7,0},{8,9},{9,10},{10,1... | collective-permute-start | bytes 196616 | tf_op jit(solution)/shard_map/ppermute | solution.py:78
  328.4 9.7 %psum.61 = f32[2,16]{0,1:T(8,128)S(1)} all-reduce(f32[2,16]{0,1:T(8,128)S(1)} %copy.183), channel_id=1, replica_groups=mesh['sect'=8,'blo'=8,'bhi'=8] {'bhi'}, use_global_device_ids=true, to_apply=%region_17.18 | all-reduce | flops 32 | bytes 256 | tf_op jit(solution)/shard_map/psum | solution.py:74
  338.1 0.2 slice_reduce_fusion.2
  338.5 0.3 convolution_bitcast_fusion.1
  338.8 0.1 fusion.57
  339.0 4.2 %collective-permute-start.6 = (f32[16,8,128]{2,0,1:T(8,128)S(1)}, f32[16,8,128]{2,0,1:T(8,128)S(1)}, u32[]{:S(2)}, u32[]{:S(2)}) collective-permute-start(f32[16,8,128]{2,0,1:T(8,128)S(1)} %maximum_select_fusion.6), channel_id=1, source_target_pairs={{0,1},{1,2},{2,3},{3,4},{4,5},{5,6},{6,7},{7,0},{8,9},{9,10},{10,1... | collective-permute-start | bytes 196616 | tf_op jit(solution)/shard_map/ppermute | solution.py:78
  343.4 13.3 %psum.62 = f32[2,16]{0,1:T(8,128)S(1)} all-reduce(f32[2,16]{0,1:T(8,128)S(1)} %copy.187), channel_id=1, replica_groups=mesh['sect'=8,'blo'=8,'bhi'=8] {'bhi'}, use_global_device_ids=true, to_apply=%region_20.21 | all-reduce | flops 32 | bytes 256 | tf_op jit(solution)/shard_map/psum | solution.py:74
  356.7 0.2 slice_reduce_fusion
  357.1 12.8 %all-gather.17.cloned.1.call-done = bf16[1,2,16,128,128]{4,3,1,0,2:T(8,128)(2,1)} async-done(((bf16[1,2,2,128,128]{4,3,1,0,2:T(8,128)(2,1)}), bf16[1,2,16,128,128]{4,3,1,0,2:T(8,128)(2,1)}) %all-gather.17.cloned.1.call-update) | async-done | bytes 1048592 | tf_op jit(solution)/shard_map/all_gather | solution.py:65
  369.9 1.5 convolution_bitcast_fusion
  371.4 0.1 fusion.11
  371.6 15.0 %psum.63 = f32[2,16]{0,1:T(8,128)S(1)} all-reduce(f32[2,16]{0,1:T(8,128)S(1)} %copy.192), channel_id=1, replica_groups=mesh['sect'=8,'blo'=8,'bhi'=8] {'bhi'}, use_global_device_ids=true, to_apply=%region_23.24 | all-reduce | flops 32 | bytes 256 | tf_op jit(solution)/shard_map/psum | solution.py:74
  387.2 13.8 %all_to_all.19 = f32[8,2,2]{2,1,0:T(2,128)S(1)} all-to-all(f32[8,2,2]{2,1,0:T(2,128)S(1)} %copy.195), channel_id=1, replica_groups=mesh['sect'=8,'blo'=8,'bhi'=8] {'sect'}, dimensions={0} | all-to-all | bytes 256 | tf_op jit(solution)/shard_map/all_to_all | solution.py:94
  401.0 0.6 squeeze.169
  401.6 0.6 squeeze.170
  (136 shorter events, 4.5 us)
Async XLA Ops:
  7.2 81.7 %copy-start = (bf16[16,16384]{1,0:T(8,128)(2,1)S(1)}, bf16[16,16384]{1,0:T(8,128)(2,1)}, u32[]{:S(2)}) copy-start(bf16[16,16384]{1,0:T(8,128)(2,1)} %param.6) | copy-start | bytes 1572868
  7.2 71.2 %all-gather.7.cloned.1.call-start = ((), (), s32[]{:S(2)}) async-start(), calls=%async_computation.3 | async-start | bytes 1179648 | tf_op jit(solution)/shard_map/all_gather | solution.py:43
  7.9 122.3 %all-gather.9.cloned.1.call-start = ((), (), s32[]{:S(2)}) async-start(), calls=%async_computation.4 | async-start | bytes 1179648 | tf_op jit(solution)/shard_map/all_gather | solution.py:65
  80.1 4.1 %copy-start.5 = (s32[1,16]{1,0:T(1,128)S(1)}, s32[1,16]{1,0:T(1,128)}, u32[]{:S(2)}) copy-start(s32[1,16]{1,0:T(1,128)} %param.4) | copy-start | bytes 196
  80.1 8.9 %copy-start.4 = (s32[128]{0:T(128)S(1)}, s32[128]{0:T(128)}, u32[]{:S(2)}) copy-start(s32[128]{0:T(128)} %param.5) | copy-start | bytes 1540
  80.1 113.8 %all-gather.11.cloned.1.call-start = ((), (), s32[]{:S(2)}) async-start(), calls=%async_computation.5 | async-start | bytes 2359296 | tf_op jit(solution)/shard_map/all_gather | solution.py:65
  82.1 175.1 %all-gather.13.cloned.1.call-start = ((), (), s32[]{:S(2)}) async-start(), calls=%async_computation.6 | async-start | bytes 2359296 | tf_op jit(solution)/shard_map/all_gather | solution.py:65
  82.9 237.3 %all-gather.15.cloned.1.call-start = ((), (), s32[]{:S(2)}) async-start(), calls=%async_computation.7 | async-start | bytes 2359296 | tf_op jit(solution)/shard_map/all_gather | solution.py:65
  85.5 9.8 %all-to-all-start = ((s32[8,1,2]{2,1,0:T(1,128)}), s32[8,1,2]{2,1,0:T(1,128)S(1)}, u32[]{:S(2)}, u32[]{:S(2)}) async-start(s32[8,1,2]{2,1,0:T(1,128)} %bitcast.4), calls=%async_computation | async-start | bytes 8192 | tf_op jit(solution)/shard_map/all_to_all | solution.py:45
  96.1 11.7 %all-to-all-start.1 = ((bf16[2,8,2056]{2,0,1:T(2,128)(2,1)}), bf16[2,8,2056]{2,0,1:T(2,128)(2,1)S(1)}, u32[]{:S(2)}, u32[]{:S(2)}) async-start(bf16[2,8,2056]{2,0,1:T(2,128)(2,1)} %copy.158), calls=%async_computation.1 | async-start | bytes 139264 | tf_op jit(solution)/shard_map/all_to_all | solution.py:52
  102.8 267.0 %all-gather.17.cloned.1.call-start = ((), (), s32[]{:S(2)}) async-start(), calls=%async_computation.8 | async-start | bytes 1179648 | tf_op jit(solution)/shard_map/all_gather | solution.py:65
  147.8 3.3 collective-permute-start
  193.9 17.4 %copy-start.3 = (bf16[2,2,16,128,128]{4,3,1,2,0:T(8,128)(2,1)S(1)}, bf16[2,2,16,128,128]{4,3,1,2,0:T(8,128)(2,1)}, u32[]{:S(2)}) copy-start(bf16[2,2,16,128,128]{4,3,1,2,0:T(8,128)(2,1)} %all-gather.11.cloned.1.call-done) | copy-start | bytes 6291460
  195.9 15.2 %collective-permute-start.1 = (f32[16,8,128]{2,0,1:T(8,128)S(1)}, f32[16,8,128]{2,0,1:T(8,128)S(1)}, u32[]{:S(2)}, u32[]{:S(2)}) collective-permute-start(f32[16,8,128]{2,0,1:T(8,128)S(1)} %maximum_select_fusion.1), channel_id=1, source_target_pairs={{0,1},{1,2},{2,3},{3,4},{4,5},{5,6},{6,7},{7,0},{8,9},{9,10},{10,1... | collective-permute-start | bytes 196616 | tf_op jit(solution)/shard_map/ppermute | solution.py:78
  211.9 18.9 %collective-permute-start.2 = (f32[16,8,128]{2,0,1:T(8,128)S(1)}, f32[16,8,128]{2,0,1:T(8,128)S(1)}, u32[]{:S(2)}, u32[]{:S(2)}) collective-permute-start(f32[16,8,128]{2,0,1:T(8,128)S(1)} %maximum_select_fusion.2), channel_id=1, source_target_pairs={{0,1},{1,2},{2,3},{3,4},{4,5},{5,6},{6,7},{7,0},{8,9},{9,10},{10,1... | collective-permute-start | bytes 196616 | tf_op jit(solution)/shard_map/ppermute | solution.py:78
  257.2 18.7 %copy-start.2 = (bf16[2,2,16,128,128]{4,3,1,2,0:T(8,128)(2,1)S(1)}, bf16[2,2,16,128,128]{4,3,1,2,0:T(8,128)(2,1)}, u32[]{:S(2)}) copy-start(bf16[2,2,16,128,128]{4,3,1,2,0:T(8,128)(2,1)} %all-gather.13.cloned.1.call-done) | copy-start | bytes 6291460
  259.2 16.5 %collective-permute-start.3 = (f32[16,8,128]{2,0,1:T(8,128)S(1)}, f32[16,8,128]{2,0,1:T(8,128)S(1)}, u32[]{:S(2)}, u32[]{:S(2)}) collective-permute-start(f32[16,8,128]{2,0,1:T(8,128)S(1)} %maximum_select_fusion.3), channel_id=1, source_target_pairs={{0,1},{1,2},{2,3},{3,4},{4,5},{5,6},{6,7},{7,0},{8,9},{9,10},{10,1... | collective-permute-start | bytes 196616 | tf_op jit(solution)/shard_map/ppermute | solution.py:78
  276.5 20.2 %collective-permute-start.4 = (f32[16,8,128]{2,0,1:T(8,128)S(1)}, f32[16,8,128]{2,0,1:T(8,128)S(1)}, u32[]{:S(2)}, u32[]{:S(2)}) collective-permute-start(f32[16,8,128]{2,0,1:T(8,128)S(1)} %maximum_select_fusion.4), channel_id=1, source_target_pairs={{0,1},{1,2},{2,3},{3,4},{4,5},{5,6},{6,7},{7,0},{8,9},{9,10},{10,1... | collective-permute-start | bytes 196616 | tf_op jit(solution)/shard_map/ppermute | solution.py:78
  320.2 18.3 %copy-start.1 = (bf16[2,2,16,128,128]{4,3,1,2,0:T(8,128)(2,1)S(1)}, bf16[2,2,16,128,128]{4,3,1,2,0:T(8,128)(2,1)}, u32[]{:S(2)}) copy-start(bf16[2,2,16,128,128]{4,3,1,2,0:T(8,128)(2,1)} %all-gather.15.cloned.1.call-done) | copy-start | bytes 6291460
  322.2 16.1 %collective-permute-start.5 = (f32[16,8,128]{2,0,1:T(8,128)S(1)}, f32[16,8,128]{2,0,1:T(8,128)S(1)}, u32[]{:S(2)}, u32[]{:S(2)}) collective-permute-start(f32[16,8,128]{2,0,1:T(8,128)S(1)} %maximum_select_fusion.5), channel_id=1, source_target_pairs={{0,1},{1,2},{2,3},{3,4},{4,5},{5,6},{6,7},{7,0},{8,9},{9,10},{10,1... | collective-permute-start | bytes 196616 | tf_op jit(solution)/shard_map/ppermute | solution.py:78
  339.0 18.0 %collective-permute-start.6 = (f32[16,8,128]{2,0,1:T(8,128)S(1)}, f32[16,8,128]{2,0,1:T(8,128)S(1)}, u32[]{:S(2)}, u32[]{:S(2)}) collective-permute-start(f32[16,8,128]{2,0,1:T(8,128)S(1)} %maximum_select_fusion.6), channel_id=1, source_target_pairs={{0,1},{1,2},{2,3},{3,4},{4,5},{5,6},{6,7},{7,0},{8,9},{9,10},{10,1... | collective-permute-start | bytes 196616 | tf_op jit(solution)/shard_map/ppermute | solution.py:78
Sparse Core Ops, SparseCore 0:
  11.2 67.1 all-gather.6
  80.5 49.6 all-gather.8
  132.3 61.5 all-gather.10
  195.8 61.3 all-gather.12
  259.1 61.0 all-gather.14
  322.2 47.6 all-gather.16

commit v8 on v6

--- a/solution.py
+++ b/solution.py
@@ -60,8 +60,10 @@
     logs = []
     batches = [[0]] + [list(range(k, min(k + 2, sites))) for k in range(1, sites, 2)]
     gathered = {}
+    first_slab, state = lax.optimization_barrier((slabs[0:1], state))
     for batch in batches:
-        got = lax.all_gather(slabs[batch[0] : batch[-1] + 1], "blo", axis=2, tiled=True)
+        piece = first_slab if batch == [0] else slabs[batch[0] : batch[-1] + 1]
+        got = lax.all_gather(piece, "blo", axis=2, tiled=True)
         for index, site in enumerate(batch):
             gathered[site] = got[index]
     for site in range(sites):

time: 335 us -> 333 us (level)
  the two profiles are of different devices: /device:TPU:64 before, /device:TPU:2 now
where the time goes in v8:
time: 333 us; the launch traced here: 332 us
  blocking collectives  202 us (61%)
  waiting for transfers between devices  63.6 us (19%)
  starting transfers between devices  26.6 us (8%)
  between operations  14.8 us (4%)
  local copies, waits for them, and re-layouts  11 us (3%)
  matrix products  9.64 us (3%)
  other arithmetic  4.1 us (1%)
    psum x8, blocking collectives, body(): norms = lax.psum(part, 'bhi')  163 us
    all_gather x5, waiting for transfers between devices, body(): got = lax.all_gather(piece, 'blo', axis=2, tiled=True)  27.2 us
    all_to_all x1, blocking collectives, body(): lax.all_to_all(jnp.concatenate([ordered, tagged], axis=2), 'bhi', 1, 1, t...  26.4 us
    all_gather x1, waiting for transfers between devices, body(): slabs = lax.all_gather(tensors[0], 'sect', axis=0, tiled=False)  25.8 us
    ppermute x7, starting transfers between devices, body(): came = lax.ppermute(rise[:, mine - 1], 'bhi', shift)  17.2 us
    all_to_all x1, blocking collectives, body(): back = lax.all_to_all(result, 'sect', 0, 0, tiled=False)  12.8 us
    all_to_all x1, starting transfers between devices, body(): lax.all_to_all(bits[0].reshape(n_sect, pick), 'sect', 0, 0, tiled=False)  9.14 us
    dot_general x8, matrix products, site_images(): jnp.einsum('rck,bckl->brcl', parts, weights, preferred_element_type=jnp.f...  8.79 us
  transfers between devices with their start and end apart: 14, of which 5 were waited for; matrix products, arithmetic and copies ran while one was open for 6% of the time, Pallas kernels for 0%

profile of v8, /device:TPU:2, one launch (start us, length us, event | category | flops | bytes accessed | tf_op | source)
XLA Modules:
  0.0 331.7 jit_solution(1339459453012040385)
XLA Ops:
  7.2 0.7 all-gather.7.cloned.1.call-update
  7.9 0.5 broadcast.258
  8.4 1.3 reduce.55
  9.7 0.7 all_to_all.12
  10.4 9.1 %all-to-all-start = ((s32[8,1,2]{2,1,0:T(1,128)}), s32[8,1,2]{2,1,0:T(1,128)S(1)}, u32[]{:S(2)}, u32[]{:S(2)}) async-start(s32[8,1,2]{2,1,0:T(1,128)} %bitcast.2), calls=%async_computation | async-start | bytes 8192 | tf_op jit(solution)/shard_map/all_to_all | solution.py:45
  19.7 0.8 fusion
  20.5 0.1 copy.111
  20.7 5.1 %all-to-all-done = s32[8,1,2]{2,1,0:T(1,128)S(1)} async-done(((s32[8,1,2]{2,1,0:T(1,128)}), s32[8,1,2]{2,1,0:T(1,128)S(1)}, u32[]{:S(2)}, u32[]{:S(2)}) %all-to-all-start) | async-done | bytes 96 | tf_op jit(solution)/shard_map/all_to_all | solution.py:45
  26.0 26.4 %all_to_all.19 = bf16[2,8,2056]{2,0,1:T(2,128)(2,1)S(1)} all-to-all(bf16[2,8,2056]{2,0,1:T(2,128)(2,1)S(1)} %copy.114), channel_id=1, replica_groups=mesh['sect'=8,'bhi'=8,'blo'=8] {'bhi'}, dimensions={1} | all-to-all | bytes 131584 | tf_op jit(solution)/shard_map/all_to_all | solution.py:51
  52.5 25.8 %all-gather.7.cloned.1.call-done = bf16[8,2,2,128,128]{4,3,2,1,0:T(8,128)(2,1)} async-done(((bf16[1,2,2,128,128]{4,3,2,1,0:T(8,128)(2,1)}), bf16[8,2,2,128,128]{4,3,2,1,0:T(8,128)(2,1)}) %all-gather.7.cloned.1.call-update) | async-done | bytes 1048592 | tf_op jit(solution)/shard_map/all_gather | solution.py:43
  78.2 1.0 fusion.56
  79.2 0.7 copy.115
  80.0 1.2 fusion.57
  81.1 0.7 copy.150
  81.9 0.7 copy.153
  82.7 0.7 copy.156
  83.6 0.3 fusion.47
  83.9 0.7 copy.135
  84.6 24.5 %all-gather.9.cloned.1.call-done = bf16[1,2,16,128,128]{4,3,1,0,2:T(8,128)(2,1)} async-done(((bf16[1,2,2,128,128]{4,3,1,0,2:T(8,128)(2,1)}), bf16[1,2,16,128,128]{4,3,1,0,2:T(8,128)(2,1)}) %all-gather.9.cloned.1.call-update) | async-done | bytes 1048592 | tf_op jit(solution)/shard_map/all_gather | solution.py:66
  109.1 1.5 convolution_bitcast_fusion
  110.6 0.1 multiply_reduce_fusion.13
  110.9 22.6 %psum.56 = f32[2,16]{0,1:T(8,128)S(1)} all-reduce(f32[2,16]{0,1:T(8,128)S(1)} %copy.119), channel_id=1, replica_groups=mesh['sect'=8,'bhi'=8,'blo'=8] {'bhi'}, use_global_device_ids=true, to_apply=%region_2.0 | all-reduce | flops 32 | bytes 256 | tf_op jit(solution)/shard_map/psum | solution.py:75
  133.5 0.2 slice_reduce_fusion.12
  133.7 3.0 collective-permute-start
  136.7 4.7 %collective-permute-done = f32[16,128]{1,0:T(8,128)S(1)} collective-permute-done((f32[16,128]{1,0:T(8,128)S(1)}, f32[16,128]{1,0:T(8,128)S(1)}, u32[]{:S(2)}, u32[]{:S(2)}) %collective-permute-start) | collective-permute-done | bytes 8224 | tf_op jit(solution)/shard_map/ppermute | solution.py:76
  141.5 2.7 all-gather.11.cloned.1.call-done
  144.2 1.6 convolution_bitcast_fusion.7
  145.9 0.1 multiply_reduce_fusion.11
  146.1 4.6 %collective-permute-start.1 = (f32[16,128]{1,0:T(8,128)S(1)}, f32[16,128]{1,0:T(8,128)S(1)}, u32[]{:S(2)}, u32[]{:S(2)}) collective-permute-start(f32[16,128]{1,0:T(8,128)S(1)} %slice_bitcast_fusion.31), channel_id=1, source_target_pairs={{0,8},{8,16},{16,24},{24,32},{32,40},{40,48},{48,56},{56,0},{1,9},... | collective-permute-start | bytes 24584 | tf_op jit(solution)/shard_map/ppermute | solution.py:76
  150.8 22.0 %psum.57 = f32[2,16]{0,1:T(8,128)S(1)} all-reduce(f32[2,16]{0,1:T(8,128)S(1)} %copy.122), channel_id=1, replica_groups=mesh['sect'=8,'bhi'=8,'blo'=8] {'bhi'}, use_global_device_ids=true, to_apply=%region_5.6 | all-reduce | flops 32 | bytes 256 | tf_op jit(solution)/shard_map/psum | solution.py:75
  172.8 0.2 slice_reduce_fusion.10
  173.2 0.3 convolution_bitcast_fusion.6
  173.5 0.1 multiply_reduce_fusion.9
  173.6 1.9 collective-permute-start.2
  175.7 20.5 %psum.58 = f32[2,16]{0,1:T(8,128)S(1)} all-reduce(f32[2,16]{0,1:T(8,128)S(1)} %copy.124), channel_id=1, replica_groups=mesh['sect'=8,'bhi'=8,'blo'=8] {'bhi'}, use_global_device_ids=true, to_apply=%region_8.9 | all-reduce | flops 32 | bytes 256 | tf_op jit(solution)/shard_map/psum | solution.py:75
  196.2 0.2 slice_reduce_fusion.8
  196.6 1.6 convolution_bitcast_fusion.5
  198.3 0.1 multiply_reduce_fusion.7
  198.4 1.9 collective-permute-start.3
  200.4 20.6 %psum.59 = f32[2,16]{0,1:T(8,128)S(1)} all-reduce(f32[2,16]{0,1:T(8,128)S(1)} %copy.127), channel_id=1, replica_groups=mesh['sect'=8,'bhi'=8,'blo'=8] {'bhi'}, use_global_device_ids=true, to_apply=%region_11.12 | all-reduce | flops 32 | bytes 256 | tf_op jit(solution)/shard_map/psum | solution.py:75
  221.0 0.2 slice_reduce_fusion.6
  221.2 0.1 reduce-precision_convert_fusion.3
  221.4 0.3 convolution_bitcast_fusion.4
  221.7 0.1 multiply_reduce_fusion.5
  221.8 1.9 collective-permute-start.4
  223.9 20.4 %psum.60 = f32[2,16]{0,1:T(8,128)S(1)} all-reduce(f32[2,16]{0,1:T(8,128)S(1)} %copy.129), channel_id=1, replica_groups=mesh['sect'=8,'bhi'=8,'blo'=8] {'bhi'}, use_global_device_ids=true, to_apply=%region_14.15 | all-reduce | flops 32 | bytes 256 | tf_op jit(solution)/shard_map/psum | solution.py:75
  244.3 0.2 slice_reduce_fusion.4
  244.7 1.7 convolution_bitcast_fusion.3
  246.4 0.1 multiply_reduce_fusion.3
  246.5 1.9 collective-permute-start.5
  248.5 20.3 %psum.61 = f32[2,16]{0,1:T(8,128)S(1)} all-reduce(f32[2,16]{0,1:T(8,128)S(1)} %copy.132), channel_id=1, replica_groups=mesh['sect'=8,'bhi'=8,'blo'=8] {'bhi'}, use_global_device_ids=true, to_apply=%region_17.18 | all-reduce | flops 32 | bytes 256 | tf_op jit(solution)/shard_map/psum | solution.py:75
  268.8 0.2 slice_reduce_fusion.2
  269.2 0.3 convolution_bitcast_fusion.2
  269.5 1.9 collective-permute-start.6
  271.5 0.1 multiply_reduce_fusion.1
  271.7 20.3 %psum.62 = f32[2,16]{0,1:T(8,128)S(1)} all-reduce(f32[2,16]{0,1:T(8,128)S(1)} %copy.134), channel_id=1, replica_groups=mesh['sect'=8,'bhi'=8,'blo'=8] {'bhi'}, use_global_device_ids=true, to_apply=%region_20.21 | all-reduce | flops 32 | bytes 256 | tf_op jit(solution)/shard_map/psum | solution.py:75
  292.0 0.2 slice_reduce_fusion
  292.4 1.5 convolution_bitcast_fusion.1
  293.9 0.1 fusion.12
  294.2 16.2 %psum.63 = f32[2,16]{0,1:T(8,128)S(1)} all-reduce(f32[2,16]{0,1:T(8,128)S(1)} %copy.136), channel_id=1, replica_groups=mesh['sect'=8,'bhi'=8,'blo'=8] {'bhi'}, use_global_device_ids=true, to_apply=%region_23.24 | all-reduce | flops 32 | bytes 256 | tf_op jit(solution)/shard_map/psum | solution.py:75
  310.4 0.1 log_add_fusion
  310.9 12.8 %all_to_all.20 = f32[8,2,2]{2,1,0:T(2,128)S(1)} all-to-all(f32[8,2,2]{2,1,0:T(2,128)S(1)} %copy.139), channel_id=1, replica_groups=mesh['sect'=8,'bhi'=8,'blo'=8] {'sect'}, dimensions={0} | all-to-all | bytes 256 | tf_op jit(solution)/shard_map/all_to_all | solution.py:92
  323.7 0.6 squeeze.190
  324.3 0.6 squeeze.191
  (106 shorter events, 3.1 us)
Async XLA Ops:
  7.2 12.4 %copy-start = (bf16[16,16384]{1,0:T(8,128)(2,1)S(1)}, bf16[16,16384]{1,0:T(8,128)(2,1)}, u32[]{:S(2)}) copy-start(bf16[16,16384]{1,0:T(8,128)(2,1)} %param.6) | copy-start | bytes 1572868
  7.2 71.1 %all-gather.7.cloned.1.call-start = ((), (), s32[]{:S(2)}) async-start(), calls=%async_computation.3 | async-start | bytes 1179648 | tf_op jit(solution)/shard_map/all_gather | solution.py:43
  10.4 15.4 %all-to-all-start = ((s32[8,1,2]{2,1,0:T(1,128)}), s32[8,1,2]{2,1,0:T(1,128)S(1)}, u32[]{:S(2)}, u32[]{:S(2)}) async-start(s32[8,1,2]{2,1,0:T(1,128)} %bitcast.2), calls=%async_computation | async-start | bytes 8192 | tf_op jit(solution)/shard_map/all_to_all | solution.py:45
  19.6 89.5 %all-gather.9.cloned.1.call-start = ((), (), s32[]{:S(2)}) async-start(), calls=%async_computation.4 | async-start | bytes 1179648 | tf_op jit(solution)/shard_map/all_gather | solution.py:66
  79.9 64.3 %all-gather.11.cloned.1.call-start = ((), (), s32[]{:S(2)}) async-start(), calls=%async_computation.5 | async-start | bytes 2359296 | tf_op jit(solution)/shard_map/all_gather | solution.py:66
  81.9 114.6 %all-gather.13.cloned.1.call-start = ((), (), s32[]{:S(2)}) async-start(), calls=%async_computation.6 | async-start | bytes 2359296 | tf_op jit(solution)/shard_map/all_gather | solution.py:66
  82.7 161.9 %all-gather.15.cloned.1.call-start = ((), (), s32[]{:S(2)}) async-start(), calls=%async_computation.7 | async-start | bytes 2359296 | tf_op jit(solution)/shard_map/all_gather | solution.py:66
  83.5 208.9 %all-gather.17.cloned.1.call-start = ((), (), s32[]{:S(2)}) async-start(), calls=%async_computation.8 | async-start | bytes 1179648 | tf_op jit(solution)/shard_map/all_gather | solution.py:66
  133.7 7.7 %collective-permute-start = (f32[16,128]{1,0:T(8,128)S(1)}, f32[16,128]{1,0:T(8,128)S(1)}, u32[]{:S(2)}, u32[]{:S(2)}) collective-permute-start(f32[16,128]{1,0:T(8,128)S(1)} %slice_bitcast_fusion.32), channel_id=1, source_target_pairs={{0,8},{8,16},{16,24},{24,32},{32,40},{40,48},{48,56},{56,0},{1,9},... | collective-permute-start | bytes 24584 | tf_op jit(solution)/shard_map/ppermute | solution.py:76
  144.2 28.9 %copy-start.3 = (bf16[2,2,16,128,128]{4,3,1,2,0:T(8,128)(2,1)S(1)}, bf16[2,2,16,128,128]{4,3,1,2,0:T(8,128)(2,1)}, u32[]{:S(2)}) copy-start(bf16[2,2,16,128,128]{4,3,1,2,0:T(8,128)(2,1)} %all-gather.11.cloned.1.call-done) | copy-start | bytes 6291460
  146.1 27.0 %collective-permute-start.1 = (f32[16,128]{1,0:T(8,128)S(1)}, f32[16,128]{1,0:T(8,128)S(1)}, u32[]{:S(2)}, u32[]{:S(2)}) collective-permute-start(f32[16,128]{1,0:T(8,128)S(1)} %slice_bitcast_fusion.31), channel_id=1, source_target_pairs={{0,8},{8,16},{16,24},{24,32},{32,40},{40,48},{48,56},{56,0},{1,9},... | collective-permute-start | bytes 24584 | tf_op jit(solution)/shard_map/ppermute | solution.py:76
  173.6 22.8 %collective-permute-start.2 = (f32[16,128]{1,0:T(8,128)S(1)}, f32[16,128]{1,0:T(8,128)S(1)}, u32[]{:S(2)}, u32[]{:S(2)}) collective-permute-start(f32[16,128]{1,0:T(8,128)S(1)} %slice_bitcast_fusion.30), channel_id=1, source_target_pairs={{0,8},{8,16},{16,24},{24,32},{32,40},{40,48},{48,56},{56,0},{1,9},... | collective-permute-start | bytes 24584 | tf_op jit(solution)/shard_map/ppermute | solution.py:76
  196.5 24.8 %copy-start.2 = (bf16[2,2,16,128,128]{4,3,1,2,0:T(8,128)(2,1)S(1)}, bf16[2,2,16,128,128]{4,3,1,2,0:T(8,128)(2,1)}, u32[]{:S(2)}) copy-start(bf16[2,2,16,128,128]{4,3,1,2,0:T(8,128)(2,1)} %all-gather.13.cloned.1.call-done) | copy-start | bytes 6291460
  198.4 22.8 %collective-permute-start.3 = (f32[16,128]{1,0:T(8,128)S(1)}, f32[16,128]{1,0:T(8,128)S(1)}, u32[]{:S(2)}, u32[]{:S(2)}) collective-permute-start(f32[16,128]{1,0:T(8,128)S(1)} %slice_bitcast_fusion.29), channel_id=1, source_target_pairs={{0,8},{8,16},{16,24},{24,32},{32,40},{40,48},{48,56},{56,0},{1,9},... | collective-permute-start | bytes 24584 | tf_op jit(solution)/shard_map/ppermute | solution.py:76
  221.8 22.7 %collective-permute-start.4 = (f32[16,128]{1,0:T(8,128)S(1)}, f32[16,128]{1,0:T(8,128)S(1)}, u32[]{:S(2)}, u32[]{:S(2)}) collective-permute-start(f32[16,128]{1,0:T(8,128)S(1)} %slice_bitcast_fusion.28), channel_id=1, source_target_pairs={{0,8},{8,16},{16,24},{24,32},{32,40},{40,48},{48,56},{56,0},{1,9},... | collective-permute-start | bytes 24584 | tf_op jit(solution)/shard_map/ppermute | solution.py:76
  244.6 24.5 %copy-start.1 = (bf16[2,2,16,128,128]{4,3,1,2,0:T(8,128)(2,1)S(1)}, bf16[2,2,16,128,128]{4,3,1,2,0:T(8,128)(2,1)}, u32[]{:S(2)}) copy-start(bf16[2,2,16,128,128]{4,3,1,2,0:T(8,128)(2,1)} %all-gather.15.cloned.1.call-done) | copy-start | bytes 6291460
  246.5 22.5 %collective-permute-start.5 = (f32[16,128]{1,0:T(8,128)S(1)}, f32[16,128]{1,0:T(8,128)S(1)}, u32[]{:S(2)}, u32[]{:S(2)}) collective-permute-start(f32[16,128]{1,0:T(8,128)S(1)} %slice_bitcast_fusion.27), channel_id=1, source_target_pairs={{0,8},{8,16},{16,24},{24,32},{32,40},{40,48},{48,56},{56,0},{1,9},... | collective-permute-start | bytes 24584 | tf_op jit(solution)/shard_map/ppermute | solution.py:76
  269.5 22.7 %collective-permute-start.6 = (f32[16,128]{1,0:T(8,128)S(1)}, f32[16,128]{1,0:T(8,128)S(1)}, u32[]{:S(2)}, u32[]{:S(2)}) collective-permute-start(f32[16,128]{1,0:T(8,128)S(1)} %slice_bitcast_fusion.26), channel_id=1, source_target_pairs={{0,8},{8,16},{16,24},{24,32},{32,40},{40,48},{48,56},{56,0},{1,9},... | collective-permute-start | bytes 24584 | tf_op jit(solution)/shard_map/ppermute | solution.py:76
Sparse Core Ops, SparseCore 0:
  11.2 66.9 all-gather.6
  80.4 28.6 all-gather.8
  111.2 32.9 all-gather.10
  146.2 33.1 all-gather.12
  181.4 33.3 all-gather.14
  216.8 30.6 all-gather.16

commit v9 on v7

--- a/solution.py
+++ b/solution.py
@@ -4,7 +4,7 @@
 from jax.sharding import Mesh
 from jax.sharding import PartitionSpec as P
 
-PARTS = 8
+PARTS = 16
 
 
 def charge_order(labels, rows, block):
@@ -61,8 +61,10 @@
     logs = []
     batches = [[0]] + [list(range(k, min(k + 2, sites))) for k in range(1, sites, 2)]
     gathered = {}
+    first_slab, state = lax.optimization_barrier((slabs[0:1], state))
     for batch in batches:
-        got = lax.all_gather(slabs[batch[0] : batch[-1] + 1], "blo", axis=2, tiled=True)
+        piece = first_slab if batch == [0] else slabs[batch[0] : batch[-1] + 1]
+        got = lax.all_gather(piece, "blo", axis=2, tiled=True)
         for index, site in enumerate(batch):
             gathered[site] = got[index]
     for site in range(sites):

time: 410 us -> 517 us (1.26)
  blocking collectives: 119 us -> 373 us
  waiting for transfers between devices: 210 us -> 66.8 us
    psum x8, blocking collectives: 105 us -> 260 us  [body(): norms = lax.psum(part, 'bhi')]
    all_gather x5 -> x3, waiting for transfers between devices: 126 us -> 0.06 us  [body(): got = lax.all_gather(piece, 'blo', axis=2, tiled=True)]
    all_gather x0 -> x2, blocking collectives: none -> 101 us  [body(): got = lax.all_gather(piece, 'blo', axis=2, tiled=True)]
    all_gather x1, waiting for transfers between devices: 70.5 us -> 54.4 us  [body(): slabs = lax.all_gather(tensors[0], 'sect', axis=0, tiled=False)]
  transfers between devices with their start and end apart: 15 -> 13, of which waited for: 9 -> 3; matrix products, arithmetic and copies ran while one was open for 5% -> 2% of each run, Pallas kernels for 0% -> 0%
where the time goes in v9:
time: 517 us; the launch traced here: 516 us
  blocking collectives  373 us (72%)
  waiting for transfers between devices  66.8 us (13%)
  starting transfers between devices  43.8 us (8%)
  between operations  14.6 us (3%)
  local copies, waits for them, and re-layouts  8.84 us (2%)
    psum x8, blocking collectives, body(): norms = lax.psum(part, 'bhi')  260 us
    all_gather x2, blocking collectives, body(): got = lax.all_gather(piece, 'blo', axis=2, tiled=True)  101 us
    all_gather x1, waiting for transfers between devices, body(): slabs = lax.all_gather(tensors[0], 'sect', axis=0, tiled=False)  54.4 us
    ppermute x7, starting transfers between devices, body(): came = lax.ppermute(send, 'bhi', shift)  29.7 us
    all_to_all x1, blocking collectives, body(): back = lax.all_to_all(result, 'sect', 0, 0, tiled=False)  12.3 us
  transfers between devices with their start and end apart: 13, of which 3 were waited for; matrix products, arithmetic and copies ran while one was open for 2% of the time, Pallas kernels for 0%

profile of v9, /device:TPU:1, one launch (start us, length us, event | category | flops | bytes accessed | tf_op | source)
XLA Modules:
  0.0 516.5 jit_solution(3088856185209286356)
XLA Ops:
  7.2 0.7 all-gather.5.cloned.1.call-update
  7.9 0.5 broadcast.230
  8.4 0.1 copy-done.5
  8.6 0.7 reduce.20
  9.2 0.7 all_to_all.12
  9.9 7.5 %all-to-all-start = ((s32[8,1,2]{2,1,0:T(1,128)}), s32[8,1,2]{2,1,0:T(1,128)S(1)}, u32[]{:S(2)}, u32[]{:S(2)}) async-start(s32[8,1,2]{2,1,0:T(1,128)} %bitcast.4), calls=%async_computation | async-start | bytes 8192 | tf_op jit(solution)/shard_map/all_to_all | solution.py:45
  17.5 0.6 copy-done.4
  18.1 0.2 convolution_convert_fusion
  18.4 5.5 %all-to-all-done = s32[8,1,2]{2,1,0:T(1,128)S(1)} async-done(((s32[8,1,2]{2,1,0:T(1,128)}), s32[8,1,2]{2,1,0:T(1,128)S(1)}, u32[]{:S(2)}, u32[]{:S(2)}) %all-to-all-start) | async-done | bytes 96 | tf_op jit(solution)/shard_map/all_to_all | solution.py:45
  24.0 54.4 %all-gather.5.cloned.1.call-done = bf16[8,2,2,128,128]{4,3,2,1,0:T(8,128)(2,1)} async-done(((bf16[1,2,2,128,128]{4,3,2,1,0:T(8,128)(2,1)}), bf16[8,2,2,128,128]{4,3,2,1,0:T(8,128)(2,1)}) %all-gather.5.cloned.1.call-update) | async-done | bytes 1048592 | tf_op jit(solution)/shard_map/all_gather | solution.py:43
  78.4 1.2 fusion.86
  79.6 0.7 copy.211
  80.4 0.7 copy.172
  81.1 6.4 %all-to-all-start.1 = ((bf16[2,16,1032]{2,0,1:T(2,128)(2,1)}), bf16[2,16,1032]{2,0,1:T(2,128)(2,1)S(1)}, u32[]{:S(2)}, u32[]{:S(2)}) async-start(bf16[2,16,1032]{2,0,1:T(2,128)(2,1)} %copy.172), calls=%async_computation.1 | async-start | bytes 147456 | tf_op jit(solution)/shard_map/all_to_all | solution.py:52
  87.5 6.1 %all-to-all-done.1 = bf16[2,16,1032]{2,0,1:T(2,128)(2,1)S(1)} async-done(((bf16[2,16,1032]{2,0,1:T(2,128)(2,1)}), bf16[2,16,1032]{2,0,1:T(2,128)(2,1)S(1)}, u32[]{:S(2)}, u32[]{:S(2)}) %all-to-all-start.1) | async-done | bytes 66080 | tf_op jit(solution)/shard_map/all_to_all | solution.py:52
  93.8 1.0 fusion.85
  94.8 0.7 copy.216
  95.6 56.1 %all_gather.19 = bf16[1,2,8,128,128]{4,3,1,0,2:T(8,128)(2,1)S(1)} all-gather(bf16[1,2,2,128,128]{4,3,1,0,2:T(8,128)(2,1)S(1)} %copy.174), channel_id=1, replica_groups=mesh['sect'=8,'blo'=4,'bhi'=16] {'blo'}, dimensions={2}, use_global_device_ids=true | all-gather | bytes 655360 | tf_op jit(solution)/shard_map/all_gather | solution.py:67
  151.7 0.2 convolution_bitcast_fusion
  152.0 0.1 fusion.93
  152.2 8.1 %collective-permute-start = (f32[32,4,128]{2,0,1:T(8,128)S(1)}, f32[32,4,128]{2,0,1:T(8,128)S(1)}, u32[]{:S(2)}, u32[]{:S(2)}) collective-permute-start(f32[32,4,128]{2,0,1:T(8,128)S(1)} %maximum_select_fusion), channel_id=1, source_target_pairs={{0,1},{1,2},{2,3},{3,4},{4,5},{5,6},{6,7},{7,8},{8,9},{9,10},{10,1... | collective-permute-start | bytes 196616 | tf_op jit(solution)/shard_map/ppermute | solution.py:80
  160.3 0.1 multiply_reduce_fusion.13
  160.4 25.3 %psum.56 = f32[2,32]{1,0:T(2,128)S(1)} all-reduce(f32[2,32]{1,0:T(2,128)S(1)} %pad_maximum_fusion.8), channel_id=1, replica_groups=mesh['sect'=8,'blo'=4,'bhi'=16] {'bhi'}, use_global_device_ids=true, to_apply=%region_2.0 | all-reduce | flops 64 | bytes 512 | tf_op jit(solution)/shard_map/psum | solution.py:76
  185.8 45.0 %all_gather.23 = bf16[1,2,8,128,128]{4,3,1,0,2:T(8,128)(2,1)S(1)} all-gather(bf16[1,2,2,128,128]{4,3,1,0,2:T(8,128)(2,1)S(1)} %copy.199), channel_id=1, replica_groups=mesh['sect'=8,'blo'=4,'bhi'=16] {'blo'}, dimensions={2}, use_global_device_ids=true | all-gather | bytes 655360 | tf_op jit(solution)/shard_map/all_gather | solution.py:67
  230.8 0.7 copy.221
  231.6 0.1 reduce-precision_convert_fusion.6
  231.7 1.3 convolution_bitcast_fusion.7
  233.0 0.1 fusion.92
  233.2 0.1 multiply_reduce_fusion.11
  233.3 5.6 %collective-permute-start.1 = (f32[32,4,128]{2,0,1:T(8,128)S(1)}, f32[32,4,128]{2,0,1:T(8,128)S(1)}, u32[]{:S(2)}, u32[]{:S(2)}) collective-permute-start(f32[32,4,128]{2,0,1:T(8,128)S(1)} %maximum_select_fusion.1), channel_id=1, source_target_pairs={{0,1},{1,2},{2,3},{3,4},{4,5},{5,6},{6,7},{7,8},{8,9},{9,10},{10,1... | collective-permute-start | bytes 196616 | tf_op jit(solution)/shard_map/ppermute | solution.py:80
  239.0 37.6 %psum.57 = f32[2,32]{1,0:T(2,128)S(1)} all-reduce(f32[2,32]{1,0:T(2,128)S(1)} %pad_maximum_fusion.9), channel_id=1, replica_groups=mesh['sect'=8,'blo'=4,'bhi'=16] {'bhi'}, use_global_device_ids=true, to_apply=%region_5.6 | all-reduce | flops 64 | bytes 512 | tf_op jit(solution)/shard_map/psum | solution.py:76
  276.6 0.1 reduce-precision_convert_fusion.5
  276.8 0.2 convolution_bitcast_fusion.6
  277.0 0.1 fusion.91
  277.2 0.1 multiply_reduce_fusion.9
  277.3 1.9 collective-permute-start.2
  279.3 34.4 %psum.58 = f32[2,32]{1,0:T(2,128)S(1)} all-reduce(f32[2,32]{1,0:T(2,128)S(1)} %pad_maximum_fusion.10), channel_id=1, replica_groups=mesh['sect'=8,'blo'=4,'bhi'=16] {'bhi'}, use_global_device_ids=true, to_apply=%region_8.9 | all-reduce | flops 64 | bytes 512 | tf_op jit(solution)/shard_map/psum | solution.py:76
  313.9 1.3 convolution_bitcast_fusion.5
  315.2 0.1 fusion.90
  315.4 0.1 multiply_reduce_fusion.7
  315.5 3.1 collective-permute-start.3
  318.7 32.2 %psum.59 = f32[2,32]{1,0:T(2,128)S(1)} all-reduce(f32[2,32]{1,0:T(2,128)S(1)} %pad_maximum_fusion.11), channel_id=1, replica_groups=mesh['sect'=8,'blo'=4,'bhi'=16] {'bhi'}, use_global_device_ids=true, to_apply=%region_11.12 | all-reduce | flops 64 | bytes 512 | tf_op jit(solution)/shard_map/psum | solution.py:76
  351.1 0.2 convolution_bitcast_fusion.4
  351.3 0.1 fusion.89
  351.5 3.6 collective-permute-start.4
  355.2 0.1 multiply_reduce_fusion.5
  355.3 32.2 %psum.60 = f32[2,32]{1,0:T(2,128)S(1)} all-reduce(f32[2,32]{1,0:T(2,128)S(1)} %pad_maximum_fusion.12), channel_id=1, replica_groups=mesh['sect'=8,'blo'=4,'bhi'=16] {'bhi'}, use_global_device_ids=true, to_apply=%region_14.15 | all-reduce | flops 64 | bytes 512 | tf_op jit(solution)/shard_map/psum | solution.py:76
  387.5 0.1 reduce-precision_convert_fusion.2
  387.7 1.3 convolution_bitcast_fusion.3
  389.0 0.1 fusion.88
  389.2 0.1 multiply_reduce_fusion.3
  389.3 3.6 collective-permute-start.5
  393.0 32.2 %psum.61 = f32[2,32]{1,0:T(2,128)S(1)} all-reduce(f32[2,32]{1,0:T(2,128)S(1)} %pad_maximum_fusion.13), channel_id=1, replica_groups=mesh['sect'=8,'blo'=4,'bhi'=16] {'bhi'}, use_global_device_ids=true, to_apply=%region_17.18 | all-reduce | flops 64 | bytes 512 | tf_op jit(solution)/shard_map/psum | solution.py:76
  425.3 0.2 convolution_bitcast_fusion.2
  425.6 0.1 fusion.87
  425.8 0.1 multiply_reduce_fusion.1
  425.9 3.6 collective-permute-start.6
  429.6 32.2 %psum.62 = f32[2,32]{1,0:T(2,128)S(1)} all-reduce(f32[2,32]{1,0:T(2,128)S(1)} %pad_maximum_fusion.14), channel_id=1, replica_groups=mesh['sect'=8,'blo'=4,'bhi'=16] {'bhi'}, use_global_device_ids=true, to_apply=%region_20.21 | all-reduce | flops 64 | bytes 512 | tf_op jit(solution)/shard_map/psum | solution.py:76
  461.9 0.2 convolution_bitcast_fusion.1
  462.2 0.1 fusion.11
  462.3 33.9 %psum.63 = f32[2,32]{1,0:T(2,128)S(1)} all-reduce(f32[2,32]{1,0:T(2,128)S(1)} %pad_maximum_fusion.15), channel_id=1, replica_groups=mesh['sect'=8,'blo'=4,'bhi'=16] {'bhi'}, use_global_device_ids=true, to_apply=%region_23.24 | all-reduce | flops 64 | bytes 512 | tf_op jit(solution)/shard_map/psum | solution.py:76
  496.4 12.3 %all_to_all.19 = f32[8,2,2]{2,1,0:T(2,128)S(1)} all-to-all(f32[8,2,2]{2,1,0:T(2,128)S(1)} %copy.226), channel_id=1, replica_groups=mesh['sect'=8,'blo'=4,'bhi'=16] {'sect'}, dimensions={0} | all-to-all | bytes 256 | tf_op jit(solution)/shard_map/all_to_all | solution.py:96
  508.8 0.6 squeeze.169
  509.4 0.6 squeeze.170
  (118 shorter events, 2.3 us)
Async XLA Ops:
  7.2 10.3 %copy-start = (bf16[16,16384]{1,0:T(8,128)(2,1)S(1)}, bf16[16,16384]{1,0:T(8,128)(2,1)}, u32[]{:S(2)}) copy-start(bf16[16,16384]{1,0:T(8,128)(2,1)} %param.6) | copy-start | bytes 1572868
  7.2 71.2 %all-gather.5.cloned.1.call-start = ((), (), s32[]{:S(2)}) async-start(), calls=%async_computation.3 | async-start | bytes 1179648 | tf_op jit(solution)/shard_map/all_gather | solution.py:43
  7.9 0.7 copy-start.5
  9.9 14.0 %all-to-all-start = ((s32[8,1,2]{2,1,0:T(1,128)}), s32[8,1,2]{2,1,0:T(1,128)S(1)}, u32[]{:S(2)}, u32[]{:S(2)}) async-start(s32[8,1,2]{2,1,0:T(1,128)} %bitcast.4), calls=%async_computation | async-start | bytes 8192 | tf_op jit(solution)/shard_map/all_to_all | solution.py:45
  17.4 214.3 %all-gather.7.cloned.1.call-start = ((), (), s32[]{:S(2)}) async-start(), calls=%async_computation.4 | async-start | bytes 1310720 | tf_op jit(solution)/shard_map/all_gather | solution.py:67
  17.5 0.7 copy-start.4
  81.1 12.6 %all-to-all-start.1 = ((bf16[2,16,1032]{2,0,1:T(2,128)(2,1)}), bf16[2,16,1032]{2,0,1:T(2,128)(2,1)S(1)}, u32[]{:S(2)}, u32[]{:S(2)}) async-start(bf16[2,16,1032]{2,0,1:T(2,128)(2,1)} %copy.172), calls=%async_computation.1 | async-start | bytes 147456 | tf_op jit(solution)/shard_map/all_to_all | solution.py:52
  87.5 226.4 %all-gather.9.cloned.1.call-start = ((), (), s32[]{:S(2)}) async-start(), calls=%async_computation.5 | async-start | bytes 1310720 | tf_op jit(solution)/shard_map/all_gather | solution.py:67
  151.7 236.0 %all-gather.11.cloned.1.call-start = ((), (), s32[]{:S(2)}) async-start(), calls=%async_computation.6 | async-start | bytes 1310720 | tf_op jit(solution)/shard_map/all_gather | solution.py:67
  152.2 79.4 %collective-permute-start = (f32[32,4,128]{2,0,1:T(8,128)S(1)}, f32[32,4,128]{2,0,1:T(8,128)S(1)}, u32[]{:S(2)}, u32[]{:S(2)}) collective-permute-start(f32[32,4,128]{2,0,1:T(8,128)S(1)} %maximum_select_fusion), channel_id=1, source_target_pairs={{0,1},{1,2},{2,3},{3,4},{4,5},{5,6},{6,7},{7,8},{8,9},{9,10},{10,1... | collective-permute-start | bytes 196616 | tf_op jit(solution)/shard_map/ppermute | solution.py:80
  233.0 43.8 %copy-start.3 = (bf16[2,2,8,128,128]{4,3,1,2,0:T(8,128)(2,1)S(1)}, bf16[2,2,8,128,128]{4,3,1,2,0:T(8,128)(2,1)}, u32[]{:S(2)}) copy-start(bf16[2,2,8,128,128]{4,3,1,2,0:T(8,128)(2,1)} %all-gather.7.cloned.1.call-done) | copy-start | bytes 3145732
  233.3 43.3 %collective-permute-start.1 = (f32[32,4,128]{2,0,1:T(8,128)S(1)}, f32[32,4,128]{2,0,1:T(8,128)S(1)}, u32[]{:S(2)}, u32[]{:S(2)}) collective-permute-start(f32[32,4,128]{2,0,1:T(8,128)S(1)} %maximum_select_fusion.1), channel_id=1, source_target_pairs={{0,1},{1,2},{2,3},{3,4},{4,5},{5,6},{6,7},{7,8},{8,9},{9,10},{10,1... | collective-permute-start | bytes 196616 | tf_op jit(solution)/shard_map/ppermute | solution.py:80
  277.3 36.4 %collective-permute-start.2 = (f32[32,4,128]{2,0,1:T(8,128)S(1)}, f32[32,4,128]{2,0,1:T(8,128)S(1)}, u32[]{:S(2)}, u32[]{:S(2)}) collective-permute-start(f32[32,4,128]{2,0,1:T(8,128)S(1)} %maximum_select_fusion.2), channel_id=1, source_target_pairs={{0,1},{1,2},{2,3},{3,4},{4,5},{5,6},{6,7},{7,8},{8,9},{9,10},{10,1... | collective-permute-start | bytes 196616 | tf_op jit(solution)/shard_map/ppermute | solution.py:80
  315.2 35.8 %copy-start.2 = (bf16[2,2,8,128,128]{4,3,1,2,0:T(8,128)(2,1)S(1)}, bf16[2,2,8,128,128]{4,3,1,2,0:T(8,128)(2,1)}, u32[]{:S(2)}) copy-start(bf16[2,2,8,128,128]{4,3,1,2,0:T(8,128)(2,1)} %all-gather.9.cloned.1.call-done) | copy-start | bytes 3145732
  315.5 35.4 %collective-permute-start.3 = (f32[32,4,128]{2,0,1:T(8,128)S(1)}, f32[32,4,128]{2,0,1:T(8,128)S(1)}, u32[]{:S(2)}, u32[]{:S(2)}) collective-permute-start(f32[32,4,128]{2,0,1:T(8,128)S(1)} %maximum_select_fusion.3), channel_id=1, source_target_pairs={{0,1},{1,2},{2,3},{3,4},{4,5},{5,6},{6,7},{7,8},{8,9},{9,10},{10,1... | collective-permute-start | bytes 196616 | tf_op jit(solution)/shard_map/ppermute | solution.py:80
  351.5 36.0 %collective-permute-start.4 = (f32[32,4,128]{2,0,1:T(8,128)S(1)}, f32[32,4,128]{2,0,1:T(8,128)S(1)}, u32[]{:S(2)}, u32[]{:S(2)}) collective-permute-start(f32[32,4,128]{2,0,1:T(8,128)S(1)} %maximum_select_fusion.4), channel_id=1, source_target_pairs={{0,1},{1,2},{2,3},{3,4},{4,5},{5,6},{6,7},{7,8},{8,9},{9,10},{10,1... | collective-permute-start | bytes 196616 | tf_op jit(solution)/shard_map/ppermute | solution.py:80
  389.0 36.3 %copy-start.1 = (bf16[2,2,8,128,128]{4,3,1,2,0:T(8,128)(2,1)S(1)}, bf16[2,2,8,128,128]{4,3,1,2,0:T(8,128)(2,1)}, u32[]{:S(2)}) copy-start(bf16[2,2,8,128,128]{4,3,1,2,0:T(8,128)(2,1)} %all-gather.11.cloned.1.call-done) | copy-start | bytes 3145732
  389.3 35.9 %collective-permute-start.5 = (f32[32,4,128]{2,0,1:T(8,128)S(1)}, f32[32,4,128]{2,0,1:T(8,128)S(1)}, u32[]{:S(2)}, u32[]{:S(2)}) collective-permute-start(f32[32,4,128]{2,0,1:T(8,128)S(1)} %maximum_select_fusion.5), channel_id=1, source_target_pairs={{0,1},{1,2},{2,3},{3,4},{4,5},{5,6},{6,7},{7,8},{8,9},{9,10},{10,1... | collective-permute-start | bytes 196616 | tf_op jit(solution)/shard_map/ppermute | solution.py:80
  425.9 35.9 %collective-permute-start.6 = (f32[32,4,128]{2,0,1:T(8,128)S(1)}, f32[32,4,128]{2,0,1:T(8,128)S(1)}, u32[]{:S(2)}, u32[]{:S(2)}) collective-permute-start(f32[32,4,128]{2,0,1:T(8,128)S(1)} %maximum_select_fusion.6), channel_id=1, source_target_pairs={{0,1},{1,2},{2,3},{3,4},{4,5},{5,6},{6,7},{7,8},{8,9},{9,10},{10,1... | collective-permute-start | bytes 196616 | tf_op jit(solution)/shard_map/ppermute | solution.py:80
Sparse Core Ops, SparseCore 0:
  11.2 67.1 all-gather.4
  80.5 75.0 all-gather.6
  157.7 73.8 all-gather.8
  233.6 60.3 all-gather.10

commit v10 on v8

--- a/solution.py
+++ b/solution.py
@@ -5,6 +5,7 @@
 from jax.sharding import PartitionSpec as P
 
 PARTS = 8
+SECT = ("sx", "sy")
 
 
 def charge_order(labels, rows, block):
@@ -27,9 +28,9 @@
 
 
 def body(bits, labels, left, tensors):
-    sect = lax.axis_index("sect")
+    sect = lax.axis_index(SECT)
     bhi = lax.axis_index("bhi")
-    n_sect = lax.axis_size("sect")
+    n_sect = lax.axis_size("sx") * lax.axis_size("sy")
     n_hi = lax.axis_size("bhi")
     n_lo = lax.axis_size("blo")
     block = tensors.shape[-1]
@@ -40,9 +41,10 @@
     pick = per_dev // n_sect
     mine = count_blocks // n_hi
 
-    slabs = lax.all_gather(tensors[0], "sect", axis=0, tiled=False)
+    slabs = lax.all_gather(tensors[0], "sy", axis=0, tiled=False)
+    slabs = lax.all_gather(slabs, "sx", axis=0, tiled=True)
 
-    pieces = lax.all_to_all(bits[0].reshape(n_sect, pick), "sect", 0, 0, tiled=False)
+    pieces = lax.all_to_all(bits[0].reshape(n_sect, pick), SECT, 0, 0, tiled=False)
     row_bits = jnp.transpose(pieces).astype(left.dtype)
 
     rows = lax.dynamic_slice_in_dim(left, sect * pick, pick, 0)
@@ -89,15 +91,16 @@
 
     result = jnp.stack([jnp.stack(probs), jnp.stack(logs)], axis=1)
     result = lax.dynamic_slice_in_dim(result, bhi * pick, pick, 2)
-    back = lax.all_to_all(result, "sect", 0, 0, tiled=False)
+    back = lax.all_to_all(result, SECT, 0, 0, tiled=False)
     out = jnp.transpose(back, (1, 0, 2)).reshape(2, bits.shape[0], n_sect * pick)
     return (out[0], out[1])
 
 
 def solution(mesh):
     n_sect, n_blk = mesh.devices.shape
-    fine = Mesh(mesh.devices.reshape(n_sect, PARTS, n_blk // PARTS), ("sect", "bhi", "blo"))
+    n_x = n_sect // 2
+    fine = Mesh(mesh.devices.reshape(n_x, 2, PARTS, n_blk // PARTS), ("sx", "sy", "bhi", "blo"))
     blk = ("bhi", "blo")
-    in_specs = (P("sect", blk), P(), P(blk, None), P("sect", None, blk, None, None))
-    out_specs = (P("sect", blk), P("sect", blk))
+    in_specs = (P(SECT, blk), P(), P(blk, None), P(SECT, None, blk, None, None))
+    out_specs = (P(SECT, blk), P(SECT, blk))
     return jax.shard_map(body, mesh=fine, in_specs=in_specs, out_specs=out_specs, check_vma=False)

time: 333 us -> 307 us (0.922)
  the two profiles are of different devices: /device:TPU:2 before, /device:TPU:64 now
where the time goes in v10:
time: 307 us
  blocking collectives  187 us (61%)
  starting transfers between devices  46.6 us (15%)
  waiting for transfers between devices  33.7 us (11%)
  between operations  14.8 us (5%)
  local copies, waits for them, and re-layouts  11 us (4%)
  matrix products  9.61 us (3%)
  other arithmetic  4.11 us (1%)
    psum x8, blocking collectives, body(): norms = lax.psum(part, 'bhi')  139 us
    ppermute x7, starting transfers between devices, body(): came = lax.ppermute(rise[:, mine - 1], 'bhi', shift)  40.8 us
    all_to_all x1, blocking collectives, body(): lax.all_to_all(jnp.concatenate([ordered, tagged], axis=2), 'bhi', 1, 1, t...  25.1 us
    all_gather x5, waiting for transfers between devices, body(): got = lax.all_gather(piece, 'blo', axis=2, tiled=True)  24.7 us
    all_to_all x1, blocking collectives, body(): back = lax.all_to_all(result, SECT, 0, 0, tiled=False)  13.7 us
    all_gather x1, blocking collectives, body(): slabs = lax.all_gather(tensors[0], 'sy', axis=0, tiled=False)  9.28 us
    dot_general x8, matrix products, site_images(): jnp.einsum('rck,bckl->brcl', parts, weights, preferred_element_type=jnp.f...  8.76 us
    all_to_all x1, waiting for transfers between devices, body(): lax.all_to_all(bits[0].reshape(n_sect, pick), SECT, 0, 0, tiled=False)  6.33 us
  transfers between devices with their start and end apart: 14, of which 4 were waited for; matrix products, arithmetic and copies ran while one was open for 6% of the time, Pallas kernels for 0%

profile of v10, /device:TPU:64, one launch (start us, length us, event | category | flops | bytes accessed | tf_op | source)
XLA Modules:
  0.0 306.6 jit_solution(3581631973935079736)
XLA Ops:
  7.2 9.3 %all_gather.21 = bf16[2,2,2,128,128]{4,3,2,1,0:T(8,128)(2,1)} all-gather(bf16[1,2,2,128,128]{4,3,2,1,0:T(8,128)(2,1)} %param.7), channel_id=1, replica_groups=mesh['sx'=4,'sy'=2,'bhi'=8,'blo'=8] {'sy'}, dimensions={0}, use_global_device_ids=true | all-gather | bytes 393216 | tf_op jit(solution)/shard_map/all_gather | solution.py:44
  16.5 0.5 broadcast.258
  17.0 1.3 reduce.55
  18.4 0.7 all_to_all.12
  19.0 5.5 %all-to-all-start = ((s32[8,1,2]{2,1,0:T(1,128)}), s32[8,1,2]{2,1,0:T(1,128)S(1)}, u32[]{:S(2)}, u32[]{:S(2)}) async-start(s32[8,1,2]{2,1,0:T(1,128)} %bitcast.2), calls=%async_computation | async-start | bytes 8192 | tf_op jit(solution)/shard_map/all_to_all | solution.py:47
  24.7 0.8 fusion
  25.6 0.1 copy.111
  25.7 6.3 %all-to-all-done = s32[8,1,2]{2,1,0:T(1,128)S(1)} async-done(((s32[8,1,2]{2,1,0:T(1,128)}), s32[8,1,2]{2,1,0:T(1,128)S(1)}, u32[]{:S(2)}, u32[]{:S(2)}) %all-to-all-start) | async-done | bytes 96 | tf_op jit(solution)/shard_map/all_to_all | solution.py:47
  32.2 25.1 %all_to_all.19 = bf16[2,8,2056]{2,0,1:T(2,128)(2,1)S(1)} all-to-all(bf16[2,8,2056]{2,0,1:T(2,128)(2,1)S(1)} %copy.114), channel_id=1, replica_groups=mesh['sx'=4,'sy'=2,'bhi'=8,'blo'=8] {'bhi'}, dimensions={1} | all-to-all | bytes 131584 | tf_op jit(solution)/shard_map/all_to_all | solution.py:53
  57.4 1.0 fusion.56
  58.4 0.7 copy.115
  59.1 1.2 fusion.57
  60.3 0.7 copy.150
  61.1 0.7 copy.153
  61.9 0.7 copy.156
  62.7 0.3 fusion.47
  63.0 0.7 copy.135
  63.8 18.9 %all-gather.9.cloned.1.call-done = bf16[1,2,16,128,128]{4,3,1,0,2:T(8,128)(2,1)} async-done(((bf16[1,2,2,128,128]{4,3,1,0,2:T(8,128)(2,1)}), bf16[1,2,16,128,128]{4,3,1,0,2:T(8,128)(2,1)}) %all-gather.9.cloned.1.call-update) | async-done | bytes 1048592 | tf_op jit(solution)/shard_map/all_gather | solution.py:68
  82.7 1.5 convolution_bitcast_fusion
  84.2 0.1 multiply_reduce_fusion.13
  84.5 21.1 %psum.56 = f32[2,16]{0,1:T(8,128)S(1)} all-reduce(f32[2,16]{0,1:T(8,128)S(1)} %copy.119), channel_id=1, replica_groups=mesh['sx'=4,'sy'=2,'bhi'=8,'blo'=8] {'bhi'}, use_global_device_ids=true, to_apply=%region_2.0 | all-reduce | flops 32 | bytes 256 | tf_op jit(solution)/shard_map/psum | solution.py:77
  105.6 0.2 slice_reduce_fusion.12
  105.8 3.8 %collective-permute-start = (f32[16,128]{1,0:T(8,128)S(1)}, f32[16,128]{1,0:T(8,128)S(1)}, u32[]{:S(2)}, u32[]{:S(2)}) collective-permute-start(f32[16,128]{1,0:T(8,128)S(1)} %slice_bitcast_fusion.32), channel_id=1, source_target_pairs={{0,8},{8,16},{16,24},{24,32},{32,40},{40,48},{48,56},{56,0},{1,9},... | collective-permute-start | bytes 24584 | tf_op jit(solution)/shard_map/ppermute | solution.py:78
  109.6 2.6 collective-permute-done
  112.3 5.7 %all-gather.11.cloned.1.call-done = bf16[2,2,16,128,128]{4,3,1,2,0:T(8,128)(2,1)} async-done(((bf16[2,2,2,128,128]{4,3,1,2,0:T(8,128)(2,1)}), bf16[2,2,16,128,128]{4,3,1,2,0:T(8,128)(2,1)}) %all-gather.11.cloned.1.call-update) | async-done | bytes 2097168 | tf_op jit(solution)/shard_map/all_gather | solution.py:68
  118.0 1.6 convolution_bitcast_fusion.7
  119.8 0.1 multiply_reduce_fusion.11
  119.9 5.4 %collective-permute-start.1 = (f32[16,128]{1,0:T(8,128)S(1)}, f32[16,128]{1,0:T(8,128)S(1)}, u32[]{:S(2)}, u32[]{:S(2)}) collective-permute-start(f32[16,128]{1,0:T(8,128)S(1)} %slice_bitcast_fusion.31), channel_id=1, source_target_pairs={{0,8},{8,16},{16,24},{24,32},{32,40},{40,48},{48,56},{56,0},{1,9},... | collective-permute-start | bytes 24584 | tf_op jit(solution)/shard_map/ppermute | solution.py:78
  125.4 18.3 %psum.57 = f32[2,16]{0,1:T(8,128)S(1)} all-reduce(f32[2,16]{0,1:T(8,128)S(1)} %copy.122), channel_id=1, replica_groups=mesh['sx'=4,'sy'=2,'bhi'=8,'blo'=8] {'bhi'}, use_global_device_ids=true, to_apply=%region_5.6 | all-reduce | flops 32 | bytes 256 | tf_op jit(solution)/shard_map/psum | solution.py:77
  143.8 0.2 slice_reduce_fusion.10
  144.1 0.3 convolution_bitcast_fusion.6
  144.5 0.1 multiply_reduce_fusion.9
  144.6 6.3 %collective-permute-start.2 = (f32[16,128]{1,0:T(8,128)S(1)}, f32[16,128]{1,0:T(8,128)S(1)}, u32[]{:S(2)}, u32[]{:S(2)}) collective-permute-start(f32[16,128]{1,0:T(8,128)S(1)} %slice_bitcast_fusion.30), channel_id=1, source_target_pairs={{0,8},{8,16},{16,24},{24,32},{32,40},{40,48},{48,56},{56,0},{1,9},... | collective-permute-start | bytes 24584 | tf_op jit(solution)/shard_map/ppermute | solution.py:78
  151.0 15.9 %psum.58 = f32[2,16]{0,1:T(8,128)S(1)} all-reduce(f32[2,16]{0,1:T(8,128)S(1)} %copy.124), channel_id=1, replica_groups=mesh['sx'=4,'sy'=2,'bhi'=8,'blo'=8] {'bhi'}, use_global_device_ids=true, to_apply=%region_8.9 | all-reduce | flops 32 | bytes 256 | tf_op jit(solution)/shard_map/psum | solution.py:77
  166.9 0.2 slice_reduce_fusion.8
  167.3 1.6 convolution_bitcast_fusion.5
  169.0 0.1 multiply_reduce_fusion.7
  169.2 6.3 %collective-permute-start.3 = (f32[16,128]{1,0:T(8,128)S(1)}, f32[16,128]{1,0:T(8,128)S(1)}, u32[]{:S(2)}, u32[]{:S(2)}) collective-permute-start(f32[16,128]{1,0:T(8,128)S(1)} %slice_bitcast_fusion.29), channel_id=1, source_target_pairs={{0,8},{8,16},{16,24},{24,32},{32,40},{40,48},{48,56},{56,0},{1,9},... | collective-permute-start | bytes 24584 | tf_op jit(solution)/shard_map/ppermute | solution.py:78
  175.6 16.1 %psum.59 = f32[2,16]{0,1:T(8,128)S(1)} all-reduce(f32[2,16]{0,1:T(8,128)S(1)} %copy.127), channel_id=1, replica_groups=mesh['sx'=4,'sy'=2,'bhi'=8,'blo'=8] {'bhi'}, use_global_device_ids=true, to_apply=%region_11.12 | all-reduce | flops 32 | bytes 256 | tf_op jit(solution)/shard_map/psum | solution.py:77
  191.7 0.2 slice_reduce_fusion.6
  192.0 0.3 convolution_bitcast_fusion.4
  192.4 0.1 multiply_reduce_fusion.5
  192.5 6.4 %collective-permute-start.4 = (f32[16,128]{1,0:T(8,128)S(1)}, f32[16,128]{1,0:T(8,128)S(1)}, u32[]{:S(2)}, u32[]{:S(2)}) collective-permute-start(f32[16,128]{1,0:T(8,128)S(1)} %slice_bitcast_fusion.28), channel_id=1, source_target_pairs={{0,8},{8,16},{16,24},{24,32},{32,40},{40,48},{48,56},{56,0},{1,9},... | collective-permute-start | bytes 24584 | tf_op jit(solution)/shard_map/ppermute | solution.py:78
  199.0 15.9 %psum.60 = f32[2,16]{0,1:T(8,128)S(1)} all-reduce(f32[2,16]{0,1:T(8,128)S(1)} %copy.129), channel_id=1, replica_groups=mesh['sx'=4,'sy'=2,'bhi'=8,'blo'=8] {'bhi'}, use_global_device_ids=true, to_apply=%region_14.15 | all-reduce | flops 32 | bytes 256 | tf_op jit(solution)/shard_map/psum | solution.py:77
  214.9 0.2 slice_reduce_fusion.4
  215.1 0.1 reduce-precision_convert_fusion.2
  215.3 1.6 convolution_bitcast_fusion.3
  217.0 0.1 multiply_reduce_fusion.3
  217.1 6.3 %collective-permute-start.5 = (f32[16,128]{1,0:T(8,128)S(1)}, f32[16,128]{1,0:T(8,128)S(1)}, u32[]{:S(2)}, u32[]{:S(2)}) collective-permute-start(f32[16,128]{1,0:T(8,128)S(1)} %slice_bitcast_fusion.27), channel_id=1, source_target_pairs={{0,8},{8,16},{16,24},{24,32},{32,40},{40,48},{48,56},{56,0},{1,9},... | collective-permute-start | bytes 24584 | tf_op jit(solution)/shard_map/ppermute | solution.py:78
  223.5 15.9 %psum.61 = f32[2,16]{0,1:T(8,128)S(1)} all-reduce(f32[2,16]{0,1:T(8,128)S(1)} %copy.132), channel_id=1, replica_groups=mesh['sx'=4,'sy'=2,'bhi'=8,'blo'=8] {'bhi'}, use_global_device_ids=true, to_apply=%region_17.18 | all-reduce | flops 32 | bytes 256 | tf_op jit(solution)/shard_map/psum | solution.py:77
  239.5 0.2 slice_reduce_fusion.2
  239.8 0.3 convolution_bitcast_fusion.2
  240.2 6.3 %collective-permute-start.6 = (f32[16,128]{1,0:T(8,128)S(1)}, f32[16,128]{1,0:T(8,128)S(1)}, u32[]{:S(2)}, u32[]{:S(2)}) collective-permute-start(f32[16,128]{1,0:T(8,128)S(1)} %slice_bitcast_fusion.26), channel_id=1, source_target_pairs={{0,8},{8,16},{16,24},{24,32},{32,40},{40,48},{48,56},{56,0},{1,9},... | collective-permute-start | bytes 24584 | tf_op jit(solution)/shard_map/ppermute | solution.py:78
  246.5 0.1 multiply_reduce_fusion.1
  246.7 16.0 %psum.62 = f32[2,16]{0,1:T(8,128)S(1)} all-reduce(f32[2,16]{0,1:T(8,128)S(1)} %copy.134), channel_id=1, replica_groups=mesh['sx'=4,'sy'=2,'bhi'=8,'blo'=8] {'bhi'}, use_global_device_ids=true, to_apply=%region_20.21 | all-reduce | flops 32 | bytes 256 | tf_op jit(solution)/shard_map/psum | solution.py:77
  262.7 0.2 slice_reduce_fusion
  263.0 0.1 reduce-precision_convert_fusion
  263.1 1.5 convolution_bitcast_fusion.1
  264.6 0.1 fusion.12
  264.9 19.4 %psum.63 = f32[2,16]{0,1:T(8,128)S(1)} all-reduce(f32[2,16]{0,1:T(8,128)S(1)} %copy.136), channel_id=1, replica_groups=mesh['sx'=4,'sy'=2,'bhi'=8,'blo'=8] {'bhi'}, use_global_device_ids=true, to_apply=%region_23.24 | all-reduce | flops 32 | bytes 256 | tf_op jit(solution)/shard_map/psum | solution.py:77
  284.3 0.1 log_add_fusion
  284.9 13.7 %all_to_all.20 = f32[8,2,2]{2,1,0:T(2,128)S(1)} all-to-all(f32[8,2,2]{2,1,0:T(2,128)S(1)} %copy.139), channel_id=1, replica_groups=mesh['sx'=4,'sy'=2,'bhi'=8,'blo'=8] {'sx','sy'}, dimensions={0} | all-to-all | bytes 256 | tf_op jit(solution)/shard_map/all_to_all | solution.py:94
  298.6 0.6 squeeze.190
  299.2 0.6 squeeze.191
  (107 shorter events, 3.1 us)
Async XLA Ops:
  7.2 17.4 %copy-start = (bf16[16,16384]{1,0:T(8,128)(2,1)S(1)}, bf16[16,16384]{1,0:T(8,128)(2,1)}, u32[]{:S(2)}) copy-start(bf16[16,16384]{1,0:T(8,128)(2,1)} %param.6) | copy-start | bytes 1572868
  7.2 50.2 %all-gather.7.cloned.1.call-start = ((), (), s32[]{:S(2)}) async-start(), calls=%async_computation.3 | async-start | bytes 1310720 | tf_op jit(solution)/shard_map/all_gather | solution.py:45
  19.0 13.0 %all-to-all-start = ((s32[8,1,2]{2,1,0:T(1,128)}), s32[8,1,2]{2,1,0:T(1,128)S(1)}, u32[]{:S(2)}, u32[]{:S(2)}) async-start(s32[8,1,2]{2,1,0:T(1,128)} %bitcast.2), calls=%async_computation | async-start | bytes 8192 | tf_op jit(solution)/shard_map/all_to_all | solution.py:47
  24.6 58.2 %all-gather.9.cloned.1.call-start = ((), (), s32[]{:S(2)}) async-start(), calls=%async_computation.4 | async-start | bytes 1179648 | tf_op jit(solution)/shard_map/all_gather | solution.py:68
  59.1 58.9 %all-gather.11.cloned.1.call-start = ((), (), s32[]{:S(2)}) async-start(), calls=%async_computation.5 | async-start | bytes 2359296 | tf_op jit(solution)/shard_map/all_gather | solution.py:68
  61.1 106.2 %all-gather.13.cloned.1.call-start = ((), (), s32[]{:S(2)}) async-start(), calls=%async_computation.6 | async-start | bytes 2359296 | tf_op jit(solution)/shard_map/all_gather | solution.py:68
  61.9 153.4 %all-gather.15.cloned.1.call-start = ((), (), s32[]{:S(2)}) async-start(), calls=%async_computation.7 | async-start | bytes 2359296 | tf_op jit(solution)/shard_map/all_gather | solution.py:68
  62.7 200.4 %all-gather.17.cloned.1.call-start = ((), (), s32[]{:S(2)}) async-start(), calls=%async_computation.8 | async-start | bytes 1179648 | tf_op jit(solution)/shard_map/all_gather | solution.py:68
  105.8 6.4 %collective-permute-start = (f32[16,128]{1,0:T(8,128)S(1)}, f32[16,128]{1,0:T(8,128)S(1)}, u32[]{:S(2)}, u32[]{:S(2)}) collective-permute-start(f32[16,128]{1,0:T(8,128)S(1)} %slice_bitcast_fusion.32), channel_id=1, source_target_pairs={{0,8},{8,16},{16,24},{24,32},{32,40},{40,48},{48,56},{56,0},{1,9},... | collective-permute-start | bytes 24584 | tf_op jit(solution)/shard_map/ppermute | solution.py:78
  118.0 26.1 %copy-start.3 = (bf16[2,2,16,128,128]{4,3,1,2,0:T(8,128)(2,1)S(1)}, bf16[2,2,16,128,128]{4,3,1,2,0:T(8,128)(2,1)}, u32[]{:S(2)}) copy-start(bf16[2,2,16,128,128]{4,3,1,2,0:T(8,128)(2,1)} %all-gather.11.cloned.1.call-done) | copy-start | bytes 6291460
  119.9 24.1 %collective-permute-start.1 = (f32[16,128]{1,0:T(8,128)S(1)}, f32[16,128]{1,0:T(8,128)S(1)}, u32[]{:S(2)}, u32[]{:S(2)}) collective-permute-start(f32[16,128]{1,0:T(8,128)S(1)} %slice_bitcast_fusion.31), channel_id=1, source_target_pairs={{0,8},{8,16},{16,24},{24,32},{32,40},{40,48},{48,56},{56,0},{1,9},... | collective-permute-start | bytes 24584 | tf_op jit(solution)/shard_map/ppermute | solution.py:78
  144.6 22.6 %collective-permute-start.2 = (f32[16,128]{1,0:T(8,128)S(1)}, f32[16,128]{1,0:T(8,128)S(1)}, u32[]{:S(2)}, u32[]{:S(2)}) collective-permute-start(f32[16,128]{1,0:T(8,128)S(1)} %slice_bitcast_fusion.30), channel_id=1, source_target_pairs={{0,8},{8,16},{16,24},{24,32},{32,40},{40,48},{48,56},{56,0},{1,9},... | collective-permute-start | bytes 24584 | tf_op jit(solution)/shard_map/ppermute | solution.py:78
  167.3 24.7 %copy-start.2 = (bf16[2,2,16,128,128]{4,3,1,2,0:T(8,128)(2,1)S(1)}, bf16[2,2,16,128,128]{4,3,1,2,0:T(8,128)(2,1)}, u32[]{:S(2)}) copy-start(bf16[2,2,16,128,128]{4,3,1,2,0:T(8,128)(2,1)} %all-gather.13.cloned.1.call-done) | copy-start | bytes 6291460
  169.2 22.8 %collective-permute-start.3 = (f32[16,128]{1,0:T(8,128)S(1)}, f32[16,128]{1,0:T(8,128)S(1)}, u32[]{:S(2)}, u32[]{:S(2)}) collective-permute-start(f32[16,128]{1,0:T(8,128)S(1)} %slice_bitcast_fusion.29), channel_id=1, source_target_pairs={{0,8},{8,16},{16,24},{24,32},{32,40},{40,48},{48,56},{56,0},{1,9},... | collective-permute-start | bytes 24584 | tf_op jit(solution)/shard_map/ppermute | solution.py:78
  192.5 22.6 %collective-permute-start.4 = (f32[16,128]{1,0:T(8,128)S(1)}, f32[16,128]{1,0:T(8,128)S(1)}, u32[]{:S(2)}, u32[]{:S(2)}) collective-permute-start(f32[16,128]{1,0:T(8,128)S(1)} %slice_bitcast_fusion.28), channel_id=1, source_target_pairs={{0,8},{8,16},{16,24},{24,32},{32,40},{40,48},{48,56},{56,0},{1,9},... | collective-permute-start | bytes 24584 | tf_op jit(solution)/shard_map/ppermute | solution.py:78
  215.3 24.5 %copy-start.1 = (bf16[2,2,16,128,128]{4,3,1,2,0:T(8,128)(2,1)S(1)}, bf16[2,2,16,128,128]{4,3,1,2,0:T(8,128)(2,1)}, u32[]{:S(2)}) copy-start(bf16[2,2,16,128,128]{4,3,1,2,0:T(8,128)(2,1)} %all-gather.15.cloned.1.call-done) | copy-start | bytes 6291460
  217.1 22.6 %collective-permute-start.5 = (f32[16,128]{1,0:T(8,128)S(1)}, f32[16,128]{1,0:T(8,128)S(1)}, u32[]{:S(2)}, u32[]{:S(2)}) collective-permute-start(f32[16,128]{1,0:T(8,128)S(1)} %slice_bitcast_fusion.27), channel_id=1, source_target_pairs={{0,8},{8,16},{16,24},{24,32},{32,40},{40,48},{48,56},{56,0},{1,9},... | collective-permute-start | bytes 24584 | tf_op jit(solution)/shard_map/ppermute | solution.py:78
  240.2 22.8 %collective-permute-start.6 = (f32[16,128]{1,0:T(8,128)S(1)}, f32[16,128]{1,0:T(8,128)S(1)}, u32[]{:S(2)}, u32[]{:S(2)}) collective-permute-start(f32[16,128]{1,0:T(8,128)S(1)} %slice_bitcast_fusion.26), channel_id=1, source_target_pairs={{0,8},{8,16},{16,24},{24,32},{32,40},{40,48},{48,56},{56,0},{1,9},... | collective-permute-start | bytes 24584 | tf_op jit(solution)/shard_map/ppermute | solution.py:78
Sparse Core Ops, SparseCore 0:
  16.7 33.9 all-gather.6
  59.2 23.4 all-gather.8
  84.9 33.1 all-gather.10
  120.0 32.7 all-gather.12
  154.8 33.4 all-gather.14
  190.3 30.6 all-gather.16

commit v11 on v10

--- a/solution.py
+++ b/solution.py
@@ -62,10 +62,8 @@
     logs = []
     batches = [[0]] + [list(range(k, min(k + 2, sites))) for k in range(1, sites, 2)]
     gathered = {}
-    first_slab, state = lax.optimization_barrier((slabs[0:1], state))
     for batch in batches:
-        piece = first_slab if batch == [0] else slabs[batch[0] : batch[-1] + 1]
-        got = lax.all_gather(piece, "blo", axis=2, tiled=True)
+        got = lax.all_gather(slabs[batch[0] : batch[-1] + 1], "blo", axis=2, tiled=True)
         for index, site in enumerate(batch):
             gathered[site] = got[index]
     for site in range(sites):

time: 307 us -> 308 us (level)
  blocking collectives: 187 us -> 154 us
  waiting for transfers between devices: 33.7 us -> 54.8 us
  starting transfers between devices: 46.6 us -> 59.7 us
    all_gather x1, waiting for transfers between devices: 0.02 us -> 34.1 us  [body(): slabs = lax.all_gather(slabs, 'sx', axis=0, tiled=True)]
    all_to_all x1 -> x0, blocking collectives: 25.1 us -> none  [body(): lax.all_to_all(jnp.concatenate([ordered, tagged], axis=2), 'bhi', 1, 1, t...]
    all_gather x5, waiting for transfers between devices: 24.7 us -> 0.1 us  [body(): lax.all_gather(slabs[batch[0]:batch[-1] + 1], 'blo', axis=2, tiled=True)]
    all_to_all x0 -> x1, starting transfers between devices: none -> 12.6 us  [body(): lax.all_to_all(jnp.concatenate([ordered, tagged], axis=2), 'bhi', 1, 1, t...]
    all_to_all x0 -> x1, waiting for transfers between devices: none -> 11.3 us  [body(): lax.all_to_all(jnp.concatenate([ordered, tagged], axis=2), 'bhi', 1, 1, t...]
    psum x8, blocking collectives: 139 us -> 134 us  [body(): norms = lax.psum(part, 'bhi')]
  transfers between devices with their start and end apart: 14 -> 15, of which waited for: 4 -> 4; matrix products, arithmetic and copies ran while one was open for 6% -> 6% of each run, Pallas kernels for 0% -> 0%
where the time goes in v11:
time: 308 us; the launch traced here: 307 us
  blocking collectives  154 us (50%)
  starting transfers between devices  59.7 us (19%)
  waiting for transfers between devices  54.8 us (18%)
  between operations  14.8 us (5%)
  local copies, waits for them, and re-layouts  11.6 us (4%)
  matrix products  8.96 us (3%)
  other arithmetic  3.41 us (1%)
    psum x8, blocking collectives, body(): norms = lax.psum(part, 'bhi')  134 us
    ppermute x7, starting transfers between devices, body(): came = lax.ppermute(rise[:, mine - 1], 'bhi', shift)  41.1 us
    all_gather x1, waiting for transfers between devices, body(): slabs = lax.all_gather(slabs, 'sx', axis=0, tiled=True)  34.1 us
    all_to_all x1, starting transfers between devices, body(): lax.all_to_all(jnp.concatenate([ordered, tagged], axis=2), 'bhi', 1, 1, t...  12.6 us
    all_to_all x1, waiting for transfers between devices, body(): lax.all_to_all(jnp.concatenate([ordered, tagged], axis=2), 'bhi', 1, 1, t...  11.3 us
    all_to_all x1, blocking collectives, body(): back = lax.all_to_all(result, SECT, 0, 0, tiled=False)  10.9 us
    all_gather x1, blocking collectives, body(): slabs = lax.all_gather(tensors[0], 'sy', axis=0, tiled=False)  9.28 us
    dot_general x8, matrix products, site_images(): jnp.einsum('rck,bckl->brcl', parts, weights, preferred_element_type=jnp.f...  8.77 us
  transfers between devices with their start and end apart: 15, of which 4 were waited for; matrix products, arithmetic and copies ran while one was open for 6% of the time, Pallas kernels for 0%

profile of v11, /device:TPU:64, one launch (start us, length us, event | category | flops | bytes accessed | tf_op | source)
XLA Modules:
  0.0 307.0 jit_solution(17741188268907290202)
XLA Ops:
  7.2 9.3 %all_gather.21 = bf16[2,2,2,128,128]{4,3,2,1,0:T(8,128)(2,1)} all-gather(bf16[1,2,2,128,128]{4,3,2,1,0:T(8,128)(2,1)} %param.7), channel_id=1, replica_groups=mesh['sx'=4,'sy'=2,'bhi'=8,'blo'=8] {'sy'}, dimensions={0}, use_global_device_ids=true | all-gather | bytes 393216 | tf_op jit(solution)/shard_map/all_gather | solution.py:44
  16.6 34.1 %all-gather.7.cloned.1.call-done = bf16[8,2,2,128,128]{4,3,2,1,0:T(8,128)(2,1)} async-done(((bf16[2,2,2,128,128]{4,3,2,1,0:T(8,128)(2,1)}), bf16[8,2,2,128,128]{4,3,2,1,0:T(8,128)(2,1)}) %all-gather.7.cloned.1.call-update) | async-done | bytes 1048592 | tf_op jit(solution)/shard_map/all_gather | solution.py:45
  50.6 1.0 fusion.56
  51.6 0.7 copy.117
  52.4 1.2 fusion.57
  53.5 0.7 copy.150
  54.4 0.7 copy.153
  55.2 0.7 copy.156
  55.9 0.5 broadcast.258
  56.4 0.7 reduce.55
  57.1 0.7 all_to_all.12
  57.8 5.8 %all-to-all-start = ((s32[8,1,2]{2,1,0:T(1,128)}), s32[8,1,2]{2,1,0:T(1,128)S(1)}, u32[]{:S(2)}, u32[]{:S(2)}) async-start(s32[8,1,2]{2,1,0:T(1,128)} %bitcast.2), calls=%async_computation | async-start | bytes 8192 | tf_op jit(solution)/shard_map/all_to_all | solution.py:47
  63.6 0.2 fusion
  63.8 0.1 copy.111
  64.0 7.0 %all-to-all-done = s32[8,1,2]{2,1,0:T(1,128)S(1)} async-done(((s32[8,1,2]{2,1,0:T(1,128)}), s32[8,1,2]{2,1,0:T(1,128)S(1)}, u32[]{:S(2)}, u32[]{:S(2)}) %all-to-all-start) | async-done | bytes 96 | tf_op jit(solution)/shard_map/all_to_all | solution.py:47
  71.1 0.7 copy.114
  71.8 12.6 %all-to-all-start.1 = ((bf16[2,8,2056]{2,0,1:T(2,128)(2,1)}), bf16[2,8,2056]{2,0,1:T(2,128)(2,1)S(1)}, u32[]{:S(2)}, u32[]{:S(2)}) async-start(bf16[2,8,2056]{2,0,1:T(2,128)(2,1)} %copy.114), calls=%async_computation.1 | async-start | bytes 139264 | tf_op jit(solution)/shard_map/all_to_all | solution.py:53
  84.4 11.3 %all-to-all-done.1 = bf16[2,8,2056]{2,0,1:T(2,128)(2,1)S(1)} async-done(((bf16[2,8,2056]{2,0,1:T(2,128)(2,1)}), bf16[2,8,2056]{2,0,1:T(2,128)(2,1)S(1)}, u32[]{:S(2)}, u32[]{:S(2)}) %all-to-all-start.1) | async-done | bytes 65824 | tf_op jit(solution)/shard_map/all_to_all | solution.py:53
  95.7 0.3 fusion.47
  96.0 0.7 copy.135
  96.7 1.5 convolution_bitcast_fusion.7
  98.3 0.1 multiply_reduce_fusion.13
  98.5 18.4 %psum.56 = f32[2,16]{0,1:T(8,128)S(1)} all-reduce(f32[2,16]{0,1:T(8,128)S(1)} %copy.119), channel_id=1, replica_groups=mesh['sx'=4,'sy'=2,'bhi'=8,'blo'=8] {'bhi'}, use_global_device_ids=true, to_apply=%region_2.0 | all-reduce | flops 32 | bytes 256 | tf_op jit(solution)/shard_map/psum | solution.py:75
  116.9 0.2 slice_reduce_fusion.12
  117.1 4.1 %collective-permute-start = (f32[16,128]{1,0:T(8,128)S(1)}, f32[16,128]{1,0:T(8,128)S(1)}, u32[]{:S(2)}, u32[]{:S(2)}) collective-permute-start(f32[16,128]{1,0:T(8,128)S(1)} %slice_bitcast_fusion.32), channel_id=1, source_target_pairs={{0,8},{8,16},{16,24},{24,32},{32,40},{40,48},{48,56},{56,0},{1,9},... | collective-permute-start | bytes 24584 | tf_op jit(solution)/shard_map/ppermute | solution.py:76
  121.3 2.3 collective-permute-done
  123.7 1.6 convolution_bitcast_fusion.6
  125.4 0.1 multiply_reduce_fusion.11
  125.6 5.4 %collective-permute-start.1 = (f32[16,128]{1,0:T(8,128)S(1)}, f32[16,128]{1,0:T(8,128)S(1)}, u32[]{:S(2)}, u32[]{:S(2)}) collective-permute-start(f32[16,128]{1,0:T(8,128)S(1)} %slice_bitcast_fusion.31), channel_id=1, source_target_pairs={{0,8},{8,16},{16,24},{24,32},{32,40},{40,48},{48,56},{56,0},{1,9},... | collective-permute-start | bytes 24584 | tf_op jit(solution)/shard_map/ppermute | solution.py:76
  131.1 15.9 %psum.57 = f32[2,16]{0,1:T(8,128)S(1)} all-reduce(f32[2,16]{0,1:T(8,128)S(1)} %copy.122), channel_id=1, replica_groups=mesh['sx'=4,'sy'=2,'bhi'=8,'blo'=8] {'bhi'}, use_global_device_ids=true, to_apply=%region_5.6 | all-reduce | flops 32 | bytes 256 | tf_op jit(solution)/shard_map/psum | solution.py:75
  147.0 0.2 slice_reduce_fusion.10
  147.3 0.3 convolution_bitcast_fusion.5
  147.7 0.1 multiply_reduce_fusion.9
  147.8 6.3 %collective-permute-start.2 = (f32[16,128]{1,0:T(8,128)S(1)}, f32[16,128]{1,0:T(8,128)S(1)}, u32[]{:S(2)}, u32[]{:S(2)}) collective-permute-start(f32[16,128]{1,0:T(8,128)S(1)} %slice_bitcast_fusion.30), channel_id=1, source_target_pairs={{0,8},{8,16},{16,24},{24,32},{32,40},{40,48},{48,56},{56,0},{1,9},... | collective-permute-start | bytes 24584 | tf_op jit(solution)/shard_map/ppermute | solution.py:76
  154.3 15.9 %psum.58 = f32[2,16]{0,1:T(8,128)S(1)} all-reduce(f32[2,16]{0,1:T(8,128)S(1)} %copy.124), channel_id=1, replica_groups=mesh['sx'=4,'sy'=2,'bhi'=8,'blo'=8] {'bhi'}, use_global_device_ids=true, to_apply=%region_8.9 | all-reduce | flops 32 | bytes 256 | tf_op jit(solution)/shard_map/psum | solution.py:75
  170.2 0.2 slice_reduce_fusion.8
  170.5 1.7 convolution_bitcast_fusion.4
  172.2 0.1 multiply_reduce_fusion.7
  172.4 6.3 %collective-permute-start.3 = (f32[16,128]{1,0:T(8,128)S(1)}, f32[16,128]{1,0:T(8,128)S(1)}, u32[]{:S(2)}, u32[]{:S(2)}) collective-permute-start(f32[16,128]{1,0:T(8,128)S(1)} %slice_bitcast_fusion.29), channel_id=1, source_target_pairs={{0,8},{8,16},{16,24},{24,32},{32,40},{40,48},{48,56},{56,0},{1,9},... | collective-permute-start | bytes 24584 | tf_op jit(solution)/shard_map/ppermute | solution.py:76
  178.8 16.0 %psum.59 = f32[2,16]{0,1:T(8,128)S(1)} all-reduce(f32[2,16]{0,1:T(8,128)S(1)} %copy.127), channel_id=1, replica_groups=mesh['sx'=4,'sy'=2,'bhi'=8,'blo'=8] {'bhi'}, use_global_device_ids=true, to_apply=%region_11.12 | all-reduce | flops 32 | bytes 256 | tf_op jit(solution)/shard_map/psum | solution.py:75
  194.8 0.2 slice_reduce_fusion.6
  195.2 0.3 convolution_bitcast_fusion.3
  195.5 0.1 multiply_reduce_fusion.5
  195.7 6.3 %collective-permute-start.4 = (f32[16,128]{1,0:T(8,128)S(1)}, f32[16,128]{1,0:T(8,128)S(1)}, u32[]{:S(2)}, u32[]{:S(2)}) collective-permute-start(f32[16,128]{1,0:T(8,128)S(1)} %slice_bitcast_fusion.28), channel_id=1, source_target_pairs={{0,8},{8,16},{16,24},{24,32},{32,40},{40,48},{48,56},{56,0},{1,9},... | collective-permute-start | bytes 24584 | tf_op jit(solution)/shard_map/ppermute | solution.py:76
  202.1 16.2 %psum.60 = f32[2,16]{0,1:T(8,128)S(1)} all-reduce(f32[2,16]{0,1:T(8,128)S(1)} %copy.129), channel_id=1, replica_groups=mesh['sx'=4,'sy'=2,'bhi'=8,'blo'=8] {'bhi'}, use_global_device_ids=true, to_apply=%region_14.15 | all-reduce | flops 32 | bytes 256 | tf_op jit(solution)/shard_map/psum | solution.py:75
  218.3 0.2 slice_reduce_fusion.4
  218.6 1.6 convolution_bitcast_fusion.2
  220.4 0.1 multiply_reduce_fusion.3
  220.5 6.3 %collective-permute-start.5 = (f32[16,128]{1,0:T(8,128)S(1)}, f32[16,128]{1,0:T(8,128)S(1)}, u32[]{:S(2)}, u32[]{:S(2)}) collective-permute-start(f32[16,128]{1,0:T(8,128)S(1)} %slice_bitcast_fusion.27), channel_id=1, source_target_pairs={{0,8},{8,16},{16,24},{24,32},{32,40},{40,48},{48,56},{56,0},{1,9},... | collective-permute-start | bytes 24584 | tf_op jit(solution)/shard_map/ppermute | solution.py:76
  226.9 15.9 %psum.61 = f32[2,16]{0,1:T(8,128)S(1)} all-reduce(f32[2,16]{0,1:T(8,128)S(1)} %copy.132), channel_id=1, replica_groups=mesh['sx'=4,'sy'=2,'bhi'=8,'blo'=8] {'bhi'}, use_global_device_ids=true, to_apply=%region_17.18 | all-reduce | flops 32 | bytes 256 | tf_op jit(solution)/shard_map/psum | solution.py:75
  242.9 0.2 slice_reduce_fusion.2
  243.2 0.3 convolution_bitcast_fusion.1
  243.5 6.3 %collective-permute-start.6 = (f32[16,128]{1,0:T(8,128)S(1)}, f32[16,128]{1,0:T(8,128)S(1)}, u32[]{:S(2)}, u32[]{:S(2)}) collective-permute-start(f32[16,128]{1,0:T(8,128)S(1)} %slice_bitcast_fusion.26), channel_id=1, source_target_pairs={{0,8},{8,16},{16,24},{24,32},{32,40},{40,48},{48,56},{56,0},{1,9},... | collective-permute-start | bytes 24584 | tf_op jit(solution)/shard_map/ppermute | solution.py:76
  249.9 0.1 multiply_reduce_fusion.1
  250.1 15.9 %psum.62 = f32[2,16]{0,1:T(8,128)S(1)} all-reduce(f32[2,16]{0,1:T(8,128)S(1)} %copy.134), channel_id=1, replica_groups=mesh['sx'=4,'sy'=2,'bhi'=8,'blo'=8] {'bhi'}, use_global_device_ids=true, to_apply=%region_20.21 | all-reduce | flops 32 | bytes 256 | tf_op jit(solution)/shard_map/psum | solution.py:75
  266.0 0.2 slice_reduce_fusion
  266.2 0.1 reduce-precision_convert_fusion
  266.4 1.5 convolution_bitcast_fusion
  267.9 0.1 fusion.12
  268.1 19.4 %psum.63 = f32[2,16]{0,1:T(8,128)S(1)} all-reduce(f32[2,16]{0,1:T(8,128)S(1)} %copy.136), channel_id=1, replica_groups=mesh['sx'=4,'sy'=2,'bhi'=8,'blo'=8] {'bhi'}, use_global_device_ids=true, to_apply=%region_23.24 | all-reduce | flops 32 | bytes 256 | tf_op jit(solution)/shard_map/psum | solution.py:75
  287.6 0.1 log_add_fusion
  288.1 10.9 %all_to_all.19 = f32[8,2,2]{2,1,0:T(2,128)S(1)} all-to-all(f32[8,2,2]{2,1,0:T(2,128)S(1)} %copy.139), channel_id=1, replica_groups=mesh['sx'=4,'sy'=2,'bhi'=8,'blo'=8] {'sx','sy'}, dimensions={0} | all-to-all | bytes 256 | tf_op jit(solution)/shard_map/all_to_all | solution.py:92
  299.0 0.6 squeeze.190
  299.6 0.6 squeeze.191
  (110 shorter events, 3.1 us)
Async XLA Ops:
  7.2 56.4 %copy-start = (bf16[16,16384]{1,0:T(8,128)(2,1)S(1)}, bf16[16,16384]{1,0:T(8,128)(2,1)}, u32[]{:S(2)}) copy-start(bf16[16,16384]{1,0:T(8,128)(2,1)} %param.6) | copy-start | bytes 1572868
  7.2 43.5 %all-gather.7.cloned.1.call-start = ((), (), s32[]{:S(2)}) async-start(), calls=%async_computation.3 | async-start | bytes 1310720 | tf_op jit(solution)/shard_map/all_gather | solution.py:45
  16.5 80.2 %all-gather.9.cloned.1.call-start = ((), (), s32[]{:S(2)}) async-start(), calls=%async_computation.4 | async-start | bytes 1179648 | tf_op jit(solution)/shard_map/all_gather | solution.py:66
  52.3 4.1 %copy-start.5 = (s32[1,16]{1,0:T(1,128)S(1)}, s32[1,16]{1,0:T(1,128)}, u32[]{:S(2)}) copy-start(s32[1,16]{1,0:T(1,128)} %param.4) | copy-start | bytes 196
  52.3 11.3 %copy-start.4 = (s32[128]{0:T(128)S(1)}, s32[128]{0:T(128)}, u32[]{:S(2)}) copy-start(s32[128]{0:T(128)} %param.5) | copy-start | bytes 1540
  52.3 71.4 %all-gather.11.cloned.1.call-start = ((), (), s32[]{:S(2)}) async-start(), calls=%async_computation.5 | async-start | bytes 2359296 | tf_op jit(solution)/shard_map/all_gather | solution.py:66
  54.3 116.2 %all-gather.13.cloned.1.call-start = ((), (), s32[]{:S(2)}) async-start(), calls=%async_computation.6 | async-start | bytes 2359296 | tf_op jit(solution)/shard_map/all_gather | solution.py:66
  55.1 163.5 %all-gather.15.cloned.1.call-start = ((), (), s32[]{:S(2)}) async-start(), calls=%async_computation.7 | async-start | bytes 2359296 | tf_op jit(solution)/shard_map/all_gather | solution.py:66
  57.8 13.3 %all-to-all-start = ((s32[8,1,2]{2,1,0:T(1,128)}), s32[8,1,2]{2,1,0:T(1,128)S(1)}, u32[]{:S(2)}, u32[]{:S(2)}) async-start(s32[8,1,2]{2,1,0:T(1,128)} %bitcast.2), calls=%async_computation | async-start | bytes 8192 | tf_op jit(solution)/shard_map/all_to_all | solution.py:47
  71.8 23.8 %all-to-all-start.1 = ((bf16[2,8,2056]{2,0,1:T(2,128)(2,1)}), bf16[2,8,2056]{2,0,1:T(2,128)(2,1)S(1)}, u32[]{:S(2)}, u32[]{:S(2)}) async-start(bf16[2,8,2056]{2,0,1:T(2,128)(2,1)} %copy.114), calls=%async_computation.1 | async-start | bytes 139264 | tf_op jit(solution)/shard_map/all_to_all | solution.py:53
  84.4 182.0 %all-gather.17.cloned.1.call-start = ((), (), s32[]{:S(2)}) async-start(), calls=%async_computation.8 | async-start | bytes 1179648 | tf_op jit(solution)/shard_map/all_gather | solution.py:66
  117.1 6.4 %collective-permute-start = (f32[16,128]{1,0:T(8,128)S(1)}, f32[16,128]{1,0:T(8,128)S(1)}, u32[]{:S(2)}, u32[]{:S(2)}) collective-permute-start(f32[16,128]{1,0:T(8,128)S(1)} %slice_bitcast_fusion.32), channel_id=1, source_target_pairs={{0,8},{8,16},{16,24},{24,32},{32,40},{40,48},{48,56},{56,0},{1,9},... | collective-permute-start | bytes 24584 | tf_op jit(solution)/shard_map/ppermute | solution.py:76
  123.7 23.6 %copy-start.3 = (bf16[2,2,16,128,128]{4,3,1,2,0:T(8,128)(2,1)S(1)}, bf16[2,2,16,128,128]{4,3,1,2,0:T(8,128)(2,1)}, u32[]{:S(2)}) copy-start(bf16[2,2,16,128,128]{4,3,1,2,0:T(8,128)(2,1)} %all-gather.11.cloned.1.call-done) | copy-start | bytes 6291460
  125.6 21.7 %collective-permute-start.1 = (f32[16,128]{1,0:T(8,128)S(1)}, f32[16,128]{1,0:T(8,128)S(1)}, u32[]{:S(2)}, u32[]{:S(2)}) collective-permute-start(f32[16,128]{1,0:T(8,128)S(1)} %slice_bitcast_fusion.31), channel_id=1, source_target_pairs={{0,8},{8,16},{16,24},{24,32},{32,40},{40,48},{48,56},{56,0},{1,9},... | collective-permute-start | bytes 24584 | tf_op jit(solution)/shard_map/ppermute | solution.py:76
  147.8 22.6 %collective-permute-start.2 = (f32[16,128]{1,0:T(8,128)S(1)}, f32[16,128]{1,0:T(8,128)S(1)}, u32[]{:S(2)}, u32[]{:S(2)}) collective-permute-start(f32[16,128]{1,0:T(8,128)S(1)} %slice_bitcast_fusion.30), channel_id=1, source_target_pairs={{0,8},{8,16},{16,24},{24,32},{32,40},{40,48},{48,56},{56,0},{1,9},... | collective-permute-start | bytes 24584 | tf_op jit(solution)/shard_map/ppermute | solution.py:76
  170.5 24.7 %copy-start.2 = (bf16[2,2,16,128,128]{4,3,1,2,0:T(8,128)(2,1)S(1)}, bf16[2,2,16,128,128]{4,3,1,2,0:T(8,128)(2,1)}, u32[]{:S(2)}) copy-start(bf16[2,2,16,128,128]{4,3,1,2,0:T(8,128)(2,1)} %all-gather.13.cloned.1.call-done) | copy-start | bytes 6291460
  172.4 22.7 %collective-permute-start.3 = (f32[16,128]{1,0:T(8,128)S(1)}, f32[16,128]{1,0:T(8,128)S(1)}, u32[]{:S(2)}, u32[]{:S(2)}) collective-permute-start(f32[16,128]{1,0:T(8,128)S(1)} %slice_bitcast_fusion.29), channel_id=1, source_target_pairs={{0,8},{8,16},{16,24},{24,32},{32,40},{40,48},{48,56},{56,0},{1,9},... | collective-permute-start | bytes 24584 | tf_op jit(solution)/shard_map/ppermute | solution.py:76
  195.7 22.8 %collective-permute-start.4 = (f32[16,128]{1,0:T(8,128)S(1)}, f32[16,128]{1,0:T(8,128)S(1)}, u32[]{:S(2)}, u32[]{:S(2)}) collective-permute-start(f32[16,128]{1,0:T(8,128)S(1)} %slice_bitcast_fusion.28), channel_id=1, source_target_pairs={{0,8},{8,16},{16,24},{24,32},{32,40},{40,48},{48,56},{56,0},{1,9},... | collective-permute-start | bytes 24584 | tf_op jit(solution)/shard_map/ppermute | solution.py:76
  218.6 24.5 %copy-start.1 = (bf16[2,2,16,128,128]{4,3,1,2,0:T(8,128)(2,1)S(1)}, bf16[2,2,16,128,128]{4,3,1,2,0:T(8,128)(2,1)}, u32[]{:S(2)}) copy-start(bf16[2,2,16,128,128]{4,3,1,2,0:T(8,128)(2,1)} %all-gather.15.cloned.1.call-done) | copy-start | bytes 6291460
  220.5 22.6 %collective-permute-start.5 = (f32[16,128]{1,0:T(8,128)S(1)}, f32[16,128]{1,0:T(8,128)S(1)}, u32[]{:S(2)}, u32[]{:S(2)}) collective-permute-start(f32[16,128]{1,0:T(8,128)S(1)} %slice_bitcast_fusion.27), channel_id=1, source_target_pairs={{0,8},{8,16},{16,24},{24,32},{32,40},{40,48},{48,56},{56,0},{1,9},... | collective-permute-start | bytes 24584 | tf_op jit(solution)/shard_map/ppermute | solution.py:76
  243.5 22.7 %collective-permute-start.6 = (f32[16,128]{1,0:T(8,128)S(1)}, f32[16,128]{1,0:T(8,128)S(1)}, u32[]{:S(2)}, u32[]{:S(2)}) collective-permute-start(f32[16,128]{1,0:T(8,128)S(1)} %slice_bitcast_fusion.26), channel_id=1, source_target_pairs={{0,8},{8,16},{16,24},{24,32},{32,40},{40,48},{48,56},{56,0},{1,9},... | collective-permute-start | bytes 24584 | tf_op jit(solution)/shard_map/ppermute | solution.py:76
Sparse Core Ops, SparseCore 0:
  16.7 33.9 all-gather.6
  52.8 29.8 all-gather.8
  84.9 33.2 all-gather.10
  120.2 32.7 all-gather.12
  155.0 33.2 all-gather.14
  190.3 30.6 all-gather.16

commit v12 on v10

--- a/solution.py
+++ b/solution.py
@@ -6,6 +6,7 @@
 
 PARTS = 8
 SECT = ("sx", "sy")
+BHI = ("bh1", "bh2")
 
 
 def charge_order(labels, rows, block):
@@ -29,9 +30,9 @@
 
 def body(bits, labels, left, tensors):
     sect = lax.axis_index(SECT)
-    bhi = lax.axis_index("bhi")
+    bhi = lax.axis_index(BHI)
     n_sect = lax.axis_size("sx") * lax.axis_size("sy")
-    n_hi = lax.axis_size("bhi")
+    n_hi = lax.axis_size("bh1") * lax.axis_size("bh2")
     n_lo = lax.axis_size("blo")
     block = tensors.shape[-1]
     count_blocks = labels.shape[0]
@@ -50,7 +51,7 @@
     rows = lax.dynamic_slice_in_dim(left, sect * pick, pick, 0)
     ordered = charge_order(labels, rows, block).reshape(pick, n_hi, mine * block)
     tagged = jnp.broadcast_to(row_bits[:, None, :], (pick, n_hi, sites))
-    spread = lax.all_to_all(jnp.concatenate([ordered, tagged], axis=2), "bhi", 1, 1, tiled=False)
+    spread = lax.all_to_all(jnp.concatenate([ordered, tagged], axis=2), BHI, 1, 1, tiled=False)
     count_rows = n_hi * pick
     spread = jnp.transpose(spread, (1, 0, 2)).reshape(count_rows, mine * block + sites)
     state = spread[:, : mine * block].reshape(count_rows, mine, block).astype(jnp.float32)
@@ -74,8 +75,9 @@
         stay = image[0]
         rise = image[1]
         part = jnp.stack([jnp.sum(stay * stay, axis=(1, 2)), jnp.sum(rise * rise, axis=(1, 2))])
-        norms = lax.psum(part, "bhi")
-        came = lax.ppermute(rise[:, mine - 1], "bhi", shift)
+        norms = lax.optimization_barrier(lax.psum(part, "bh2"))
+        norms = lax.psum(norms, "bh1")
+        came = lax.ppermute(rise[:, mine - 1], BHI, shift)
         raised = jnp.concatenate([came[:, None], rise[:, : mine - 1]], axis=1)
         norm_zero = norms[0]
         norm_one = norms[1]
@@ -99,8 +101,9 @@
 def solution(mesh):
     n_sect, n_blk = mesh.devices.shape
     n_x = n_sect // 2
-    fine = Mesh(mesh.devices.reshape(n_x, 2, PARTS, n_blk // PARTS), ("sx", "sy", "bhi", "blo"))
-    blk = ("bhi", "blo")
+    grid = mesh.devices.reshape(n_x, 2, PARTS // 2, 2, n_blk // PARTS)
+    fine = Mesh(grid, ("sx", "sy", "bh1", "bh2", "blo"))
+    blk = ("bh1", "bh2", "blo")
     in_specs = (P(SECT, blk), P(), P(blk, None), P(SECT, None, blk, None, None))
     out_specs = (P(SECT, blk), P(SECT, blk))
     return jax.shard_map(body, mesh=fine, in_specs=in_specs, out_specs=out_specs, check_vma=False)

time: 307 us -> 317 us (1.033)
  the two profiles are of different devices: /device:TPU:64 before, /device:TPU:2 now
where the time goes in v12:
time: 317 us; the launch traced here: 316 us
  blocking collectives  212 us (67%)
  starting transfers between devices  35.5 us (11%)
  waiting for transfers between devices  28.7 us (9%)
  between operations  14.8 us (5%)
  local copies, waits for them, and re-layouts  11 us (3%)
  matrix products  9.59 us (3%)
  other arithmetic  4.11 us (1%)
    psum x8, blocking collectives, body(): norms = lax.psum(norms, 'bh1')  115 us
    psum x8, blocking collectives, body(): norms = lax.optimization_barrier(lax.psum(part, 'bh2'))  48.1 us
    ppermute x7, starting transfers between devices, body(): came = lax.ppermute(rise[:, mine - 1], BHI, shift)  27.9 us
    all_to_all x1, blocking collectives, body(): lax.all_to_all(jnp.concatenate([ordered, tagged], axis=2), BHI, 1, 1, til...  27.1 us
    all_gather x5, waiting for transfers between devices, body(): got = lax.all_gather(piece, 'blo', axis=2, tiled=True)  19.5 us
    all_to_all x1, blocking collectives, body(): back = lax.all_to_all(result, SECT, 0, 0, tiled=False)  12.8 us
    all_gather x1, blocking collectives, body(): slabs = lax.all_gather(tensors[0], 'sy', axis=0, tiled=False)  9.28 us
    dot_general x8, matrix products, site_images(): jnp.einsum('rck,bckl->brcl', parts, weights, preferred_element_type=jnp.f...  8.74 us
  transfers between devices with their start and end apart: 14, of which 4 were waited for; matrix products, arithmetic and copies ran while one was open for 6% of the time, Pallas kernels for 0%

profile of v12, /device:TPU:2, one launch (start us, length us, event | category | flops | bytes accessed | tf_op | source)
XLA Modules:
  0.0 315.7 jit_solution(16331787611435094546)
XLA Ops:
  7.2 9.3 %all_gather.21 = bf16[2,2,2,128,128]{4,3,2,1,0:T(8,128)(2,1)} all-gather(bf16[1,2,2,128,128]{4,3,2,1,0:T(8,128)(2,1)} %param.7), channel_id=1, replica_groups=mesh['sx'=4,'sy'=2,'bh1'=4,'bh2'=2,'blo'=8] {'sy'}, dimensions={0}, use_global_device_ids=true | all-gather | bytes 393216 | tf_op jit(solution)/shard_map/all_gather | solution.py:45
  16.5 0.5 broadcast.258
  17.0 1.3 reduce.55
  18.4 0.7 all_to_all.12
  19.0 7.4 %all-to-all-start = ((s32[8,1,2]{2,1,0:T(1,128)}), s32[8,1,2]{2,1,0:T(1,128)S(1)}, u32[]{:S(2)}, u32[]{:S(2)}) async-start(s32[8,1,2]{2,1,0:T(1,128)} %bitcast.2), calls=%async_computation | async-start | bytes 8192 | tf_op jit(solution)/shard_map/all_to_all | solution.py:48
  26.6 0.8 fusion
  27.6 5.1 %all-to-all-done = s32[8,1,2]{2,1,0:T(1,128)S(1)} async-done(((s32[8,1,2]{2,1,0:T(1,128)}), s32[8,1,2]{2,1,0:T(1,128)S(1)}, u32[]{:S(2)}, u32[]{:S(2)}) %all-to-all-start) | async-done | bytes 96 | tf_op jit(solution)/shard_map/all_to_all | solution.py:48
  32.9 27.1 %all_to_all.19 = bf16[2,8,2056]{2,0,1:T(2,128)(2,1)S(1)} all-to-all(bf16[2,8,2056]{2,0,1:T(2,128)(2,1)S(1)} %copy.114), channel_id=1, replica_groups=mesh['sx'=4,'sy'=2,'bh1'=4,'bh2'=2,'blo'=8] {'bh1','bh2'}, dimensions={1} | all-to-all | bytes 131584 | tf_op jit(solution)/shard_map/all_to_all | solution.py:54
  60.1 1.0 fusion.56
  61.1 0.7 copy.115
  61.8 1.2 fusion.57
  63.0 0.7 copy.150
  63.8 0.7 copy.153
  64.6 0.7 copy.156
  65.4 0.3 fusion.47
  65.7 0.7 copy.135
  66.5 16.9 %all-gather.9.cloned.1.call-done = bf16[1,2,16,128,128]{4,3,1,0,2:T(8,128)(2,1)} async-done(((bf16[1,2,2,128,128]{4,3,1,0,2:T(8,128)(2,1)}), bf16[1,2,16,128,128]{4,3,1,0,2:T(8,128)(2,1)}) %all-gather.9.cloned.1.call-update) | async-done | bytes 1048592 | tf_op jit(solution)/shard_map/all_gather | solution.py:69
  83.4 1.5 convolution_bitcast_fusion
  85.0 0.1 multiply_reduce_fusion.13
  85.2 5.9 %psum.112 = f32[2,16]{0,1:T(8,128)S(1)} all-reduce(f32[2,16]{0,1:T(8,128)S(1)} %copy.119), channel_id=1, replica_groups=mesh['sx'=4,'sy'=2,'bh1'=4,'bh2'=2,'blo'=8] {'bh2'}, use_global_device_ids=true, to_apply=%region_2.0 | all-reduce | flops 32 | bytes 256 | tf_op jit(solution)/shard_map/psum | solution.py:78
  91.1 17.2 %psum.113 = f32[2,16]{0,1:T(8,128)S(1)} all-reduce(f32[2,16]{0,1:T(8,128)S(1)} %psum.112), channel_id=1, replica_groups=mesh['sx'=4,'sy'=2,'bh1'=4,'bh2'=2,'blo'=8] {'bh1'}, use_global_device_ids=true, to_apply=%region_3.0 | all-reduce | flops 32 | bytes 256 | tf_op jit(solution)/shard_map/psum | solution.py:79
  108.2 0.2 slice_reduce_fusion.12
  108.4 3.7 %collective-permute-start = (f32[16,128]{1,0:T(8,128)S(1)}, f32[16,128]{1,0:T(8,128)S(1)}, u32[]{:S(2)}, u32[]{:S(2)}) collective-permute-start(f32[16,128]{1,0:T(8,128)S(1)} %slice_bitcast_fusion.32), channel_id=1, source_target_pairs={{0,8},{8,16},{16,24},{24,32},{32,40},{40,48},{48,56},{56,0},{1,9},... | collective-permute-start | bytes 24584 | tf_op jit(solution)/shard_map/ppermute | solution.py:80
  112.1 3.9 %collective-permute-done = f32[16,128]{1,0:T(8,128)S(1)} collective-permute-done((f32[16,128]{1,0:T(8,128)S(1)}, f32[16,128]{1,0:T(8,128)S(1)}, u32[]{:S(2)}, u32[]{:S(2)}) %collective-permute-start) | collective-permute-done | bytes 8224 | tf_op jit(solution)/shard_map/ppermute | solution.py:80
  116.2 2.5 all-gather.11.cloned.1.call-done
  118.7 1.6 convolution_bitcast_fusion.7
  120.4 0.1 multiply_reduce_fusion.11
  120.5 4.5 %collective-permute-start.1 = (f32[16,128]{1,0:T(8,128)S(1)}, f32[16,128]{1,0:T(8,128)S(1)}, u32[]{:S(2)}, u32[]{:S(2)}) collective-permute-start(f32[16,128]{1,0:T(8,128)S(1)} %slice_bitcast_fusion.31), channel_id=1, source_target_pairs={{0,8},{8,16},{16,24},{24,32},{32,40},{40,48},{48,56},{56,0},{1,9},... | collective-permute-start | bytes 24584 | tf_op jit(solution)/shard_map/ppermute | solution.py:80
  125.1 6.7 %psum.114 = f32[2,16]{0,1:T(8,128)S(1)} all-reduce(f32[2,16]{0,1:T(8,128)S(1)} %copy.122), channel_id=1, replica_groups=mesh['sx'=4,'sy'=2,'bh1'=4,'bh2'=2,'blo'=8] {'bh2'}, use_global_device_ids=true, to_apply=%region_6.7 | all-reduce | flops 32 | bytes 256 | tf_op jit(solution)/shard_map/psum | solution.py:78
  131.9 16.1 %psum.115 = f32[2,16]{0,1:T(8,128)S(1)} all-reduce(f32[2,16]{0,1:T(8,128)S(1)} %psum.114), channel_id=1, replica_groups=mesh['sx'=4,'sy'=2,'bh1'=4,'bh2'=2,'blo'=8] {'bh1'}, use_global_device_ids=true, to_apply=%region_7.8 | all-reduce | flops 32 | bytes 256 | tf_op jit(solution)/shard_map/psum | solution.py:79
  148.0 0.2 slice_reduce_fusion.10
  148.3 0.3 convolution_bitcast_fusion.6
  148.7 0.1 multiply_reduce_fusion.9
  148.8 5.0 %collective-permute-start.2 = (f32[16,128]{1,0:T(8,128)S(1)}, f32[16,128]{1,0:T(8,128)S(1)}, u32[]{:S(2)}, u32[]{:S(2)}) collective-permute-start(f32[16,128]{1,0:T(8,128)S(1)} %slice_bitcast_fusion.30), channel_id=1, source_target_pairs={{0,8},{8,16},{16,24},{24,32},{32,40},{40,48},{48,56},{56,0},{1,9},... | collective-permute-start | bytes 24584 | tf_op jit(solution)/shard_map/ppermute | solution.py:80
  153.9 5.9 %psum.116 = f32[2,16]{0,1:T(8,128)S(1)} all-reduce(f32[2,16]{0,1:T(8,128)S(1)} %copy.124), channel_id=1, replica_groups=mesh['sx'=4,'sy'=2,'bh1'=4,'bh2'=2,'blo'=8] {'bh2'}, use_global_device_ids=true, to_apply=%region_10.11 | all-reduce | flops 32 | bytes 256 | tf_op jit(solution)/shard_map/psum | solution.py:78
  159.8 11.4 %psum.117 = f32[2,16]{0,1:T(8,128)S(1)} all-reduce(f32[2,16]{0,1:T(8,128)S(1)} %psum.116), channel_id=1, replica_groups=mesh['sx'=4,'sy'=2,'bh1'=4,'bh2'=2,'blo'=8] {'bh1'}, use_global_device_ids=true, to_apply=%region_11.12 | all-reduce | flops 32 | bytes 256 | tf_op jit(solution)/shard_map/psum | solution.py:79
  171.2 0.2 slice_reduce_fusion.8
  171.5 1.6 convolution_bitcast_fusion.5
  173.4 4.6 %collective-permute-start.3 = (f32[16,128]{1,0:T(8,128)S(1)}, f32[16,128]{1,0:T(8,128)S(1)}, u32[]{:S(2)}, u32[]{:S(2)}) collective-permute-start(f32[16,128]{1,0:T(8,128)S(1)} %slice_bitcast_fusion.29), channel_id=1, source_target_pairs={{0,8},{8,16},{16,24},{24,32},{32,40},{40,48},{48,56},{56,0},{1,9},... | collective-permute-start | bytes 24584 | tf_op jit(solution)/shard_map/ppermute | solution.py:80
  178.1 6.0 %psum.118 = f32[2,16]{0,1:T(8,128)S(1)} all-reduce(f32[2,16]{0,1:T(8,128)S(1)} %copy.127), channel_id=1, replica_groups=mesh['sx'=4,'sy'=2,'bh1'=4,'bh2'=2,'blo'=8] {'bh2'}, use_global_device_ids=true, to_apply=%region_14.15 | all-reduce | flops 32 | bytes 256 | tf_op jit(solution)/shard_map/psum | solution.py:78
  184.1 13.7 %psum.119 = f32[2,16]{0,1:T(8,128)S(1)} all-reduce(f32[2,16]{0,1:T(8,128)S(1)} %psum.118), channel_id=1, replica_groups=mesh['sx'=4,'sy'=2,'bh1'=4,'bh2'=2,'blo'=8] {'bh1'}, use_global_device_ids=true, to_apply=%region_15.16 | all-reduce | flops 32 | bytes 256 | tf_op jit(solution)/shard_map/psum | solution.py:79
  197.9 0.2 slice_reduce_fusion.6
  198.2 0.3 convolution_bitcast_fusion.4
  198.7 2.7 collective-permute-start.4
  201.5 5.9 %psum.120 = f32[2,16]{0,1:T(8,128)S(1)} all-reduce(f32[2,16]{0,1:T(8,128)S(1)} %copy.129), channel_id=1, replica_groups=mesh['sx'=4,'sy'=2,'bh1'=4,'bh2'=2,'blo'=8] {'bh2'}, use_global_device_ids=true, to_apply=%region_18.19 | all-reduce | flops 32 | bytes 256 | tf_op jit(solution)/shard_map/psum | solution.py:78
  207.4 15.9 %psum.121 = f32[2,16]{0,1:T(8,128)S(1)} all-reduce(f32[2,16]{0,1:T(8,128)S(1)} %psum.120), channel_id=1, replica_groups=mesh['sx'=4,'sy'=2,'bh1'=4,'bh2'=2,'blo'=8] {'bh1'}, use_global_device_ids=true, to_apply=%region_19.20 | all-reduce | flops 32 | bytes 256 | tf_op jit(solution)/shard_map/psum | solution.py:79
  223.3 0.2 slice_reduce_fusion.4
  223.6 1.6 convolution_bitcast_fusion.3
  225.5 2.5 collective-permute-start.5
  228.1 5.9 %psum.122 = f32[2,16]{0,1:T(8,128)S(1)} all-reduce(f32[2,16]{0,1:T(8,128)S(1)} %copy.132), channel_id=1, replica_groups=mesh['sx'=4,'sy'=2,'bh1'=4,'bh2'=2,'blo'=8] {'bh2'}, use_global_device_ids=true, to_apply=%region_22.23 | all-reduce | flops 32 | bytes 256 | tf_op jit(solution)/shard_map/psum | solution.py:78
  234.0 13.5 %psum.123 = f32[2,16]{0,1:T(8,128)S(1)} all-reduce(f32[2,16]{0,1:T(8,128)S(1)} %psum.122), channel_id=1, replica_groups=mesh['sx'=4,'sy'=2,'bh1'=4,'bh2'=2,'blo'=8] {'bh1'}, use_global_device_ids=true, to_apply=%region_23.24 | all-reduce | flops 32 | bytes 256 | tf_op jit(solution)/shard_map/psum | solution.py:79
  247.5 0.2 slice_reduce_fusion.2
  247.8 0.3 convolution_bitcast_fusion.2
  248.2 4.8 %collective-permute-start.6 = (f32[16,128]{1,0:T(8,128)S(1)}, f32[16,128]{1,0:T(8,128)S(1)}, u32[]{:S(2)}, u32[]{:S(2)}) collective-permute-start(f32[16,128]{1,0:T(8,128)S(1)} %slice_bitcast_fusion.26), channel_id=1, source_target_pairs={{0,8},{8,16},{16,24},{24,32},{32,40},{40,48},{48,56},{56,0},{1,9},... | collective-permute-start | bytes 24584 | tf_op jit(solution)/shard_map/ppermute | solution.py:80
  253.0 0.1 multiply_reduce_fusion.1
  253.3 5.9 %psum.124 = f32[2,16]{0,1:T(8,128)S(1)} all-reduce(f32[2,16]{0,1:T(8,128)S(1)} %copy.134), channel_id=1, replica_groups=mesh['sx'=4,'sy'=2,'bh1'=4,'bh2'=2,'blo'=8] {'bh2'}, use_global_device_ids=true, to_apply=%region_26.27 | all-reduce | flops 32 | bytes 256 | tf_op jit(solution)/shard_map/psum | solution.py:78
  259.1 11.3 %psum.125 = f32[2,16]{0,1:T(8,128)S(1)} all-reduce(f32[2,16]{0,1:T(8,128)S(1)} %psum.124), channel_id=1, replica_groups=mesh['sx'=4,'sy'=2,'bh1'=4,'bh2'=2,'blo'=8] {'bh1'}, use_global_device_ids=true, to_apply=%region_27.28 | all-reduce | flops 32 | bytes 256 | tf_op jit(solution)/shard_map/psum | solution.py:79
  270.4 0.2 slice_reduce_fusion
  270.8 1.5 convolution_bitcast_fusion.1
  272.6 6.1 %psum.126 = f32[2,16]{0,1:T(8,128)S(1)} all-reduce(f32[2,16]{0,1:T(8,128)S(1)} %copy.136), channel_id=1, replica_groups=mesh['sx'=4,'sy'=2,'bh1'=4,'bh2'=2,'blo'=8] {'bh2'}, use_global_device_ids=true, to_apply=%region_30.31 | all-reduce | flops 32 | bytes 256 | tf_op jit(solution)/shard_map/psum | solution.py:78
  278.6 15.6 %psum.127 = f32[2,16]{0,1:T(8,128)S(1)} all-reduce(f32[2,16]{0,1:T(8,128)S(1)} %psum.126), channel_id=1, replica_groups=mesh['sx'=4,'sy'=2,'bh1'=4,'bh2'=2,'blo'=8] {'bh1'}, use_global_device_ids=true, to_apply=%region_31.32 | all-reduce | flops 32 | bytes 256 | tf_op jit(solution)/shard_map/psum | solution.py:79
  294.8 12.8 %all_to_all.20 = f32[8,2,2]{2,1,0:T(2,128)S(1)} all-to-all(f32[8,2,2]{2,1,0:T(2,128)S(1)} %copy.139), channel_id=1, replica_groups=mesh['sx'=4,'sy'=2,'bh1'=4,'bh2'=2,'blo'=8] {'sx','sy'}, dimensions={0} | all-to-all | bytes 256 | tf_op jit(solution)/shard_map/all_to_all | solution.py:96
  307.6 0.6 squeeze.190
  308.2 0.6 squeeze.191
  (115 shorter events, 4.1 us)
Async XLA Ops:
  7.2 19.3 %copy-start = (bf16[16,16384]{1,0:T(8,128)(2,1)S(1)}, bf16[16,16384]{1,0:T(8,128)(2,1)}, u32[]{:S(2)}) copy-start(bf16[16,16384]{1,0:T(8,128)(2,1)} %param.6) | copy-start | bytes 1572868
  7.2 52.9 %all-gather.7.cloned.1.call-start = ((), (), s32[]{:S(2)}) async-start(), calls=%async_computation.3 | async-start | bytes 1310720 | tf_op jit(solution)/shard_map/all_gather | solution.py:46
  19.0 13.6 %all-to-all-start = ((s32[8,1,2]{2,1,0:T(1,128)}), s32[8,1,2]{2,1,0:T(1,128)S(1)}, u32[]{:S(2)}, u32[]{:S(2)}) async-start(s32[8,1,2]{2,1,0:T(1,128)} %bitcast.2), calls=%async_computation | async-start | bytes 8192 | tf_op jit(solution)/shard_map/all_to_all | solution.py:48
  26.5 57.0 %all-gather.9.cloned.1.call-start = ((), (), s32[]{:S(2)}) async-start(), calls=%async_computation.4 | async-start | bytes 1179648 | tf_op jit(solution)/shard_map/all_gather | solution.py:69
  61.8 56.9 %all-gather.11.cloned.1.call-start = ((), (), s32[]{:S(2)}) async-start(), calls=%async_computation.5 | async-start | bytes 2359296 | tf_op jit(solution)/shard_map/all_gather | solution.py:69
  63.8 107.8 %all-gather.13.cloned.1.call-start = ((), (), s32[]{:S(2)}) async-start(), calls=%async_computation.6 | async-start | bytes 2359296 | tf_op jit(solution)/shard_map/all_gather | solution.py:69
  64.6 159.1 %all-gather.15.cloned.1.call-start = ((), (), s32[]{:S(2)}) async-start(), calls=%async_computation.7 | async-start | bytes 2359296 | tf_op jit(solution)/shard_map/all_gather | solution.py:69
  65.4 205.4 %all-gather.17.cloned.1.call-start = ((), (), s32[]{:S(2)}) async-start(), calls=%async_computation.8 | async-start | bytes 1179648 | tf_op jit(solution)/shard_map/all_gather | solution.py:69
  108.4 7.7 %collective-permute-start = (f32[16,128]{1,0:T(8,128)S(1)}, f32[16,128]{1,0:T(8,128)S(1)}, u32[]{:S(2)}, u32[]{:S(2)}) collective-permute-start(f32[16,128]{1,0:T(8,128)S(1)} %slice_bitcast_fusion.32), channel_id=1, source_target_pairs={{0,8},{8,16},{16,24},{24,32},{32,40},{40,48},{48,56},{56,0},{1,9},... | collective-permute-start | bytes 24584 | tf_op jit(solution)/shard_map/ppermute | solution.py:80
  118.7 29.6 %copy-start.3 = (bf16[2,2,16,128,128]{4,3,1,2,0:T(8,128)(2,1)S(1)}, bf16[2,2,16,128,128]{4,3,1,2,0:T(8,128)(2,1)}, u32[]{:S(2)}) copy-start(bf16[2,2,16,128,128]{4,3,1,2,0:T(8,128)(2,1)} %all-gather.11.cloned.1.call-done) | copy-start | bytes 6291460
  120.5 27.7 %collective-permute-start.1 = (f32[16,128]{1,0:T(8,128)S(1)}, f32[16,128]{1,0:T(8,128)S(1)}, u32[]{:S(2)}, u32[]{:S(2)}) collective-permute-start(f32[16,128]{1,0:T(8,128)S(1)} %slice_bitcast_fusion.31), channel_id=1, source_target_pairs={{0,8},{8,16},{16,24},{24,32},{32,40},{40,48},{48,56},{56,0},{1,9},... | collective-permute-start | bytes 24584 | tf_op jit(solution)/shard_map/ppermute | solution.py:80
  148.8 22.6 %collective-permute-start.2 = (f32[16,128]{1,0:T(8,128)S(1)}, f32[16,128]{1,0:T(8,128)S(1)}, u32[]{:S(2)}, u32[]{:S(2)}) collective-permute-start(f32[16,128]{1,0:T(8,128)S(1)} %slice_bitcast_fusion.30), channel_id=1, source_target_pairs={{0,8},{8,16},{16,24},{24,32},{32,40},{40,48},{48,56},{56,0},{1,9},... | collective-permute-start | bytes 24584 | tf_op jit(solution)/shard_map/ppermute | solution.py:80
  171.5 26.7 %copy-start.2 = (bf16[2,2,16,128,128]{4,3,1,2,0:T(8,128)(2,1)S(1)}, bf16[2,2,16,128,128]{4,3,1,2,0:T(8,128)(2,1)}, u32[]{:S(2)}) copy-start(bf16[2,2,16,128,128]{4,3,1,2,0:T(8,128)(2,1)} %all-gather.13.cloned.1.call-done) | copy-start | bytes 6291460
  173.4 24.7 %collective-permute-start.3 = (f32[16,128]{1,0:T(8,128)S(1)}, f32[16,128]{1,0:T(8,128)S(1)}, u32[]{:S(2)}, u32[]{:S(2)}) collective-permute-start(f32[16,128]{1,0:T(8,128)S(1)} %slice_bitcast_fusion.29), channel_id=1, source_target_pairs={{0,8},{8,16},{16,24},{24,32},{32,40},{40,48},{48,56},{56,0},{1,9},... | collective-permute-start | bytes 24584 | tf_op jit(solution)/shard_map/ppermute | solution.py:80
  198.7 24.8 %collective-permute-start.4 = (f32[16,128]{1,0:T(8,128)S(1)}, f32[16,128]{1,0:T(8,128)S(1)}, u32[]{:S(2)}, u32[]{:S(2)}) collective-permute-start(f32[16,128]{1,0:T(8,128)S(1)} %slice_bitcast_fusion.28), channel_id=1, source_target_pairs={{0,8},{8,16},{16,24},{24,32},{32,40},{40,48},{48,56},{56,0},{1,9},... | collective-permute-start | bytes 24584 | tf_op jit(solution)/shard_map/ppermute | solution.py:80
  223.6 24.2 %copy-start.1 = (bf16[2,2,16,128,128]{4,3,1,2,0:T(8,128)(2,1)S(1)}, bf16[2,2,16,128,128]{4,3,1,2,0:T(8,128)(2,1)}, u32[]{:S(2)}) copy-start(bf16[2,2,16,128,128]{4,3,1,2,0:T(8,128)(2,1)} %all-gather.15.cloned.1.call-done) | copy-start | bytes 6291460
  225.5 22.2 %collective-permute-start.5 = (f32[16,128]{1,0:T(8,128)S(1)}, f32[16,128]{1,0:T(8,128)S(1)}, u32[]{:S(2)}, u32[]{:S(2)}) collective-permute-start(f32[16,128]{1,0:T(8,128)S(1)} %slice_bitcast_fusion.27), channel_id=1, source_target_pairs={{0,8},{8,16},{16,24},{24,32},{32,40},{40,48},{48,56},{56,0},{1,9},... | collective-permute-start | bytes 24584 | tf_op jit(solution)/shard_map/ppermute | solution.py:80
  248.2 22.5 %collective-permute-start.6 = (f32[16,128]{1,0:T(8,128)S(1)}, f32[16,128]{1,0:T(8,128)S(1)}, u32[]{:S(2)}, u32[]{:S(2)}) collective-permute-start(f32[16,128]{1,0:T(8,128)S(1)} %slice_bitcast_fusion.26), channel_id=1, source_target_pairs={{0,8},{8,16},{16,24},{24,32},{32,40},{40,48},{48,56},{56,0},{1,9},... | collective-permute-start | bytes 24584 | tf_op jit(solution)/shard_map/ppermute | solution.py:80
Sparse Core Ops, SparseCore 0:
  16.7 33.7 all-gather.6
  61.9 21.4 all-gather.8
  85.6 33.0 all-gather.10
  120.7 32.5 all-gather.12
  155.3 33.3 all-gather.14
  190.8 30.3 all-gather.16

commit v13 on v12

--- a/solution.py
+++ b/solution.py
@@ -6,7 +6,7 @@
 
 PARTS = 8
 SECT = ("sx", "sy")
-BHI = ("bh1", "bh2")
+BHI = ("bh1", "bh2", "bh3")
 
 
 def charge_order(labels, rows, block):
@@ -32,7 +32,7 @@
     sect = lax.axis_index(SECT)
     bhi = lax.axis_index(BHI)
     n_sect = lax.axis_size("sx") * lax.axis_size("sy")
-    n_hi = lax.axis_size("bh1") * lax.axis_size("bh2")
+    n_hi = lax.axis_size("bh1") * lax.axis_size("bh2") * lax.axis_size("bh3")
     n_lo = lax.axis_size("blo")
     block = tensors.shape[-1]
     count_blocks = labels.shape[0]
@@ -75,7 +75,8 @@
         stay = image[0]
         rise = image[1]
         part = jnp.stack([jnp.sum(stay * stay, axis=(1, 2)), jnp.sum(rise * rise, axis=(1, 2))])
-        norms = lax.optimization_barrier(lax.psum(part, "bh2"))
+        norms = lax.optimization_barrier(lax.psum(part, "bh3"))
+        norms = lax.optimization_barrier(lax.psum(norms, "bh2"))
         norms = lax.psum(norms, "bh1")
         came = lax.ppermute(rise[:, mine - 1], BHI, shift)
         raised = jnp.concatenate([came[:, None], rise[:, : mine - 1]], axis=1)
@@ -101,9 +102,9 @@
 def solution(mesh):
     n_sect, n_blk = mesh.devices.shape
     n_x = n_sect // 2
-    grid = mesh.devices.reshape(n_x, 2, PARTS // 2, 2, n_blk // PARTS)
-    fine = Mesh(grid, ("sx", "sy", "bh1", "bh2", "blo"))
-    blk = ("bh1", "bh2", "blo")
+    grid = mesh.devices.reshape(n_x, 2, PARTS // 4, 2, 2, n_blk // PARTS)
+    fine = Mesh(grid, ("sx", "sy", "bh1", "bh2", "bh3", "blo"))
+    blk = ("bh1", "bh2", "bh3", "blo")
     in_specs = (P(SECT, blk), P(), P(blk, None), P(SECT, None, blk, None, None))
     out_specs = (P(SECT, blk), P(SECT, blk))
     return jax.shard_map(body, mesh=fine, in_specs=in_specs, out_specs=out_specs, check_vma=False)

time: 317 us -> 381 us (1.20)
  blocking collectives: 212 us -> 280 us
    psum x8 -> x16, blocking collectives: 48.1 us -> 120 us  [the longest x8 71.5 us: body(): norms = lax.optimization_barrier(lax.psum(norms, 'bh2'))]
    psum x8, blocking collectives: 115 us -> 110 us  [body(): norms = lax.psum(norms, 'bh1')]
  transfers between devices with their start and end apart: 14 -> 14, of which waited for: 4 -> 3; matrix products, arithmetic and copies ran while one was open for 6% -> 5% of each run, Pallas kernels for 0% -> 0%
where the time goes in v13:
time: 381 us; the launch traced here: 380 us
  blocking collectives  280 us (73%)
  starting transfers between devices  34.5 us (9%)
  waiting for transfers between devices  26.2 us (7%)
  between operations  14.8 us (4%)
  local copies, waits for them, and re-layouts  11 us (3%)
  matrix products  9.62 us (3%)
  other arithmetic  4.09 us (1%)
    psum x8, blocking collectives, body(): norms = lax.psum(norms, 'bh1')  110 us
    psum x8, blocking collectives, body(): norms = lax.optimization_barrier(lax.psum(norms, 'bh2'))  71.5 us
    psum x8, blocking collectives, body(): norms = lax.optimization_barrier(lax.psum(part, 'bh3'))  48.9 us
    all_to_all x1, blocking collectives, body(): lax.all_to_all(jnp.concatenate([ordered, tagged], axis=2), BHI, 1, 1, til...  27.1 us
    ppermute x7, starting transfers between devices, body(): came = lax.ppermute(rise[:, mine - 1], BHI, shift)  26.8 us
    all_gather x5, waiting for transfers between devices, body(): got = lax.all_gather(piece, 'blo', axis=2, tiled=True)  17 us
    all_to_all x1, blocking collectives, body(): back = lax.all_to_all(result, SECT, 0, 0, tiled=False)  12.7 us
    all_gather x1, blocking collectives, body(): slabs = lax.all_gather(tensors[0], 'sy', axis=0, tiled=False)  9.28 us
  transfers between devices with their start and end apart: 14, of which 3 were waited for; matrix products, arithmetic and copies ran while one was open for 5% of the time, Pallas kernels for 0%

profile of v13, /device:TPU:2, one launch (start us, length us, event | category | flops | bytes accessed | tf_op | source)
XLA Modules:
  0.0 380.0 jit_solution(12462670500788356977)
XLA Ops:
  7.2 9.3 %all_gather.21 = bf16[2,2,2,128,128]{4,3,2,1,0:T(8,128)(2,1)} all-gather(bf16[1,2,2,128,128]{4,3,2,1,0:T(8,128)(2,1)} %param.7), channel_id=1, replica_groups=mesh['sx'=4,'sy'=2,'bh1'=2,'bh2'=2,'bh3'=2,'blo'=8] {'sy'}, dimensions={0}, use_global_device_ids=true | all-gather | bytes 393216 | tf_op jit(solution)/shard_map/all_gather | solution.py:45
  16.5 0.5 broadcast.258
  17.0 1.3 reduce.55
  18.4 0.7 all_to_all.12
  19.0 7.4 %all-to-all-start = ((s32[8,1,2]{2,1,0:T(1,128)}), s32[8,1,2]{2,1,0:T(1,128)S(1)}, u32[]{:S(2)}, u32[]{:S(2)}) async-start(s32[8,1,2]{2,1,0:T(1,128)} %bitcast.2), calls=%async_computation | async-start | bytes 8192 | tf_op jit(solution)/shard_map/all_to_all | solution.py:48
  26.6 0.8 fusion
  27.6 5.1 %all-to-all-done = s32[8,1,2]{2,1,0:T(1,128)S(1)} async-done(((s32[8,1,2]{2,1,0:T(1,128)}), s32[8,1,2]{2,1,0:T(1,128)S(1)}, u32[]{:S(2)}, u32[]{:S(2)}) %all-to-all-start) | async-done | bytes 96 | tf_op jit(solution)/shard_map/all_to_all | solution.py:48
  32.9 27.1 %all_to_all.19 = bf16[2,8,2056]{2,0,1:T(2,128)(2,1)S(1)} all-to-all(bf16[2,8,2056]{2,0,1:T(2,128)(2,1)S(1)} %copy.114), channel_id=1, replica_groups=mesh['sx'=4,'sy'=2,'bh1'=2,'bh2'=2,'bh3'=2,'blo'=8] {'bh1','bh2','bh3'}, dimensions={1} | all-to-all | bytes 131584 | tf_op jit(solution)/shard_map/all_to_all | solution.py:54
  60.1 1.0 fusion.56
  61.1 0.7 copy.115
  61.8 1.2 fusion.57
  63.0 0.7 copy.150
  63.8 0.7 copy.153
  64.6 0.7 copy.156
  65.4 0.3 fusion.47
  65.7 0.7 copy.135
  66.5 16.9 %all-gather.9.cloned.1.call-done = bf16[1,2,16,128,128]{4,3,1,0,2:T(8,128)(2,1)} async-done(((bf16[1,2,2,128,128]{4,3,1,0,2:T(8,128)(2,1)}), bf16[1,2,16,128,128]{4,3,1,0,2:T(8,128)(2,1)}) %all-gather.9.cloned.1.call-update) | async-done | bytes 1048592 | tf_op jit(solution)/shard_map/all_gather | solution.py:69
  83.4 1.5 convolution_bitcast_fusion
  85.2 5.9 %psum.168 = f32[2,16]{0,1:T(8,128)S(1)} all-reduce(f32[2,16]{0,1:T(8,128)S(1)} %copy.119), channel_id=1, replica_groups=mesh['sx'=4,'sy'=2,'bh1'=2,'bh2'=2,'bh3'=2,'blo'=8] {'bh3'}, use_global_device_ids=true, to_apply=%region_2.0 | all-reduce | flops 32 | bytes 256 | tf_op jit(solution)/shard_map/psum | solution.py:78
  91.1 8.9 %psum.169 = f32[2,16]{0,1:T(8,128)S(1)} all-reduce(f32[2,16]{0,1:T(8,128)S(1)} %psum.168), channel_id=1, replica_groups=mesh['sx'=4,'sy'=2,'bh1'=2,'bh2'=2,'bh3'=2,'blo'=8] {'bh2'}, use_global_device_ids=true, to_apply=%region_3.0 | all-reduce | flops 32 | bytes 256 | tf_op jit(solution)/shard_map/psum | solution.py:79
  100.0 14.2 %psum.170 = f32[2,16]{0,1:T(8,128)S(1)} all-reduce(f32[2,16]{0,1:T(8,128)S(1)} %psum.169), channel_id=1, replica_groups=mesh['sx'=4,'sy'=2,'bh1'=2,'bh2'=2,'bh3'=2,'blo'=8] {'bh1'}, use_global_device_ids=true, to_apply=%region_4.0 | all-reduce | flops 32 | bytes 256 | tf_op jit(solution)/shard_map/psum | solution.py:80
  114.1 0.2 slice_reduce_fusion.12
  114.3 4.2 %collective-permute-start = (f32[16,128]{1,0:T(8,128)S(1)}, f32[16,128]{1,0:T(8,128)S(1)}, u32[]{:S(2)}, u32[]{:S(2)}) collective-permute-start(f32[16,128]{1,0:T(8,128)S(1)} %slice_bitcast_fusion.32), channel_id=1, source_target_pairs={{0,8},{8,16},{16,24},{24,32},{32,40},{40,48},{48,56},{56,0},{1,9},... | collective-permute-start | bytes 24584 | tf_op jit(solution)/shard_map/ppermute | solution.py:81
  118.6 4.0 %collective-permute-done = f32[16,128]{1,0:T(8,128)S(1)} collective-permute-done((f32[16,128]{1,0:T(8,128)S(1)}, f32[16,128]{1,0:T(8,128)S(1)}, u32[]{:S(2)}, u32[]{:S(2)}) %collective-permute-start) | collective-permute-done | bytes 8224 | tf_op jit(solution)/shard_map/ppermute | solution.py:81
  122.7 1.6 convolution_bitcast_fusion.7
  124.5 3.1 collective-permute-start.1
  127.7 7.3 %psum.171 = f32[2,16]{0,1:T(8,128)S(1)} all-reduce(f32[2,16]{0,1:T(8,128)S(1)} %copy.122), channel_id=1, replica_groups=mesh['sx'=4,'sy'=2,'bh1'=2,'bh2'=2,'bh3'=2,'blo'=8] {'bh3'}, use_global_device_ids=true, to_apply=%region_7.8 | all-reduce | flops 32 | bytes 256 | tf_op jit(solution)/shard_map/psum | solution.py:78
  135.1 9.0 %psum.172 = f32[2,16]{0,1:T(8,128)S(1)} all-reduce(f32[2,16]{0,1:T(8,128)S(1)} %psum.171), channel_id=1, replica_groups=mesh['sx'=4,'sy'=2,'bh1'=2,'bh2'=2,'bh3'=2,'blo'=8] {'bh2'}, use_global_device_ids=true, to_apply=%region_8.9 | all-reduce | flops 32 | bytes 256 | tf_op jit(solution)/shard_map/psum | solution.py:79
  144.1 13.8 %psum.173 = f32[2,16]{0,1:T(8,128)S(1)} all-reduce(f32[2,16]{0,1:T(8,128)S(1)} %psum.172), channel_id=1, replica_groups=mesh['sx'=4,'sy'=2,'bh1'=2,'bh2'=2,'bh3'=2,'blo'=8] {'bh1'}, use_global_device_ids=true, to_apply=%region_9.10 | all-reduce | flops 32 | bytes 256 | tf_op jit(solution)/shard_map/psum | solution.py:80
  157.9 0.2 slice_reduce_fusion.10
  158.2 0.3 convolution_bitcast_fusion.6
  158.7 4.8 %collective-permute-start.2 = (f32[16,128]{1,0:T(8,128)S(1)}, f32[16,128]{1,0:T(8,128)S(1)}, u32[]{:S(2)}, u32[]{:S(2)}) collective-permute-start(f32[16,128]{1,0:T(8,128)S(1)} %slice_bitcast_fusion.30), channel_id=1, source_target_pairs={{0,8},{8,16},{16,24},{24,32},{32,40},{40,48},{48,56},{56,0},{1,9},... | collective-permute-start | bytes 24584 | tf_op jit(solution)/shard_map/ppermute | solution.py:81
  163.5 6.3 %psum.174 = f32[2,16]{0,1:T(8,128)S(1)} all-reduce(f32[2,16]{0,1:T(8,128)S(1)} %copy.124), channel_id=1, replica_groups=mesh['sx'=4,'sy'=2,'bh1'=2,'bh2'=2,'bh3'=2,'blo'=8] {'bh3'}, use_global_device_ids=true, to_apply=%region_12.13 | all-reduce | flops 32 | bytes 256 | tf_op jit(solution)/shard_map/psum | solution.py:78
  169.8 8.9 %psum.175 = f32[2,16]{0,1:T(8,128)S(1)} all-reduce(f32[2,16]{0,1:T(8,128)S(1)} %psum.174), channel_id=1, replica_groups=mesh['sx'=4,'sy'=2,'bh1'=2,'bh2'=2,'bh3'=2,'blo'=8] {'bh2'}, use_global_device_ids=true, to_apply=%region_13.14 | all-reduce | flops 32 | bytes 256 | tf_op jit(solution)/shard_map/psum | solution.py:79
  178.7 13.8 %psum.176 = f32[2,16]{0,1:T(8,128)S(1)} all-reduce(f32[2,16]{0,1:T(8,128)S(1)} %psum.175), channel_id=1, replica_groups=mesh['sx'=4,'sy'=2,'bh1'=2,'bh2'=2,'bh3'=2,'blo'=8] {'bh1'}, use_global_device_ids=true, to_apply=%region_14.15 | all-reduce | flops 32 | bytes 256 | tf_op jit(solution)/shard_map/psum | solution.py:80
  192.6 0.2 slice_reduce_fusion.8
  192.9 1.6 convolution_bitcast_fusion.5
  194.8 4.8 %collective-permute-start.3 = (f32[16,128]{1,0:T(8,128)S(1)}, f32[16,128]{1,0:T(8,128)S(1)}, u32[]{:S(2)}, u32[]{:S(2)}) collective-permute-start(f32[16,128]{1,0:T(8,128)S(1)} %slice_bitcast_fusion.29), channel_id=1, source_target_pairs={{0,8},{8,16},{16,24},{24,32},{32,40},{40,48},{48,56},{56,0},{1,9},... | collective-permute-start | bytes 24584 | tf_op jit(solution)/shard_map/ppermute | solution.py:81
  199.7 6.0 %psum.177 = f32[2,16]{0,1:T(8,128)S(1)} all-reduce(f32[2,16]{0,1:T(8,128)S(1)} %copy.127), channel_id=1, replica_groups=mesh['sx'=4,'sy'=2,'bh1'=2,'bh2'=2,'bh3'=2,'blo'=8] {'bh3'}, use_global_device_ids=true, to_apply=%region_17.18 | all-reduce | flops 32 | bytes 256 | tf_op jit(solution)/shard_map/psum | solution.py:78
  205.7 9.1 %psum.178 = f32[2,16]{0,1:T(8,128)S(1)} all-reduce(f32[2,16]{0,1:T(8,128)S(1)} %psum.177), channel_id=1, replica_groups=mesh['sx'=4,'sy'=2,'bh1'=2,'bh2'=2,'bh3'=2,'blo'=8] {'bh2'}, use_global_device_ids=true, to_apply=%region_18.19 | all-reduce | flops 32 | bytes 256 | tf_op jit(solution)/shard_map/psum | solution.py:79
  214.8 13.7 %psum.179 = f32[2,16]{0,1:T(8,128)S(1)} all-reduce(f32[2,16]{0,1:T(8,128)S(1)} %psum.178), channel_id=1, replica_groups=mesh['sx'=4,'sy'=2,'bh1'=2,'bh2'=2,'bh3'=2,'blo'=8] {'bh1'}, use_global_device_ids=true, to_apply=%region_19.20 | all-reduce | flops 32 | bytes 256 | tf_op jit(solution)/shard_map/psum | solution.py:80
  228.8 0.3 convolution_bitcast_fusion.4
  229.3 4.8 %collective-permute-start.4 = (f32[16,128]{1,0:T(8,128)S(1)}, f32[16,128]{1,0:T(8,128)S(1)}, u32[]{:S(2)}, u32[]{:S(2)}) collective-permute-start(f32[16,128]{1,0:T(8,128)S(1)} %slice_bitcast_fusion.28), channel_id=1, source_target_pairs={{0,8},{8,16},{16,24},{24,32},{32,40},{40,48},{48,56},{56,0},{1,9},... | collective-permute-start | bytes 24584 | tf_op jit(solution)/shard_map/ppermute | solution.py:81
  234.2 5.9 %psum.180 = f32[2,16]{0,1:T(8,128)S(1)} all-reduce(f32[2,16]{0,1:T(8,128)S(1)} %copy.129), channel_id=1, replica_groups=mesh['sx'=4,'sy'=2,'bh1'=2,'bh2'=2,'bh3'=2,'blo'=8] {'bh3'}, use_global_device_ids=true, to_apply=%region_22.23 | all-reduce | flops 32 | bytes 256 | tf_op jit(solution)/shard_map/psum | solution.py:78
  240.0 8.9 %psum.181 = f32[2,16]{0,1:T(8,128)S(1)} all-reduce(f32[2,16]{0,1:T(8,128)S(1)} %psum.180), channel_id=1, replica_groups=mesh['sx'=4,'sy'=2,'bh1'=2,'bh2'=2,'bh3'=2,'blo'=8] {'bh2'}, use_global_device_ids=true, to_apply=%region_23.24 | all-reduce | flops 32 | bytes 256 | tf_op jit(solution)/shard_map/psum | solution.py:79
  248.9 13.7 %psum.182 = f32[2,16]{0,1:T(8,128)S(1)} all-reduce(f32[2,16]{0,1:T(8,128)S(1)} %psum.181), channel_id=1, replica_groups=mesh['sx'=4,'sy'=2,'bh1'=2,'bh2'=2,'bh3'=2,'blo'=8] {'bh1'}, use_global_device_ids=true, to_apply=%region_24.25 | all-reduce | flops 32 | bytes 256 | tf_op jit(solution)/shard_map/psum | solution.py:80
  262.6 0.2 slice_reduce_fusion.4
  263.0 1.7 convolution_bitcast_fusion.3
  264.8 1.9 collective-permute-start.5
  266.9 5.9 %psum.183 = f32[2,16]{0,1:T(8,128)S(1)} all-reduce(f32[2,16]{0,1:T(8,128)S(1)} %copy.132), channel_id=1, replica_groups=mesh['sx'=4,'sy'=2,'bh1'=2,'bh2'=2,'bh3'=2,'blo'=8] {'bh3'}, use_global_device_ids=true, to_apply=%region_27.28 | all-reduce | flops 32 | bytes 256 | tf_op jit(solution)/shard_map/psum | solution.py:78
  272.8 8.9 %psum.184 = f32[2,16]{0,1:T(8,128)S(1)} all-reduce(f32[2,16]{0,1:T(8,128)S(1)} %psum.183), channel_id=1, replica_groups=mesh['sx'=4,'sy'=2,'bh1'=2,'bh2'=2,'bh3'=2,'blo'=8] {'bh2'}, use_global_device_ids=true, to_apply=%region_28.29 | all-reduce | flops 32 | bytes 256 | tf_op jit(solution)/shard_map/psum | solution.py:79
  281.7 13.7 %psum.185 = f32[2,16]{0,1:T(8,128)S(1)} all-reduce(f32[2,16]{0,1:T(8,128)S(1)} %psum.184), channel_id=1, replica_groups=mesh['sx'=4,'sy'=2,'bh1'=2,'bh2'=2,'bh3'=2,'blo'=8] {'bh1'}, use_global_device_ids=true, to_apply=%region_29.30 | all-reduce | flops 32 | bytes 256 | tf_op jit(solution)/shard_map/psum | solution.py:80
  295.7 0.3 convolution_bitcast_fusion.2
  296.1 3.3 collective-permute-start.6
  299.6 5.9 %psum.186 = f32[2,16]{0,1:T(8,128)S(1)} all-reduce(f32[2,16]{0,1:T(8,128)S(1)} %copy.134), channel_id=1, replica_groups=mesh['sx'=4,'sy'=2,'bh1'=2,'bh2'=2,'bh3'=2,'blo'=8] {'bh3'}, use_global_device_ids=true, to_apply=%region_32.33 | all-reduce | flops 32 | bytes 256 | tf_op jit(solution)/shard_map/psum | solution.py:78
  305.5 8.9 %psum.187 = f32[2,16]{0,1:T(8,128)S(1)} all-reduce(f32[2,16]{0,1:T(8,128)S(1)} %psum.186), channel_id=1, replica_groups=mesh['sx'=4,'sy'=2,'bh1'=2,'bh2'=2,'bh3'=2,'blo'=8] {'bh2'}, use_global_device_ids=true, to_apply=%region_33.34 | all-reduce | flops 32 | bytes 256 | tf_op jit(solution)/shard_map/psum | solution.py:79
  314.4 13.7 %psum.188 = f32[2,16]{0,1:T(8,128)S(1)} all-reduce(f32[2,16]{0,1:T(8,128)S(1)} %psum.187), channel_id=1, replica_groups=mesh['sx'=4,'sy'=2,'bh1'=2,'bh2'=2,'bh3'=2,'blo'=8] {'bh1'}, use_global_device_ids=true, to_apply=%region_34.35 | all-reduce | flops 32 | bytes 256 | tf_op jit(solution)/shard_map/psum | solution.py:80
  328.5 1.5 convolution_bitcast_fusion.1
  330.2 5.9 %psum.189 = f32[2,16]{0,1:T(8,128)S(1)} all-reduce(f32[2,16]{0,1:T(8,128)S(1)} %copy.136), channel_id=1, replica_groups=mesh['sx'=4,'sy'=2,'bh1'=2,'bh2'=2,'bh3'=2,'blo'=8] {'bh3'}, use_global_device_ids=true, to_apply=%region_37.38 | all-reduce | flops 32 | bytes 256 | tf_op jit(solution)/shard_map/psum | solution.py:78
  336.1 8.9 %psum.190 = f32[2,16]{0,1:T(8,128)S(1)} all-reduce(f32[2,16]{0,1:T(8,128)S(1)} %psum.189), channel_id=1, replica_groups=mesh['sx'=4,'sy'=2,'bh1'=2,'bh2'=2,'bh3'=2,'blo'=8] {'bh2'}, use_global_device_ids=true, to_apply=%region_38.39 | all-reduce | flops 32 | bytes 256 | tf_op jit(solution)/shard_map/psum | solution.py:79
  345.0 13.7 %psum.191 = f32[2,16]{0,1:T(8,128)S(1)} all-reduce(f32[2,16]{0,1:T(8,128)S(1)} %psum.190), channel_id=1, replica_groups=mesh['sx'=4,'sy'=2,'bh1'=2,'bh2'=2,'bh3'=2,'blo'=8] {'bh1'}, use_global_device_ids=true, to_apply=%region_39.40 | all-reduce | flops 32 | bytes 256 | tf_op jit(solution)/shard_map/psum | solution.py:80
  359.2 12.7 %all_to_all.20 = f32[8,2,2]{2,1,0:T(2,128)S(1)} all-to-all(f32[8,2,2]{2,1,0:T(2,128)S(1)} %copy.139), channel_id=1, replica_groups=mesh['sx'=4,'sy'=2,'bh1'=2,'bh2'=2,'bh3'=2,'blo'=8] {'sx','sy'}, dimensions={0} | all-to-all | bytes 256 | tf_op jit(solution)/shard_map/all_to_all | solution.py:97
  371.9 0.6 squeeze.190
  372.5 0.6 squeeze.191
  (123 shorter events, 5.1 us)
Async XLA Ops:
  7.2 19.3 %copy-start = (bf16[16,16384]{1,0:T(8,128)(2,1)S(1)}, bf16[16,16384]{1,0:T(8,128)(2,1)}, u32[]{:S(2)}) copy-start(bf16[16,16384]{1,0:T(8,128)(2,1)} %param.6) | copy-start | bytes 1572868
  7.2 52.9 %all-gather.7.cloned.1.call-start = ((), (), s32[]{:S(2)}) async-start(), calls=%async_computation.3 | async-start | bytes 1310720 | tf_op jit(solution)/shard_map/all_gather | solution.py:46
  19.0 13.6 %all-to-all-start = ((s32[8,1,2]{2,1,0:T(1,128)}), s32[8,1,2]{2,1,0:T(1,128)S(1)}, u32[]{:S(2)}, u32[]{:S(2)}) async-start(s32[8,1,2]{2,1,0:T(1,128)} %bitcast.2), calls=%async_computation | async-start | bytes 8192 | tf_op jit(solution)/shard_map/all_to_all | solution.py:48
  26.5 57.0 %all-gather.9.cloned.1.call-start = ((), (), s32[]{:S(2)}) async-start(), calls=%async_computation.4 | async-start | bytes 1179648 | tf_op jit(solution)/shard_map/all_gather | solution.py:69
  61.8 60.9 %all-gather.11.cloned.1.call-start = ((), (), s32[]{:S(2)}) async-start(), calls=%async_computation.5 | async-start | bytes 2359296 | tf_op jit(solution)/shard_map/all_gather | solution.py:69
  63.8 129.2 %all-gather.13.cloned.1.call-start = ((), (), s32[]{:S(2)}) async-start(), calls=%async_computation.6 | async-start | bytes 2359296 | tf_op jit(solution)/shard_map/all_gather | solution.py:69
  64.6 198.4 %all-gather.15.cloned.1.call-start = ((), (), s32[]{:S(2)}) async-start(), calls=%async_computation.7 | async-start | bytes 2359296 | tf_op jit(solution)/shard_map/all_gather | solution.py:69
  65.4 263.1 %all-gather.17.cloned.1.call-start = ((), (), s32[]{:S(2)}) async-start(), calls=%async_computation.8 | async-start | bytes 1179648 | tf_op jit(solution)/shard_map/all_gather | solution.py:69
  114.3 8.2 %collective-permute-start = (f32[16,128]{1,0:T(8,128)S(1)}, f32[16,128]{1,0:T(8,128)S(1)}, u32[]{:S(2)}, u32[]{:S(2)}) collective-permute-start(f32[16,128]{1,0:T(8,128)S(1)} %slice_bitcast_fusion.32), channel_id=1, source_target_pairs={{0,8},{8,16},{16,24},{24,32},{32,40},{40,48},{48,56},{56,0},{1,9},... | collective-permute-start | bytes 24584 | tf_op jit(solution)/shard_map/ppermute | solution.py:81
  122.7 35.5 %copy-start.3 = (bf16[2,2,16,128,128]{4,3,1,2,0:T(8,128)(2,1)S(1)}, bf16[2,2,16,128,128]{4,3,1,2,0:T(8,128)(2,1)}, u32[]{:S(2)}) copy-start(bf16[2,2,16,128,128]{4,3,1,2,0:T(8,128)(2,1)} %all-gather.11.cloned.1.call-done) | copy-start | bytes 6291460
  124.5 33.5 %collective-permute-start.1 = (f32[16,128]{1,0:T(8,128)S(1)}, f32[16,128]{1,0:T(8,128)S(1)}, u32[]{:S(2)}, u32[]{:S(2)}) collective-permute-start(f32[16,128]{1,0:T(8,128)S(1)} %slice_bitcast_fusion.31), channel_id=1, source_target_pairs={{0,8},{8,16},{16,24},{24,32},{32,40},{40,48},{48,56},{56,0},{1,9},... | collective-permute-start | bytes 24584 | tf_op jit(solution)/shard_map/ppermute | solution.py:81
  158.7 34.1 %collective-permute-start.2 = (f32[16,128]{1,0:T(8,128)S(1)}, f32[16,128]{1,0:T(8,128)S(1)}, u32[]{:S(2)}, u32[]{:S(2)}) collective-permute-start(f32[16,128]{1,0:T(8,128)S(1)} %slice_bitcast_fusion.30), channel_id=1, source_target_pairs={{0,8},{8,16},{16,24},{24,32},{32,40},{40,48},{48,56},{56,0},{1,9},... | collective-permute-start | bytes 24584 | tf_op jit(solution)/shard_map/ppermute | solution.py:81
  192.9 35.9 %copy-start.2 = (bf16[2,2,16,128,128]{4,3,1,2,0:T(8,128)(2,1)S(1)}, bf16[2,2,16,128,128]{4,3,1,2,0:T(8,128)(2,1)}, u32[]{:S(2)}) copy-start(bf16[2,2,16,128,128]{4,3,1,2,0:T(8,128)(2,1)} %all-gather.13.cloned.1.call-done) | copy-start | bytes 6291460
  194.8 33.9 %collective-permute-start.3 = (f32[16,128]{1,0:T(8,128)S(1)}, f32[16,128]{1,0:T(8,128)S(1)}, u32[]{:S(2)}, u32[]{:S(2)}) collective-permute-start(f32[16,128]{1,0:T(8,128)S(1)} %slice_bitcast_fusion.29), channel_id=1, source_target_pairs={{0,8},{8,16},{16,24},{24,32},{32,40},{40,48},{48,56},{56,0},{1,9},... | collective-permute-start | bytes 24584 | tf_op jit(solution)/shard_map/ppermute | solution.py:81
  229.3 33.5 %collective-permute-start.4 = (f32[16,128]{1,0:T(8,128)S(1)}, f32[16,128]{1,0:T(8,128)S(1)}, u32[]{:S(2)}, u32[]{:S(2)}) collective-permute-start(f32[16,128]{1,0:T(8,128)S(1)} %slice_bitcast_fusion.28), channel_id=1, source_target_pairs={{0,8},{8,16},{16,24},{24,32},{32,40},{40,48},{48,56},{56,0},{1,9},... | collective-permute-start | bytes 24584 | tf_op jit(solution)/shard_map/ppermute | solution.py:81
  263.0 32.7 %copy-start.1 = (bf16[2,2,16,128,128]{4,3,1,2,0:T(8,128)(2,1)S(1)}, bf16[2,2,16,128,128]{4,3,1,2,0:T(8,128)(2,1)}, u32[]{:S(2)}) copy-start(bf16[2,2,16,128,128]{4,3,1,2,0:T(8,128)(2,1)} %all-gather.15.cloned.1.call-done) | copy-start | bytes 6291460
  264.8 30.7 %collective-permute-start.5 = (f32[16,128]{1,0:T(8,128)S(1)}, f32[16,128]{1,0:T(8,128)S(1)}, u32[]{:S(2)}, u32[]{:S(2)}) collective-permute-start(f32[16,128]{1,0:T(8,128)S(1)} %slice_bitcast_fusion.27), channel_id=1, source_target_pairs={{0,8},{8,16},{16,24},{24,32},{32,40},{40,48},{48,56},{56,0},{1,9},... | collective-permute-start | bytes 24584 | tf_op jit(solution)/shard_map/ppermute | solution.py:81
  296.1 32.3 %collective-permute-start.6 = (f32[16,128]{1,0:T(8,128)S(1)}, f32[16,128]{1,0:T(8,128)S(1)}, u32[]{:S(2)}, u32[]{:S(2)}) collective-permute-start(f32[16,128]{1,0:T(8,128)S(1)} %slice_bitcast_fusion.26), channel_id=1, source_target_pairs={{0,8},{8,16},{16,24},{24,32},{32,40},{40,48},{48,56},{56,0},{1,9},... | collective-permute-start | bytes 24584 | tf_op jit(solution)/shard_map/ppermute | solution.py:81
Sparse Core Ops, SparseCore 0:
  16.7 33.7 all-gather.6
  61.9 21.4 all-gather.8
  85.6 33.2 all-gather.10
  120.9 32.7 all-gather.12
  155.7 33.3 all-gather.14
  191.1 30.3 all-gather.16

commit v14 on v10

--- a/solution.py
+++ b/solution.py
@@ -6,6 +6,7 @@
 
 PARTS = 8
 SECT = ("sx", "sy")
+GATHER = ("g1", "g2")
 
 
 def charge_order(labels, rows, block):
@@ -32,7 +33,7 @@
     bhi = lax.axis_index("bhi")
     n_sect = lax.axis_size("sx") * lax.axis_size("sy")
     n_hi = lax.axis_size("bhi")
-    n_lo = lax.axis_size("blo")
+    n_lo = lax.axis_size("g1")
     block = tensors.shape[-1]
     count_blocks = labels.shape[0]
     width = count_blocks * block
@@ -48,7 +49,8 @@
     row_bits = jnp.transpose(pieces).astype(left.dtype)
 
     rows = lax.dynamic_slice_in_dim(left, sect * pick, pick, 0)
-    ordered = charge_order(labels, rows, block).reshape(pick, n_hi, mine * block)
+    ordered = charge_order(labels, rows, block).reshape(pick, n_lo, n_hi, mine // n_lo, block)
+    ordered = jnp.transpose(ordered, (0, 2, 1, 3, 4)).reshape(pick, n_hi, mine * block)
     tagged = jnp.broadcast_to(row_bits[:, None, :], (pick, n_hi, sites))
     spread = lax.all_to_all(jnp.concatenate([ordered, tagged], axis=2), "bhi", 1, 1, tiled=False)
     count_rows = n_hi * pick
@@ -65,7 +67,7 @@
     first_slab, state = lax.optimization_barrier((slabs[0:1], state))
     for batch in batches:
         piece = first_slab if batch == [0] else slabs[batch[0] : batch[-1] + 1]
-        got = lax.all_gather(piece, "blo", axis=2, tiled=True)
+        got = lax.all_gather(piece, GATHER, axis=2, tiled=True)
         for index, site in enumerate(batch):
             gathered[site] = got[index]
     for site in range(sites):
@@ -75,8 +77,12 @@
         rise = image[1]
         part = jnp.stack([jnp.sum(stay * stay, axis=(1, 2)), jnp.sum(rise * rise, axis=(1, 2))])
         norms = lax.psum(part, "bhi")
-        came = lax.ppermute(rise[:, mine - 1], "bhi", shift)
-        raised = jnp.concatenate([came[:, None], rise[:, : mine - 1]], axis=1)
+        rise4 = rise.reshape(count_rows, n_lo, mine // n_lo, block)
+        send = rise4[:, :, mine // n_lo - 1]
+        send = jnp.where(bhi == n_hi - 1, jnp.roll(send, 1, axis=1), send)
+        came = lax.ppermute(send, "bhi", shift)
+        raised = jnp.concatenate([came[:, :, None], rise4[:, :, : mine // n_lo - 1]], axis=2)
+        raised = raised.reshape(count_rows, mine, block)
         norm_zero = norms[0]
         norm_one = norms[1]
         choose = carried_bits[site] == 1
@@ -99,8 +105,9 @@
 def solution(mesh):
     n_sect, n_blk = mesh.devices.shape
     n_x = n_sect // 2
-    fine = Mesh(mesh.devices.reshape(n_x, 2, PARTS, n_blk // PARTS), ("sx", "sy", "bhi", "blo"))
-    blk = ("bhi", "blo")
+    grid = mesh.devices.reshape(n_x, 2, 2, PARTS, n_blk // (2 * PARTS))
+    fine = Mesh(grid, ("sx", "sy", "g1", "bhi", "g2"))
+    blk = ("g1", "bhi", "g2")
     in_specs = (P(SECT, blk), P(), P(blk, None), P(SECT, None, blk, None, None))
     out_specs = (P(SECT, blk), P(SECT, blk))
     return jax.shard_map(body, mesh=fine, in_specs=in_specs, out_specs=out_specs, check_vma=False)

time: 307 us -> 464 us (1.51)
  the two profiles are of different devices: /device:TPU:64 before, /device:TPU:288 now
where the time goes in v14:
time: 464 us
  blocking collectives  322 us (69%)
  waiting for transfers between devices  73.4 us (16%)
  starting transfers between devices  27.5 us (6%)
  between operations  14.9 us (3%)
  local copies, waits for them, and re-layouts  10.8 us (2%)
  matrix products  9.59 us (2%)
  other arithmetic  5.11 us (1%)
    psum x8, blocking collectives, body(): norms = lax.psum(part, 'bhi')  283 us
    all_gather x5, waiting for transfers between devices, body(): got = lax.all_gather(piece, GATHER, axis=2, tiled=True)  58.4 us
    ppermute x7, starting transfers between devices, body(): came = lax.ppermute(send, 'bhi', shift)  21.8 us
    all_to_all x1, blocking collectives, body(): lax.all_to_all(jnp.concatenate([ordered, tagged], axis=2), 'bhi', 1, 1, t...  15.1 us
    all_to_all x1, blocking collectives, body(): back = lax.all_to_all(result, SECT, 0, 0, tiled=False)  14.7 us
    all_gather x1, blocking collectives, body(): slabs = lax.all_gather(tensors[0], 'sy', axis=0, tiled=False)  9.28 us
  transfers between devices with their start and end apart: 14, of which 5 were waited for; matrix products, arithmetic and copies ran while one was open for 4% of the time, Pallas kernels for 0%

profile of v14, /device:TPU:288, one launch (start us, length us, event | category | flops | bytes accessed | tf_op | source)
XLA Modules:
  0.0 463.7 jit_solution(17794693754409918976)
XLA Ops:
  7.2 9.3 %all_gather.21 = bf16[2,2,2,128,128]{4,3,2,1,0:T(8,128)(2,1)} all-gather(bf16[1,2,2,128,128]{4,3,2,1,0:T(8,128)(2,1)} %param.7), channel_id=1, replica_groups=mesh['sx'=4,'sy'=2,'g1'=2,'bhi'=8,'g2'=4] {'sy'}, dimensions={0}, use_global_device_ids=true | all-gather | bytes 393216 | tf_op jit(solution)/shard_map/all_gather | solution.py:45
  16.5 0.5 broadcast.258
  17.0 1.3 reduce.62
  18.4 0.7 all_to_all.12
  19.0 5.5 %all-to-all-start = ((s32[8,1,2]{2,1,0:T(1,128)}), s32[8,1,2]{2,1,0:T(1,128)S(1)}, u32[]{:S(2)}, u32[]{:S(2)}) async-start(s32[8,1,2]{2,1,0:T(1,128)} %bitcast.4), calls=%async_computation | async-start | bytes 8192 | tf_op jit(solution)/shard_map/all_to_all | solution.py:48
  24.7 0.8 convolution_convert_fusion
  25.6 6.5 %all-to-all-done = s32[8,1,2]{2,1,0:T(1,128)S(1)} async-done(((s32[8,1,2]{2,1,0:T(1,128)}), s32[8,1,2]{2,1,0:T(1,128)S(1)}, u32[]{:S(2)}, u32[]{:S(2)}) %all-to-all-start) | async-done | bytes 96 | tf_op jit(solution)/shard_map/all_to_all | solution.py:48
  32.2 15.1 %all_to_all.19 = bf16[2,8,2056]{2,0,1:T(2,128)(2,1)S(1)} all-to-all(bf16[2,8,2056]{2,0,1:T(2,128)(2,1)S(1)} %copy.134), channel_id=1, replica_groups=mesh['sx'=4,'sy'=2,'g1'=2,'bhi'=8,'g2'=4] {'bhi'}, dimensions={1} | all-to-all | bytes 131584 | tf_op jit(solution)/shard_map/all_to_all | solution.py:55
  47.4 0.7 all-gather.7.cloned.1.call-done
  48.1 1.0 fusion.55
  49.1 0.7 copy.135
  49.8 1.2 fusion.56
  51.0 0.7 copy.175
  51.8 0.7 copy.178
  52.6 0.7 copy.181
  53.4 0.3 fusion.46
  53.7 0.7 copy.161
  54.5 44.3 %all-gather.9.cloned.1.call-done = bf16[1,2,16,128,128]{4,3,1,0,2:T(8,128)(2,1)} async-done(((bf16[1,2,2,128,128]{4,3,1,0,2:T(8,128)(2,1)}), bf16[1,2,16,128,128]{4,3,1,0,2:T(8,128)(2,1)}) %all-gather.9.cloned.1.call-update) | async-done | bytes 1048592 | tf_op jit(solution)/shard_map/all_gather | solution.py:70
  98.7 1.5 convolution_bitcast_fusion
  100.3 0.1 fusion.63
  100.6 35.8 %psum.56 = f32[2,16]{0,1:T(8,128)S(1)} all-reduce(f32[2,16]{0,1:T(8,128)S(1)} %copy.138), channel_id=1, replica_groups=mesh['sx'=4,'sy'=2,'g1'=2,'bhi'=8,'g2'=4] {'bhi'}, use_global_device_ids=true, to_apply=%region_2.0 | all-reduce | flops 32 | bytes 256 | tf_op jit(solution)/shard_map/psum | solution.py:79
  136.4 0.2 slice_reduce_fusion.12
  136.6 1.9 collective-permute-start
  138.6 7.8 %collective-permute-done = f32[16,2,128]{2,0,1:T(8,128)S(1)} collective-permute-done((f32[16,2,128]{2,0,1:T(8,128)S(1)}, f32[16,2,128]{2,0,1:T(8,128)S(1)}, u32[]{:S(2)}, u32[]{:S(2)}) %collective-permute-start) | collective-permute-done | bytes 16416 | tf_op jit(solution)/shard_map/ppermute | solution.py:83
  146.5 14.1 %all-gather.11.cloned.1.call-done = bf16[2,2,16,128,128]{4,3,1,2,0:T(8,128)(2,1)} async-done(((bf16[2,2,2,128,128]{4,3,1,2,0:T(8,128)(2,1)}), bf16[2,2,16,128,128]{4,3,1,2,0:T(8,128)(2,1)}) %all-gather.11.cloned.1.call-update) | async-done | bytes 2097168 | tf_op jit(solution)/shard_map/all_gather | solution.py:70
  160.6 1.6 convolution_bitcast_fusion.7
  162.3 0.1 fusion.62
  162.4 0.1 multiply_reduce_fusion.11
  162.6 1.9 collective-permute-start.1
  164.6 45.2 %psum.57 = f32[2,16]{0,1:T(8,128)S(1)} all-reduce(f32[2,16]{0,1:T(8,128)S(1)} %copy.141), channel_id=1, replica_groups=mesh['sx'=4,'sy'=2,'g1'=2,'bhi'=8,'g2'=4] {'bhi'}, use_global_device_ids=true, to_apply=%region_5.6 | all-reduce | flops 32 | bytes 256 | tf_op jit(solution)/shard_map/psum | solution.py:79
  209.8 0.2 slice_reduce_fusion.10
  210.2 0.3 convolution_bitcast_fusion.6
  210.5 0.1 fusion.61
  210.8 2.3 collective-permute-start.2
  213.2 34.0 %psum.58 = f32[2,16]{0,1:T(8,128)S(1)} all-reduce(f32[2,16]{0,1:T(8,128)S(1)} %copy.144), channel_id=1, replica_groups=mesh['sx'=4,'sy'=2,'g1'=2,'bhi'=8,'g2'=4] {'bhi'}, use_global_device_ids=true, to_apply=%region_8.9 | all-reduce | flops 32 | bytes 256 | tf_op jit(solution)/shard_map/psum | solution.py:79
  247.2 0.2 slice_reduce_fusion.8
  247.6 1.6 convolution_bitcast_fusion.5
  249.3 0.1 fusion.60
  249.6 3.9 collective-permute-start.3
  253.6 40.5 %psum.59 = f32[2,16]{0,1:T(8,128)S(1)} all-reduce(f32[2,16]{0,1:T(8,128)S(1)} %copy.148), channel_id=1, replica_groups=mesh['sx'=4,'sy'=2,'g1'=2,'bhi'=8,'g2'=4] {'bhi'}, use_global_device_ids=true, to_apply=%region_11.12 | all-reduce | flops 32 | bytes 256 | tf_op jit(solution)/shard_map/psum | solution.py:79
  294.1 0.2 slice_reduce_fusion.6
  294.4 0.3 convolution_bitcast_fusion.4
  294.8 0.1 fusion.59
  294.9 0.1 multiply_reduce_fusion.5
  295.1 4.2 collective-permute-start.4
  299.4 29.6 %psum.60 = f32[2,16]{0,1:T(8,128)S(1)} all-reduce(f32[2,16]{0,1:T(8,128)S(1)} %copy.151), channel_id=1, replica_groups=mesh['sx'=4,'sy'=2,'g1'=2,'bhi'=8,'g2'=4] {'bhi'}, use_global_device_ids=true, to_apply=%region_14.15 | all-reduce | flops 32 | bytes 256 | tf_op jit(solution)/shard_map/psum | solution.py:79
  329.0 0.2 slice_reduce_fusion.4
  329.4 1.7 convolution_bitcast_fusion.3
  331.1 0.1 fusion.58
  331.4 4.4 collective-permute-start.5
  335.9 32.2 %psum.61 = f32[2,16]{0,1:T(8,128)S(1)} all-reduce(f32[2,16]{0,1:T(8,128)S(1)} %copy.155), channel_id=1, replica_groups=mesh['sx'=4,'sy'=2,'g1'=2,'bhi'=8,'g2'=4] {'bhi'}, use_global_device_ids=true, to_apply=%region_17.18 | all-reduce | flops 32 | bytes 256 | tf_op jit(solution)/shard_map/psum | solution.py:79
  368.1 0.2 slice_reduce_fusion.2
  368.5 0.3 convolution_bitcast_fusion.2
  368.8 0.1 fusion.57
  368.9 3.1 collective-permute-start.6
  372.1 0.1 multiply_reduce_fusion.1
  372.3 32.0 %psum.62 = f32[2,16]{0,1:T(8,128)S(1)} all-reduce(f32[2,16]{0,1:T(8,128)S(1)} %copy.158), channel_id=1, replica_groups=mesh['sx'=4,'sy'=2,'g1'=2,'bhi'=8,'g2'=4] {'bhi'}, use_global_device_ids=true, to_apply=%region_20.21 | all-reduce | flops 32 | bytes 256 | tf_op jit(solution)/shard_map/psum | solution.py:79
  404.3 0.2 slice_reduce_fusion
  404.7 1.5 convolution_bitcast_fusion.1
  406.2 0.1 fusion.11
  406.4 34.0 %psum.63 = f32[2,16]{0,1:T(8,128)S(1)} all-reduce(f32[2,16]{0,1:T(8,128)S(1)} %copy.162), channel_id=1, replica_groups=mesh['sx'=4,'sy'=2,'g1'=2,'bhi'=8,'g2'=4] {'bhi'}, use_global_device_ids=true, to_apply=%region_23.24 | all-reduce | flops 32 | bytes 256 | tf_op jit(solution)/shard_map/psum | solution.py:79
  441.0 14.7 %all_to_all.20 = f32[8,2,2]{2,1,0:T(2,128)S(1)} all-to-all(f32[8,2,2]{2,1,0:T(2,128)S(1)} %copy.165), channel_id=1, replica_groups=mesh['sx'=4,'sy'=2,'g1'=2,'bhi'=8,'g2'=4] {'sx','sy'}, dimensions={0} | all-to-all | bytes 256 | tf_op jit(solution)/shard_map/all_to_all | solution.py:100
  455.7 0.6 squeeze.169
  456.3 0.6 squeeze.170
  (128 shorter events, 4.0 us)
Async XLA Ops:
  7.2 17.4 %copy-start = (bf16[16,16384]{1,0:T(8,128)(2,1)S(1)}, bf16[16,16384]{1,0:T(8,128)(2,1)}, u32[]{:S(2)}) copy-start(bf16[16,16384]{1,0:T(8,128)(2,1)} %param.6) | copy-start | bytes 1572868
  7.2 40.9 %all-gather.7.cloned.1.call-start = ((), (), s32[]{:S(2)}) async-start(), calls=%async_computation.3 | async-start | bytes 1310720 | tf_op jit(solution)/shard_map/all_gather | solution.py:46
  19.0 13.0 %all-to-all-start = ((s32[8,1,2]{2,1,0:T(1,128)}), s32[8,1,2]{2,1,0:T(1,128)S(1)}, u32[]{:S(2)}, u32[]{:S(2)}) async-start(s32[8,1,2]{2,1,0:T(1,128)} %bitcast.4), calls=%async_computation | async-start | bytes 8192 | tf_op jit(solution)/shard_map/all_to_all | solution.py:48
  24.6 74.2 %all-gather.9.cloned.1.call-start = ((), (), s32[]{:S(2)}) async-start(), calls=%async_computation.4 | async-start | bytes 1179648 | tf_op jit(solution)/shard_map/all_gather | solution.py:70
  49.8 110.8 %all-gather.11.cloned.1.call-start = ((), (), s32[]{:S(2)}) async-start(), calls=%async_computation.5 | async-start | bytes 2359296 | tf_op jit(solution)/shard_map/all_gather | solution.py:70
  51.8 195.8 %all-gather.13.cloned.1.call-start = ((), (), s32[]{:S(2)}) async-start(), calls=%async_computation.6 | async-start | bytes 2359296 | tf_op jit(solution)/shard_map/all_gather | solution.py:70
  52.6 276.8 %all-gather.15.cloned.1.call-start = ((), (), s32[]{:S(2)}) async-start(), calls=%async_computation.7 | async-start | bytes 2359296 | tf_op jit(solution)/shard_map/all_gather | solution.py:70
  53.4 351.3 %all-gather.17.cloned.1.call-start = ((), (), s32[]{:S(2)}) async-start(), calls=%async_computation.8 | async-start | bytes 1179648 | tf_op jit(solution)/shard_map/all_gather | solution.py:70
  136.6 9.8 %collective-permute-start = (f32[16,2,128]{2,0,1:T(8,128)S(1)}, f32[16,2,128]{2,0,1:T(8,128)S(1)}, u32[]{:S(2)}, u32[]{:S(2)}) collective-permute-start(f32[16,2,128]{2,0,1:T(8,128)S(1)} %maximum_select_fusion), channel_id=1, source_target_pairs={{0,4},{4,8},{8,12},{12,16},{16,20},{20,24},{24,28},{28,0},{1,5},{5... | collective-permute-start | bytes 49160 | tf_op jit(solution)/shard_map/ppermute | solution.py:83
  160.6 49.6 %copy-start.3 = (bf16[2,2,16,128,128]{4,3,1,2,0:T(8,128)(2,1)S(1)}, bf16[2,2,16,128,128]{4,3,1,2,0:T(8,128)(2,1)}, u32[]{:S(2)}) copy-start(bf16[2,2,16,128,128]{4,3,1,2,0:T(8,128)(2,1)} %all-gather.11.cloned.1.call-done) | copy-start | bytes 6291460
  162.6 47.5 %collective-permute-start.1 = (f32[16,2,128]{2,0,1:T(8,128)S(1)}, f32[16,2,128]{2,0,1:T(8,128)S(1)}, u32[]{:S(2)}, u32[]{:S(2)}) collective-permute-start(f32[16,2,128]{2,0,1:T(8,128)S(1)} %maximum_select_fusion.1), channel_id=1, source_target_pairs={{0,4},{4,8},{8,12},{12,16},{16,20},{20,24},{24,28},{28,0},{1,5},{5... | collective-permute-start | bytes 49160 | tf_op jit(solution)/shard_map/ppermute | solution.py:83
  210.8 36.6 %collective-permute-start.2 = (f32[16,2,128]{2,0,1:T(8,128)S(1)}, f32[16,2,128]{2,0,1:T(8,128)S(1)}, u32[]{:S(2)}, u32[]{:S(2)}) collective-permute-start(f32[16,2,128]{2,0,1:T(8,128)S(1)} %maximum_select_fusion.2), channel_id=1, source_target_pairs={{0,4},{4,8},{8,12},{12,16},{16,20},{20,24},{24,28},{28,0},{1,5},{5... | collective-permute-start | bytes 49160 | tf_op jit(solution)/shard_map/ppermute | solution.py:83
  247.6 46.9 %copy-start.2 = (bf16[2,2,16,128,128]{4,3,1,2,0:T(8,128)(2,1)S(1)}, bf16[2,2,16,128,128]{4,3,1,2,0:T(8,128)(2,1)}, u32[]{:S(2)}) copy-start(bf16[2,2,16,128,128]{4,3,1,2,0:T(8,128)(2,1)} %all-gather.13.cloned.1.call-done) | copy-start | bytes 6291460
  249.6 44.7 %collective-permute-start.3 = (f32[16,2,128]{2,0,1:T(8,128)S(1)}, f32[16,2,128]{2,0,1:T(8,128)S(1)}, u32[]{:S(2)}, u32[]{:S(2)}) collective-permute-start(f32[16,2,128]{2,0,1:T(8,128)S(1)} %maximum_select_fusion.3), channel_id=1, source_target_pairs={{0,4},{4,8},{8,12},{12,16},{16,20},{20,24},{24,28},{28,0},{1,5},{5... | collective-permute-start | bytes 49160 | tf_op jit(solution)/shard_map/ppermute | solution.py:83
  295.1 34.2 %collective-permute-start.4 = (f32[16,2,128]{2,0,1:T(8,128)S(1)}, f32[16,2,128]{2,0,1:T(8,128)S(1)}, u32[]{:S(2)}, u32[]{:S(2)}) collective-permute-start(f32[16,2,128]{2,0,1:T(8,128)S(1)} %maximum_select_fusion.4), channel_id=1, source_target_pairs={{0,4},{4,8},{8,12},{12,16},{16,20},{20,24},{24,28},{28,0},{1,5},{5... | collective-permute-start | bytes 49160 | tf_op jit(solution)/shard_map/ppermute | solution.py:83
  329.4 39.1 %copy-start.1 = (bf16[2,2,16,128,128]{4,3,1,2,0:T(8,128)(2,1)S(1)}, bf16[2,2,16,128,128]{4,3,1,2,0:T(8,128)(2,1)}, u32[]{:S(2)}) copy-start(bf16[2,2,16,128,128]{4,3,1,2,0:T(8,128)(2,1)} %all-gather.15.cloned.1.call-done) | copy-start | bytes 6291460
  331.4 36.9 %collective-permute-start.5 = (f32[16,2,128]{2,0,1:T(8,128)S(1)}, f32[16,2,128]{2,0,1:T(8,128)S(1)}, u32[]{:S(2)}, u32[]{:S(2)}) collective-permute-start(f32[16,2,128]{2,0,1:T(8,128)S(1)} %maximum_select_fusion.5), channel_id=1, source_target_pairs={{0,4},{4,8},{8,12},{12,16},{16,20},{20,24},{24,28},{28,0},{1,5},{5... | collective-permute-start | bytes 49160 | tf_op jit(solution)/shard_map/ppermute | solution.py:83
  368.9 35.5 %collective-permute-start.6 = (f32[16,2,128]{2,0,1:T(8,128)S(1)}, f32[16,2,128]{2,0,1:T(8,128)S(1)}, u32[]{:S(2)}, u32[]{:S(2)}) collective-permute-start(f32[16,2,128]{2,0,1:T(8,128)S(1)} %maximum_select_fusion.6), channel_id=1, source_target_pairs={{0,4},{4,8},{8,12},{12,16},{16,20},{20,24},{24,28},{28,0},{1,5},{5... | collective-permute-start | bytes 49160 | tf_op jit(solution)/shard_map/ppermute | solution.py:83
Sparse Core Ops, SparseCore 0:
  16.7 31.3 all-gather.6
  50.2 48.4 all-gather.8
  100.9 59.6 all-gather.10
  162.6 64.7 all-gather.12
  229.3 67.0 all-gather.14
  298.4 57.9 all-gather.16

commit v15 on v11

--- a/solution.py
+++ b/solution.py
@@ -48,13 +48,14 @@
     row_bits = jnp.transpose(pieces).astype(left.dtype)
 
     rows = lax.dynamic_slice_in_dim(left, sect * pick, pick, 0)
-    ordered = charge_order(labels, rows, block).reshape(pick, n_hi, mine * block)
-    tagged = jnp.broadcast_to(row_bits[:, None, :], (pick, n_hi, sites))
-    spread = lax.all_to_all(jnp.concatenate([ordered, tagged], axis=2), "bhi", 1, 1, tiled=False)
+    ordered = charge_order(labels, rows, block).reshape(pick, width)
+    tagged = jnp.concatenate([ordered, row_bits], axis=1)
+    spread = lax.all_gather(tagged, "bhi", axis=0, tiled=False)
     count_rows = n_hi * pick
-    spread = jnp.transpose(spread, (1, 0, 2)).reshape(count_rows, mine * block + sites)
-    state = spread[:, : mine * block].reshape(count_rows, mine, block).astype(jnp.float32)
-    carried_bits = jnp.transpose(spread[:, mine * block :])
+    spread = spread.reshape(count_rows, width + sites)
+    state = lax.dynamic_slice_in_dim(spread, bhi * mine * block, mine * block, 1)
+    state = state.reshape(count_rows, mine, block).astype(jnp.float32)
+    carried_bits = jnp.transpose(spread[:, width:])
 
     total = jnp.zeros((count_rows,), jnp.float32)
     shift = [(q, (q + 1) % n_hi) for q in range(n_hi)]

time: 308 us -> 317 us (1.029)
  blocking collectives: 154 us -> 188 us
  starting transfers between devices: 59.7 us -> 45.8 us
  waiting for transfers between devices: 54.8 us -> 43.6 us
    all_gather x0 -> x1, blocking collectives: none -> 33.3 us  [body(): spread = lax.all_gather(tagged, 'bhi', axis=0, tiled=False)]
    all_to_all x1 -> x0, starting transfers between devices: 12.6 us -> none  [body(): lax.all_to_all(jnp.concatenate([ordered, tagged], axis=2), 'bhi', 1, 1, t...]
    all_to_all x1 -> x0, waiting for transfers between devices: 11.3 us -> none  [body(): lax.all_to_all(jnp.concatenate([ordered, tagged], axis=2), 'bhi', 1, 1, t...]
  transfers between devices with their start and end apart: 15 -> 14, of which waited for: 4 -> 3; matrix products, arithmetic and copies ran while one was open for 6% -> 6% of each run, Pallas kernels for 0% -> 0%
where the time goes in v15:
time: 317 us
  blocking collectives  188 us (59%)
  starting transfers between devices  45.8 us (14%)
  waiting for transfers between devices  43.6 us (14%)
  between operations  14.8 us (5%)
  local copies, waits for them, and re-layouts  11.3 us (4%)
  matrix products  9 us (3%)
  other arithmetic  3.55 us (1%)
    psum x8, blocking collectives, body(): norms = lax.psum(part, 'bhi')  136 us
    ppermute x7, starting transfers between devices, body(): came = lax.ppermute(rise[:, mine - 1], 'bhi', shift)  39.8 us
    all_gather x1, waiting for transfers between devices, body(): slabs = lax.all_gather(slabs, 'sx', axis=0, tiled=True)  34.1 us
    all_gather x1, blocking collectives, body(): spread = lax.all_gather(tagged, 'bhi', axis=0, tiled=False)  33.3 us
    all_to_all x1, blocking collectives, body(): back = lax.all_to_all(result, SECT, 0, 0, tiled=False)  10.1 us
    all_gather x1, blocking collectives, body(): slabs = lax.all_gather(tensors[0], 'sy', axis=0, tiled=False)  9.28 us
    dot_general x8, matrix products, site_images(): jnp.einsum('rck,bckl->brcl', parts, weights, preferred_element_type=jnp.f...  8.8 us
    all_to_all x1, waiting for transfers between devices, body(): lax.all_to_all(bits[0].reshape(n_sect, pick), SECT, 0, 0, tiled=False)  6.93 us
  transfers between devices with their start and end apart: 14, of which 3 were waited for; matrix products, arithmetic and copies ran while one was open for 6% of the time, Pallas kernels for 0%

profile of v15, /device:TPU:64, one launch (start us, length us, event | category | flops | bytes accessed | tf_op | source)
XLA Modules:
  0.0 316.6 jit_solution(9443128284229524408)
XLA Ops:
  7.2 9.3 %all_gather.29 = bf16[2,2,2,128,128]{4,3,2,1,0:T(8,128)(2,1)} all-gather(bf16[1,2,2,128,128]{4,3,2,1,0:T(8,128)(2,1)} %param.7), channel_id=1, replica_groups=mesh['sx'=4,'sy'=2,'bhi'=8,'blo'=8] {'sy'}, dimensions={0}, use_global_device_ids=true | all-gather | bytes 393216 | tf_op jit(solution)/shard_map/all_gather | solution.py:44
  16.6 34.1 %all-gather.9.cloned.1.call-done = bf16[8,2,2,128,128]{4,3,2,1,0:T(8,128)(2,1)} async-done(((bf16[2,2,2,128,128]{4,3,2,1,0:T(8,128)(2,1)}), bf16[8,2,2,128,128]{4,3,2,1,0:T(8,128)(2,1)}) %all-gather.9.cloned.1.call-update) | async-done | bytes 1048592 | tf_op jit(solution)/shard_map/all_gather | solution.py:45
  50.6 1.0 fusion.56
  51.6 0.7 copy.113
  52.4 1.2 fusion.57
  53.5 0.7 copy.146
  54.4 0.7 copy.149
  55.2 0.7 copy.152
  55.9 0.5 broadcast.257
  56.4 0.7 reduce.55
  57.1 0.7 all_to_all.9
  57.8 5.8 %all-to-all-start = ((s32[8,1,2]{2,1,0:T(1,128)}), s32[8,1,2]{2,1,0:T(1,128)S(1)}, u32[]{:S(2)}, u32[]{:S(2)}) async-start(s32[8,1,2]{2,1,0:T(1,128)} %bitcast.2), calls=%async_computation | async-start | bytes 8192 | tf_op jit(solution)/shard_map/all_to_all | solution.py:47
  63.7 0.2 fusion
  63.9 0.1 copy.108
  64.1 6.9 %all-to-all-done = s32[8,1,2]{2,1,0:T(1,128)S(1)} async-done(((s32[8,1,2]{2,1,0:T(1,128)}), s32[8,1,2]{2,1,0:T(1,128)S(1)}, u32[]{:S(2)}, u32[]{:S(2)}) %all-to-all-start) | async-done | bytes 96 | tf_op jit(solution)/shard_map/all_to_all | solution.py:47
  71.2 33.3 %all-gather.1 = bf16[8,2,16392]{2,1,0:T(2,128)(2,1)S(1)} all-gather(bf16[1,2,16392]{2,1,0:T(2,128)(2,1)S(1)} %maximum_bitcast_fusion.16), channel_id=2, replica_groups=mesh['sx'=4,'sy'=2,'bhi'=8,'blo'=8] {'bhi'}, dimensions={0}, use_global_device_ids=true | all-gather | bytes 590112 | tf_op jit(solution)/shard_map/all_gather | solution.py:53
  104.5 0.4 reshape.189
  104.9 0.3 fusion.47
  105.2 0.1 reduce-precision_convert_fusion.7
  105.3 0.7 copy.131
  106.0 1.5 convolution_bitcast_fusion.7
  107.6 0.1 multiply_reduce_fusion.13
  107.8 18.3 %psum.56 = f32[2,16]{0,1:T(8,128)S(1)} all-reduce(f32[2,16]{0,1:T(8,128)S(1)} %copy.115), channel_id=1, replica_groups=mesh['sx'=4,'sy'=2,'bhi'=8,'blo'=8] {'bhi'}, use_global_device_ids=true, to_apply=%region_2.0 | all-reduce | flops 32 | bytes 256 | tf_op jit(solution)/shard_map/psum | solution.py:76
  126.1 0.2 slice_reduce_fusion.12
  126.3 4.0 %collective-permute-start = (f32[16,128]{1,0:T(8,128)S(1)}, f32[16,128]{1,0:T(8,128)S(1)}, u32[]{:S(2)}, u32[]{:S(2)}) collective-permute-start(f32[16,128]{1,0:T(8,128)S(1)} %slice_bitcast_fusion.32), channel_id=1, source_target_pairs={{0,8},{8,16},{16,24},{24,32},{32,40},{40,48},{48,56},{56,0},{1,9},... | collective-permute-start | bytes 24584 | tf_op jit(solution)/shard_map/ppermute | solution.py:77
  130.4 2.4 collective-permute-done
  133.0 1.6 convolution_bitcast_fusion.6
  134.7 0.1 multiply_reduce_fusion.11
  134.8 5.2 %collective-permute-start.1 = (f32[16,128]{1,0:T(8,128)S(1)}, f32[16,128]{1,0:T(8,128)S(1)}, u32[]{:S(2)}, u32[]{:S(2)}) collective-permute-start(f32[16,128]{1,0:T(8,128)S(1)} %slice_bitcast_fusion.31), channel_id=1, source_target_pairs={{0,8},{8,16},{16,24},{24,32},{32,40},{40,48},{48,56},{56,0},{1,9},... | collective-permute-start | bytes 24584 | tf_op jit(solution)/shard_map/ppermute | solution.py:77
  140.1 16.2 %psum.57 = f32[2,16]{0,1:T(8,128)S(1)} all-reduce(f32[2,16]{0,1:T(8,128)S(1)} %copy.118), channel_id=1, replica_groups=mesh['sx'=4,'sy'=2,'bhi'=8,'blo'=8] {'bhi'}, use_global_device_ids=true, to_apply=%region_5.6 | all-reduce | flops 32 | bytes 256 | tf_op jit(solution)/shard_map/psum | solution.py:76
  156.3 0.2 slice_reduce_fusion.10
  156.7 0.3 convolution_bitcast_fusion.5
  157.0 0.1 multiply_reduce_fusion.9
  157.1 6.2 %collective-permute-start.2 = (f32[16,128]{1,0:T(8,128)S(1)}, f32[16,128]{1,0:T(8,128)S(1)}, u32[]{:S(2)}, u32[]{:S(2)}) collective-permute-start(f32[16,128]{1,0:T(8,128)S(1)} %slice_bitcast_fusion.30), channel_id=1, source_target_pairs={{0,8},{8,16},{16,24},{24,32},{32,40},{40,48},{48,56},{56,0},{1,9},... | collective-permute-start | bytes 24584 | tf_op jit(solution)/shard_map/ppermute | solution.py:77
  163.5 16.2 %psum.58 = f32[2,16]{0,1:T(8,128)S(1)} all-reduce(f32[2,16]{0,1:T(8,128)S(1)} %copy.120), channel_id=1, replica_groups=mesh['sx'=4,'sy'=2,'bhi'=8,'blo'=8] {'bhi'}, use_global_device_ids=true, to_apply=%region_8.9 | all-reduce | flops 32 | bytes 256 | tf_op jit(solution)/shard_map/psum | solution.py:76
  179.7 0.2 slice_reduce_fusion.8
  180.1 1.7 convolution_bitcast_fusion.4
  181.8 0.1 multiply_reduce_fusion.7
  182.0 6.2 %collective-permute-start.3 = (f32[16,128]{1,0:T(8,128)S(1)}, f32[16,128]{1,0:T(8,128)S(1)}, u32[]{:S(2)}, u32[]{:S(2)}) collective-permute-start(f32[16,128]{1,0:T(8,128)S(1)} %slice_bitcast_fusion.29), channel_id=1, source_target_pairs={{0,8},{8,16},{16,24},{24,32},{32,40},{40,48},{48,56},{56,0},{1,9},... | collective-permute-start | bytes 24584 | tf_op jit(solution)/shard_map/ppermute | solution.py:77
  188.2 16.2 %psum.59 = f32[2,16]{0,1:T(8,128)S(1)} all-reduce(f32[2,16]{0,1:T(8,128)S(1)} %copy.123), channel_id=1, replica_groups=mesh['sx'=4,'sy'=2,'bhi'=8,'blo'=8] {'bhi'}, use_global_device_ids=true, to_apply=%region_11.12 | all-reduce | flops 32 | bytes 256 | tf_op jit(solution)/shard_map/psum | solution.py:76
  204.5 0.2 slice_reduce_fusion.6
  204.8 0.3 convolution_bitcast_fusion.3
  205.1 0.1 multiply_reduce_fusion.5
  205.3 6.0 %collective-permute-start.4 = (f32[16,128]{1,0:T(8,128)S(1)}, f32[16,128]{1,0:T(8,128)S(1)}, u32[]{:S(2)}, u32[]{:S(2)}) collective-permute-start(f32[16,128]{1,0:T(8,128)S(1)} %slice_bitcast_fusion.28), channel_id=1, source_target_pairs={{0,8},{8,16},{16,24},{24,32},{32,40},{40,48},{48,56},{56,0},{1,9},... | collective-permute-start | bytes 24584 | tf_op jit(solution)/shard_map/ppermute | solution.py:77
  211.4 16.2 %psum.60 = f32[2,16]{0,1:T(8,128)S(1)} all-reduce(f32[2,16]{0,1:T(8,128)S(1)} %copy.125), channel_id=1, replica_groups=mesh['sx'=4,'sy'=2,'bhi'=8,'blo'=8] {'bhi'}, use_global_device_ids=true, to_apply=%region_14.15 | all-reduce | flops 32 | bytes 256 | tf_op jit(solution)/shard_map/psum | solution.py:76
  227.6 0.2 slice_reduce_fusion.4
  227.9 1.6 convolution_bitcast_fusion.2
  229.6 0.1 multiply_reduce_fusion.3
  229.8 6.1 %collective-permute-start.5 = (f32[16,128]{1,0:T(8,128)S(1)}, f32[16,128]{1,0:T(8,128)S(1)}, u32[]{:S(2)}, u32[]{:S(2)}) collective-permute-start(f32[16,128]{1,0:T(8,128)S(1)} %slice_bitcast_fusion.27), channel_id=1, source_target_pairs={{0,8},{8,16},{16,24},{24,32},{32,40},{40,48},{48,56},{56,0},{1,9},... | collective-permute-start | bytes 24584 | tf_op jit(solution)/shard_map/ppermute | solution.py:77
  236.0 16.2 %psum.61 = f32[2,16]{0,1:T(8,128)S(1)} all-reduce(f32[2,16]{0,1:T(8,128)S(1)} %copy.128), channel_id=1, replica_groups=mesh['sx'=4,'sy'=2,'bhi'=8,'blo'=8] {'bhi'}, use_global_device_ids=true, to_apply=%region_17.18 | all-reduce | flops 32 | bytes 256 | tf_op jit(solution)/shard_map/psum | solution.py:76
  252.1 0.2 slice_reduce_fusion.2
  252.5 0.3 convolution_bitcast_fusion.1
  252.8 6.1 %collective-permute-start.6 = (f32[16,128]{1,0:T(8,128)S(1)}, f32[16,128]{1,0:T(8,128)S(1)}, u32[]{:S(2)}, u32[]{:S(2)}) collective-permute-start(f32[16,128]{1,0:T(8,128)S(1)} %slice_bitcast_fusion.26), channel_id=1, source_target_pairs={{0,8},{8,16},{16,24},{24,32},{32,40},{40,48},{48,56},{56,0},{1,9},... | collective-permute-start | bytes 24584 | tf_op jit(solution)/shard_map/ppermute | solution.py:77
  258.9 0.1 multiply_reduce_fusion.1
  259.1 16.2 %psum.62 = f32[2,16]{0,1:T(8,128)S(1)} all-reduce(f32[2,16]{0,1:T(8,128)S(1)} %copy.130), channel_id=1, replica_groups=mesh['sx'=4,'sy'=2,'bhi'=8,'blo'=8] {'bhi'}, use_global_device_ids=true, to_apply=%region_20.21 | all-reduce | flops 32 | bytes 256 | tf_op jit(solution)/shard_map/psum | solution.py:76
  275.4 0.2 slice_reduce_fusion
  275.6 0.1 reduce-precision_convert_fusion
  275.7 1.5 convolution_bitcast_fusion
  277.3 0.1 fusion.12
  277.5 20.4 %psum.63 = f32[2,16]{0,1:T(8,128)S(1)} all-reduce(f32[2,16]{0,1:T(8,128)S(1)} %copy.132), channel_id=1, replica_groups=mesh['sx'=4,'sy'=2,'bhi'=8,'blo'=8] {'bhi'}, use_global_device_ids=true, to_apply=%region_23.24 | all-reduce | flops 32 | bytes 256 | tf_op jit(solution)/shard_map/psum | solution.py:76
  297.9 0.1 log_add_fusion
  298.4 10.1 %all_to_all.14 = f32[8,2,2]{2,1,0:T(2,128)S(1)} all-to-all(f32[8,2,2]{2,1,0:T(2,128)S(1)} %copy.135), channel_id=1, replica_groups=mesh['sx'=4,'sy'=2,'bhi'=8,'blo'=8] {'sx','sy'}, dimensions={0} | all-to-all | bytes 256 | tf_op jit(solution)/shard_map/all_to_all | solution.py:93
  308.5 0.6 squeeze.190
  309.1 0.6 squeeze.191
  (107 shorter events, 3.1 us)
Async XLA Ops:
  7.2 56.4 %copy-start = (bf16[16,16384]{1,0:T(8,128)(2,1)S(1)}, bf16[16,16384]{1,0:T(8,128)(2,1)}, u32[]{:S(2)}) copy-start(bf16[16,16384]{1,0:T(8,128)(2,1)} %param.6) | copy-start | bytes 1572868
  7.2 43.5 %all-gather.9.cloned.1.call-start = ((), (), s32[]{:S(2)}) async-start(), calls=%async_computation.2 | async-start | bytes 1310720 | tf_op jit(solution)/shard_map/all_gather | solution.py:45
  16.5 89.5 %all-gather.11.cloned.1.call-start = ((), (), s32[]{:S(2)}) async-start(), calls=%async_computation.3 | async-start | bytes 1179648 | tf_op jit(solution)/shard_map/all_gather | solution.py:67
  52.3 4.1 %copy-start.5 = (s32[1,16]{1,0:T(1,128)S(1)}, s32[1,16]{1,0:T(1,128)}, u32[]{:S(2)}) copy-start(s32[1,16]{1,0:T(1,128)} %param.4) | copy-start | bytes 196
  52.3 11.4 %copy-start.4 = (s32[128]{0:T(128)S(1)}, s32[128]{0:T(128)}, u32[]{:S(2)}) copy-start(s32[128]{0:T(128)} %param.5) | copy-start | bytes 1540
  52.3 80.6 %all-gather.13.cloned.1.call-start = ((), (), s32[]{:S(2)}) async-start(), calls=%async_computation.4 | async-start | bytes 2359296 | tf_op jit(solution)/shard_map/all_gather | solution.py:67
  54.3 125.7 %all-gather.15.cloned.1.call-start = ((), (), s32[]{:S(2)}) async-start(), calls=%async_computation.5 | async-start | bytes 2359296 | tf_op jit(solution)/shard_map/all_gather | solution.py:67
  55.1 172.8 %all-gather.17.cloned.1.call-start = ((), (), s32[]{:S(2)}) async-start(), calls=%async_computation.6 | async-start | bytes 2359296 | tf_op jit(solution)/shard_map/all_gather | solution.py:67
  57.8 13.3 %all-to-all-start = ((s32[8,1,2]{2,1,0:T(1,128)}), s32[8,1,2]{2,1,0:T(1,128)S(1)}, u32[]{:S(2)}, u32[]{:S(2)}) async-start(s32[8,1,2]{2,1,0:T(1,128)} %bitcast.2), calls=%async_computation | async-start | bytes 8192 | tf_op jit(solution)/shard_map/all_to_all | solution.py:47
  63.5 212.2 %all-gather.19.cloned.1.call-start = ((), (), s32[]{:S(2)}) async-start(), calls=%async_computation.7 | async-start | bytes 1179648 | tf_op jit(solution)/shard_map/all_gather | solution.py:67
  126.3 6.5 %collective-permute-start = (f32[16,128]{1,0:T(8,128)S(1)}, f32[16,128]{1,0:T(8,128)S(1)}, u32[]{:S(2)}, u32[]{:S(2)}) collective-permute-start(f32[16,128]{1,0:T(8,128)S(1)} %slice_bitcast_fusion.32), channel_id=1, source_target_pairs={{0,8},{8,16},{16,24},{24,32},{32,40},{40,48},{48,56},{56,0},{1,9},... | collective-permute-start | bytes 24584 | tf_op jit(solution)/shard_map/ppermute | solution.py:77
  132.9 23.7 %copy-start.3 = (bf16[2,2,16,128,128]{4,3,1,2,0:T(8,128)(2,1)S(1)}, bf16[2,2,16,128,128]{4,3,1,2,0:T(8,128)(2,1)}, u32[]{:S(2)}) copy-start(bf16[2,2,16,128,128]{4,3,1,2,0:T(8,128)(2,1)} %all-gather.13.cloned.1.call-done) | copy-start | bytes 6291460
  134.8 21.7 %collective-permute-start.1 = (f32[16,128]{1,0:T(8,128)S(1)}, f32[16,128]{1,0:T(8,128)S(1)}, u32[]{:S(2)}, u32[]{:S(2)}) collective-permute-start(f32[16,128]{1,0:T(8,128)S(1)} %slice_bitcast_fusion.31), channel_id=1, source_target_pairs={{0,8},{8,16},{16,24},{24,32},{32,40},{40,48},{48,56},{56,0},{1,9},... | collective-permute-start | bytes 24584 | tf_op jit(solution)/shard_map/ppermute | solution.py:77
  157.1 22.8 %collective-permute-start.2 = (f32[16,128]{1,0:T(8,128)S(1)}, f32[16,128]{1,0:T(8,128)S(1)}, u32[]{:S(2)}, u32[]{:S(2)}) collective-permute-start(f32[16,128]{1,0:T(8,128)S(1)} %slice_bitcast_fusion.30), channel_id=1, source_target_pairs={{0,8},{8,16},{16,24},{24,32},{32,40},{40,48},{48,56},{56,0},{1,9},... | collective-permute-start | bytes 24584 | tf_op jit(solution)/shard_map/ppermute | solution.py:77
  180.1 24.7 %copy-start.2 = (bf16[2,2,16,128,128]{4,3,1,2,0:T(8,128)(2,1)S(1)}, bf16[2,2,16,128,128]{4,3,1,2,0:T(8,128)(2,1)}, u32[]{:S(2)}) copy-start(bf16[2,2,16,128,128]{4,3,1,2,0:T(8,128)(2,1)} %all-gather.15.cloned.1.call-done) | copy-start | bytes 6291460
  182.0 22.7 %collective-permute-start.3 = (f32[16,128]{1,0:T(8,128)S(1)}, f32[16,128]{1,0:T(8,128)S(1)}, u32[]{:S(2)}, u32[]{:S(2)}) collective-permute-start(f32[16,128]{1,0:T(8,128)S(1)} %slice_bitcast_fusion.29), channel_id=1, source_target_pairs={{0,8},{8,16},{16,24},{24,32},{32,40},{40,48},{48,56},{56,0},{1,9},... | collective-permute-start | bytes 24584 | tf_op jit(solution)/shard_map/ppermute | solution.py:77
  205.3 22.5 %collective-permute-start.4 = (f32[16,128]{1,0:T(8,128)S(1)}, f32[16,128]{1,0:T(8,128)S(1)}, u32[]{:S(2)}, u32[]{:S(2)}) collective-permute-start(f32[16,128]{1,0:T(8,128)S(1)} %slice_bitcast_fusion.28), channel_id=1, source_target_pairs={{0,8},{8,16},{16,24},{24,32},{32,40},{40,48},{48,56},{56,0},{1,9},... | collective-permute-start | bytes 24584 | tf_op jit(solution)/shard_map/ppermute | solution.py:77
  227.9 24.5 %copy-start.1 = (bf16[2,2,16,128,128]{4,3,1,2,0:T(8,128)(2,1)S(1)}, bf16[2,2,16,128,128]{4,3,1,2,0:T(8,128)(2,1)}, u32[]{:S(2)}) copy-start(bf16[2,2,16,128,128]{4,3,1,2,0:T(8,128)(2,1)} %all-gather.17.cloned.1.call-done) | copy-start | bytes 6291460
  229.8 22.5 %collective-permute-start.5 = (f32[16,128]{1,0:T(8,128)S(1)}, f32[16,128]{1,0:T(8,128)S(1)}, u32[]{:S(2)}, u32[]{:S(2)}) collective-permute-start(f32[16,128]{1,0:T(8,128)S(1)} %slice_bitcast_fusion.27), channel_id=1, source_target_pairs={{0,8},{8,16},{16,24},{24,32},{32,40},{40,48},{48,56},{56,0},{1,9},... | collective-permute-start | bytes 24584 | tf_op jit(solution)/shard_map/ppermute | solution.py:77
  252.8 22.8 %collective-permute-start.6 = (f32[16,128]{1,0:T(8,128)S(1)}, f32[16,128]{1,0:T(8,128)S(1)}, u32[]{:S(2)}, u32[]{:S(2)}) collective-permute-start(f32[16,128]{1,0:T(8,128)S(1)} %slice_bitcast_fusion.26), channel_id=1, source_target_pairs={{0,8},{8,16},{16,24},{24,32},{32,40},{40,48},{48,56},{56,0},{1,9},... | collective-permute-start | bytes 24584 | tf_op jit(solution)/shard_map/ppermute | solution.py:77
Sparse Core Ops, SparseCore 0:
  16.7 33.9 all-gather.8
  52.8 31.6 all-gather.10
  86.7 32.6 all-gather.12
  121.4 32.5 all-gather.14
  156.0 32.8 all-gather.16
  190.9 30.2 all-gather.18

commit v16 on v10

--- a/solution.py
+++ b/solution.py
@@ -44,17 +44,18 @@
     slabs = lax.all_gather(tensors[0], "sy", axis=0, tiled=False)
     slabs = lax.all_gather(slabs, "sx", axis=0, tiled=True)
 
-    pieces = lax.all_to_all(bits[0].reshape(n_sect, pick), SECT, 0, 0, tiled=False)
-    row_bits = jnp.transpose(pieces).astype(left.dtype)
-
     rows = lax.dynamic_slice_in_dim(left, sect * pick, pick, 0)
     ordered = charge_order(labels, rows, block).reshape(pick, n_hi, mine * block)
-    tagged = jnp.broadcast_to(row_bits[:, None, :], (pick, n_hi, sites))
-    spread = lax.all_to_all(jnp.concatenate([ordered, tagged], axis=2), "bhi", 1, 1, tiled=False)
+    spread = lax.all_to_all(ordered, "bhi", 1, 1, tiled=False)
     count_rows = n_hi * pick
-    spread = jnp.transpose(spread, (1, 0, 2)).reshape(count_rows, mine * block + sites)
-    state = spread[:, : mine * block].reshape(count_rows, mine, block).astype(jnp.float32)
-    carried_bits = jnp.transpose(spread[:, mine * block :])
+    state = jnp.transpose(spread, (1, 0, 2)).reshape(count_rows, mine, block).astype(jnp.float32)
+
+    first_slab, state, late_bits = lax.optimization_barrier((slabs[0:1], state, bits))
+    pieces = lax.all_to_all(late_bits[0].reshape(n_sect, pick), SECT, 0, 0, tiled=False)
+    row_bits = pieces.reshape(1, sites * pick)
+    row_bits = jnp.broadcast_to(row_bits, (n_hi, sites * pick))
+    carried_bits = lax.all_to_all(row_bits, "bhi", 0, 0, tiled=False).reshape(n_hi, sites, pick)
+    carried_bits = jnp.transpose(carried_bits, (1, 0, 2)).reshape(sites, count_rows)
 
     total = jnp.zeros((count_rows,), jnp.float32)
     shift = [(q, (q + 1) % n_hi) for q in range(n_hi)]
@@ -62,7 +63,6 @@
     logs = []
     batches = [[0]] + [list(range(k, min(k + 2, sites))) for k in range(1, sites, 2)]
     gathered = {}
-    first_slab, state = lax.optimization_barrier((slabs[0:1], state))
     for batch in batches:
         piece = first_slab if batch == [0] else slabs[batch[0] : batch[-1] + 1]
         got = lax.all_gather(piece, "blo", axis=2, tiled=True)

time: 307 us -> 304 us (level)
  the two profiles are of different devices: /device:TPU:64 before, /device:TPU:2 now
where the time goes in v16:
time: 304 us; the launch traced here: 302 us
  blocking collectives  201 us (66%)
  starting transfers between devices  36.9 us (12%)
  waiting for transfers between devices  25.2 us (8%)
  between operations  14.8 us (5%)
  local copies, waits for them, and re-layouts  11.6 us (4%)
  matrix products  9.62 us (3%)
  other arithmetic  3.77 us (1%)
    psum x8, blocking collectives, body(): norms = lax.psum(part, 'bhi')  152 us
    all_to_all x1, blocking collectives, body(): spread = lax.all_to_all(ordered, 'bhi', 1, 1, tiled=False)  28.4 us
    ppermute x7, starting transfers between devices, body(): came = lax.ppermute(rise[:, mine - 1], 'bhi', shift)  16.9 us
    all_to_all x1, starting transfers between devices, body(): lax.all_to_all(row_bits, 'bhi', 0, 0, tiled=False)  12.2 us
    all_to_all x1, waiting for transfers between devices, body(): lax.all_to_all(row_bits, 'bhi', 0, 0, tiled=False)  11.7 us
    all_to_all x1, blocking collectives, body(): back = lax.all_to_all(result, SECT, 0, 0, tiled=False)  10.6 us
    all_gather x1, blocking collectives, body(): slabs = lax.all_gather(tensors[0], 'sy', axis=0, tiled=False)  9.28 us
    dot_general x8, matrix products, site_images(): jnp.einsum('rck,bckl->brcl', parts, weights, preferred_element_type=jnp.f...  8.77 us
  transfers between devices with their start and end apart: 15, of which 4 were waited for; matrix products, arithmetic and copies ran while one was open for 6% of the time, Pallas kernels for 0%

profile of v16, /device:TPU:2, one launch (start us, length us, event | category | flops | bytes accessed | tf_op | source)
XLA Modules:
  0.0 302.4 jit_solution(7585402370580309476)
XLA Ops:
  7.2 9.3 %all_gather.21 = bf16[2,2,2,128,128]{4,3,2,1,0:T(8,128)(2,1)} all-gather(bf16[1,2,2,128,128]{4,3,2,1,0:T(8,128)(2,1)} %param.7), channel_id=1, replica_groups=mesh['sx'=4,'sy'=2,'bhi'=8,'blo'=8] {'sy'}, dimensions={0}, use_global_device_ids=true | all-gather | bytes 393216 | tf_op jit(solution)/shard_map/all_gather | solution.py:44
  16.7 0.8 fusion
  17.5 0.1 copy.58
  17.8 28.4 %all_to_all.25 = bf16[2,8,2048]{2,0,1:T(2,128)(2,1)S(1)} all-to-all(bf16[2,8,2048]{2,0,1:T(2,128)(2,1)S(1)} %copy.59), channel_id=1, replica_groups=mesh['sx'=4,'sy'=2,'bhi'=8,'blo'=8] {'bhi'}, dimensions={1} | all-to-all | bytes 131072 | tf_op jit(solution)/shard_map/all_to_all | solution.py:49
  46.3 0.1 reshape.344
  46.4 3.7 %all-gather.7.cloned.1.call-done = bf16[8,2,2,128,128]{4,3,2,1,0:T(8,128)(2,1)} async-done(((bf16[2,2,2,128,128]{4,3,2,1,0:T(8,128)(2,1)}), bf16[8,2,2,128,128]{4,3,2,1,0:T(8,128)(2,1)}) %all-gather.7.cloned.1.call-update) | async-done | bytes 1048592 | tf_op jit(solution)/shard_map/all_gather | solution.py:45
  50.1 1.0 fusion.71
  51.1 0.7 copy.63
  51.8 1.2 fusion.70
  53.0 0.7 copy.102
  53.8 0.7 copy.105
  54.6 0.7 copy.108
  55.4 0.5 broadcast.271
  55.9 0.7 reduce.16
  56.6 0.7 all_to_all.17
  57.2 7.6 %all-to-all-start.1 = ((s32[8,1,2]{2,1,0:T(1,128)}), s32[8,1,2]{2,1,0:T(1,128)S(1)}, u32[]{:S(2)}, u32[]{:S(2)}) async-start(s32[8,1,2]{2,1,0:T(1,128)} %bitcast.3), calls=%async_computation.1 | async-start | bytes 8192 | tf_op jit(solution)/shard_map/all_to_all | solution.py:54
  64.8 6.2 %all-to-all-done.1 = s32[8,1,2]{2,1,0:T(1,128)S(1)} async-done(((s32[8,1,2]{2,1,0:T(1,128)}), s32[8,1,2]{2,1,0:T(1,128)S(1)}, u32[]{:S(2)}, u32[]{:S(2)}) %all-to-all-start.1) | async-done | bytes 96 | tf_op jit(solution)/shard_map/all_to_all | solution.py:54
  71.0 0.7 reduce.17
  71.8 0.6 broadcast_in_dim.83
  72.4 12.2 %all-to-all-start.2 = ((s32[8,1,16]{2,1,0:T(1,128)}), s32[8,1,16]{2,1,0:T(1,128)S(1)}, u32[]{:S(2)}, u32[]{:S(2)}) async-start(s32[8,1,16]{2,1,0:T(1,128)} %broadcast_in_dim.83), calls=%async_computation.2 | async-start | bytes 8192 | tf_op jit(solution)/shard_map/all_to_all | solution.py:57
  84.6 0.7 copy.90
  85.3 11.7 %all-to-all-done.2 = s32[8,1,16]{2,1,0:T(1,128)S(1)} async-done(((s32[8,1,16]{2,1,0:T(1,128)}), s32[8,1,16]{2,1,0:T(1,128)S(1)}, u32[]{:S(2)}, u32[]{:S(2)}) %all-to-all-start.2) | async-done | bytes 544 | tf_op jit(solution)/shard_map/all_to_all | solution.py:57
  97.7 0.1 copy.71
  99.3 1.5 convolution_bitcast_fusion
  100.8 0.1 multiply_reduce_fusion.13
  101.0 16.6 %psum.56 = f32[2,16]{1,0:T(2,128)S(1)} all-reduce(f32[2,16]{1,0:T(2,128)S(1)} %pad_maximum_fusion), channel_id=1, replica_groups=mesh['sx'=4,'sy'=2,'bhi'=8,'blo'=8] {'bhi'}, use_global_device_ids=true, to_apply=%region_2.0 | all-reduce | flops 32 | bytes 256 | tf_op jit(solution)/shard_map/psum | solution.py:77
  117.6 4.2 %collective-permute-start = (f32[16,128]{1,0:T(8,128)S(1)}, f32[16,128]{1,0:T(8,128)S(1)}, u32[]{:S(2)}, u32[]{:S(2)}) collective-permute-start(f32[16,128]{1,0:T(8,128)S(1)} %slice_bitcast_fusion.32), channel_id=1, source_target_pairs={{0,8},{8,16},{16,24},{24,32},{32,40},{40,48},{48,56},{56,0},{1,9},... | collective-permute-start | bytes 24584 | tf_op jit(solution)/shard_map/ppermute | solution.py:78
  121.9 3.4 %collective-permute-done = f32[16,128]{1,0:T(8,128)S(1)} collective-permute-done((f32[16,128]{1,0:T(8,128)S(1)}, f32[16,128]{1,0:T(8,128)S(1)}, u32[]{:S(2)}, u32[]{:S(2)}) %collective-permute-start) | collective-permute-done | bytes 8224 | tf_op jit(solution)/shard_map/ppermute | solution.py:78
  125.4 1.6 convolution_bitcast_fusion.7
  127.1 0.1 multiply_reduce_fusion.11
  127.2 3.1 %collective-permute-start.1 = (f32[16,128]{1,0:T(8,128)S(1)}, f32[16,128]{1,0:T(8,128)S(1)}, u32[]{:S(2)}, u32[]{:S(2)}) collective-permute-start(f32[16,128]{1,0:T(8,128)S(1)} %slice_bitcast_fusion.31), channel_id=1, source_target_pairs={{0,8},{8,16},{16,24},{24,32},{32,40},{40,48},{48,56},{56,0},{1,9},... | collective-permute-start | bytes 24584 | tf_op jit(solution)/shard_map/ppermute | solution.py:78
  130.3 19.1 %psum.57 = f32[2,16]{1,0:T(2,128)S(1)} all-reduce(f32[2,16]{1,0:T(2,128)S(1)} %pad_maximum_fusion.1), channel_id=1, replica_groups=mesh['sx'=4,'sy'=2,'bhi'=8,'blo'=8] {'bhi'}, use_global_device_ids=true, to_apply=%region_5.6 | all-reduce | flops 32 | bytes 256 | tf_op jit(solution)/shard_map/psum | solution.py:77
  149.4 0.1 reduce-precision_convert_fusion.5
  149.6 0.3 convolution_bitcast_fusion.6
  149.9 0.1 multiply_reduce_fusion.9
  150.0 1.9 collective-permute-start.2
  152.0 20.1 %psum.58 = f32[2,16]{1,0:T(2,128)S(1)} all-reduce(f32[2,16]{1,0:T(2,128)S(1)} %pad_maximum_fusion.2), channel_id=1, replica_groups=mesh['sx'=4,'sy'=2,'bhi'=8,'blo'=8] {'bhi'}, use_global_device_ids=true, to_apply=%region_8.9 | all-reduce | flops 32 | bytes 256 | tf_op jit(solution)/shard_map/psum | solution.py:77
  172.1 0.1 reduce-precision_convert_fusion.4
  172.2 1.6 convolution_bitcast_fusion.5
  174.0 0.1 multiply_reduce_fusion.7
  174.1 1.9 collective-permute-start.3
  176.0 20.2 %psum.59 = f32[2,16]{1,0:T(2,128)S(1)} all-reduce(f32[2,16]{1,0:T(2,128)S(1)} %pad_maximum_fusion.3), channel_id=1, replica_groups=mesh['sx'=4,'sy'=2,'bhi'=8,'blo'=8] {'bhi'}, use_global_device_ids=true, to_apply=%region_11.12 | all-reduce | flops 32 | bytes 256 | tf_op jit(solution)/shard_map/psum | solution.py:77
  196.3 0.1 reduce-precision_convert_fusion.3
  196.4 0.3 convolution_bitcast_fusion.4
  196.7 0.1 multiply_reduce_fusion.5
  196.9 1.9 collective-permute-start.4
  198.8 20.2 %psum.60 = f32[2,16]{1,0:T(2,128)S(1)} all-reduce(f32[2,16]{1,0:T(2,128)S(1)} %pad_maximum_fusion.4), channel_id=1, replica_groups=mesh['sx'=4,'sy'=2,'bhi'=8,'blo'=8] {'bhi'}, use_global_device_ids=true, to_apply=%region_14.15 | all-reduce | flops 32 | bytes 256 | tf_op jit(solution)/shard_map/psum | solution.py:77
  219.0 0.1 reduce-precision_convert_fusion.2
  219.2 1.7 convolution_bitcast_fusion.3
  220.9 0.1 multiply_reduce_fusion.3
  221.0 1.9 collective-permute-start.5
  223.0 20.1 %psum.61 = f32[2,16]{1,0:T(2,128)S(1)} all-reduce(f32[2,16]{1,0:T(2,128)S(1)} %pad_maximum_fusion.5), channel_id=1, replica_groups=mesh['sx'=4,'sy'=2,'bhi'=8,'blo'=8] {'bhi'}, use_global_device_ids=true, to_apply=%region_17.18 | all-reduce | flops 32 | bytes 256 | tf_op jit(solution)/shard_map/psum | solution.py:77
  243.1 0.1 reduce-precision_convert_fusion.1
  243.2 0.3 convolution_bitcast_fusion.2
  243.6 1.9 collective-permute-start.6
  245.5 0.1 multiply_reduce_fusion.1
  245.6 20.1 %psum.62 = f32[2,16]{1,0:T(2,128)S(1)} all-reduce(f32[2,16]{1,0:T(2,128)S(1)} %pad_maximum_fusion.6), channel_id=1, replica_groups=mesh['sx'=4,'sy'=2,'bhi'=8,'blo'=8] {'bhi'}, use_global_device_ids=true, to_apply=%region_20.21 | all-reduce | flops 32 | bytes 256 | tf_op jit(solution)/shard_map/psum | solution.py:77
  265.7 0.1 reduce-precision_convert_fusion
  265.9 1.5 convolution_bitcast_fusion.1
  267.4 0.1 fusion.12
  267.6 16.0 %psum.63 = f32[2,16]{1,0:T(2,128)S(1)} all-reduce(f32[2,16]{1,0:T(2,128)S(1)} %pad_maximum_fusion.7), channel_id=1, replica_groups=mesh['sx'=4,'sy'=2,'bhi'=8,'blo'=8] {'bhi'}, use_global_device_ids=true, to_apply=%region_23.24 | all-reduce | flops 32 | bytes 256 | tf_op jit(solution)/shard_map/psum | solution.py:77
  283.7 10.6 %all_to_all.26 = f32[8,2,2]{2,1,0:T(2,128)S(1)} all-to-all(f32[8,2,2]{2,1,0:T(2,128)S(1)} %copy.91), channel_id=1, replica_groups=mesh['sx'=4,'sy'=2,'bhi'=8,'blo'=8] {'sx','sy'}, dimensions={0} | all-to-all | bytes 256 | tf_op jit(solution)/shard_map/all_to_all | solution.py:94
  294.3 0.6 squeeze.190
  294.9 0.6 squeeze.191
  (115 shorter events, 3.9 us)
Async XLA Ops:
  7.2 9.4 %copy-start = (bf16[16,16384]{1,0:T(8,128)(2,1)S(1)}, bf16[16,16384]{1,0:T(8,128)(2,1)}, u32[]{:S(2)}) copy-start(bf16[16,16384]{1,0:T(8,128)(2,1)} %param.6) | copy-start | bytes 1572868
  7.2 42.9 %all-gather.7.cloned.1.call-start = ((), (), s32[]{:S(2)}) async-start(), calls=%async_computation.4 | async-start | bytes 1310720 | tf_op jit(solution)/shard_map/all_gather | solution.py:45
  16.5 82.7 %all-gather.9.cloned.1.call-start = ((), (), s32[]{:S(2)}) async-start(), calls=%async_computation.5 | async-start | bytes 1179648 | tf_op jit(solution)/shard_map/all_gather | solution.py:68
  51.8 4.1 %copy-start.4 = (s32[1,16]{1,0:T(1,128)S(1)}, s32[1,16]{1,0:T(1,128)}, u32[]{:S(2)}) copy-start(s32[1,16]{1,0:T(1,128)} %param.4) | copy-start | bytes 196
  51.8 73.6 %all-gather.11.cloned.1.call-start = ((), (), s32[]{:S(2)}) async-start(), calls=%async_computation.6 | async-start | bytes 2359296 | tf_op jit(solution)/shard_map/all_gather | solution.py:68
  53.8 118.4 %all-gather.13.cloned.1.call-start = ((), (), s32[]{:S(2)}) async-start(), calls=%async_computation.7 | async-start | bytes 2359296 | tf_op jit(solution)/shard_map/all_gather | solution.py:68
  54.6 164.6 %all-gather.15.cloned.1.call-start = ((), (), s32[]{:S(2)}) async-start(), calls=%async_computation.8 | async-start | bytes 2359296 | tf_op jit(solution)/shard_map/all_gather | solution.py:68
  57.2 13.8 %all-to-all-start.1 = ((s32[8,1,2]{2,1,0:T(1,128)}), s32[8,1,2]{2,1,0:T(1,128)S(1)}, u32[]{:S(2)}, u32[]{:S(2)}) async-start(s32[8,1,2]{2,1,0:T(1,128)} %bitcast.3), calls=%async_computation.1 | async-start | bytes 8192 | tf_op jit(solution)/shard_map/all_to_all | solution.py:54
  72.4 24.7 %all-to-all-start.2 = ((s32[8,1,16]{2,1,0:T(1,128)}), s32[8,1,16]{2,1,0:T(1,128)S(1)}, u32[]{:S(2)}, u32[]{:S(2)}) async-start(s32[8,1,16]{2,1,0:T(1,128)} %broadcast_in_dim.83), calls=%async_computation.2 | async-start | bytes 8192 | tf_op jit(solution)/shard_map/all_to_all | solution.py:57
  84.5 181.3 %all-gather.17.cloned.1.call-start = ((), (), s32[]{:S(2)}) async-start(), calls=%async_computation.9 | async-start | bytes 1179648 | tf_op jit(solution)/shard_map/all_gather | solution.py:68
  117.6 7.6 %collective-permute-start = (f32[16,128]{1,0:T(8,128)S(1)}, f32[16,128]{1,0:T(8,128)S(1)}, u32[]{:S(2)}, u32[]{:S(2)}) collective-permute-start(f32[16,128]{1,0:T(8,128)S(1)} %slice_bitcast_fusion.32), channel_id=1, source_target_pairs={{0,8},{8,16},{16,24},{24,32},{32,40},{40,48},{48,56},{56,0},{1,9},... | collective-permute-start | bytes 24584 | tf_op jit(solution)/shard_map/ppermute | solution.py:78
  125.4 24.2 %copy-start.3 = (bf16[2,2,16,128,128]{4,3,1,2,0:T(8,128)(2,1)S(1)}, bf16[2,2,16,128,128]{4,3,1,2,0:T(8,128)(2,1)}, u32[]{:S(2)}) copy-start(bf16[2,2,16,128,128]{4,3,1,2,0:T(8,128)(2,1)} %all-gather.11.cloned.1.call-done) | copy-start | bytes 6291460
  127.2 22.2 %collective-permute-start.1 = (f32[16,128]{1,0:T(8,128)S(1)}, f32[16,128]{1,0:T(8,128)S(1)}, u32[]{:S(2)}, u32[]{:S(2)}) collective-permute-start(f32[16,128]{1,0:T(8,128)S(1)} %slice_bitcast_fusion.31), channel_id=1, source_target_pairs={{0,8},{8,16},{16,24},{24,32},{32,40},{40,48},{48,56},{56,0},{1,9},... | collective-permute-start | bytes 24584 | tf_op jit(solution)/shard_map/ppermute | solution.py:78
  150.0 22.0 %collective-permute-start.2 = (f32[16,128]{1,0:T(8,128)S(1)}, f32[16,128]{1,0:T(8,128)S(1)}, u32[]{:S(2)}, u32[]{:S(2)}) collective-permute-start(f32[16,128]{1,0:T(8,128)S(1)} %slice_bitcast_fusion.30), channel_id=1, source_target_pairs={{0,8},{8,16},{16,24},{24,32},{32,40},{40,48},{48,56},{56,0},{1,9},... | collective-permute-start | bytes 24584 | tf_op jit(solution)/shard_map/ppermute | solution.py:78
  172.2 24.1 %copy-start.2 = (bf16[2,2,16,128,128]{4,3,1,2,0:T(8,128)(2,1)S(1)}, bf16[2,2,16,128,128]{4,3,1,2,0:T(8,128)(2,1)}, u32[]{:S(2)}) copy-start(bf16[2,2,16,128,128]{4,3,1,2,0:T(8,128)(2,1)} %all-gather.13.cloned.1.call-done) | copy-start | bytes 6291460
  174.1 22.2 %collective-permute-start.3 = (f32[16,128]{1,0:T(8,128)S(1)}, f32[16,128]{1,0:T(8,128)S(1)}, u32[]{:S(2)}, u32[]{:S(2)}) collective-permute-start(f32[16,128]{1,0:T(8,128)S(1)} %slice_bitcast_fusion.29), channel_id=1, source_target_pairs={{0,8},{8,16},{16,24},{24,32},{32,40},{40,48},{48,56},{56,0},{1,9},... | collective-permute-start | bytes 24584 | tf_op jit(solution)/shard_map/ppermute | solution.py:78
  196.9 22.2 %collective-permute-start.4 = (f32[16,128]{1,0:T(8,128)S(1)}, f32[16,128]{1,0:T(8,128)S(1)}, u32[]{:S(2)}, u32[]{:S(2)}) collective-permute-start(f32[16,128]{1,0:T(8,128)S(1)} %slice_bitcast_fusion.28), channel_id=1, source_target_pairs={{0,8},{8,16},{16,24},{24,32},{32,40},{40,48},{48,56},{56,0},{1,9},... | collective-permute-start | bytes 24584 | tf_op jit(solution)/shard_map/ppermute | solution.py:78
  219.2 24.0 %copy-start.1 = (bf16[2,2,16,128,128]{4,3,1,2,0:T(8,128)(2,1)S(1)}, bf16[2,2,16,128,128]{4,3,1,2,0:T(8,128)(2,1)}, u32[]{:S(2)}) copy-start(bf16[2,2,16,128,128]{4,3,1,2,0:T(8,128)(2,1)} %all-gather.15.cloned.1.call-done) | copy-start | bytes 6291460
  221.0 22.1 %collective-permute-start.5 = (f32[16,128]{1,0:T(8,128)S(1)}, f32[16,128]{1,0:T(8,128)S(1)}, u32[]{:S(2)}, u32[]{:S(2)}) collective-permute-start(f32[16,128]{1,0:T(8,128)S(1)} %slice_bitcast_fusion.27), channel_id=1, source_target_pairs={{0,8},{8,16},{16,24},{24,32},{32,40},{40,48},{48,56},{56,0},{1,9},... | collective-permute-start | bytes 24584 | tf_op jit(solution)/shard_map/ppermute | solution.py:78
  243.6 22.2 %collective-permute-start.6 = (f32[16,128]{1,0:T(8,128)S(1)}, f32[16,128]{1,0:T(8,128)S(1)}, u32[]{:S(2)}, u32[]{:S(2)}) collective-permute-start(f32[16,128]{1,0:T(8,128)S(1)} %slice_bitcast_fusion.26), channel_id=1, source_target_pairs={{0,8},{8,16},{16,24},{24,32},{32,40},{40,48},{48,56},{56,0},{1,9},... | collective-permute-start | bytes 24584 | tf_op jit(solution)/shard_map/ppermute | solution.py:78
Sparse Core Ops, SparseCore 0:
  16.7 33.4 all-gather.6
  52.3 31.1 all-gather.8
  85.6 33.0 all-gather.10
  120.7 33.0 all-gather.12
  155.8 33.0 all-gather.14
  190.9 30.5 all-gather.16

commit v17 on v16

--- a/solution.py
+++ b/solution.py
@@ -91,7 +91,10 @@
 
     result = jnp.stack([jnp.stack(probs), jnp.stack(logs)], axis=1)
     result = lax.dynamic_slice_in_dim(result, bhi * pick, pick, 2)
-    back = lax.all_to_all(result, SECT, 0, 0, tiled=False)
+    n_x = lax.axis_size("sx")
+    back = result.reshape(n_x, n_sect // n_x, 2, pick)
+    back = lax.all_to_all(back, "sy", 1, 1, tiled=False)
+    back = lax.all_to_all(back, "sx", 0, 0, tiled=False).reshape(n_sect, 2, pick)
     out = jnp.transpose(back, (1, 0, 2)).reshape(2, bits.shape[0], n_sect * pick)
     return (out[0], out[1])
 

time: 304 us -> 309 us (1.016)
  blocking collectives: 201 us -> 205 us
    all_to_all x1 -> x2, blocking collectives: 10.6 us -> 15.2 us  [the longest x1 7.61 us: body(): back = lax.all_to_all(back, 'sy', 1, 1, tiled=False)]
where the time goes in v17:
time: 309 us; the launch traced here: 307 us
  blocking collectives  205 us (66%)
  starting transfers between devices  36.9 us (12%)
  waiting for transfers between devices  25.2 us (8%)
  between operations  14.8 us (5%)
  local copies, waits for them, and re-layouts  12.1 us (4%)
  matrix products  9.62 us (3%)
  other arithmetic  3.77 us (1%)
    psum x8, blocking collectives, body(): norms = lax.psum(part, 'bhi')  152 us
    all_to_all x1, blocking collectives, body(): spread = lax.all_to_all(ordered, 'bhi', 1, 1, tiled=False)  28.4 us
    ppermute x7, starting transfers between devices, body(): came = lax.ppermute(rise[:, mine - 1], 'bhi', shift)  16.9 us
    all_to_all x1, starting transfers between devices, body(): lax.all_to_all(row_bits, 'bhi', 0, 0, tiled=False)  12.2 us
    all_to_all x1, waiting for transfers between devices, body(): lax.all_to_all(row_bits, 'bhi', 0, 0, tiled=False)  11.7 us
    all_gather x1, blocking collectives, body(): slabs = lax.all_gather(tensors[0], 'sy', axis=0, tiled=False)  9.28 us
    dot_general x8, matrix products, site_images(): jnp.einsum('rck,bckl->brcl', parts, weights, preferred_element_type=jnp.f...  8.77 us
    all_to_all x1, blocking collectives, body(): back = lax.all_to_all(back, 'sy', 1, 1, tiled=False)  7.61 us
  transfers between devices with their start and end apart: 15, of which 4 were waited for; matrix products, arithmetic and copies ran while one was open for 6% of the time, Pallas kernels for 0%

profile of v17, /device:TPU:2, one launch (start us, length us, event | category | flops | bytes accessed | tf_op | source)
XLA Modules:
  0.0 307.4 jit_solution(15426584001289474532)
XLA Ops:
  7.2 9.3 %all_gather.21 = bf16[2,2,2,128,128]{4,3,2,1,0:T(8,128)(2,1)} all-gather(bf16[1,2,2,128,128]{4,3,2,1,0:T(8,128)(2,1)} %param.7), channel_id=1, replica_groups=mesh['sx'=4,'sy'=2,'bhi'=8,'blo'=8] {'sy'}, dimensions={0}, use_global_device_ids=true | all-gather | bytes 393216 | tf_op jit(solution)/shard_map/all_gather | solution.py:44
  16.7 0.8 fusion
  17.5 0.1 copy.64
  17.8 28.4 %all_to_all.30 = bf16[2,8,2048]{2,0,1:T(2,128)(2,1)S(1)} all-to-all(bf16[2,8,2048]{2,0,1:T(2,128)(2,1)S(1)} %copy.65), channel_id=1, replica_groups=mesh['sx'=4,'sy'=2,'bhi'=8,'blo'=8] {'bhi'}, dimensions={1} | all-to-all | bytes 131072 | tf_op jit(solution)/shard_map/all_to_all | solution.py:49
  46.3 0.1 reshape.352
  46.4 3.7 %all-gather.7.cloned.1.call-done = bf16[8,2,2,128,128]{4,3,2,1,0:T(8,128)(2,1)} async-done(((bf16[2,2,2,128,128]{4,3,2,1,0:T(8,128)(2,1)}), bf16[8,2,2,128,128]{4,3,2,1,0:T(8,128)(2,1)}) %all-gather.7.cloned.1.call-update) | async-done | bytes 1048592 | tf_op jit(solution)/shard_map/all_gather | solution.py:45
  50.1 1.0 fusion.71
  51.1 0.7 copy.69
  51.8 1.2 fusion.70
  53.0 0.7 copy.115
  53.8 0.7 copy.118
  54.6 0.7 copy.121
  55.4 0.5 broadcast.265
  55.9 0.7 reduce.8
  56.6 0.7 all_to_all.20
  57.2 7.6 %all-to-all-start.1 = ((s32[8,1,2]{2,1,0:T(1,128)}), s32[8,1,2]{2,1,0:T(1,128)S(1)}, u32[]{:S(2)}, u32[]{:S(2)}) async-start(s32[8,1,2]{2,1,0:T(1,128)} %bitcast.3), calls=%async_computation.1 | async-start | bytes 8192 | tf_op jit(solution)/shard_map/all_to_all | solution.py:54
  64.8 6.2 %all-to-all-done.1 = s32[8,1,2]{2,1,0:T(1,128)S(1)} async-done(((s32[8,1,2]{2,1,0:T(1,128)}), s32[8,1,2]{2,1,0:T(1,128)S(1)}, u32[]{:S(2)}, u32[]{:S(2)}) %all-to-all-start.1) | async-done | bytes 96 | tf_op jit(solution)/shard_map/all_to_all | solution.py:54
  71.0 0.7 reduce.9
  71.8 0.6 broadcast_in_dim.83
  72.4 12.2 %all-to-all-start.2 = ((s32[8,1,16]{2,1,0:T(1,128)}), s32[8,1,16]{2,1,0:T(1,128)S(1)}, u32[]{:S(2)}, u32[]{:S(2)}) async-start(s32[8,1,16]{2,1,0:T(1,128)} %broadcast_in_dim.83), calls=%async_computation.2 | async-start | bytes 8192 | tf_op jit(solution)/shard_map/all_to_all | solution.py:57
  84.6 0.7 copy.96
  85.3 11.7 %all-to-all-done.2 = s32[8,1,16]{2,1,0:T(1,128)S(1)} async-done(((s32[8,1,16]{2,1,0:T(1,128)}), s32[8,1,16]{2,1,0:T(1,128)S(1)}, u32[]{:S(2)}, u32[]{:S(2)}) %all-to-all-start.2) | async-done | bytes 544 | tf_op jit(solution)/shard_map/all_to_all | solution.py:57
  99.3 1.5 convolution_bitcast_fusion
  100.8 0.1 multiply_reduce_fusion.13
  101.0 16.6 %psum.56 = f32[2,16]{1,0:T(2,128)S(1)} all-reduce(f32[2,16]{1,0:T(2,128)S(1)} %pad_maximum_fusion), channel_id=1, replica_groups=mesh['sx'=4,'sy'=2,'bhi'=8,'blo'=8] {'bhi'}, use_global_device_ids=true, to_apply=%region_2.0 | all-reduce | flops 32 | bytes 256 | tf_op jit(solution)/shard_map/psum | solution.py:77
  117.6 4.2 %collective-permute-start = (f32[16,128]{1,0:T(8,128)S(1)}, f32[16,128]{1,0:T(8,128)S(1)}, u32[]{:S(2)}, u32[]{:S(2)}) collective-permute-start(f32[16,128]{1,0:T(8,128)S(1)} %slice_bitcast_fusion.32), channel_id=1, source_target_pairs={{0,8},{8,16},{16,24},{24,32},{32,40},{40,48},{48,56},{56,0},{1,9},... | collective-permute-start | bytes 24584 | tf_op jit(solution)/shard_map/ppermute | solution.py:78
  121.9 3.4 %collective-permute-done = f32[16,128]{1,0:T(8,128)S(1)} collective-permute-done((f32[16,128]{1,0:T(8,128)S(1)}, f32[16,128]{1,0:T(8,128)S(1)}, u32[]{:S(2)}, u32[]{:S(2)}) %collective-permute-start) | collective-permute-done | bytes 8224 | tf_op jit(solution)/shard_map/ppermute | solution.py:78
  125.4 1.6 convolution_bitcast_fusion.7
  127.1 0.1 multiply_reduce_fusion.11
  127.2 3.1 collective-permute-start.1
  130.3 19.1 %psum.57 = f32[2,16]{1,0:T(2,128)S(1)} all-reduce(f32[2,16]{1,0:T(2,128)S(1)} %pad_maximum_fusion.1), channel_id=1, replica_groups=mesh['sx'=4,'sy'=2,'bhi'=8,'blo'=8] {'bhi'}, use_global_device_ids=true, to_apply=%region_5.6 | all-reduce | flops 32 | bytes 256 | tf_op jit(solution)/shard_map/psum | solution.py:77
  149.4 0.1 reduce-precision_convert_fusion.5
  149.6 0.3 convolution_bitcast_fusion.6
  149.9 0.1 multiply_reduce_fusion.9
  150.0 1.9 collective-permute-start.2
  152.0 20.1 %psum.58 = f32[2,16]{1,0:T(2,128)S(1)} all-reduce(f32[2,16]{1,0:T(2,128)S(1)} %pad_maximum_fusion.2), channel_id=1, replica_groups=mesh['sx'=4,'sy'=2,'bhi'=8,'blo'=8] {'bhi'}, use_global_device_ids=true, to_apply=%region_8.9 | all-reduce | flops 32 | bytes 256 | tf_op jit(solution)/shard_map/psum | solution.py:77
  172.1 0.1 reduce-precision_convert_fusion.4
  172.2 1.6 convolution_bitcast_fusion.5
  174.0 0.1 multiply_reduce_fusion.7
  174.1 1.9 collective-permute-start.3
  176.0 20.2 %psum.59 = f32[2,16]{1,0:T(2,128)S(1)} all-reduce(f32[2,16]{1,0:T(2,128)S(1)} %pad_maximum_fusion.3), channel_id=1, replica_groups=mesh['sx'=4,'sy'=2,'bhi'=8,'blo'=8] {'bhi'}, use_global_device_ids=true, to_apply=%region_11.12 | all-reduce | flops 32 | bytes 256 | tf_op jit(solution)/shard_map/psum | solution.py:77
  196.4 0.3 convolution_bitcast_fusion.4
  196.7 0.1 multiply_reduce_fusion.5
  196.9 1.9 collective-permute-start.4
  198.8 20.2 %psum.60 = f32[2,16]{1,0:T(2,128)S(1)} all-reduce(f32[2,16]{1,0:T(2,128)S(1)} %pad_maximum_fusion.4), channel_id=1, replica_groups=mesh['sx'=4,'sy'=2,'bhi'=8,'blo'=8] {'bhi'}, use_global_device_ids=true, to_apply=%region_14.15 | all-reduce | flops 32 | bytes 256 | tf_op jit(solution)/shard_map/psum | solution.py:77
  219.0 0.1 reduce-precision_convert_fusion.2
  219.2 1.7 convolution_bitcast_fusion.3
  220.9 0.1 multiply_reduce_fusion.3
  221.0 1.9 collective-permute-start.5
  223.0 20.1 %psum.61 = f32[2,16]{1,0:T(2,128)S(1)} all-reduce(f32[2,16]{1,0:T(2,128)S(1)} %pad_maximum_fusion.5), channel_id=1, replica_groups=mesh['sx'=4,'sy'=2,'bhi'=8,'blo'=8] {'bhi'}, use_global_device_ids=true, to_apply=%region_17.18 | all-reduce | flops 32 | bytes 256 | tf_op jit(solution)/shard_map/psum | solution.py:77
  243.1 0.1 reduce-precision_convert_fusion.1
  243.2 0.3 convolution_bitcast_fusion.2
  243.6 1.9 collective-permute-start.6
  245.5 0.1 multiply_reduce_fusion.1
  245.6 20.1 %psum.62 = f32[2,16]{1,0:T(2,128)S(1)} all-reduce(f32[2,16]{1,0:T(2,128)S(1)} %pad_maximum_fusion.6), channel_id=1, replica_groups=mesh['sx'=4,'sy'=2,'bhi'=8,'blo'=8] {'bhi'}, use_global_device_ids=true, to_apply=%region_20.21 | all-reduce | flops 32 | bytes 256 | tf_op jit(solution)/shard_map/psum | solution.py:77
  265.9 1.5 convolution_bitcast_fusion.1
  267.4 0.1 fusion.12
  267.6 16.0 %psum.63 = f32[2,16]{1,0:T(2,128)S(1)} all-reduce(f32[2,16]{1,0:T(2,128)S(1)} %pad_maximum_fusion.7), channel_id=1, replica_groups=mesh['sx'=4,'sy'=2,'bhi'=8,'blo'=8] {'bhi'}, use_global_device_ids=true, to_apply=%region_23.24 | all-reduce | flops 32 | bytes 256 | tf_op jit(solution)/shard_map/psum | solution.py:77
  283.7 0.1 copy.98
  283.8 7.6 %all_to_all.31 = f32[4,2,2,2]{0,3,2,1:T(2,128)S(1)} all-to-all(f32[4,2,2,2]{0,3,2,1:T(2,128)S(1)} %copy.98), channel_id=1, replica_groups=mesh['sx'=4,'sy'=2,'bhi'=8,'blo'=8] {'sy'}, dimensions={1} | all-to-all | bytes 256 | tf_op jit(solution)/shard_map/all_to_all | solution.py:96
  291.5 0.1 copy.99
  291.6 7.6 %all_to_all.32 = f32[4,2,2,2]{1,3,2,0:T(2,128)S(1)} all-to-all(f32[4,2,2,2]{1,3,2,0:T(2,128)S(1)} %copy.99), channel_id=1, replica_groups=mesh['sx'=4,'sy'=2,'bhi'=8,'blo'=8] {'sx'}, dimensions={0} | all-to-all | bytes 256 | tf_op jit(solution)/shard_map/all_to_all | solution.py:97
  299.3 0.6 squeeze.190
  300.0 0.6 squeeze.191
  (121 shorter events, 4.4 us)
Async XLA Ops:
  7.2 9.4 %copy-start = (bf16[16,16384]{1,0:T(8,128)(2,1)S(1)}, bf16[16,16384]{1,0:T(8,128)(2,1)}, u32[]{:S(2)}) copy-start(bf16[16,16384]{1,0:T(8,128)(2,1)} %param.6) | copy-start | bytes 1572868
  7.2 42.9 %all-gather.7.cloned.1.call-start = ((), (), s32[]{:S(2)}) async-start(), calls=%async_computation.5 | async-start | bytes 1310720 | tf_op jit(solution)/shard_map/all_gather | solution.py:45
  16.5 82.7 %all-gather.9.cloned.1.call-start = ((), (), s32[]{:S(2)}) async-start(), calls=%async_computation.6 | async-start | bytes 1179648 | tf_op jit(solution)/shard_map/all_gather | solution.py:68
  51.8 4.1 %copy-start.4 = (s32[1,16]{1,0:T(1,128)S(1)}, s32[1,16]{1,0:T(1,128)}, u32[]{:S(2)}) copy-start(s32[1,16]{1,0:T(1,128)} %param.4) | copy-start | bytes 196
  51.8 73.6 %all-gather.11.cloned.1.call-start = ((), (), s32[]{:S(2)}) async-start(), calls=%async_computation.7 | async-start | bytes 2359296 | tf_op jit(solution)/shard_map/all_gather | solution.py:68
  53.8 118.4 %all-gather.13.cloned.1.call-start = ((), (), s32[]{:S(2)}) async-start(), calls=%async_computation.8 | async-start | bytes 2359296 | tf_op jit(solution)/shard_map/all_gather | solution.py:68
  54.6 164.6 %all-gather.15.cloned.1.call-start = ((), (), s32[]{:S(2)}) async-start(), calls=%async_computation.9 | async-start | bytes 2359296 | tf_op jit(solution)/shard_map/all_gather | solution.py:68
  57.2 13.8 %all-to-all-start.1 = ((s32[8,1,2]{2,1,0:T(1,128)}), s32[8,1,2]{2,1,0:T(1,128)S(1)}, u32[]{:S(2)}, u32[]{:S(2)}) async-start(s32[8,1,2]{2,1,0:T(1,128)} %bitcast.3), calls=%async_computation.1 | async-start | bytes 8192 | tf_op jit(solution)/shard_map/all_to_all | solution.py:54
  72.4 24.7 %all-to-all-start.2 = ((s32[8,1,16]{2,1,0:T(1,128)}), s32[8,1,16]{2,1,0:T(1,128)S(1)}, u32[]{:S(2)}, u32[]{:S(2)}) async-start(s32[8,1,16]{2,1,0:T(1,128)} %broadcast_in_dim.83), calls=%async_computation.2 | async-start | bytes 8192 | tf_op jit(solution)/shard_map/all_to_all | solution.py:57
  84.5 181.3 %all-gather.17.cloned.1.call-start = ((), (), s32[]{:S(2)}) async-start(), calls=%async_computation.10 | async-start | bytes 1179648 | tf_op jit(solution)/shard_map/all_gather | solution.py:68
  117.6 7.6 %collective-permute-start = (f32[16,128]{1,0:T(8,128)S(1)}, f32[16,128]{1,0:T(8,128)S(1)}, u32[]{:S(2)}, u32[]{:S(2)}) collective-permute-start(f32[16,128]{1,0:T(8,128)S(1)} %slice_bitcast_fusion.32), channel_id=1, source_target_pairs={{0,8},{8,16},{16,24},{24,32},{32,40},{40,48},{48,56},{56,0},{1,9},... | collective-permute-start | bytes 24584 | tf_op jit(solution)/shard_map/ppermute | solution.py:78
  125.4 24.2 %copy-start.3 = (bf16[2,2,16,128,128]{4,3,1,2,0:T(8,128)(2,1)S(1)}, bf16[2,2,16,128,128]{4,3,1,2,0:T(8,128)(2,1)}, u32[]{:S(2)}) copy-start(bf16[2,2,16,128,128]{4,3,1,2,0:T(8,128)(2,1)} %all-gather.11.cloned.1.call-done) | copy-start | bytes 6291460
  127.2 22.2 %collective-permute-start.1 = (f32[16,128]{1,0:T(8,128)S(1)}, f32[16,128]{1,0:T(8,128)S(1)}, u32[]{:S(2)}, u32[]{:S(2)}) collective-permute-start(f32[16,128]{1,0:T(8,128)S(1)} %slice_bitcast_fusion.31), channel_id=1, source_target_pairs={{0,8},{8,16},{16,24},{24,32},{32,40},{40,48},{48,56},{56,0},{1,9},... | collective-permute-start | bytes 24584 | tf_op jit(solution)/shard_map/ppermute | solution.py:78
  150.0 22.0 %collective-permute-start.2 = (f32[16,128]{1,0:T(8,128)S(1)}, f32[16,128]{1,0:T(8,128)S(1)}, u32[]{:S(2)}, u32[]{:S(2)}) collective-permute-start(f32[16,128]{1,0:T(8,128)S(1)} %slice_bitcast_fusion.30), channel_id=1, source_target_pairs={{0,8},{8,16},{16,24},{24,32},{32,40},{40,48},{48,56},{56,0},{1,9},... | collective-permute-start | bytes 24584 | tf_op jit(solution)/shard_map/ppermute | solution.py:78
  172.2 24.1 %copy-start.2 = (bf16[2,2,16,128,128]{4,3,1,2,0:T(8,128)(2,1)S(1)}, bf16[2,2,16,128,128]{4,3,1,2,0:T(8,128)(2,1)}, u32[]{:S(2)}) copy-start(bf16[2,2,16,128,128]{4,3,1,2,0:T(8,128)(2,1)} %all-gather.13.cloned.1.call-done) | copy-start | bytes 6291460
  174.1 22.2 %collective-permute-start.3 = (f32[16,128]{1,0:T(8,128)S(1)}, f32[16,128]{1,0:T(8,128)S(1)}, u32[]{:S(2)}, u32[]{:S(2)}) collective-permute-start(f32[16,128]{1,0:T(8,128)S(1)} %slice_bitcast_fusion.29), channel_id=1, source_target_pairs={{0,8},{8,16},{16,24},{24,32},{32,40},{40,48},{48,56},{56,0},{1,9},... | collective-permute-start | bytes 24584 | tf_op jit(solution)/shard_map/ppermute | solution.py:78
  196.9 22.2 %collective-permute-start.4 = (f32[16,128]{1,0:T(8,128)S(1)}, f32[16,128]{1,0:T(8,128)S(1)}, u32[]{:S(2)}, u32[]{:S(2)}) collective-permute-start(f32[16,128]{1,0:T(8,128)S(1)} %slice_bitcast_fusion.28), channel_id=1, source_target_pairs={{0,8},{8,16},{16,24},{24,32},{32,40},{40,48},{48,56},{56,0},{1,9},... | collective-permute-start | bytes 24584 | tf_op jit(solution)/shard_map/ppermute | solution.py:78
  219.2 24.0 %copy-start.1 = (bf16[2,2,16,128,128]{4,3,1,2,0:T(8,128)(2,1)S(1)}, bf16[2,2,16,128,128]{4,3,1,2,0:T(8,128)(2,1)}, u32[]{:S(2)}) copy-start(bf16[2,2,16,128,128]{4,3,1,2,0:T(8,128)(2,1)} %all-gather.15.cloned.1.call-done) | copy-start | bytes 6291460
  221.0 22.1 %collective-permute-start.5 = (f32[16,128]{1,0:T(8,128)S(1)}, f32[16,128]{1,0:T(8,128)S(1)}, u32[]{:S(2)}, u32[]{:S(2)}) collective-permute-start(f32[16,128]{1,0:T(8,128)S(1)} %slice_bitcast_fusion.27), channel_id=1, source_target_pairs={{0,8},{8,16},{16,24},{24,32},{32,40},{40,48},{48,56},{56,0},{1,9},... | collective-permute-start | bytes 24584 | tf_op jit(solution)/shard_map/ppermute | solution.py:78
  243.6 22.2 %collective-permute-start.6 = (f32[16,128]{1,0:T(8,128)S(1)}, f32[16,128]{1,0:T(8,128)S(1)}, u32[]{:S(2)}, u32[]{:S(2)}) collective-permute-start(f32[16,128]{1,0:T(8,128)S(1)} %slice_bitcast_fusion.26), channel_id=1, source_target_pairs={{0,8},{8,16},{16,24},{24,32},{32,40},{40,48},{48,56},{56,0},{1,9},... | collective-permute-start | bytes 24584 | tf_op jit(solution)/shard_map/ppermute | solution.py:78
Sparse Core Ops, SparseCore 0:
  16.7 33.4 all-gather.6
  52.3 31.1 all-gather.8
  85.6 33.0 all-gather.10
  120.7 33.0 all-gather.12
  155.8 33.0 all-gather.14
  190.9 30.5 all-gather.16
